TPU v7x, 32 devices: a whole 2x2x4 slice. The times are simulated.
32 devices in a mesh: row: 16 (over z, x, core), col: 2 (over y).
Axes of the slice: x: 2, y: 2, z: 4, core: 2. Of those that a mesh axis runs over, the one named last changes fastest.
Arguments:
- slab: float32 [8192, 1024], P('row', 'col'), may hold values from -6 to 6
- leaf_v: float32 [8192, 256], P('row', 'col'), may hold values from -0.25 to 0.25
- leaf_t: float32 [4096, 256], P('row', 'col'), may hold values from -0.1875 to 0.1875
- tree_v: float32 [4096, 256], P('row', 'col'), may hold values from -0.375 to 0.375
- tree_t: float32 [4096, 256], P('row', 'col'), may hold values from -0.1875 to 0.1875
Outputs:
- updated_slab: float32 [8192, 1024], P('row', 'col')
All inputs are finite; a program needn't handle non-finite values.
Results may differ from a plain program's by a relative error of at most 0.0001.
Values sent between devices are 32-bit elements; how exact they have to be, the bound alone decides.
No kernel may reach another device: no remote copies, remote signals or barrier semaphores. Data moves between devices by JAX's collectives and lax.ppermute only.
A program may use at most 64 MiB of HBM per device.

v0:
```python
import jax
import jax.numpy as jnp
from jax import lax
from jax.sharding import PartitionSpec as P


def swapped(array, axis, bit):
    return lax.ppermute(array, axis, [(i, i ^ 1 << bit) for i in range(lax.axis_size(axis))])


def product(left, right):
    return jnp.dot(left, right, precision=lax.Precision.HIGHEST, preferred_element_type=jnp.float32)


def product_left_t(left, right):
    return lax.dot_general(
        left,
        right,
        (((0,), (0,)), ((), ())),
        precision=lax.Precision.HIGHEST,
        preferred_element_type=jnp.float32,
    )


def unit_lower(raw):
    row_ids = lax.broadcasted_iota(jnp.int32, raw.shape, 0)
    col_ids = lax.broadcasted_iota(jnp.int32, raw.shape, 1)
    diagonal = jnp.where(row_ids == col_ids, 1.0, 0.0).astype(raw.dtype)
    return jnp.where(row_ids > col_ids, raw, 0.0) + diagonal


def on_device(slab, leaf_v, leaf_t, tree_v, tree_t):
    leaf_full, leaf_tri = (
        lax.all_gather(leaf_v, "col", axis=1, tiled=True),
        lax.all_gather(leaf_t, "col", axis=1, tiled=True),
    )
    tree_full, tree_tri = (
        lax.all_gather(tree_v, "col", axis=1, tiled=True),
        lax.all_gather(tree_t, "col", axis=1, tiled=True),
    )
    width = leaf_tri.shape[0]
    leaf_vectors = unit_lower(leaf_full)
    leaf_factor = jnp.triu(leaf_tri)
    leaf_w = product_left_t(leaf_factor, product_left_t(leaf_vectors, slab))
    current = slab[:width] - product(leaf_vectors[:width], leaf_w)
    remainder = slab[width:] - product(leaf_vectors[width:], leaf_w)
    tree_vectors = jnp.triu(tree_full)
    tree_factor = jnp.triu(tree_tri)
    position = lax.axis_index("row")
    levels = lax.axis_size("row").bit_length() - 1
    for level in range(levels):
        step = 1 << level
        phase = position % (2 * step)
        is_lower = phase == 0
        is_upper = phase == step
        projected = product_left_t(tree_vectors, current)
        outgoing = jnp.where(is_upper, projected, current)
        received, partner_factor = swapped((outgoing, tree_factor), "row", level)
        merged = jnp.where(is_upper, received + projected, current + received)
        pair_factor = jnp.where(is_upper, tree_factor, partner_factor)
        update = product_left_t(pair_factor, merged)
        raised = current - product(tree_vectors, update)
        lowered = current - update
        current = jnp.where(is_upper, raised, jnp.where(is_lower, lowered, current))
    return jnp.concatenate([current, remainder], axis=0)


def solution(mesh):
    in_specs = (P("row", "col"), P("row", "col"), P("row", "col"), P("row", "col"), P("row", "col"))
    out_specs = P("row", "col")
    return jax.shard_map(
        on_device, mesh=mesh, in_specs=in_specs, out_specs=out_specs, check_vma=False
    )
```

profile of v0, /device:TPU:0, one launch (start us, length us, event | category | flops | bytes accessed | tf_op | source)
XLA Modules:
  0.0 124.4 jit_solution(8653530077791594265)
XLA Ops:
  0.0 10.3 %all_gather.12 = f32[512,256]{1,0:T(8,128)S(1)} all-gather(f32[512,128]{1,0:T(8,128)} %param.6), channel_id=1, replica_groups=mesh['row'=16,'col'=2] {'col'}, dimensions={1}, use_global_device_ids=true | all-gather | bytes 786432 | tf_op jit(solution)/shard_map/all_gather | solution.py:34
  10.4 1.1 fusion.41
  11.5 5.8 %all_gather.13 = f32[256,256]{1,0:T(8,128)S(1)} all-gather(f32[256,128]{1,0:T(8,128)S(1)} %copy-done.4), channel_id=1, replica_groups=mesh['row'=16,'col'=2] {'col'}, dimensions={1}, use_global_device_ids=true | all-gather | bytes 393216 | tf_op jit(solution)/shard_map/all_gather | solution.py:35
  17.3 5.6 %all_gather.14 = f32[256,256]{1,0:T(8,128)S(1)} all-gather(f32[256,128]{1,0:T(8,128)S(1)} %copy-done.5), channel_id=1, replica_groups=mesh['row'=16,'col'=2] {'col'}, dimensions={1}, use_global_device_ids=true | all-gather | bytes 393216 | tf_op jit(solution)/shard_map/all_gather | solution.py:38
  22.9 0.7 fusion.26
  23.6 0.6 convolution_subtract_fusion.5
  24.3 1.5 %broadcast_select_fusion = (f32[256,512]{1,0:T(8,128)}, f32[256,512]{1,0:T(8,128)S(1)}) fusion(f32[256,512]{1,0:T(8,128)S(1)} %convolution_subtract_fusion.5, pred[]{:T(512)S(6)} %eq.35, f32[256,256]{1,0:T(8,128)S(1)} %all_gather.14, s32[256]{0:T(256)S(1)} %iota_add_fusion), kind=kOutput, calls=%fused_computation.46 | convolution fusion | flops 402915328 | bytes 1836033 | tf_op jit(solution)/shard_map/dot_general | solution.py:16
  25.8 6.8 %all_gather.15 = f32[256,256]{1,0:T(8,128)S(1)} all-gather(f32[256,128]{1,0:T(8,128)S(1)} %copy-done.6), channel_id=1, replica_groups=mesh['row'=16,'col'=2] {'col'}, dimensions={1}, use_global_device_ids=true | all-gather | bytes 393216 | tf_op jit(solution)/shard_map/all_gather | solution.py:39
  32.5 0.1 fusion.28
  32.7 1.5 %collective-permute-done = f32[256,256]{1,0:T(8,128)S(1)} collective-permute-done((f32[256,256]{1,0:T(8,128)S(1)}, f32[256,256]{1,0:T(8,128)S(1)}, u32[]{:S(2)}, u32[]{:S(2)}) %collective-permute-start) | collective-permute-done | bytes 262176 | tf_op jit(solution)/shard_map/ppermute | solution.py:8
  34.2 1.7 %fusion.16 = f32[256,512]{1,0:T(8,128)S(1)} fusion(f32[256,512]{1,0:T(8,128)S(1)} %convolution_subtract_fusion.5, f32[256,512]{1,0:T(8,128)} %collective-permute-done.1, f32[256,512]{1,0:T(8,128)S(1)} %get-tuple-element.6, f32[256,256]{1,0:T(8,128)S(1)} %fusion.28, f32[256,256]{1,0:T(8,128)S(1)} %collective-permute-done, pred[]{:T(512)S(6)} %eq.35), kind=kOutput, calls=%fused_computation.27 | convolution fusion | flops 403111936 | bytes 2621441 | tf_op jit(solution)/shard_map/dot_general | solution.py:16
  36.0 0.7 fusion
  36.7 1.5 %broadcast_select_fusion.1 = (f32[256,512]{1,0:T(8,128)}, f32[256,512]{1,0:T(8,128)S(1)}) fusion(f32[256,512]{1,0:T(8,128)S(1)} %fusion, pred[]{:T(512)S(6)} %eq.34, f32[256,256]{1,0:T(8,128)S(1)} %all_gather.14, s32[256]{0:T(256)S(1)} %iota_add_fusion), kind=kOutput, calls=%fused_computation.48 | convolution fusion | flops 402915328 | bytes 1836033 | tf_op jit(solution)/shard_map/dot_general | solution.py:16
  38.2 1.7 %collective-permute-start.3 = (f32[256,512]{1,0:T(8,128)}, f32[256,512]{1,0:T(8,128)}, u32[]{:S(2)}, u32[]{:S(2)}) collective-permute-start(f32[256,512]{1,0:T(8,128)} %get-tuple-element.7), channel_id=1, source_target_pairs={{0,4},{2,6},{4,0},{6,2},{8,12},{10,14},{12,8},{14,10},{16,20},{18,... | collective-permute-start | bytes 1572872 | tf_op jit(solution)/shard_map/ppermute | solution.py:8
  39.8 0.4 collective-permute-start.2
  40.2 17.8 %collective-permute-done.2 = f32[256,256]{1,0:T(8,128)S(1)} collective-permute-done((f32[256,256]{1,0:T(8,128)S(1)}, f32[256,256]{1,0:T(8,128)S(1)}, u32[]{:S(2)}, u32[]{:S(2)}) %collective-permute-start.2) | collective-permute-done | bytes 262176 | tf_op jit(solution)/shard_map/ppermute | solution.py:8
  58.0 1.7 %fusion.12 = f32[256,512]{1,0:T(8,128)S(1)} fusion(f32[256,512]{1,0:T(8,128)S(1)} %fusion, f32[256,512]{1,0:T(8,128)} %collective-permute-done.3, f32[256,512]{1,0:T(8,128)S(1)} %get-tuple-element.8, f32[256,256]{1,0:T(8,128)S(1)} %fusion.28, f32[256,256]{1,0:T(8,128)S(1)} %collective-permute-done.2, pred[]{:T(512)S(6)} %eq.34), kind=kOutput, calls=%fused_computation.23 | convolution fusion | flops 403111936 | bytes 2621441 | tf_op jit(solution)/shard_map/dot_general | solution.py:16
  59.7 0.7 fusion.1
  60.4 1.5 %broadcast_select_fusion.2 = (f32[256,512]{1,0:T(8,128)}, f32[256,512]{1,0:T(8,128)S(1)}) fusion(f32[256,512]{1,0:T(8,128)S(1)} %fusion.1, pred[]{:T(512)S(6)} %eq.33, f32[256,256]{1,0:T(8,128)S(1)} %all_gather.14, s32[256]{0:T(256)S(1)} %iota_add_fusion), kind=kOutput, calls=%fused_computation.50 | convolution fusion | flops 402915328 | bytes 1836033 | tf_op jit(solution)/shard_map/dot_general | solution.py:16
  61.9 1.8 %collective-permute-start.5 = (f32[256,512]{1,0:T(8,128)}, f32[256,512]{1,0:T(8,128)}, u32[]{:S(2)}, u32[]{:S(2)}) collective-permute-start(f32[256,512]{1,0:T(8,128)} %get-tuple-element.9), channel_id=1, source_target_pairs={{0,8},{2,10},{4,12},{6,14},{8,0},{10,2},{12,4},{14,6},{16,24},{18,... | collective-permute-start | bytes 1572872 | tf_op jit(solution)/shard_map/ppermute | solution.py:8
  63.7 0.3 collective-permute-start.4
  63.9 17.0 %collective-permute-done.4 = f32[256,256]{1,0:T(8,128)S(1)} collective-permute-done((f32[256,256]{1,0:T(8,128)S(1)}, f32[256,256]{1,0:T(8,128)S(1)}, u32[]{:S(2)}, u32[]{:S(2)}) %collective-permute-start.4) | collective-permute-done | bytes 262176 | tf_op jit(solution)/shard_map/ppermute | solution.py:8
  80.9 1.7 %fusion.8 = f32[256,512]{1,0:T(8,128)S(1)} fusion(f32[256,512]{1,0:T(8,128)S(1)} %fusion.1, f32[256,512]{1,0:T(8,128)} %collective-permute-done.5, f32[256,512]{1,0:T(8,128)S(1)} %get-tuple-element.10, f32[256,256]{1,0:T(8,128)S(1)} %fusion.28, f32[256,256]{1,0:T(8,128)S(1)} %collective-permute-done.4, pred[]{:T(512)S(6)} %eq.33), kind=kOutput, calls=%fused_computation.19 | convolution fusion | flops 403111936 | bytes 2621441 | tf_op jit(solution)/shard_map/dot_general | solution.py:16
  82.6 0.7 fusion.2
  83.3 1.7 %broadcast_select_fusion.3 = (f32[256,512]{1,0:T(8,128)}, f32[256,512]{1,0:T(8,128)}) fusion(f32[256,512]{1,0:T(8,128)S(1)} %fusion.2, pred[]{:T(512)S(6)} %eq.32, f32[256,256]{1,0:T(8,128)S(1)} %all_gather.14, s32[256]{0:T(256)S(1)} %iota_add_fusion), kind=kOutput, calls=%fused_computation.52 | convolution fusion | flops 402915328 | bytes 1836033 | tf_op jit(solution)/shard_map/dot_general | solution.py:16
  85.0 2.8 %collective-permute-start.7 = (f32[256,512]{1,0:T(8,128)}, f32[256,512]{1,0:T(8,128)}, u32[]{:S(2)}, u32[]{:S(2)}) collective-permute-start(f32[256,512]{1,0:T(8,128)} %get-tuple-element.11), channel_id=1, source_target_pairs={{0,16},{2,18},{4,20},{6,22},{8,24},{10,26},{12,28},{14,30},{16,0},... | collective-permute-start | bytes 1572872 | tf_op jit(solution)/shard_map/ppermute | solution.py:8
  87.8 0.2 collective-permute-start.6
  87.9 0.6 convolution_subtract_fusion
  88.6 32.4 %collective-permute-done.6 = f32[256,256]{1,0:T(8,128)S(1)} collective-permute-done((f32[256,256]{1,0:T(8,128)S(1)}, f32[256,256]{1,0:T(8,128)S(1)}, u32[]{:S(2)}, u32[]{:S(2)}) %collective-permute-start.6) | collective-permute-done | bytes 262176 | tf_op jit(solution)/shard_map/ppermute | solution.py:8
  120.9 1.7 %fusion.4 = f32[256,512]{1,0:T(8,128)S(1)} fusion(f32[256,512]{1,0:T(8,128)S(1)} %fusion.2, f32[256,512]{1,0:T(8,128)} %collective-permute-done.7, f32[256,512]{1,0:T(8,128)S(1)} %copy-done.3, f32[256,256]{1,0:T(8,128)S(1)} %fusion.28, f32[256,256]{1,0:T(8,128)S(1)} %collective-permute-done.6, pred[]{:T(512)S(6)} %eq.32), kind=kOutput, calls=%fused_computation.15 | convolution fusion | flops 403111936 | bytes 2621441 | tf_op jit(solution)/shard_map/dot_general | solution.py:16
  122.7 0.7 fusion.3
  123.4 1.0 pad_maximum_fusion
  (22 shorter events, 0.2 us)
Async XLA Ops:
  0.0 10.4 %copy-start = (f32[512,512]{1,0:T(8,128)S(1)}, f32[512,512]{1,0:T(8,128)}, u32[]{:S(2)}) copy-start(f32[512,512]{1,0:T(8,128)} %param.5) | copy-start | bytes 3145732
  10.4 13.2 %copy-start.1 = (f32[512,256]{1,0:T(8,128)}, f32[512,256]{1,0:T(8,128)S(1)}, u32[]{:S(2)}) copy-start(f32[512,256]{1,0:T(8,128)S(1)} %select_add_fusion) | copy-start | bytes 1572868
  10.4 1.1 copy-start.4
  11.5 5.8 %copy-start.5 = (f32[256,128]{1,0:T(8,128)S(1)}, f32[256,128]{1,0:T(8,128)}, u32[]{:S(2)}) copy-start(f32[256,128]{1,0:T(8,128)} %param.8) | copy-start | bytes 393220
  24.3 1.5 %copy-start.6 = (f32[256,128]{1,0:T(8,128)S(1)}, f32[256,128]{1,0:T(8,128)}, u32[]{:S(2)}) copy-start(f32[256,128]{1,0:T(8,128)} %param.9) | copy-start | bytes 393220
  25.8 8.5 %collective-permute-start.1 = (f32[256,512]{1,0:T(8,128)}, f32[256,512]{1,0:T(8,128)}, u32[]{:S(2)}, u32[]{:S(2)}) collective-permute-start(f32[256,512]{1,0:T(8,128)} %get-tuple-element.5), channel_id=1, source_target_pairs={{0,2},{2,0},{4,6},{6,4},{8,10},{10,8},{12,14},{14,12},{16,18},{18,... | collective-permute-start | bytes 1572872 | tf_op jit(solution)/shard_map/ppermute | solution.py:8
  32.6 1.6 %collective-permute-start = (f32[256,256]{1,0:T(8,128)S(1)}, f32[256,256]{1,0:T(8,128)S(1)}, u32[]{:S(2)}, u32[]{:S(2)}) collective-permute-start(f32[256,256]{1,0:T(8,128)S(1)} %fusion.28), channel_id=1, source_target_pairs={{0,2},{2,0},{4,6},{6,4},{8,10},{10,8},{12,14},{14,12},{16,18},{18,... | collective-permute-start | bytes 786440 | tf_op jit(solution)/shard_map/ppermute | solution.py:8
  38.2 19.8 %collective-permute-start.3 = (f32[256,512]{1,0:T(8,128)}, f32[256,512]{1,0:T(8,128)}, u32[]{:S(2)}, u32[]{:S(2)}) collective-permute-start(f32[256,512]{1,0:T(8,128)} %get-tuple-element.7), channel_id=1, source_target_pairs={{0,4},{2,6},{4,0},{6,2},{8,12},{10,14},{12,8},{14,10},{16,20},{18,... | collective-permute-start | bytes 1572872 | tf_op jit(solution)/shard_map/ppermute | solution.py:8
  39.8 18.1 %collective-permute-start.2 = (f32[256,256]{1,0:T(8,128)S(1)}, f32[256,256]{1,0:T(8,128)S(1)}, u32[]{:S(2)}, u32[]{:S(2)}) collective-permute-start(f32[256,256]{1,0:T(8,128)S(1)} %fusion.28), channel_id=1, source_target_pairs={{0,4},{2,6},{4,0},{6,2},{8,12},{10,14},{12,8},{14,10},{16,20},{18,... | collective-permute-start | bytes 786440 | tf_op jit(solution)/shard_map/ppermute | solution.py:8
  61.9 19.0 %collective-permute-start.5 = (f32[256,512]{1,0:T(8,128)}, f32[256,512]{1,0:T(8,128)}, u32[]{:S(2)}, u32[]{:S(2)}) collective-permute-start(f32[256,512]{1,0:T(8,128)} %get-tuple-element.9), channel_id=1, source_target_pairs={{0,8},{2,10},{4,12},{6,14},{8,0},{10,2},{12,4},{14,6},{16,24},{18,... | collective-permute-start | bytes 1572872 | tf_op jit(solution)/shard_map/ppermute | solution.py:8
  63.7 17.2 %collective-permute-start.4 = (f32[256,256]{1,0:T(8,128)S(1)}, f32[256,256]{1,0:T(8,128)S(1)}, u32[]{:S(2)}, u32[]{:S(2)}) collective-permute-start(f32[256,256]{1,0:T(8,128)S(1)} %fusion.28), channel_id=1, source_target_pairs={{0,8},{2,10},{4,12},{6,14},{8,0},{10,2},{12,4},{14,6},{16,24},{18,... | collective-permute-start | bytes 786440 | tf_op jit(solution)/shard_map/ppermute | solution.py:8
  83.3 4.6 %copy-start.2 = (f32[512,256]{1,0:T(8,128)S(1)}, f32[512,256]{1,0:T(8,128)}, u32[]{:S(2)}) copy-start(f32[512,256]{1,0:T(8,128)} %copy-done.1) | copy-start | bytes 1572868
  85.0 35.9 %collective-permute-start.7 = (f32[256,512]{1,0:T(8,128)}, f32[256,512]{1,0:T(8,128)}, u32[]{:S(2)}, u32[]{:S(2)}) collective-permute-start(f32[256,512]{1,0:T(8,128)} %get-tuple-element.11), channel_id=1, source_target_pairs={{0,16},{2,18},{4,20},{6,22},{8,24},{10,26},{12,28},{14,30},{16,0},... | collective-permute-start | bytes 1572872 | tf_op jit(solution)/shard_map/ppermute | solution.py:8
  87.8 33.2 %collective-permute-start.6 = (f32[256,256]{1,0:T(8,128)S(1)}, f32[256,256]{1,0:T(8,128)S(1)}, u32[]{:S(2)}, u32[]{:S(2)}) collective-permute-start(f32[256,256]{1,0:T(8,128)S(1)} %fusion.28), channel_id=1, source_target_pairs={{0,16},{2,18},{4,20},{6,22},{8,24},{10,26},{12,28},{14,30},{16,0},... | collective-permute-start | bytes 786440 | tf_op jit(solution)/shard_map/ppermute | solution.py:8
  87.9 33.0 %copy-start.3 = (f32[256,512]{1,0:T(8,128)S(1)}, f32[256,512]{1,0:T(8,128)}, u32[]{:S(2)}) copy-start(f32[256,512]{1,0:T(8,128)} %get-tuple-element.12) | copy-start | bytes 1572868
where the time goes:
time: 125 us; the launch traced here: 124 us
  waiting for transfers between devices  68.6 us (55%)
  blocking collectives  28.5 us (23%)
  matrix products  18.8 us (15%)
  starting transfers between devices  7.05 us (6%)
    ppermute x8, waiting for transfers between devices, swapped(): lax.ppermute(array, axis, [(i, i ^ 1 << bit) for i in range(lax.axis_size...  68.6 us
    dot_general x10, matrix products, product_left_t(): lax.dot_general(left, right, (((0,), (0,)), ((), ())), precision=lax.Prec...  14.9 us
    all_gather x1, blocking collectives, on_device(): lax.all_gather(leaf_v, 'col', axis=1, tiled=True)  10.3 us
    ppermute x8, starting transfers between devices, swapped(): lax.ppermute(array, axis, [(i, i ^ 1 << bit) for i in range(lax.axis_size...  7.05 us
    all_gather x1, blocking collectives, on_device(): lax.all_gather(tree_t, 'col', axis=1, tiled=True)  6.75 us
    all_gather x1, blocking collectives, on_device(): lax.all_gather(leaf_t, 'col', axis=1, tiled=True)  5.78 us
    all_gather x1, blocking collectives, on_device(): lax.all_gather(tree_v, 'col', axis=1, tiled=True)  5.63 us
    dot_general x6, matrix products, product(): jnp.dot(left, right, precision=lax.Precision.HIGHEST, preferred_element_t...  3.94 us
  transfers between devices with their start and end apart: 8, of which 4 were waited for; matrix products, arithmetic and copies ran while one was open for 1% of the time, Pallas kernels for 0%

commit v1 on v0

v1 whole, which is shorter than its diff:
```python
import jax
import jax.numpy as jnp
from jax import lax
from jax.sharding import PartitionSpec as P


def product(left, right):
    return jnp.dot(left, right, precision=lax.Precision.HIGHEST, preferred_element_type=jnp.float32)


def product_left_t(left, right):
    return lax.dot_general(
        left,
        right,
        (((0,), (0,)), ((), ())),
        precision=lax.Precision.HIGHEST,
        preferred_element_type=jnp.float32,
    )


def unit_lower(raw):
    row_ids = lax.broadcasted_iota(jnp.int32, raw.shape, 0)
    col_ids = lax.broadcasted_iota(jnp.int32, raw.shape, 1)
    diagonal = jnp.where(row_ids == col_ids, 1.0, 0.0).astype(raw.dtype)
    return jnp.where(row_ids > col_ids, raw, 0.0) + diagonal


def col_gather(parts):
    n_col = lax.axis_size("col")
    me = lax.axis_index("col")
    by_shift = [parts]
    for shift in range(1, n_col):
        perm = [(i, (i + shift) % n_col) for i in range(n_col)]
        by_shift.append(lax.ppermute(parts, "col", perm))
    joined = []
    for a in range(len(parts)):
        stacked = jnp.stack([got[a] for got in by_shift])
        blocks = [stacked[(me - b) % n_col] for b in range(n_col)]
        joined.append(jnp.concatenate(blocks, axis=1))
    return joined


def on_device(slab, leaf_v, leaf_t, tree_v, tree_t):
    n_row = lax.axis_size("row")
    levels = n_row.bit_length() - 1
    position = lax.axis_index("row")

    leaf_full, leaf_tri = col_gather((leaf_v, leaf_t))
    tree_full, tree_tri = col_gather((tree_v, tree_t))
    width = leaf_tri.shape[0]

    leaf_vectors = unit_lower(leaf_full)
    leaf_factor = jnp.triu(leaf_tri)
    leaf_w = product_left_t(leaf_factor, product_left_t(leaf_vectors, slab))
    current = slab[:width] - product(leaf_vectors[:width], leaf_w)
    remainder = slab[width:] - product(leaf_vectors[width:], leaf_w)

    tree_vectors = jnp.triu(tree_full)
    tree_factor = jnp.triu(tree_tri)
    tree_joint = product(tree_vectors, tree_factor)

    partner_factors = []
    for level in range(levels):
        step = 1 << level
        pairs = [(i + step, i) for i in range(0, n_row, 2 * step)]
        partner_factors.append(lax.ppermute((tree_factor, tree_joint), "row", pairs))

    for level in range(levels):
        if level < 2:
            wanted = partner_factors[0] if level == 0 else partner_factors[1:]
            current, wanted = lax.optimization_barrier((current, wanted))
            if level == 0:
                partner_factors[0] = wanted
            else:
                partner_factors[1:] = wanted
        step = 1 << level
        phase = position % (2 * step)
        role = jnp.where(phase == 0, 1, jnp.where(phase == step, 2, 0))
        pairs = []
        for i in range(0, n_row, 2 * step):
            pairs += [(i, i + step), (i + step, i)]
        received = lax.ppermute(current, "row", pairs)
        their_factor, their_joint = partner_factors[level]

        def idle_pre(g, sf):
            return g

        def lower_pre(g, sf):
            return g - product_left_t(sf, g)

        def upper_pre(g, sf):
            return product_left_t(tree_joint, g)

        early = lax.switch(role, (idle_pre, lower_pre, upper_pre), current, their_factor)

        def idle_post(g, e, r, sj):
            return g

        def lower_post(g, e, r, sj):
            return e - product_left_t(sj, r)

        def upper_post(g, e, r, sj):
            return g - product(tree_vectors, product_left_t(tree_factor, r) + e)

        current = lax.switch(role, (idle_post, lower_post, upper_post), current, early, received, their_joint)
    return jnp.concatenate([current, remainder], axis=0)


def solution(mesh):
    in_specs = (P("row", "col"), P("row", "col"), P("row", "col"), P("row", "col"), P("row", "col"))
    out_specs = P("row", "col")
    return jax.shard_map(
        on_device, mesh=mesh, in_specs=in_specs, out_specs=out_specs, check_vma=False
    )
```

time: 125 us -> 96.1 us (0.77)
  waiting for transfers between devices: 68.6 us -> 39.8 us
  blocking collectives: 28.5 us -> 0 us
  starting transfers between devices: 7.05 us -> 22.3 us
  local copies, waits for them, and re-layouts: 0.04 us -> 9.84 us
  matrix products: 18.8 us -> 20.2 us
    ppermute x8 -> x16, waiting for transfers between devices: 68.6 us -> 39.8 us  [the longest x4 18.9 us: on_device(): received = lax.ppermute(current, 'row', pairs)]
    all_gather x4 -> x0, blocking collectives: 28.5 us -> none  [the longest x1 10.3 us: on_device(): lax.all_gather(leaf_v, 'col', axis=1, tiled=True)]
    ppermute x8 -> x16, starting transfers between devices: 7.05 us -> 22.3 us  [the longest x8 10.3 us: on_device(): lax.ppermute((tree_factor, tree_joint), 'row', pairs)]
    dot_general x10, matrix products: 14.9 us -> 17.8 us  [product_left_t(): lax.dot_general(left, right, (((0,), (0,)), ((), ())), precision=lax.Prec...]
    sub x0 -> x3, local copies, waits for them, and re-layouts: none -> 2.67 us  [lower_post(): return e - product_left_t(sj, r)]
    another operation x0 -> x3, local copies, waits for them, and re-layouts: none -> 2.22 us
    cond x0 -> x2, local copies, waits for them, and re-layouts: none -> 1.99 us  [on_device(): lax.switch(role, (idle_post, lower_post, upper_post), current, early, rec...]
    unnamed x14 -> x20, local copies, waits for them, and re-layouts: 0.04 us -> 1.97 us
  transfers between devices with their start and end apart: 8 -> 16, of which waited for: 4 -> 8; matrix products, arithmetic and copies ran while one was open for 1% -> 18% of each run, Pallas kernels for 0% -> 0%
where the time goes in v1:
time: 96.1 us; the launch traced here: 95.4 us
  waiting for transfers between devices  39.8 us (41%)
  starting transfers between devices  22.3 us (23%)
  matrix products  20.2 us (21%)
  local copies, waits for them, and re-layouts  9.84 us (10%)
  other arithmetic  2.38 us (2%)
    ppermute x4, waiting for transfers between devices, on_device(): received = lax.ppermute(current, 'row', pairs)  18.9 us
    dot_general x10, matrix products, product_left_t(): lax.dot_general(left, right, (((0,), (0,)), ((), ())), precision=lax.Prec...  17.8 us
    ppermute x4, waiting for transfers between devices, col_gather(): by_shift.append(lax.ppermute(parts, 'col', perm))  11.9 us
    ppermute x8, starting transfers between devices, on_device(): lax.ppermute((tree_factor, tree_joint), 'row', pairs)  10.3 us
    ppermute x8, waiting for transfers between devices, on_device(): lax.ppermute((tree_factor, tree_joint), 'row', pairs)  9.02 us
    ppermute x4, starting transfers between devices, on_device(): received = lax.ppermute(current, 'row', pairs)  6.94 us
    ppermute x4, starting transfers between devices, col_gather(): by_shift.append(lax.ppermute(parts, 'col', perm))  5.04 us
    sub x3, local copies, waits for them, and re-layouts, lower_post(): return e - product_left_t(sj, r)  2.67 us
  transfers between devices with their start and end apart: 16, of which 8 were waited for; matrix products, arithmetic and copies ran while one was open for 18% of the time, Pallas kernels for 0%

profile of v1, /device:TPU:0, one launch (start us, length us, event | category | flops | bytes accessed | tf_op | source)
XLA Modules:
  0.0 95.4 jit_solution(11776196414745702068)
XLA Ops:
  0.0 3.0 %collective-permute-start.4 = (f32[256,128]{1,0:T(8,128)}, f32[256,128]{1,0:T(8,128)S(1)}, u32[]{:S(2)}, u32[]{:S(2)}) collective-permute-start(f32[256,128]{1,0:T(8,128)} %param.32), channel_id=1, source_target_pairs={{0,1},{1,0},{2,3},{3,2},{4,5},{5,4},{6,7},{7,6},{8,9},{9,8},{10,11... | collective-permute-start | bytes 393224 | tf_op jit(solution)/shard_map/ppermute | solution.py:34
  3.0 2.0 %collective-permute-start.1 = (f32[256,128]{1,0:T(8,128)}, f32[256,128]{1,0:T(8,128)S(1)}, u32[]{:S(2)}, u32[]{:S(2)}) collective-permute-start(f32[256,128]{1,0:T(8,128)} %param.31), channel_id=1, source_target_pairs={{0,1},{1,0},{2,3},{3,2},{4,5},{5,4},{6,7},{7,6},{8,9},{9,8},{10,11... | collective-permute-start | bytes 393224 | tf_op jit(solution)/shard_map/ppermute | solution.py:34
  5.0 2.5 %collective-permute-done.4 = f32[256,128]{1,0:T(8,128)S(1)} collective-permute-done((f32[256,128]{1,0:T(8,128)}, f32[256,128]{1,0:T(8,128)S(1)}, u32[]{:S(2)}, u32[]{:S(2)}) %collective-permute-start.4) | collective-permute-done | bytes 131104 | tf_op jit(solution)/shard_map/ppermute | solution.py:34
  8.5 9.4 %collective-permute-done.2 = f32[256,128]{1,0:T(8,128)S(1)} collective-permute-done((f32[256,128]{1,0:T(8,128)}, f32[256,128]{1,0:T(8,128)S(1)}, u32[]{:S(2)}, u32[]{:S(2)}) %collective-permute-start.2) | collective-permute-done | bytes 131104 | tf_op jit(solution)/shard_map/ppermute | solution.py:34
  18.1 1.3 %collective-permute-start.3 = (f32[256,256]{1,0:T(8,128)S(1)}, f32[256,256]{1,0:T(8,128)S(1)}, u32[]{:S(2)}, u32[]{:S(2)}) collective-permute-start(f32[256,256]{1,0:T(8,128)S(1)} %get-tuple-element.238), channel_id=1, source_target_pairs={{2,0},{6,4},{10,8},{14,12},{18,16},{22,20},{26,24},{30,28},{3,1},{... | collective-permute-start | bytes 786440 | tf_op jit(solution)/shard_map/ppermute | solution.py:66
  19.8 1.3 %collective-permute-start.5 = (f32[256,256]{1,0:T(8,128)S(1)}, f32[256,256]{1,0:T(8,128)S(1)}, u32[]{:S(2)}, u32[]{:S(2)}) collective-permute-start(f32[256,256]{1,0:T(8,128)S(1)} %fusion.36), channel_id=1, source_target_pairs={{2,0},{6,4},{10,8},{14,12},{18,16},{22,20},{26,24},{30,28},{3,1},{... | collective-permute-start | bytes 786440 | tf_op jit(solution)/shard_map/ppermute | solution.py:66
  32.1 3.1 %collective-permute-done.7 = f32[256,256]{1,0:T(8,128)S(1)} collective-permute-done((f32[256,256]{1,0:T(8,128)S(1)}, f32[256,256]{1,0:T(8,128)S(1)}, u32[]{:S(2)}, u32[]{:S(2)}) %collective-permute-start.7) | collective-permute-done | bytes 262176 | tf_op jit(solution)/shard_map/ppermute | solution.py:66
  37.8 1.6 %conditional.8 = (f32[256,512]{1,0:T(8,128)S(1)}) conditional(s32[]{:T(128)} %clamp.19, f32[256,512]{1,0:T(8,128)S(1)} %convolution_subtract_fusion.9, (f32[256,256]{1,0:T(8,128)}, f32[256,512]{1,0:T(8,128)S(1)}) %tuple.139, (f32[256,256]{1,0:T(8,128)S(1)}, f32[256,512]{1,0:T(8,128)S(1)}) %tuple.81), branch_computations={%region_0.1_spmd, %region_1.2_spmd, %region_2.3_spmd} | conditional | flops 402784256 | bytes 1310728 | solution.py:94
  37.9 1.6 %convolution_subtract_fusion = f32[256,512]{1,0:T(8,128)S(1)} fusion(f32[256,512]{1,0:T(8,128)S(1)} %get-tuple-element.133, f32[256,256]{1,0:T(8,128)} %get-tuple-element.134), kind=kOutput, calls=%fused_computation | convolution fusion | flops 402784256 | bytes 1310720 | tf_op jit(solution)/shard_map/cond/branch_1_fun/dot_general | solution.py:12
  39.5 1.8 %conditional.9 = (f32[256,512]{0,1:T(8,128)S(1)}) conditional(s32[]{:T(128)} %clamp.19, (f32[256,512]{1,0:T(8,128)S(1)}) %tuple.104, (f32[256,256]{1,0:T(8,128)}, f32[256,512]{1,0:T(8,128)S(1)}, f32[256,512]{1,0:T(8,128)S(1)}) %tuple.138, (f32[256,256]{1,0:T(8,128)S(1)}, f32[256,512]{1,0:T(8,128)S(1)}, f32[256,512]{1,0:T(8,128)S(1)}, ...), branch_computations={%region_3.4_spmd, %region_4.5_spmd, %region_5.6_spmd} | conditional | flops 805568512 | bytes 6815780 | solution.py:105
  39.5 1.6 %convolution_subtract_fusion.1 = f32[256,512]{1,0:T(8,128)S(1)} fusion(f32[256,512]{1,0:T(8,128)S(1)} %get-tuple-element.137, f32[256,256]{1,0:T(8,128)} %get-tuple-element.144, f32[256,512]{1,0:T(8,128)S(1)} %get-tuple-element.146), kind=kOutput, calls=%fused_computation.1 | convolution fusion | flops 402784256 | bytes 1835008 | tf_op jit(solution)/shard_map/cond/branch_1_fun/dot_general | solution.py:12
  41.3 3.1 %collective-permute-done.11 = f32[256,256]{1,0:T(8,128)} collective-permute-done((f32[256,256]{1,0:T(8,128)S(1)}, f32[256,256]{1,0:T(8,128)}, u32[]{:S(2)}, u32[]{:S(2)}) %collective-permute-start.11) | collective-permute-done | bytes 262176 | tf_op jit(solution)/shard_map/ppermute | solution.py:66
  44.5 2.8 %collective-permute-done.12 = f32[256,256]{1,0:T(8,128)} collective-permute-done((f32[256,256]{1,0:T(8,128)S(1)}, f32[256,256]{1,0:T(8,128)}, u32[]{:S(2)}, u32[]{:S(2)}) %collective-permute-start.12) | collective-permute-done | bytes 262176 | tf_op jit(solution)/shard_map/ppermute | solution.py:66
  48.3 1.9 %collective-permute-start.13 = (f32[256,512]{1,0:T(8,128)}, f32[256,512]{1,0:T(8,128)S(1)}, u32[]{:S(2)}, u32[]{:S(2)}) collective-permute-start(f32[256,512]{1,0:T(8,128)} %copy.12), channel_id=1, source_target_pairs={{0,4},{4,0},{8,12},{12,8},{16,20},{20,16},{24,28},{28,24},{1,5},{5... | collective-permute-start | bytes 1572872 | tf_op jit(solution)/shard_map/ppermute | solution.py:82
  50.2 3.2 %conditional.10 = (f32[256,512]{1,0:T(8,128)S(1)}) conditional(s32[]{:T(128)} %clamp.18, f32[256,512]{1,0:T(8,128)} %copy.12, (f32[256,256]{1,0:T(8,128)}, f32[256,512]{0,1:T(8,128)S(1)}) %tuple.137, (f32[256,256]{1,0:T(8,128)S(1)}, f32[256,512]{0,1:T(8,128)S(1)}) %tuple.86), branch_computations={%region_6.7_spmd, %region_7.8_spmd, %region_8.9_spmd} | conditional | flops 402784256 | bytes 2883592 | solution.py:94
  51.2 2.2 %convolution_subtract_fusion.2 = f32[256,512]{1,0:T(8,128)S(1)} fusion(f32[256,512]{1,0:T(8,128)} %copy.14, f32[256,256]{1,0:T(8,128)} %get-tuple-element.154, f32[256,512]{0,1:T(8,128)S(1)} %get-tuple-element.215), kind=kOutput, calls=%fused_computation.5 | convolution fusion | flops 402784256 | bytes 1835008 | tf_op jit(solution)/shard_map/cond/branch_1_fun/dot_general | solution.py:12
  53.4 6.1 %collective-permute-done.13 = f32[256,512]{1,0:T(8,128)S(1)} collective-permute-done((f32[256,512]{1,0:T(8,128)}, f32[256,512]{1,0:T(8,128)S(1)}, u32[]{:S(2)}, u32[]{:S(2)}) %collective-permute-start.13) | collective-permute-done | bytes 524320 | tf_op jit(solution)/shard_map/ppermute | solution.py:82
  59.5 3.8 %conditional.11 = (f32[256,512]{0,1:T(8,128)S(1)}) conditional(s32[]{:T(128)} %clamp.18, f32[256,512]{0,1:T(8,128)S(1)} %get-tuple-element.243, (f32[256,256]{1,0:T(8,128)}, f32[256,512]{1,0:T(8,128)S(1)}, f32[256,512]{1,0:T(8,128)S(1)}) %tuple.87, (f32[256,256]{1,0:T(8,128)S(1)}, f32[256,512]{1,0:T(8,128)S(1)}, ...), branch_computations={%region_9.10_spmd, %region_10.11_spmd, %region_11.12_spmd} | conditional | flops 805568512 | bytes 3670024 | solution.py:105
  59.5 2.4 %convolution_subtract_fusion.3 = f32[256,512]{1,0:T(8,128)} fusion(f32[256,512]{1,0:T(8,128)S(1)} %get-tuple-element.157, f32[256,256]{1,0:T(8,128)} %get-tuple-element.158, f32[256,512]{1,0:T(8,128)S(1)} %get-tuple-element.159), kind=kOutput, calls=%fused_computation.6 | convolution fusion | flops 402784256 | bytes 1835008 | tf_op jit(solution)/shard_map/cond/branch_1_fun/dot_general | solution.py:12
  64.3 1.9 %collective-permute-start.14 = (f32[256,512]{1,0:T(8,128)}, f32[256,512]{1,0:T(8,128)S(1)}, u32[]{:S(2)}, u32[]{:S(2)}) collective-permute-start(f32[256,512]{1,0:T(8,128)} %copy.16), channel_id=1, source_target_pairs={{0,8},{8,0},{16,24},{24,16},{1,9},{9,1},{17,25},{25,17}} | collective-permute-start | bytes 1572872 | tf_op jit(solution)/shard_map/ppermute | solution.py:82
  66.3 3.2 %conditional.12 = (f32[256,512]{1,0:T(8,128)S(1)}) conditional(s32[]{:T(128)} %clamp.17, f32[256,512]{1,0:T(8,128)} %copy.16, (f32[256,256]{1,0:T(8,128)}, f32[256,512]{0,1:T(8,128)S(1)}) %tuple.89, (f32[256,256]{1,0:T(8,128)S(1)}, f32[256,512]{0,1:T(8,128)S(1)}) %tuple.90), branch_computations={%region_12.13_spmd, %region_13.14_spmd, %region_14.15_spmd} | conditional | flops 402784256 | bytes 2883592 | solution.py:94
  67.3 2.2 %convolution_subtract_fusion.4 = f32[256,512]{1,0:T(8,128)S(1)} fusion(f32[256,512]{1,0:T(8,128)} %copy.18, f32[256,256]{1,0:T(8,128)} %get-tuple-element.166, f32[256,512]{0,1:T(8,128)S(1)} %get-tuple-element.219), kind=kOutput, calls=%fused_computation.10 | convolution fusion | flops 402784256 | bytes 1835008 | tf_op jit(solution)/shard_map/cond/branch_1_fun/dot_general | solution.py:12
  69.5 6.1 %collective-permute-done.14 = f32[256,512]{1,0:T(8,128)S(1)} collective-permute-done((f32[256,512]{1,0:T(8,128)}, f32[256,512]{1,0:T(8,128)S(1)}, u32[]{:S(2)}, u32[]{:S(2)}) %collective-permute-start.14) | collective-permute-done | bytes 524320 | tf_op jit(solution)/shard_map/ppermute | solution.py:82
  75.6 3.6 %conditional.13 = (f32[256,512]{0,1:T(8,128)S(1)}) conditional(s32[]{:T(128)} %clamp.17, f32[256,512]{0,1:T(8,128)S(1)} %get-tuple-element.245, (f32[256,256]{1,0:T(8,128)}, f32[256,512]{1,0:T(8,128)S(1)}, f32[256,512]{1,0:T(8,128)S(1)}) %tuple.91, (f32[256,256]{1,0:T(8,128)S(1)}, f32[256,512]{1,0:T(8,128)S(1)}, ...), branch_computations={%region_15.16_spmd, %region_16.17_spmd, %region_17.18_spmd} | conditional | flops 805568512 | bytes 3670024 | solution.py:105
  75.6 2.4 %convolution_subtract_fusion.5 = f32[256,512]{1,0:T(8,128)} fusion(f32[256,512]{1,0:T(8,128)S(1)} %get-tuple-element.169, f32[256,256]{1,0:T(8,128)} %get-tuple-element.170, f32[256,512]{1,0:T(8,128)S(1)} %get-tuple-element.171), kind=kOutput, calls=%fused_computation.11 | convolution fusion | flops 402784256 | bytes 1835008 | tf_op jit(solution)/shard_map/cond/branch_1_fun/dot_general | solution.py:12
  80.2 1.9 %collective-permute-start.15 = (f32[256,512]{1,0:T(8,128)}, f32[256,512]{1,0:T(8,128)}, u32[]{:S(2)}, u32[]{:S(2)}) collective-permute-start(f32[256,512]{1,0:T(8,128)} %copy.20), channel_id=1, source_target_pairs={{0,16},{16,0},{1,17},{17,1}} | collective-permute-start | bytes 1572872 | tf_op jit(solution)/shard_map/ppermute | solution.py:82
  82.2 1.4 %convolution_subtract_fusion.8 = f32[256,512]{1,0:T(8,128)} fusion(f32[256,512]{1,0:T(8,128)S(1)} %fusion.11, f32[512,512]{1,0:T(8,128)S(1)} %copy-done.1, f32[512,256]{1,0:T(8,128)S(1)} %fusion.4), kind=kOutput, calls=%fused_computation.20 | convolution fusion | flops 402784256 | bytes 1835008 | tf_op jit(solution)/shard_map/dot_general | solution.py:8
  83.6 2.2 %conditional.14 = (f32[256,512]{1,0:T(8,128)S(1)}) conditional(s32[]{:T(128)} %clamp.16, f32[256,512]{1,0:T(8,128)S(1)} %copy-done.3, (f32[256,256]{1,0:T(8,128)}, f32[256,512]{0,1:T(8,128)S(1)}) %tuple.93, (f32[256,256]{1,0:T(8,128)S(1)}, f32[256,512]{0,1:T(8,128)S(1)}) %tuple.94), branch_computations={%region_18.19_spmd, %region_19.20_spmd, %region_20.21_spmd} | conditional | flops 402784256 | bytes 2883592 | solution.py:94
  83.8 2.0 %convolution_subtract_fusion.6 = f32[256,512]{1,0:T(8,128)S(1)} fusion(f32[256,512]{1,0:T(8,128)S(1)} %copy.22, f32[256,256]{1,0:T(8,128)} %get-tuple-element.178, f32[256,512]{0,1:T(8,128)S(1)} %get-tuple-element.223), kind=kOutput, calls=%fused_computation.15 | convolution fusion | flops 402784256 | bytes 1835008 | tf_op jit(solution)/shard_map/cond/branch_1_fun/dot_general | solution.py:12
  85.8 6.7 %collective-permute-done.15 = f32[256,512]{1,0:T(8,128)} collective-permute-done((f32[256,512]{1,0:T(8,128)}, f32[256,512]{1,0:T(8,128)}, u32[]{:S(2)}, u32[]{:S(2)}) %collective-permute-start.15) | collective-permute-done | bytes 524320 | tf_op jit(solution)/shard_map/ppermute | solution.py:82
  92.5 1.8 %conditional.15 = (f32[256,512]{1,0:T(8,128)S(1)}) conditional(s32[]{:T(128)} %clamp.16, f32[256,512]{0,1:T(8,128)S(1)} %get-tuple-element.247, (f32[256,256]{1,0:T(8,128)}, f32[256,512]{1,0:T(8,128)}, f32[256,512]{1,0:T(8,128)S(1)}) %tuple.95, (f32[256,256]{1,0:T(8,128)S(1)}, f32[256,512]{1,0:T(8,128)}, ...), branch_computations={%region_21.22_spmd, %region_22.23_spmd, %region_23.24_spmd} | conditional | flops 805568512 | bytes 4718600 | solution.py:105
  92.5 1.8 %convolution_subtract_fusion.7 = f32[256,512]{1,0:T(8,128)S(1)} fusion(f32[256,512]{1,0:T(8,128)S(1)} %get-tuple-element.181, f32[256,256]{1,0:T(8,128)} %get-tuple-element.182, f32[256,512]{1,0:T(8,128)} %get-tuple-element.183), kind=kOutput, calls=%fused_computation.16 | convolution fusion | flops 402784256 | bytes 1835008 | tf_op jit(solution)/shard_map/cond/branch_1_fun/dot_general | solution.py:12
  (58 shorter events, 24.0 us)
Async XLA Ops:
  0.0 7.5 %collective-permute-start.4 = (f32[256,128]{1,0:T(8,128)}, f32[256,128]{1,0:T(8,128)S(1)}, u32[]{:S(2)}, u32[]{:S(2)}) collective-permute-start(f32[256,128]{1,0:T(8,128)} %param.32), channel_id=1, source_target_pairs={{0,1},{1,0},{2,3},{3,2},{4,5},{5,4},{6,7},{7,6},{8,9},{9,8},{10,11... | collective-permute-start | bytes 393224 | tf_op jit(solution)/shard_map/ppermute | solution.py:34
  3.0 18.2 %collective-permute-start = (f32[512,128]{1,0:T(8,128)}, f32[512,128]{1,0:T(8,128)S(1)}, u32[]{:S(2)}, u32[]{:S(2)}) collective-permute-start(f32[512,128]{1,0:T(8,128)} %param.30), channel_id=1, source_target_pairs={{0,1},{1,0},{2,3},{3,2},{4,5},{5,4},{6,7},{7,6},{8,9},{9,8},{10,11... | collective-permute-start | bytes 786440 | tf_op jit(solution)/shard_map/ppermute | solution.py:34
  3.0 18.1 %collective-permute-start.1 = (f32[256,128]{1,0:T(8,128)}, f32[256,128]{1,0:T(8,128)S(1)}, u32[]{:S(2)}, u32[]{:S(2)}) collective-permute-start(f32[256,128]{1,0:T(8,128)} %param.31), channel_id=1, source_target_pairs={{0,1},{1,0},{2,3},{3,2},{4,5},{5,4},{6,7},{7,6},{8,9},{9,8},{10,11... | collective-permute-start | bytes 393224 | tf_op jit(solution)/shard_map/ppermute | solution.py:34
  5.0 12.9 %collective-permute-start.2 = (f32[256,128]{1,0:T(8,128)}, f32[256,128]{1,0:T(8,128)S(1)}, u32[]{:S(2)}, u32[]{:S(2)}) collective-permute-start(f32[256,128]{1,0:T(8,128)} %param.33), channel_id=1, source_target_pairs={{0,1},{1,0},{2,3},{3,2},{4,5},{5,4},{6,7},{7,6},{8,9},{9,8},{10,11... | collective-permute-start | bytes 393224 | tf_op jit(solution)/shard_map/ppermute | solution.py:34
  7.5 10.4 %copy-start.9 = (f32[256,128]{1,0:T(8,128)S(1)}, f32[256,128]{1,0:T(8,128)}, u32[]{:S(2)}) copy-start(f32[256,128]{1,0:T(8,128)} %param.33) | copy-start | bytes 393220
  18.1 7.6 %collective-permute-start.3 = (f32[256,256]{1,0:T(8,128)S(1)}, f32[256,256]{1,0:T(8,128)S(1)}, u32[]{:S(2)}, u32[]{:S(2)}) collective-permute-start(f32[256,256]{1,0:T(8,128)S(1)} %get-tuple-element.238), channel_id=1, source_target_pairs={{2,0},{6,4},{10,8},{14,12},{18,16},{22,20},{26,24},{30,28},{3,1},{... | collective-permute-start | bytes 786440 | tf_op jit(solution)/shard_map/ppermute | solution.py:66
  19.4 1.7 %copy-start.10 = (f32[256,128]{1,0:T(8,128)S(1)}, f32[256,128]{1,0:T(8,128)}, u32[]{:S(2)}) copy-start(f32[256,128]{1,0:T(8,128)} %param.31) | copy-start | bytes 393220
  19.8 5.9 %collective-permute-start.5 = (f32[256,256]{1,0:T(8,128)S(1)}, f32[256,256]{1,0:T(8,128)S(1)}, u32[]{:S(2)}, u32[]{:S(2)}) collective-permute-start(f32[256,256]{1,0:T(8,128)S(1)} %fusion.36), channel_id=1, source_target_pairs={{2,0},{6,4},{10,8},{14,12},{18,16},{22,20},{26,24},{30,28},{3,1},{... | collective-permute-start | bytes 786440 | tf_op jit(solution)/shard_map/ppermute | solution.py:66
  21.1 1.0 copy-start.5
  22.1 1.2 %copy-start = (f32[512,512]{1,0:T(8,128)S(1)}, f32[512,512]{1,0:T(8,128)}, u32[]{:S(2)}) copy-start(f32[512,512]{1,0:T(8,128)} %param.29) | copy-start | bytes 3145732
  25.7 10.8 %copy-start.8 = (f32[256,256]{1,0:T(8,128)}, f32[256,256]{1,0:T(8,128)S(1)}, u32[]{:S(2)}) copy-start(f32[256,256]{1,0:T(8,128)S(1)} %collective-permute-done.3) | copy-start | bytes 786436
  25.7 10.8 %copy-start.7 = (f32[256,256]{1,0:T(8,128)}, f32[256,256]{1,0:T(8,128)S(1)}, u32[]{:S(2)}) copy-start(f32[256,256]{1,0:T(8,128)S(1)} %collective-permute-done.5) | copy-start | bytes 786436
  25.7 10.8 %collective-permute-start.6 = (f32[256,512]{1,0:T(8,128)S(1)}, f32[256,512]{1,0:T(8,128)S(1)}, u32[]{:S(2)}, u32[]{:S(2)}) collective-permute-start(f32[256,512]{1,0:T(8,128)S(1)} %convolution_subtract_fusion.9), channel_id=1, source_target_pairs={{0,2},{2,0},{4,6},{6,4},{8,10},{10,8},{12,14},{14,12},{16,18},{18,... | collective-permute-start | bytes 1572872 | tf_op jit(solution)/shard_map/ppermute | solution.py:82
  26.9 8.3 %collective-permute-start.7 = (f32[256,256]{1,0:T(8,128)S(1)}, f32[256,256]{1,0:T(8,128)S(1)}, u32[]{:S(2)}, u32[]{:S(2)}) collective-permute-start(f32[256,256]{1,0:T(8,128)S(1)} %get-tuple-element.238), channel_id=1, source_target_pairs={{4,0},{12,8},{20,16},{28,24},{5,1},{13,9},{21,17},{29,25}} | collective-permute-start | bytes 786440 | tf_op jit(solution)/shard_map/ppermute | solution.py:66
  28.2 13.1 %collective-permute-start.8 = (f32[256,256]{1,0:T(8,128)S(1)}, f32[256,256]{1,0:T(8,128)}, u32[]{:S(2)}, u32[]{:S(2)}) collective-permute-start(f32[256,256]{1,0:T(8,128)S(1)} %fusion.36), channel_id=1, source_target_pairs={{4,0},{12,8},{20,16},{28,24},{5,1},{13,9},{21,17},{29,25}} | collective-permute-start | bytes 786440 | tf_op jit(solution)/shard_map/ppermute | solution.py:66
  29.5 11.8 %collective-permute-start.9 = (f32[256,256]{1,0:T(8,128)S(1)}, f32[256,256]{1,0:T(8,128)}, u32[]{:S(2)}, u32[]{:S(2)}) collective-permute-start(f32[256,256]{1,0:T(8,128)S(1)} %get-tuple-element.238), channel_id=1, source_target_pairs={{8,0},{24,16},{9,1},{25,17}} | collective-permute-start | bytes 786440 | tf_op jit(solution)/shard_map/ppermute | solution.py:66
  30.8 10.5 %collective-permute-start.10 = (f32[256,256]{1,0:T(8,128)S(1)}, f32[256,256]{1,0:T(8,128)}, u32[]{:S(2)}, u32[]{:S(2)}) collective-permute-start(f32[256,256]{1,0:T(8,128)S(1)} %fusion.36), channel_id=1, source_target_pairs={{8,0},{24,16},{9,1},{25,17}} | collective-permute-start | bytes 786440 | tf_op jit(solution)/shard_map/ppermute | solution.py:66
  35.2 1.3 %copy-start.6 = (f32[256,256]{1,0:T(8,128)}, f32[256,256]{1,0:T(8,128)S(1)}, u32[]{:S(2)}) copy-start(f32[256,256]{1,0:T(8,128)S(1)} %collective-permute-done.7) | copy-start | bytes 786436
  35.2 9.3 %collective-permute-start.11 = (f32[256,256]{1,0:T(8,128)S(1)}, f32[256,256]{1,0:T(8,128)}, u32[]{:S(2)}, u32[]{:S(2)}) collective-permute-start(f32[256,256]{1,0:T(8,128)S(1)} %get-tuple-element.238), channel_id=1, source_target_pairs={{16,0},{17,1}} | collective-permute-start | bytes 786440 | tf_op jit(solution)/shard_map/ppermute | solution.py:66
  36.5 10.7 %collective-permute-start.12 = (f32[256,256]{1,0:T(8,128)S(1)}, f32[256,256]{1,0:T(8,128)}, u32[]{:S(2)}, u32[]{:S(2)}) collective-permute-start(f32[256,256]{1,0:T(8,128)S(1)} %fusion.36), channel_id=1, source_target_pairs={{16,0},{17,1}} | collective-permute-start | bytes 786440 | tf_op jit(solution)/shard_map/ppermute | solution.py:66
  48.3 11.3 %collective-permute-start.13 = (f32[256,512]{1,0:T(8,128)}, f32[256,512]{1,0:T(8,128)S(1)}, u32[]{:S(2)}, u32[]{:S(2)}) collective-permute-start(f32[256,512]{1,0:T(8,128)} %copy.12), channel_id=1, source_target_pairs={{0,4},{4,0},{8,12},{12,8},{16,20},{20,16},{24,28},{28,24},{1,5},{5... | collective-permute-start | bytes 1572872 | tf_op jit(solution)/shard_map/ppermute | solution.py:82
  64.3 11.3 %collective-permute-start.14 = (f32[256,512]{1,0:T(8,128)}, f32[256,512]{1,0:T(8,128)S(1)}, u32[]{:S(2)}, u32[]{:S(2)}) collective-permute-start(f32[256,512]{1,0:T(8,128)} %copy.16), channel_id=1, source_target_pairs={{0,8},{8,0},{16,24},{24,16},{1,9},{9,1},{17,25},{25,17}} | collective-permute-start | bytes 1572872 | tf_op jit(solution)/shard_map/ppermute | solution.py:82
  79.2 2.9 %copy-start.1 = (f32[512,512]{1,0:T(8,128)S(1)}, f32[512,512]{1,0:T(8,128)}, u32[]{:S(2)}) copy-start(f32[512,512]{1,0:T(8,128)} %param.29) | copy-start | bytes 3145732
  80.2 12.3 %collective-permute-start.15 = (f32[256,512]{1,0:T(8,128)}, f32[256,512]{1,0:T(8,128)}, u32[]{:S(2)}, u32[]{:S(2)}) collective-permute-start(f32[256,512]{1,0:T(8,128)} %copy.20), channel_id=1, source_target_pairs={{0,16},{16,0},{1,17},{17,1}} | collective-permute-start | bytes 1572872 | tf_op jit(solution)/shard_map/ppermute | solution.py:82
  82.2 1.4 %copy-start.3 = (f32[256,512]{1,0:T(8,128)S(1)}, f32[256,512]{1,0:T(8,128)}, u32[]{:S(2)}) copy-start(f32[256,512]{1,0:T(8,128)} %copy.20) | copy-start | bytes 1572868
  92.5 1.8 %copy-start.4 = (f32[256,512]{1,0:T(8,128)S(1)}, f32[256,512]{1,0:T(8,128)}, u32[]{:S(2)}) copy-start(f32[256,512]{1,0:T(8,128)} %convolution_subtract_fusion.8) | copy-start | bytes 1572868

commit v2 on v1

v2 whole, which is shorter than its diff:
```python
import jax
import jax.numpy as jnp
from jax import lax
from jax.sharding import PartitionSpec as P


def product(left, right):
    return jnp.dot(left, right, precision=lax.Precision.HIGHEST, preferred_element_type=jnp.float32)


def product_left_t(left, right):
    return lax.dot_general(
        left,
        right,
        (((0,), (0,)), ((), ())),
        precision=lax.Precision.HIGHEST,
        preferred_element_type=jnp.float32,
    )


def unit_lower(raw):
    row_ids = lax.broadcasted_iota(jnp.int32, raw.shape, 0)
    col_ids = lax.broadcasted_iota(jnp.int32, raw.shape, 1)
    diagonal = jnp.where(row_ids == col_ids, 1.0, 0.0).astype(raw.dtype)
    return jnp.where(row_ids > col_ids, raw, 0.0) + diagonal


def col_gather(part):
    n_col = lax.axis_size("col")
    me = lax.axis_index("col")
    by_shift = [part]
    for shift in range(1, n_col):
        perm = [(i, (i + shift) % n_col) for i in range(n_col)]
        by_shift.append(lax.ppermute(part, "col", perm))
    stacked = jnp.stack(by_shift)
    blocks = [stacked[(me - b) % n_col] for b in range(n_col)]
    return jnp.concatenate(blocks, axis=1)


def on_device(slab, leaf_v, leaf_t, tree_v, tree_t):
    n_row = lax.axis_size("row")
    levels = n_row.bit_length() - 1
    position = lax.axis_index("row")
    rows = leaf_v.shape[0]
    width = leaf_t.shape[0]

    gathered = col_gather(jnp.concatenate([leaf_v, leaf_t, tree_v, tree_t], axis=0))
    leaf_full = gathered[:rows]
    leaf_tri = gathered[rows:rows + width]
    tree_full = gathered[rows + width:rows + 2 * width]
    tree_tri = gathered[rows + 2 * width:]

    leaf_vectors = unit_lower(leaf_full)
    leaf_factor = jnp.triu(leaf_tri)
    leaf_w = product_left_t(leaf_factor, product_left_t(leaf_vectors, slab))
    leafed = slab - product(leaf_vectors, leaf_w)
    current = leafed[:width]

    tree_vectors = jnp.triu(tree_full)
    tree_factor = jnp.triu(tree_tri)
    tree_joint = product(tree_vectors, tree_factor)
    own_pair = jnp.stack([tree_factor, tree_joint])

    partner_factors = []
    for level in range(levels):
        step = 1 << level
        pairs = [(i + step, i) for i in range(0, n_row, 2 * step)]
        partner_factors.append(lax.ppermute(own_pair, "row", pairs))

    zeros = jnp.zeros_like(tree_factor)
    result = current
    for level in range(levels):
        if level < 2:
            wanted = partner_factors[0] if level == 0 else partner_factors[1:]
            current, wanted = lax.optimization_barrier((current, wanted))
            if level == 0:
                partner_factors[0] = wanted
            else:
                partner_factors[1:] = wanted
        step = 1 << level
        phase = position % (2 * step)
        is_lower = phase == 0
        is_upper = phase == step
        their = partner_factors[level]
        first = jnp.where(is_lower, their[0], jnp.where(is_upper, tree_joint, zeros))
        second = jnp.where(is_lower, their[1], jnp.where(is_upper, tree_factor, zeros))
        pairs = []
        for i in range(0, n_row, 2 * step):
            pairs += [(i, i + step), (i + step, i)]
        received = lax.ppermute(current, "row", pairs)
        early = product_left_t(first, current)
        early, received = lax.optimization_barrier((early, received))
        update = early + product_left_t(second, received)
        result = jnp.where(is_upper, current - product(tree_vectors, update), result)
        current = jnp.where(is_lower, current - update, current)
    top = jnp.where(position == 0, current, result)
    return lax.dynamic_update_slice(leafed, top, (0, 0))


def solution(mesh):
    in_specs = (P("row", "col"), P("row", "col"), P("row", "col"), P("row", "col"), P("row", "col"))
    out_specs = P("row", "col")
    return jax.shard_map(
        on_device, mesh=mesh, in_specs=in_specs, out_specs=out_specs, check_vma=False
    )
```

time: 96.1 us -> 87.4 us (0.909)
  waiting for transfers between devices: 39.8 us -> 48.9 us
  starting transfers between devices: 22.3 us -> 15.3 us
  local copies, waits for them, and re-layouts: 9.84 us -> 5.29 us
  matrix products: 20.2 us -> 15.9 us
  other arithmetic: 2.38 us -> 1.21 us
    ppermute x12 -> x5, starting transfers between devices: 15.4 us -> 8.18 us  [the longest x4 5.14 us: on_device(): partner_factors.append(lax.ppermute(own_pair, 'row', pairs))]
    dot_general x10, matrix products: 17.8 us -> 11 us  [product_left_t(): lax.dot_general(left, right, (((0,), (0,)), ((), ())), precision=lax.Prec...]
    ppermute x12 -> x5, waiting for transfers between devices: 20.9 us -> 25.8 us  [the longest x1 14.7 us: col_gather(): by_shift.append(lax.ppermute(part, 'col', perm))]
    ppermute x4, waiting for transfers between devices: 18.9 us -> 23.1 us  [on_device(): received = lax.ppermute(current, 'row', pairs)]
    unnamed x20 -> x25, local copies, waits for them, and re-layouts: 1.97 us -> 5.24 us
    sub x3 -> x0, local copies, waits for them, and re-layouts: 2.67 us -> none  [lower_post(): return e - product_left_t(sj, r)]
    dot_general x3 -> x6, matrix products: 2.4 us -> 4.84 us  [product(): jnp.dot(left, right, precision=lax.Precision.HIGHEST, preferred_element_t...]
    another operation x3 -> x0, local copies, waits for them, and re-layouts: 2.22 us -> none
  transfers between devices with their start and end apart: 16 -> 9, of which waited for: 8 -> 6; matrix products, arithmetic and copies ran while one was open for 18% -> 12% of each run, Pallas kernels for 0% -> 0%
where the time goes in v2:
time: 87.4 us; the launch traced here: 86.9 us
  waiting for transfers between devices  48.9 us (56%)
  matrix products  15.9 us (18%)
  starting transfers between devices  15.3 us (18%)
  local copies, waits for them, and re-layouts  5.29 us (6%)
  other arithmetic  1.21 us (1%)
    ppermute x4, waiting for transfers between devices, on_device(): received = lax.ppermute(current, 'row', pairs)  23.1 us
    ppermute x1, waiting for transfers between devices, col_gather(): by_shift.append(lax.ppermute(part, 'col', perm))  14.7 us
    ppermute x4, waiting for transfers between devices, on_device(): partner_factors.append(lax.ppermute(own_pair, 'row', pairs))  11 us
    dot_general x10, matrix products, product_left_t(): lax.dot_general(left, right, (((0,), (0,)), ((), ())), precision=lax.Prec...  11 us
    ppermute x4, starting transfers between devices, on_device(): received = lax.ppermute(current, 'row', pairs)  7.15 us
    unnamed x25, local copies, waits for them, and re-layouts  5.24 us
    ppermute x4, starting transfers between devices, on_device(): partner_factors.append(lax.ppermute(own_pair, 'row', pairs))  5.14 us
    dot_general x6, matrix products, product(): jnp.dot(left, right, precision=lax.Precision.HIGHEST, preferred_element_t...  4.84 us
  transfers between devices with their start and end apart: 9, of which 6 were waited for; matrix products, arithmetic and copies ran while one was open for 12% of the time, Pallas kernels for 0%

profile of v2, /device:TPU:0, one launch (start us, length us, event | category | flops | bytes accessed | tf_op | source)
XLA Modules:
  0.0 86.9 jit_solution(169180674318700401)
XLA Ops:
  0.0 1.0 %constant_dynamic-update-slice_fusion.3 = f32[1280,128]{1,0:T(8,128)S(1)} fusion(f32[512,128]{1,0:T(8,128)} %param.6), kind=kLoop, calls=%fused_computation.108 | loop fusion | bytes 524288
  1.0 0.9 %constant_dynamic-update-slice_fusion.2 = f32[1280,128]{1,0:T(8,128)S(1)} fusion(f32[1280,128]{1,0:T(8,128)S(1)} %constant_dynamic-update-slice_fusion.3, f32[256,128]{1,0:T(8,128)} %param.7), kind=kLoop, calls=%fused_computation.107 | loop fusion | bytes 262144
  1.9 0.9 %constant_dynamic-update-slice_fusion.1 = f32[1280,128]{1,0:T(8,128)S(1)} fusion(f32[1280,128]{1,0:T(8,128)S(1)} %constant_dynamic-update-slice_fusion.2, f32[256,128]{1,0:T(8,128)} %param.8), kind=kLoop, calls=%fused_computation.106 | loop fusion | bytes 262144
  2.9 3.0 %collective-permute-start = (f32[1280,128]{1,0:T(8,128)S(1)}, f32[1280,128]{1,0:T(8,128)S(1)}, u32[]{:S(2)}, u32[]{:S(2)}) collective-permute-start(f32[1280,128]{1,0:T(8,128)S(1)} %constant_dynamic-update-slice_fusion), channel_id=1, source_target_pairs={{0,1},{1,0},{2,3},{3,2},{4,5},{5,4},{6,7},{7,6},{8,9},{9,8},{10,11... | collective-permute-start | bytes 1966088 | tf_op jit(solution)/shard_map/ppermute | solution.py:34
  5.9 14.7 %collective-permute-done = f32[1280,128]{1,0:T(8,128)S(1)} collective-permute-done((f32[1280,128]{1,0:T(8,128)S(1)}, f32[1280,128]{1,0:T(8,128)S(1)}, u32[]{:S(2)}, u32[]{:S(2)}) %collective-permute-start) | collective-permute-done | bytes 655392 | tf_op jit(solution)/shard_map/ppermute | solution.py:34
  21.4 0.8 pad_maximum_fusion
  22.3 1.3 %collective-permute-start.1 = (f32[2,256,256]{2,1,0:T(8,128)}, f32[2,256,256]{2,1,0:T(8,128)S(1)}, u32[]{:S(2)}, u32[]{:S(2)}) collective-permute-start(f32[2,256,256]{2,1,0:T(8,128)} %pad_maximum_fusion), channel_id=1, source_target_pairs={{2,0},{6,4},{10,8},{14,12},{18,16},{22,20},{26,24},{30,28},{3,1},{... | collective-permute-start | bytes 1572872 | tf_op jit(solution)/shard_map/ppermute | solution.py:68
  23.6 1.1 %fusion.85 = f32[256,512]{1,0:T(8,128)S(1)} fusion(f32[512,512]{1,0:T(8,128)S(1)} %copy-done.1, f32[1280,128]{1,0:T(8,128)S(1)} %get-tuple-element.36, f32[1280,128]{1,0:T(8,128)S(1)} %get-tuple-element.35), kind=kOutput, calls=%fused_computation.120 | convolution fusion | flops 806092800 | bytes 2883584 | tf_op jit(solution)/shard_map/dot_general | solution.py:12
  24.7 0.7 fusion.17
  25.4 1.0 %convolution_subtract_fusion = f32[512,512]{1,0:T(8,128)S(1)} fusion(f32[512,512]{1,0:T(8,128)S(1)} %copy-done.1, f32[256,512]{1,0:T(8,128)S(1)} %fusion.17, f32[1280,128]{1,0:T(8,128)S(1)} %get-tuple-element.36, f32[1280,128]{1,0:T(8,128)S(1)} %get-tuple-element.35), kind=kOutput, calls=%fused_computation.10 | convolution fusion | flops 806354944 | bytes 3932160 | tf_op jit(solution)/shard_map/dot_general | solution.py:8
  26.5 1.2 %collective-permute-start.2 = (f32[256,512]{1,0:T(8,128)S(1)}, f32[256,512]{1,0:T(8,128)}, u32[]{:S(2)}, u32[]{:S(2)}) collective-permute-start(f32[256,512]{1,0:T(8,128)S(1)} %slice.56), channel_id=1, source_target_pairs={{0,2},{2,0},{4,6},{6,4},{8,10},{10,8},{12,14},{14,12},{16,18},{18,... | collective-permute-start | bytes 1572872 | tf_op jit(solution)/shard_map/ppermute | solution.py:90
  27.7 1.3 %collective-permute-start.3 = (f32[2,256,256]{2,1,0:T(8,128)}, f32[2,256,256]{2,1,0:T(8,128)S(1)}, u32[]{:S(2)}, u32[]{:S(2)}) collective-permute-start(f32[2,256,256]{2,1,0:T(8,128)} %pad_maximum_fusion), channel_id=1, source_target_pairs={{4,0},{12,8},{20,16},{28,24},{5,1},{13,9},{21,17},{29,25}} | collective-permute-start | bytes 1572872 | tf_op jit(solution)/shard_map/ppermute | solution.py:68
  29.0 1.3 %collective-permute-start.4 = (f32[2,256,256]{2,1,0:T(8,128)}, f32[2,256,256]{2,1,0:T(8,128)S(1)}, u32[]{:S(2)}, u32[]{:S(2)}) collective-permute-start(f32[2,256,256]{2,1,0:T(8,128)} %pad_maximum_fusion), channel_id=1, source_target_pairs={{8,0},{24,16},{9,1},{25,17}} | collective-permute-start | bytes 1572872 | tf_op jit(solution)/shard_map/ppermute | solution.py:68
  30.3 1.3 %collective-permute-start.5 = (f32[2,256,256]{2,1,0:T(8,128)}, f32[2,256,256]{2,1,0:T(8,128)S(1)}, u32[]{:S(2)}, u32[]{:S(2)}) collective-permute-start(f32[2,256,256]{2,1,0:T(8,128)} %pad_maximum_fusion), channel_id=1, source_target_pairs={{16,0},{17,1}} | collective-permute-start | bytes 1572872 | tf_op jit(solution)/shard_map/ppermute | solution.py:68
  31.6 0.6 fusion.27
  32.3 2.6 %subtract_select_fusion.3 = (f32[256,512]{1,0:T(8,128)S(1)}, f32[256,512]{1,0:T(8,128)}) fusion(f32[256,512]{1,0:T(8,128)S(1)} %slice.56, pred[]{:T(512)S(6)} %eq.42, f32[256,512]{1,0:T(8,128)S(1)} %fusion.27, f32[256,512]{1,0:T(8,128)} %collective-permute-done.2, f32[256,256]{1,0:T(8,128)S(1)} %get-tuple-element.33, f32[2,256,256]{2,1,0:T(8,128)} %copy-done.7, ...), kind=kOutput, calls=%fused_computation.24 | convolution fusion | flops 403177472 | bytes 3147264 | tf_op jit(solution)/shard_map/dot_general | solution.py:12
  34.9 4.1 %collective-permute-done.3 = f32[2,256,256]{2,1,0:T(8,128)S(1)} collective-permute-done((f32[2,256,256]{2,1,0:T(8,128)}, f32[2,256,256]{2,1,0:T(8,128)S(1)}, u32[]{:S(2)}, u32[]{:S(2)}) %collective-permute-start.3) | collective-permute-done | bytes 524320 | tf_op jit(solution)/shard_map/ppermute | solution.py:68
  39.0 6.9 %collective-permute-done.4 = f32[2,256,256]{2,1,0:T(8,128)S(1)} collective-permute-done((f32[2,256,256]{2,1,0:T(8,128)}, f32[2,256,256]{2,1,0:T(8,128)S(1)}, u32[]{:S(2)}, u32[]{:S(2)}) %collective-permute-start.4) | collective-permute-done | bytes 524320 | tf_op jit(solution)/shard_map/ppermute | solution.py:68
  45.9 0.8 copy-done.3
  46.7 0.8 copy-done.8
  47.5 1.9 %collective-permute-start.6 = (f32[256,512]{1,0:T(8,128)S(1)}, f32[256,512]{1,0:T(8,128)}, u32[]{:S(2)}, u32[]{:S(2)}) collective-permute-start(f32[256,512]{1,0:T(8,128)S(1)} %get-tuple-element.23), channel_id=1, source_target_pairs={{0,4},{4,0},{8,12},{12,8},{16,20},{20,16},{24,28},{28,24},{1,5},{5... | collective-permute-start | bytes 1572872 | tf_op jit(solution)/shard_map/ppermute | solution.py:90
  49.5 1.7 %fusion.25 = f32[256,512]{1,0:T(8,128)S(1)} fusion(f32[256,512]{1,0:T(8,128)S(1)} %get-tuple-element.23, f32[256,256]{1,0:T(8,128)S(1)} %fusion.87, f32[2,256,256]{2,1,0:T(8,128)} %copy-done.5, pred[]{:T(512)S(6)} %eq.44, pred[]{:T(512)S(6)} %eq.41), kind=kOutput, calls=%fused_computation.53 | convolution fusion | flops 402784256 | bytes 1572866 | tf_op jit(solution)/shard_map/dot_general | solution.py:12
  51.2 7.5 %collective-permute-done.6 = f32[256,512]{1,0:T(8,128)} collective-permute-done((f32[256,512]{1,0:T(8,128)S(1)}, f32[256,512]{1,0:T(8,128)}, u32[]{:S(2)}, u32[]{:S(2)}) %collective-permute-start.6) | collective-permute-done | bytes 524320 | tf_op jit(solution)/shard_map/ppermute | solution.py:90
  58.7 1.7 %subtract_select_fusion.2 = (f32[256,512]{1,0:T(8,128)S(1)}, f32[256,512]{1,0:T(8,128)S(1)}) fusion(f32[256,512]{1,0:T(8,128)S(1)} %get-tuple-element.23, pred[]{:T(512)S(6)} %eq.41, f32[256,512]{1,0:T(8,128)S(1)} %fusion.25, f32[256,512]{1,0:T(8,128)} %collective-permute-done.6, f32[256,256]{1,0:T(8,128)S(1)} %get-tuple-element.33, ...), kind=kOutput, calls=%fused_computation.23 | convolution fusion | flops 403177472 | bytes 3147264 | tf_op jit(solution)/shard_map/dot_general | solution.py:12
  60.4 1.9 %collective-permute-start.7 = (f32[256,512]{1,0:T(8,128)S(1)}, f32[256,512]{1,0:T(8,128)S(1)}, u32[]{:S(2)}, u32[]{:S(2)}) collective-permute-start(f32[256,512]{1,0:T(8,128)S(1)} %get-tuple-element.39), channel_id=1, source_target_pairs={{0,8},{8,0},{16,24},{24,16},{1,9},{9,1},{17,25},{25,17}} | collective-permute-start | bytes 1572872 | tf_op jit(solution)/shard_map/ppermute | solution.py:90
  63.4 0.6 fusion.23
  64.0 7.4 %collective-permute-done.7 = f32[256,512]{1,0:T(8,128)S(1)} collective-permute-done((f32[256,512]{1,0:T(8,128)S(1)}, f32[256,512]{1,0:T(8,128)S(1)}, u32[]{:S(2)}, u32[]{:S(2)}) %collective-permute-start.7) | collective-permute-done | bytes 524320 | tf_op jit(solution)/shard_map/ppermute | solution.py:90
  71.5 0.7 subtract_select_fusion.1
  72.2 2.1 %collective-permute-start.8 = (f32[256,512]{1,0:T(8,128)S(1)}, f32[256,512]{1,0:T(8,128)S(1)}, u32[]{:S(2)}, u32[]{:S(2)}) collective-permute-start(f32[256,512]{1,0:T(8,128)S(1)} %get-tuple-element.41), channel_id=1, source_target_pairs={{0,16},{16,0},{1,17},{17,1}} | collective-permute-start | bytes 1572872 | tf_op jit(solution)/shard_map/ppermute | solution.py:90
  76.0 8.2 %collective-permute-done.8 = f32[256,512]{1,0:T(8,128)S(1)} collective-permute-done((f32[256,512]{1,0:T(8,128)S(1)}, f32[256,512]{1,0:T(8,128)S(1)}, u32[]{:S(2)}, u32[]{:S(2)}) %collective-permute-start.8) | collective-permute-done | bytes 524320 | tf_op jit(solution)/shard_map/ppermute | solution.py:90
  84.1 0.6 fusion.20
  85.4 1.5 %fusion.5 = f32[512,512]{1,0:T(8,128)} fusion(f32[512,512]{1,0:T(8,128)} %copy-done, f32[256,512]{1,0:T(8,128)S(1)} %convolution_subtract_fusion.4, f32[256,512]{1,0:T(8,128)S(1)} %fusion.1, f32[256,512]{1,0:T(8,128)S(1)} %get-tuple-element.39, f32[256,256]{1,0:T(8,128)S(1)} %get-tuple-element.34, f32[256,512]{1,0:T(8,128)S(1)} %get-tuple-element.41, ...), kind=kOutput, calls=%fused_computation.19 | convolution fusion | flops 403701760 | bytes 4980740 | tf_op jit(solution)/shard_map/dot_general | solution.py:8
  (33 shorter events, 4.2 us)
Async XLA Ops:
  0.0 2.8 %copy-start.10 = (f32[256,128]{1,0:T(8,128)S(1)}, f32[256,128]{1,0:T(8,128)}, u32[]{:S(2)}) copy-start(f32[256,128]{1,0:T(8,128)} %param.9) | copy-start | bytes 393220
  2.9 17.8 %collective-permute-start = (f32[1280,128]{1,0:T(8,128)S(1)}, f32[1280,128]{1,0:T(8,128)S(1)}, u32[]{:S(2)}, u32[]{:S(2)}) collective-permute-start(f32[1280,128]{1,0:T(8,128)S(1)} %constant_dynamic-update-slice_fusion), channel_id=1, source_target_pairs={{0,1},{1,0},{2,3},{3,2},{4,5},{5,4},{6,7},{7,6},{8,9},{9,8},{10,11... | collective-permute-start | bytes 1966088 | tf_op jit(solution)/shard_map/ppermute | solution.py:34
  21.0 2.5 %copy-start.1 = (f32[512,512]{1,0:T(8,128)S(1)}, f32[512,512]{1,0:T(8,128)}, u32[]{:S(2)}) copy-start(f32[512,512]{1,0:T(8,128)} %param.5) | copy-start | bytes 3145732
  22.3 4.2 %collective-permute-start.1 = (f32[2,256,256]{2,1,0:T(8,128)}, f32[2,256,256]{2,1,0:T(8,128)S(1)}, u32[]{:S(2)}, u32[]{:S(2)}) collective-permute-start(f32[2,256,256]{2,1,0:T(8,128)} %pad_maximum_fusion), channel_id=1, source_target_pairs={{2,0},{6,4},{10,8},{14,12},{18,16},{22,20},{26,24},{30,28},{3,1},{... | collective-permute-start | bytes 1572872 | tf_op jit(solution)/shard_map/ppermute | solution.py:68
  26.4 35.9 %copy-start = (f32[512,512]{1,0:T(8,128)}, f32[512,512]{1,0:T(8,128)S(1)}, u32[]{:S(2)}) copy-start(f32[512,512]{1,0:T(8,128)S(1)} %convolution_subtract_fusion) | copy-start | bytes 3145732
  26.5 5.8 %copy-start.7 = (f32[2,256,256]{2,1,0:T(8,128)}, f32[2,256,256]{2,1,0:T(8,128)S(1)}, u32[]{:S(2)}) copy-start(f32[2,256,256]{2,1,0:T(8,128)S(1)} %collective-permute-done.1) | copy-start | bytes 1572868
  26.5 5.8 %collective-permute-start.2 = (f32[256,512]{1,0:T(8,128)S(1)}, f32[256,512]{1,0:T(8,128)}, u32[]{:S(2)}, u32[]{:S(2)}) collective-permute-start(f32[256,512]{1,0:T(8,128)S(1)} %slice.56), channel_id=1, source_target_pairs={{0,2},{2,0},{4,6},{6,4},{8,10},{10,8},{12,14},{14,12},{16,18},{18,... | collective-permute-start | bytes 1572872 | tf_op jit(solution)/shard_map/ppermute | solution.py:90
  27.7 11.3 %collective-permute-start.3 = (f32[2,256,256]{2,1,0:T(8,128)}, f32[2,256,256]{2,1,0:T(8,128)S(1)}, u32[]{:S(2)}, u32[]{:S(2)}) collective-permute-start(f32[2,256,256]{2,1,0:T(8,128)} %pad_maximum_fusion), channel_id=1, source_target_pairs={{4,0},{12,8},{20,16},{28,24},{5,1},{13,9},{21,17},{29,25}} | collective-permute-start | bytes 1572872 | tf_op jit(solution)/shard_map/ppermute | solution.py:68
  29.0 16.9 %collective-permute-start.4 = (f32[2,256,256]{2,1,0:T(8,128)}, f32[2,256,256]{2,1,0:T(8,128)S(1)}, u32[]{:S(2)}, u32[]{:S(2)}) collective-permute-start(f32[2,256,256]{2,1,0:T(8,128)} %pad_maximum_fusion), channel_id=1, source_target_pairs={{8,0},{24,16},{9,1},{25,17}} | collective-permute-start | bytes 1572872 | tf_op jit(solution)/shard_map/ppermute | solution.py:68
  30.3 15.6 %collective-permute-start.5 = (f32[2,256,256]{2,1,0:T(8,128)}, f32[2,256,256]{2,1,0:T(8,128)S(1)}, u32[]{:S(2)}, u32[]{:S(2)}) collective-permute-start(f32[2,256,256]{2,1,0:T(8,128)} %pad_maximum_fusion), channel_id=1, source_target_pairs={{16,0},{17,1}} | collective-permute-start | bytes 1572872 | tf_op jit(solution)/shard_map/ppermute | solution.py:68
  39.0 7.7 %copy-start.5 = (f32[2,256,256]{2,1,0:T(8,128)}, f32[2,256,256]{2,1,0:T(8,128)S(1)}, u32[]{:S(2)}) copy-start(f32[2,256,256]{2,1,0:T(8,128)S(1)} %collective-permute-done.3) | copy-start | bytes 1572868
  45.9 0.8 copy-start.3
  46.7 0.8 copy-start.8
  47.5 11.2 %collective-permute-start.6 = (f32[256,512]{1,0:T(8,128)S(1)}, f32[256,512]{1,0:T(8,128)}, u32[]{:S(2)}, u32[]{:S(2)}) collective-permute-start(f32[256,512]{1,0:T(8,128)S(1)} %get-tuple-element.23), channel_id=1, source_target_pairs={{0,4},{4,0},{8,12},{12,8},{16,20},{20,16},{24,28},{28,24},{1,5},{5... | collective-permute-start | bytes 1572872 | tf_op jit(solution)/shard_map/ppermute | solution.py:90
  49.5 9.2 %copy-start.6 = (f32[2,256,256]{2,1,0:T(8,128)S(1)}, f32[2,256,256]{2,1,0:T(8,128)}, u32[]{:S(2)}) copy-start(f32[2,256,256]{2,1,0:T(8,128)} %copy-done.5) | copy-start | bytes 1572868
  51.1 11.2 %copy-start.2 = (f32[256,512]{1,0:T(8,128)S(1)}, f32[256,512]{1,0:T(8,128)}, u32[]{:S(2)}) copy-start(f32[256,512]{1,0:T(8,128)} %get-tuple-element.38) | copy-start | bytes 1572868
  60.4 11.1 %collective-permute-start.7 = (f32[256,512]{1,0:T(8,128)S(1)}, f32[256,512]{1,0:T(8,128)S(1)}, u32[]{:S(2)}, u32[]{:S(2)}) collective-permute-start(f32[256,512]{1,0:T(8,128)S(1)} %get-tuple-element.39), channel_id=1, source_target_pairs={{0,8},{8,0},{16,24},{24,16},{1,9},{9,1},{17,25},{25,17}} | collective-permute-start | bytes 1572872 | tf_op jit(solution)/shard_map/ppermute | solution.py:90
  62.4 1.0 %copy-start.4 = (f32[2,256,256]{2,1,0:T(8,128)S(1)}, f32[2,256,256]{2,1,0:T(8,128)}, u32[]{:S(2)}) copy-start(f32[2,256,256]{2,1,0:T(8,128)} %copy-done.3) | copy-start | bytes 1572868
  72.2 12.0 %collective-permute-start.8 = (f32[256,512]{1,0:T(8,128)S(1)}, f32[256,512]{1,0:T(8,128)S(1)}, u32[]{:S(2)}, u32[]{:S(2)}) collective-permute-start(f32[256,512]{1,0:T(8,128)S(1)} %get-tuple-element.41), channel_id=1, source_target_pairs={{0,16},{16,0},{1,17},{17,1}} | collective-permute-start | bytes 1572872 | tf_op jit(solution)/shard_map/ppermute | solution.py:90
  74.3 1.0 %copy-start.9 = (f32[2,256,256]{2,1,0:T(8,128)S(1)}, f32[2,256,256]{2,1,0:T(8,128)}, u32[]{:S(2)}) copy-start(f32[2,256,256]{2,1,0:T(8,128)} %copy-done.8) | copy-start | bytes 1572868

commit v3 on v2

--- a/solution.py
+++ b/solution.py
@@ -59,41 +59,64 @@
     tree_vectors = jnp.triu(tree_full)
     tree_factor = jnp.triu(tree_tri)
     tree_joint = product(tree_vectors, tree_factor)
-    own_pair = jnp.stack([tree_factor, tree_joint])
+    own3 = jnp.stack([tree_vectors, tree_factor, tree_joint])
+
+    core = position % 2
+    base = position - core
+    cols = slab.shape[1]
+    half = cols // 2
+    swap = [(p, p ^ 1) for p in range(n_row)]
+    mate3 = lax.ppermute(own3, "row", swap)
+    odd3 = jnp.where(core == 1, own3, mate3)
+    even3 = jnp.where(core == 0, own3, mate3)
 
     partner_factors = []
-    for level in range(levels):
+    for level in range(1, levels):
         step = 1 << level
-        pairs = [(i + step, i) for i in range(0, n_row, 2 * step)]
-        partner_factors.append(lax.ppermute(own_pair, "row", pairs))
+        pairs = []
+        for i in range(0, n_row, 2 * step):
+            pairs += [(i + step, i), (i + step + 1, i + 1)]
+        partner_factors.append(lax.ppermute(even3[1:], "row", pairs))
+
+    is_lower = core == 0
+    received = lax.ppermute(current, "row", swap)
+    own_h = lax.dynamic_slice(current, (0, core * half), (width, half))
+    early = product_left_t(jnp.where(is_lower, odd3[1], odd3[2]), own_h)
+    early, received = lax.optimization_barrier((early, received))
+    recv_h = lax.dynamic_slice(received, (0, core * half), (width, half))
+    update = early + product_left_t(jnp.where(is_lower, odd3[2], odd3[1]), recv_h)
+    upper_h = jnp.where(is_lower, recv_h, own_h)
+    level0_out = upper_h - product(odd3[0], update)
+    chain = jnp.where(is_lower, own_h, recv_h) - update
 
     zeros = jnp.zeros_like(tree_factor)
-    result = current
-    for level in range(levels):
-        if level < 2:
-            wanted = partner_factors[0] if level == 0 else partner_factors[1:]
-            current, wanted = lax.optimization_barrier((current, wanted))
-            if level == 0:
-                partner_factors[0] = wanted
-            else:
-                partner_factors[1:] = wanted
+    result = chain
+    for level in range(1, levels):
+        if level == 1:
+            chain, partner_factors = lax.optimization_barrier((chain, partner_factors))
         step = 1 << level
-        phase = position % (2 * step)
+        phase = base % (2 * step)
         is_lower = phase == 0
         is_upper = phase == step
-        their = partner_factors[level]
-        first = jnp.where(is_lower, their[0], jnp.where(is_upper, tree_joint, zeros))
-        second = jnp.where(is_lower, their[1], jnp.where(is_upper, tree_factor, zeros))
+        their = partner_factors[level - 1]
+        first = jnp.where(is_lower, their[0], jnp.where(is_upper, even3[2], zeros))
+        second = jnp.where(is_lower, their[1], jnp.where(is_upper, even3[1], zeros))
         pairs = []
         for i in range(0, n_row, 2 * step):
-            pairs += [(i, i + step), (i + step, i)]
-        received = lax.ppermute(current, "row", pairs)
-        early = product_left_t(first, current)
+            for c in range(2):
+                pairs += [(i + c, i + step + c), (i + step + c, i + c)]
+        received = lax.ppermute(chain, "row", pairs)
+        early = product_left_t(first, chain)
         early, received = lax.optimization_barrier((early, received))
         update = early + product_left_t(second, received)
-        result = jnp.where(is_upper, current - product(tree_vectors, update), result)
-        current = jnp.where(is_lower, current - update, current)
-    top = jnp.where(position == 0, current, result)
+        result = jnp.where(is_upper, chain - product(even3[0], update), result)
+        chain = jnp.where(is_lower, chain - update, chain)
+    base_out = jnp.where(base == 0, chain, result)
+
+    keep = jnp.where(core == 0, base_out, level0_out)
+    give = jnp.where(core == 0, level0_out, base_out)
+    got = lax.ppermute(give, "row", swap)
+    top = jnp.concatenate([jnp.where(core == 0, keep, got), jnp.where(core == 0, got, keep)], axis=1)
     return lax.dynamic_update_slice(leafed, top, (0, 0))
 
 

time: 87.4 us -> 90.7 us (1.038)
  starting transfers between devices: 15.3 us -> 11.4 us
  matrix products: 15.9 us -> 19.2 us
  waiting for transfers between devices: 48.9 us -> 51.2 us
  local copies, waits for them, and re-layouts: 5.29 us -> 7.29 us
    ppermute x8 -> x9, starting transfers between devices: 12.3 us -> 8.42 us  [the longest x3 3.86 us: on_device(): partner_factors.append(lax.ppermute(even3[1:], 'row', pairs))]
    ppermute x8 -> x9, waiting for transfers between devices: 34.2 us -> 36.9 us  [the longest x3 21 us: on_device(): partner_factors.append(lax.ppermute(even3[1:], 'row', pairs))]
    dot_general x10, matrix products: 11 us -> 13.5 us  [product_left_t(): lax.dot_general(left, right, (((0,), (0,)), ((), ())), precision=lax.Prec...]
    unnamed x25 -> x18, local copies, waits for them, and re-layouts: 5.24 us -> 3.82 us
    dynamic_update_slice x0 -> x1, local copies, waits for them, and re-layouts: none -> 1.31 us  [on_device(): return lax.dynamic_update_slice(leafed, top, (0, 0))]
    optimization_barrier x0 -> x4, local copies, waits for them, and re-layouts: none -> 1.23 us  [on_device(): early, received = lax.optimization_barrier((early, received))]
  transfers between devices with their start and end apart: 9 -> 10, of which waited for: 6 -> 7; matrix products, arithmetic and copies ran while one was open for 12% -> 16% of each run, Pallas kernels for 0% -> 0%
where the time goes in v3:
time: 90.7 us; the launch traced here: 90.2 us
  waiting for transfers between devices  51.2 us (56%)
  matrix products  19.2 us (21%)
  starting transfers between devices  11.4 us (13%)
  local copies, waits for them, and re-layouts  7.29 us (8%)
    ppermute x3, waiting for transfers between devices, on_device(): partner_factors.append(lax.ppermute(even3[1:], 'row', pairs))  21 us
    ppermute x1, waiting for transfers between devices, col_gather(): by_shift.append(lax.ppermute(part, 'col', perm))  14.4 us
    ppermute x3, waiting for transfers between devices, on_device(): received = lax.ppermute(chain, 'row', pairs)  14.3 us
    dot_general x10, matrix products, product_left_t(): lax.dot_general(left, right, (((0,), (0,)), ((), ())), precision=lax.Prec...  13.5 us
    dot_general x6, matrix products, product(): jnp.dot(left, right, precision=lax.Precision.HIGHEST, preferred_element_t...  5.64 us
    ppermute x3, starting transfers between devices, on_device(): partner_factors.append(lax.ppermute(even3[1:], 'row', pairs))  3.86 us
    ppermute x3, starting transfers between devices, on_device(): received = lax.ppermute(chain, 'row', pairs)  3.85 us
    unnamed x18, local copies, waits for them, and re-layouts  3.82 us
  transfers between devices with their start and end apart: 10, of which 7 were waited for; matrix products, arithmetic and copies ran while one was open for 16% of the time, Pallas kernels for 0%

profile of v3, /device:TPU:0, one launch (start us, length us, event | category | flops | bytes accessed | tf_op | source)
XLA Modules:
  0.0 90.2 jit_solution(2616776272238461585)
XLA Ops:
  0.0 1.1 %constant_dynamic-update-slice_fusion.3 = f32[1280,128]{1,0:T(8,128)S(1)} fusion(f32[512,128]{1,0:T(8,128)} %param.6), kind=kLoop, calls=%fused_computation.129 | loop fusion | bytes 524288
  1.1 0.9 %constant_dynamic-update-slice_fusion.2 = f32[1280,128]{1,0:T(8,128)S(1)} fusion(f32[1280,128]{1,0:T(8,128)S(1)} %constant_dynamic-update-slice_fusion.3, f32[256,128]{1,0:T(8,128)} %param.7), kind=kLoop, calls=%fused_computation.128 | loop fusion | bytes 262144
  2.0 0.9 %constant_dynamic-update-slice_fusion.1 = f32[1280,128]{1,0:T(8,128)S(1)} fusion(f32[1280,128]{1,0:T(8,128)S(1)} %constant_dynamic-update-slice_fusion.2, f32[256,128]{1,0:T(8,128)} %param.8), kind=kLoop, calls=%fused_computation.127 | loop fusion | bytes 262144
  2.9 3.0 %collective-permute-start = (f32[1280,128]{1,0:T(8,128)S(1)}, f32[1280,128]{1,0:T(8,128)S(1)}, u32[]{:S(2)}, u32[]{:S(2)}) collective-permute-start(f32[1280,128]{1,0:T(8,128)S(1)} %constant_dynamic-update-slice_fusion), channel_id=1, source_target_pairs={{0,1},{1,0},{2,3},{3,2},{4,5},{5,4},{6,7},{7,6},{8,9},{9,8},{10,11... | collective-permute-start | bytes 1966088 | tf_op jit(solution)/shard_map/ppermute | solution.py:34
  6.3 14.4 %collective-permute-done = f32[1280,128]{1,0:T(8,128)S(1)} collective-permute-done((f32[1280,128]{1,0:T(8,128)S(1)}, f32[1280,128]{1,0:T(8,128)S(1)}, u32[]{:S(2)}, u32[]{:S(2)}) %collective-permute-start) | collective-permute-done | bytes 655392 | tf_op jit(solution)/shard_map/ppermute | solution.py:34
  21.6 1.1 %fusion.106 = f32[256,512]{1,0:T(8,128)S(1)} fusion(f32[512,512]{1,0:T(8,128)S(1)} %copy-done, f32[1280,128]{1,0:T(8,128)S(1)} %get-tuple-element.34, f32[1280,128]{1,0:T(8,128)S(1)} %get-tuple-element.33), kind=kOutput, calls=%fused_computation.141 | convolution fusion | flops 806092800 | bytes 2883584 | tf_op jit(solution)/shard_map/dot_general | solution.py:12
  22.8 0.7 fusion.15
  23.5 1.1 %convolution_subtract_fusion = f32[512,512]{0,1:T(8,128)S(1)} fusion(f32[512,512]{0,1:T(8,128)S(1)} %copy.6, f32[256,512]{1,0:T(8,128)S(1)} %fusion.15, f32[1280,128]{1,0:T(8,128)S(1)} %get-tuple-element.34, f32[1280,128]{1,0:T(8,128)S(1)} %get-tuple-element.33), kind=kOutput, calls=%fused_computation.10 | convolution fusion | flops 806354944 | bytes 3932160 | tf_op jit(solution)/shard_map/dot_general | solution.py:8
  25.3 0.9 slice.91
  26.2 1.3 %collective-permute-start.3 = (f32[2,256,256]{2,1,0:T(8,128)}, f32[2,256,256]{2,1,0:T(8,128)}, u32[]{:S(2)}, u32[]{:S(2)}) collective-permute-start(f32[2,256,256]{2,1,0:T(8,128)} %slice.91), channel_id=1, source_target_pairs={{4,0},{6,2},{12,8},{14,10},{20,16},{22,18},{28,24},{30,26},{5,1},{... | collective-permute-start | bytes 1572872 | tf_op jit(solution)/shard_map/ppermute | solution.py:79
  27.5 1.3 %collective-permute-start.4 = (f32[2,256,256]{2,1,0:T(8,128)}, f32[2,256,256]{2,1,0:T(8,128)}, u32[]{:S(2)}, u32[]{:S(2)}) collective-permute-start(f32[2,256,256]{2,1,0:T(8,128)} %slice.91), channel_id=1, source_target_pairs={{8,0},{10,2},{24,16},{26,18},{9,1},{11,3},{25,17},{27,19}} | collective-permute-start | bytes 1572872 | tf_op jit(solution)/shard_map/ppermute | solution.py:79
  28.8 1.3 %collective-permute-start.5 = (f32[2,256,256]{2,1,0:T(8,128)}, f32[2,256,256]{2,1,0:T(8,128)}, u32[]{:S(2)}, u32[]{:S(2)}) collective-permute-start(f32[2,256,256]{2,1,0:T(8,128)} %slice.91), channel_id=1, source_target_pairs={{16,0},{18,2},{17,1},{19,3}} | collective-permute-start | bytes 1572872 | tf_op jit(solution)/shard_map/ppermute | solution.py:79
  30.7 0.8 copy.7
  31.6 2.2 %select_subtract_fusion.1 = (f32[256,256]{0,1:T(8,128)S(1)}, f32[256,256]{0,1:T(8,128)}) fusion(f32[256,512]{0,1:T(8,128)} %collective-permute-done.2, s32[]{:T(128)S(6)} %select_n.255, f32[256,512]{0,1:T(8,128)S(1)} %slice.86, pred[]{:T(512)S(6)} %eq.43, f32[256,256]{0,1:T(8,128)} %copy.7, f32[3,256,256]{2,1,0:T(8,128)S(1)} %get-tuple-element.30), kind=kOutput, calls=%fused_computation.82 | convolution fusion | flops 201588736 | bytes 2099200 | tf_op jit(solution)/shard_map/dot_general | solution.py:12
  33.8 8.5 %collective-permute-done.3 = f32[2,256,256]{2,1,0:T(8,128)} collective-permute-done((f32[2,256,256]{2,1,0:T(8,128)}, f32[2,256,256]{2,1,0:T(8,128)}, u32[]{:S(2)}, u32[]{:S(2)}) %collective-permute-start.3) | collective-permute-done | bytes 524320 | tf_op jit(solution)/shard_map/ppermute | solution.py:79
  42.3 12.5 %collective-permute-done.4 = f32[2,256,256]{2,1,0:T(8,128)} collective-permute-done((f32[2,256,256]{2,1,0:T(8,128)}, f32[2,256,256]{2,1,0:T(8,128)}, u32[]{:S(2)}, u32[]{:S(2)}) %collective-permute-start.4) | collective-permute-done | bytes 524320 | tf_op jit(solution)/shard_map/ppermute | solution.py:79
  54.8 1.5 %fusion.29 = f32[256,256]{1,0:T(8,128)S(1)} fusion(f32[256,256]{0,1:T(8,128)S(1)} %get-tuple-element.19, f32[2,256,256]{2,1,0:T(8,128)} %collective-permute-done.3, f32[3,256,256]{2,1,0:T(8,128)S(1)} %get-tuple-element.29, pred[]{:T(512)S(6)} %eq.49, pred[]{:T(512)S(6)} %eq.47), kind=kOutput, calls=%fused_computation.55 | convolution fusion | flops 201457664 | bytes 1048578 | tf_op jit(solution)/shard_map/dot_general | solution.py:12
  56.4 5.8 %collective-permute-done.6 = f32[256,256]{0,1:T(8,128)S(1)} collective-permute-done((f32[256,256]{0,1:T(8,128)S(1)}, f32[256,256]{0,1:T(8,128)S(1)}, u32[]{:S(2)}, u32[]{:S(2)}) %collective-permute-start.6) | collective-permute-done | bytes 262176 | tf_op jit(solution)/shard_map/ppermute | solution.py:108
  62.3 1.4 %subtract_select_fusion.2 = (f32[256,256]{0,1:T(8,128)S(1)}, f32[256,256]{0,1:T(8,128)S(1)}) fusion(f32[256,256]{0,1:T(8,128)S(1)} %get-tuple-element.19, pred[]{:T(512)S(6)} %eq.47, f32[256,256]{0,1:T(8,128)S(1)} %copy.8, f32[256,256]{0,1:T(8,128)S(1)} %collective-permute-done.6, f32[2,256,256]{2,1,0:T(8,128)} %collective-permute-done.3, ...), kind=kOutput, calls=%fused_computation.32 | convolution fusion | flops 201654272 | bytes 1836544 | tf_op jit(solution)/shard_map/dot_general | solution.py:12
  63.7 1.9 %collective-permute-start.7 = (f32[256,256]{0,1:T(8,128)S(1)}, f32[256,256]{0,1:T(8,128)}, u32[]{:S(2)}, u32[]{:S(2)}) collective-permute-start(f32[256,256]{0,1:T(8,128)S(1)} %get-tuple-element.39), channel_id=1, source_target_pairs={{0,8},{8,0},{2,10},{10,2},{16,24},{24,16},{18,26},{26,18},{1,9},{9... | collective-permute-start | bytes 786440 | tf_op jit(solution)/shard_map/ppermute | solution.py:108
  65.6 1.5 %fusion.25 = f32[256,256]{1,0:T(8,128)S(1)} fusion(f32[256,256]{0,1:T(8,128)S(1)} %get-tuple-element.39, f32[2,256,256]{2,1,0:T(8,128)} %collective-permute-done.4, f32[3,256,256]{2,1,0:T(8,128)S(1)} %get-tuple-element.29, pred[]{:T(512)S(6)} %eq.50, pred[]{:T(512)S(6)} %eq.46), kind=kOutput, calls=%fused_computation.51 | convolution fusion | flops 201457664 | bytes 1048578 | tf_op jit(solution)/shard_map/dot_general | solution.py:12
  67.2 1.1 %fusion = f32[256,256]{0,1:T(8,128)} fusion(f32[256,256]{0,1:T(8,128)S(1)} %get-tuple-element.19, f32[3,256,256]{2,1,0:T(8,128)S(1)} %get-tuple-element.29, pred[]{:T(512)S(6)} %eq.49, f32[256,256]{0,1:T(8,128)S(1)} %copy.8, f32[256,256]{0,1:T(8,128)S(1)} %get-tuple-element.40), kind=kOutput, calls=%fused_computation.12 | convolution fusion | flops 201523200 | bytes 1310721 | tf_op jit(solution)/shard_map/dot_general | solution.py:8
  68.3 3.9 %collective-permute-done.7 = f32[256,256]{0,1:T(8,128)} collective-permute-done((f32[256,256]{0,1:T(8,128)S(1)}, f32[256,256]{0,1:T(8,128)}, u32[]{:S(2)}, u32[]{:S(2)}) %collective-permute-start.7) | collective-permute-done | bytes 262176 | tf_op jit(solution)/shard_map/ppermute | solution.py:108
  72.3 1.5 %subtract_select_fusion.1 = (f32[256,256]{0,1:T(8,128)S(1)}, f32[256,256]{0,1:T(8,128)S(1)}) fusion(f32[256,256]{0,1:T(8,128)S(1)} %get-tuple-element.39, pred[]{:T(512)S(6)} %eq.46, f32[256,256]{0,1:T(8,128)S(1)} %copy.9, f32[256,256]{0,1:T(8,128)} %collective-permute-done.7, f32[2,256,256]{2,1,0:T(8,128)} %collective-permute-done.4, ...), kind=kOutput, calls=%fused_computation.31 | convolution fusion | flops 201654272 | bytes 1836544 | tf_op jit(solution)/shard_map/dot_general | solution.py:12
  73.8 1.9 %collective-permute-start.8 = (f32[256,256]{0,1:T(8,128)S(1)}, f32[256,256]{0,1:T(8,128)}, u32[]{:S(2)}, u32[]{:S(2)}) collective-permute-start(f32[256,256]{0,1:T(8,128)S(1)} %get-tuple-element.41), channel_id=1, source_target_pairs={{0,16},{16,0},{2,18},{18,2},{1,17},{17,1},{3,19},{19,3}} | collective-permute-start | bytes 786440 | tf_op jit(solution)/shard_map/ppermute | solution.py:108
  75.7 1.5 %fusion.21 = f32[256,256]{1,0:T(8,128)S(1)} fusion(f32[256,256]{0,1:T(8,128)S(1)} %get-tuple-element.41, f32[2,256,256]{2,1,0:T(8,128)} %collective-permute-done.5, f32[3,256,256]{2,1,0:T(8,128)S(1)} %get-tuple-element.29, pred[]{:T(512)S(6)} %eq.51, pred[]{:T(512)S(6)} %eq.45), kind=kOutput, calls=%fused_computation.47 | convolution fusion | flops 201457664 | bytes 1048578 | tf_op jit(solution)/shard_map/dot_general | solution.py:12
  77.3 1.1 %fusion.1 = f32[256,256]{0,1:T(8,128)} fusion(f32[256,256]{0,1:T(8,128)S(1)} %copy-done.3, f32[256,256]{0,1:T(8,128)S(1)} %get-tuple-element.39, f32[3,256,256]{2,1,0:T(8,128)S(1)} %get-tuple-element.29, pred[]{:T(512)S(6)} %eq.50, f32[256,256]{0,1:T(8,128)S(1)} %copy.9, f32[256,256]{0,1:T(8,128)S(1)} %get-tuple-element.42), kind=kOutput, calls=%fused_computation.14 | convolution fusion | flops 201523200 | bytes 1572865 | tf_op jit(solution)/shard_map/dot_general | solution.py:8
  78.4 4.7 %collective-permute-done.8 = f32[256,256]{0,1:T(8,128)} collective-permute-done((f32[256,256]{0,1:T(8,128)S(1)}, f32[256,256]{0,1:T(8,128)}, u32[]{:S(2)}, u32[]{:S(2)}) %collective-permute-start.8) | collective-permute-done | bytes 262176 | tf_op jit(solution)/shard_map/ppermute | solution.py:108
  83.2 1.4 %fusion.19 = f32[256,256]{0,1:T(8,128)S(1)} fusion(f32[256,256]{0,1:T(8,128)} %collective-permute-done.8, f32[2,256,256]{2,1,0:T(8,128)} %collective-permute-done.5, f32[3,256,256]{2,1,0:T(8,128)S(1)} %get-tuple-element.29, pred[]{:T(512)S(6)} %eq.51, pred[]{:T(512)S(6)} %eq.45), kind=kOutput, calls=%fused_computation.45 | convolution fusion | flops 201457664 | bytes 1048578 | tf_op jit(solution)/shard_map/dot_general | solution.py:12
  85.7 1.5 %broadcast_select_fusion.4 = (f32[256,256]{0,1:T(8,128)S(1)}, f32[256,256]{0,1:T(8,128)S(1)}) fusion(f32[256,256]{0,1:T(8,128)S(1)} %fusion.3, pred[]{:T(512)S(6)} %eq.43, f32[256,256]{0,1:T(8,128)S(1)} %copy-done.2, f32[256,256]{0,1:T(8,128)S(1)} %copy-done.5, f32[3,256,256]{2,1,0:T(8,128)} %copy-done.1, f32[256,512]{0,1:T(8,128)S(1)} %slice.86, ...), kind=kOutput, calls=%fused_computation.121 | convolution fusion | flops 201588736 | bytes 2097157 | tf_op jit(solution)/shard_map/dot_general | solution.py:8
  87.2 1.5 %collective-permute-done.9 = f32[256,256]{0,1:T(8,128)S(1)} collective-permute-done((f32[256,256]{0,1:T(8,128)S(1)}, f32[256,256]{0,1:T(8,128)S(1)}, u32[]{:S(2)}, u32[]{:S(2)}) %collective-permute-start.9) | collective-permute-done | bytes 262176 | tf_op jit(solution)/shard_map/ppermute | solution.py:118
  88.9 1.3 %copy.11 = f32[512,512]{1,0:T(8,128)} copy(f32[512,512]{0,1:T(8,128)S(1)} %maximum_dynamic-update-slice_fusion) | data formatting | bytes 2097152 | tf_op jit(solution)/shard_map/dynamic_update_slice | solution.py:120
  (37 shorter events, 4.2 us)
Async XLA Ops:
  0.0 2.9 %copy-start.6 = (f32[256,128]{1,0:T(8,128)S(1)}, f32[256,128]{1,0:T(8,128)}, u32[]{:S(2)}) copy-start(f32[256,128]{1,0:T(8,128)} %param.9) | copy-start | bytes 393220
  0.0 6.0 %copy-start = (f32[512,512]{1,0:T(8,128)S(1)}, f32[512,512]{1,0:T(8,128)}, u32[]{:S(2)}) copy-start(f32[512,512]{1,0:T(8,128)} %param.5) | copy-start | bytes 3145732
  2.9 17.8 %collective-permute-start = (f32[1280,128]{1,0:T(8,128)S(1)}, f32[1280,128]{1,0:T(8,128)S(1)}, u32[]{:S(2)}, u32[]{:S(2)}) collective-permute-start(f32[1280,128]{1,0:T(8,128)S(1)} %constant_dynamic-update-slice_fusion), channel_id=1, source_target_pairs={{0,1},{1,0},{2,3},{3,2},{4,5},{5,4},{6,7},{7,6},{8,9},{9,8},{10,11... | collective-permute-start | bytes 1966088 | tf_op jit(solution)/shard_map/ppermute | solution.py:34
  21.6 3.6 %collective-permute-start.1 = (f32[3,256,256]{2,1,0:T(8,128)S(1)}, f32[3,256,256]{2,1,0:T(8,128)S(1)}, u32[]{:S(2)}, u32[]{:S(2)}) collective-permute-start(f32[3,256,256]{2,1,0:T(8,128)S(1)} %pad_maximum_fusion), channel_id=1, source_target_pairs={{0,2},{2,0},{4,6},{6,4},{8,10},{10,8},{12,14},{14,12},{16,18},{18,... | collective-permute-start | bytes 2359304 | tf_op jit(solution)/shard_map/ppermute | solution.py:69
  24.6 6.1 %collective-permute-start.2 = (f32[256,512]{0,1:T(8,128)S(1)}, f32[256,512]{0,1:T(8,128)}, u32[]{:S(2)}, u32[]{:S(2)}) collective-permute-start(f32[256,512]{0,1:T(8,128)S(1)} %slice.86), channel_id=1, source_target_pairs={{0,2},{2,0},{4,6},{6,4},{8,10},{10,8},{12,14},{14,12},{16,18},{18,... | collective-permute-start | bytes 1572872 | tf_op jit(solution)/shard_map/ppermute | solution.py:82
  25.3 6.3 %copy-start.1 = (f32[3,256,256]{2,1,0:T(8,128)}, f32[3,256,256]{2,1,0:T(8,128)S(1)}, u32[]{:S(2)}) copy-start(f32[3,256,256]{2,1,0:T(8,128)S(1)} %get-tuple-element.30) | copy-start | bytes 2359300
  26.2 16.1 %collective-permute-start.3 = (f32[2,256,256]{2,1,0:T(8,128)}, f32[2,256,256]{2,1,0:T(8,128)}, u32[]{:S(2)}, u32[]{:S(2)}) collective-permute-start(f32[2,256,256]{2,1,0:T(8,128)} %slice.91), channel_id=1, source_target_pairs={{4,0},{6,2},{12,8},{14,10},{20,16},{22,18},{28,24},{30,26},{5,1},{... | collective-permute-start | bytes 1572872 | tf_op jit(solution)/shard_map/ppermute | solution.py:79
  27.5 27.3 %collective-permute-start.4 = (f32[2,256,256]{2,1,0:T(8,128)}, f32[2,256,256]{2,1,0:T(8,128)}, u32[]{:S(2)}, u32[]{:S(2)}) collective-permute-start(f32[2,256,256]{2,1,0:T(8,128)} %slice.91), channel_id=1, source_target_pairs={{8,0},{10,2},{24,16},{26,18},{9,1},{11,3},{25,17},{27,19}} | collective-permute-start | bytes 1572872 | tf_op jit(solution)/shard_map/ppermute | solution.py:79
  28.8 26.0 %collective-permute-start.5 = (f32[2,256,256]{2,1,0:T(8,128)}, f32[2,256,256]{2,1,0:T(8,128)}, u32[]{:S(2)}, u32[]{:S(2)}) collective-permute-start(f32[2,256,256]{2,1,0:T(8,128)} %slice.91), channel_id=1, source_target_pairs={{16,0},{18,2},{17,1},{19,3}} | collective-permute-start | bytes 1572872 | tf_op jit(solution)/shard_map/ppermute | solution.py:79
  54.8 7.4 %collective-permute-start.6 = (f32[256,256]{0,1:T(8,128)S(1)}, f32[256,256]{0,1:T(8,128)S(1)}, u32[]{:S(2)}, u32[]{:S(2)}) collective-permute-start(f32[256,256]{0,1:T(8,128)S(1)} %get-tuple-element.19), channel_id=1, source_target_pairs={{0,4},{4,0},{2,6},{6,2},{8,12},{12,8},{10,14},{14,10},{16,20},{20,... | collective-permute-start | bytes 786440 | tf_op jit(solution)/shard_map/ppermute | solution.py:108
  63.7 8.5 %collective-permute-start.7 = (f32[256,256]{0,1:T(8,128)S(1)}, f32[256,256]{0,1:T(8,128)}, u32[]{:S(2)}, u32[]{:S(2)}) collective-permute-start(f32[256,256]{0,1:T(8,128)S(1)} %get-tuple-element.39), channel_id=1, source_target_pairs={{0,8},{8,0},{2,10},{10,2},{16,24},{24,16},{18,26},{26,18},{1,9},{9... | collective-permute-start | bytes 786440 | tf_op jit(solution)/shard_map/ppermute | solution.py:108
  72.3 5.0 %copy-start.3 = (f32[256,256]{0,1:T(8,128)S(1)}, f32[256,256]{0,1:T(8,128)}, u32[]{:S(2)}) copy-start(f32[256,256]{0,1:T(8,128)} %fusion) | copy-start | bytes 786436
  73.8 9.3 %collective-permute-start.8 = (f32[256,256]{0,1:T(8,128)S(1)}, f32[256,256]{0,1:T(8,128)}, u32[]{:S(2)}, u32[]{:S(2)}) collective-permute-start(f32[256,256]{0,1:T(8,128)S(1)} %get-tuple-element.41), channel_id=1, source_target_pairs={{0,16},{16,0},{2,18},{18,2},{1,17},{17,1},{3,19},{19,3}} | collective-permute-start | bytes 786440 | tf_op jit(solution)/shard_map/ppermute | solution.py:108
  78.4 6.2 %copy-start.4 = (f32[256,256]{0,1:T(8,128)S(1)}, f32[256,256]{0,1:T(8,128)}, u32[]{:S(2)}) copy-start(f32[256,256]{0,1:T(8,128)} %fusion.1) | copy-start | bytes 786436
  84.7 1.0 %copy-start.2 = (f32[256,256]{0,1:T(8,128)S(1)}, f32[256,256]{0,1:T(8,128)}, u32[]{:S(2)}) copy-start(f32[256,256]{0,1:T(8,128)} %copy.7) | copy-start | bytes 786436
  84.7 1.0 %copy-start.5 = (f32[256,256]{0,1:T(8,128)S(1)}, f32[256,256]{0,1:T(8,128)}, u32[]{:S(2)}) copy-start(f32[256,256]{0,1:T(8,128)} %get-tuple-element.38) | copy-start | bytes 786436
  87.2 1.6 %collective-permute-start.9 = (f32[256,256]{0,1:T(8,128)S(1)}, f32[256,256]{0,1:T(8,128)S(1)}, u32[]{:S(2)}, u32[]{:S(2)}) collective-permute-start(f32[256,256]{0,1:T(8,128)S(1)} %get-tuple-element.43), channel_id=1, source_target_pairs={{0,2},{2,0},{4,6},{6,4},{8,10},{10,8},{12,14},{14,12},{16,18},{18,... | collective-permute-start | bytes 786440 | tf_op jit(solution)/shard_map/ppermute | solution.py:118

commit v4 on v3

--- a/solution.py
+++ b/solution.py
@@ -70,13 +70,25 @@
     odd3 = jnp.where(core == 1, own3, mate3)
     even3 = jnp.where(core == 0, own3, mate3)
 
+    row_ids = lax.broadcasted_iota(jnp.int32, tree_factor.shape, 0)
+    col_ids = lax.broadcasted_iota(jnp.int32, tree_factor.shape, 1)
+    even_s, even_m = even3[1], even3[2]
+    packed = jnp.where(row_ids <= col_ids, even_s, even_m.T)
+    diag_m = jnp.sum(jnp.where(row_ids == col_ids, even_m, 0.0), axis=0, keepdims=True)
+    packed = jnp.concatenate([packed, jnp.broadcast_to(diag_m, (8, width))], axis=0)
     partner_factors = []
     for level in range(1, levels):
         step = 1 << level
         pairs = []
         for i in range(0, n_row, 2 * step):
             pairs += [(i + step, i), (i + step + 1, i + 1)]
-        partner_factors.append(lax.ppermute(even3[1:], "row", pairs))
+        partner_factors.append(lax.ppermute(packed, "row", pairs))
+
+    def unpack(got):
+        square = got[:width]
+        their_s = jnp.where(row_ids <= col_ids, square, 0.0)
+        their_m = jnp.where(row_ids < col_ids, square.T, jnp.where(row_ids == col_ids, got[width:width + 1], 0.0))
+        return their_s, their_m
 
     is_lower = core == 0
     received = lax.ppermute(current, "row", swap)
@@ -93,12 +105,15 @@
     result = chain
     for level in range(1, levels):
         if level == 1:
-            chain, partner_factors = lax.optimization_barrier((chain, partner_factors))
+            chain, partner_factors[0] = lax.optimization_barrier((chain, partner_factors[0]))
+        if level == 2:
+            chain, rest = lax.optimization_barrier((chain, partner_factors[1:]))
+            partner_factors[1:] = rest
         step = 1 << level
         phase = base % (2 * step)
         is_lower = phase == 0
         is_upper = phase == step
-        their = partner_factors[level - 1]
+        their = unpack(partner_factors[level - 1])
         first = jnp.where(is_lower, their[0], jnp.where(is_upper, even3[2], zeros))
         second = jnp.where(is_lower, their[1], jnp.where(is_upper, even3[1], zeros))
         pairs = []
@@ -117,7 +132,7 @@
     give = jnp.where(core == 0, level0_out, base_out)
     got = lax.ppermute(give, "row", swap)
     top = jnp.concatenate([jnp.where(core == 0, keep, got), jnp.where(core == 0, got, keep)], axis=1)
-    return lax.dynamic_update_slice(leafed, top, (0, 0))
+    return jnp.concatenate([top, leafed[width:]], axis=0)
 
 
 def solution(mesh):

time: 90.7 us -> 79.5 us (0.88)
  waiting for transfers between devices: 51.2 us -> 36 us
  starting transfers between devices: 11.4 us -> 17.1 us
  matrix products: 19.2 us -> 14.9 us
  other arithmetic: 0.66 us -> 2.52 us
    ppermute x3, waiting for transfers between devices: 21 us -> 8.61 us  [on_device(): partner_factors.append(lax.ppermute(packed, 'row', pairs))]
    ppermute x3, starting transfers between devices: 3.85 us -> 9.5 us  [on_device(): received = lax.ppermute(chain, 'row', pairs)]
    ppermute x3, waiting for transfers between devices: 14.3 us -> 11.2 us  [on_device(): received = lax.ppermute(chain, 'row', pairs)]
    slice x1 -> x5, local copies, waits for them, and re-layouts: 0.88 us -> 3.95 us  [the longest x3 2.13 us: unpack(): got[width:width + 1]]
    dot_general x10, matrix products: 13.5 us -> 10.9 us  [product_left_t(): lax.dot_general(left, right, (((0,), (0,)), ((), ())), precision=lax.Prec...]
    concatenate x0 -> x2, other arithmetic: none -> 1.85 us  [the longest x1 1.07 us: on_device(): return jnp.concatenate([top, leafed[width:]], axis=0)]
    dot_general x6, matrix products: 5.64 us -> 4.04 us  [product(): jnp.dot(left, right, precision=lax.Precision.HIGHEST, preferred_element_t...]
    dynamic_update_slice x1 -> x0, local copies, waits for them, and re-layouts: 1.31 us -> none  [on_device(): return lax.dynamic_update_slice(leafed, top, (0, 0))]
  transfers between devices with their start and end apart: 10 -> 10, of which waited for: 7 -> 6; matrix products, arithmetic and copies ran while one was open for 16% -> 17% of each run, Pallas kernels for 0% -> 0%
where the time goes in v4:
time: 79.5 us; the launch traced here: 78.9 us
  waiting for transfers between devices  36 us (45%)
  starting transfers between devices  17.1 us (22%)
  matrix products  14.9 us (19%)
  local copies, waits for them, and re-layouts  8.06 us (10%)
  other arithmetic  2.52 us (3%)
    ppermute x1, waiting for transfers between devices, col_gather(): by_shift.append(lax.ppermute(part, 'col', perm))  14.7 us
    ppermute x3, waiting for transfers between devices, on_device(): received = lax.ppermute(chain, 'row', pairs)  11.2 us
    dot_general x10, matrix products, product_left_t(): lax.dot_general(left, right, (((0,), (0,)), ((), ())), precision=lax.Prec...  10.9 us
    ppermute x3, starting transfers between devices, on_device(): received = lax.ppermute(chain, 'row', pairs)  9.5 us
    ppermute x3, waiting for transfers between devices, on_device(): partner_factors.append(lax.ppermute(packed, 'row', pairs))  8.61 us
    dot_general x6, matrix products, product(): jnp.dot(left, right, precision=lax.Precision.HIGHEST, preferred_element_t...  4.04 us
    ppermute x3, starting transfers between devices, on_device(): partner_factors.append(lax.ppermute(packed, 'row', pairs))  3.86 us
    unnamed x7, local copies, waits for them, and re-layouts  3.8 us
  transfers between devices with their start and end apart: 10, of which 6 were waited for; matrix products, arithmetic and copies ran while one was open for 17% of the time, Pallas kernels for 0%

profile of v4, /device:TPU:0, one launch (start us, length us, event | category | flops | bytes accessed | tf_op | source)
XLA Modules:
  0.0 78.9 jit_solution(14421717835043067181)
XLA Ops:
  0.0 1.0 %constant_dynamic-update-slice_fusion.3 = f32[1280,128]{1,0:T(8,128)S(1)} fusion(f32[512,128]{1,0:T(8,128)} %param.6), kind=kLoop, calls=%fused_computation.140 | loop fusion | bytes 524288
  1.0 0.9 %constant_dynamic-update-slice_fusion.2 = f32[1280,128]{1,0:T(8,128)S(1)} fusion(f32[1280,128]{1,0:T(8,128)S(1)} %constant_dynamic-update-slice_fusion.3, f32[256,128]{1,0:T(8,128)} %param.7), kind=kLoop, calls=%fused_computation.139 | loop fusion | bytes 262144
  1.9 0.9 %constant_dynamic-update-slice_fusion.1 = f32[1280,128]{1,0:T(8,128)S(1)} fusion(f32[1280,128]{1,0:T(8,128)S(1)} %constant_dynamic-update-slice_fusion.2, f32[256,128]{1,0:T(8,128)} %param.8), kind=kLoop, calls=%fused_computation.138 | loop fusion | bytes 262144
  2.9 3.0 %collective-permute-start = (f32[1280,128]{1,0:T(8,128)S(1)}, f32[1280,128]{1,0:T(8,128)S(1)}, u32[]{:S(2)}, u32[]{:S(2)}) collective-permute-start(f32[1280,128]{1,0:T(8,128)S(1)} %constant_dynamic-update-slice_fusion), channel_id=1, source_target_pairs={{0,1},{1,0},{2,3},{3,2},{4,5},{5,4},{6,7},{7,6},{8,9},{9,8},{10,11... | collective-permute-start | bytes 1966088 | tf_op jit(solution)/shard_map/ppermute | solution.py:34
  5.9 14.7 %collective-permute-done = f32[1280,128]{1,0:T(8,128)S(1)} collective-permute-done((f32[1280,128]{1,0:T(8,128)S(1)}, f32[1280,128]{1,0:T(8,128)S(1)}, u32[]{:S(2)}, u32[]{:S(2)}) %collective-permute-start) | collective-permute-done | bytes 655392 | tf_op jit(solution)/shard_map/ppermute | solution.py:34
  20.9 1.0 %copy-done = f32[512,512]{1,0:T(8,128)S(1)} copy-done((f32[512,512]{1,0:T(8,128)S(1)}, f32[512,512]{1,0:T(8,128)}, u32[]{:S(2)}) %copy-start) | copy-done | bytes 1048600
  21.9 1.1 %fusion.107 = f32[256,512]{1,0:T(8,128)S(1)} fusion(f32[512,512]{1,0:T(8,128)S(1)} %copy-done, f32[1280,128]{1,0:T(8,128)S(1)} %get-tuple-element.36, f32[1280,128]{1,0:T(8,128)S(1)} %get-tuple-element.35), kind=kOutput, calls=%fused_computation.152 | convolution fusion | flops 806092800 | bytes 2883584 | tf_op jit(solution)/shard_map/dot_general | solution.py:12
  23.6 0.7 fusion.15
  24.4 1.1 %convolution_subtract_fusion = f32[512,512]{1,0:T(8,128)S(1)} fusion(f32[512,512]{1,0:T(8,128)S(1)} %copy-done, f32[256,512]{1,0:T(8,128)S(1)} %fusion.15, f32[1280,128]{1,0:T(8,128)S(1)} %get-tuple-element.36, f32[1280,128]{1,0:T(8,128)S(1)} %get-tuple-element.35), kind=kOutput, calls=%fused_computation.10 | convolution fusion | flops 806354944 | bytes 3932160 | tf_op jit(solution)/shard_map/dot_general | solution.py:8
  26.2 0.7 fusion.112
  27.3 0.8 pad_maximum_fusion.2
  28.1 1.3 %collective-permute-start.6 = (f32[264,256]{0,1:T(8,128)}, f32[264,256]{0,1:T(8,128)}, u32[]{:S(2)}, u32[]{:S(2)}) collective-permute-start(f32[264,256]{0,1:T(8,128)} %pad_maximum_fusion.2), channel_id=1, source_target_pairs={{16,0},{18,2},{17,1},{19,3}} | collective-permute-start | bytes 811016 | tf_op jit(solution)/shard_map/ppermute | solution.py:85
  29.3 1.3 %collective-permute-start.5 = (f32[264,256]{0,1:T(8,128)}, f32[264,256]{0,1:T(8,128)S(1)}, u32[]{:S(2)}, u32[]{:S(2)}) collective-permute-start(f32[264,256]{0,1:T(8,128)} %pad_maximum_fusion.2), channel_id=1, source_target_pairs={{8,0},{10,2},{24,16},{26,18},{9,1},{11,3},{25,17},{27,19}} | collective-permute-start | bytes 811016 | tf_op jit(solution)/shard_map/ppermute | solution.py:85
  30.6 1.3 %collective-permute-start.3 = (f32[264,256]{0,1:T(8,128)}, f32[264,256]{0,1:T(8,128)}, u32[]{:S(2)}, u32[]{:S(2)}) collective-permute-start(f32[264,256]{0,1:T(8,128)} %pad_maximum_fusion.2), channel_id=1, source_target_pairs={{4,0},{6,2},{12,8},{14,10},{20,16},{22,18},{28,24},{30,26},{5,1},{... | collective-permute-start | bytes 811016 | tf_op jit(solution)/shard_map/ppermute | solution.py:85
  32.6 1.1 %copy.33 = f32[1,256,256]{1,2,0:T(8,128)S(1)} copy(f32[1,256,256]{2,1,0:T(8,128)} %get-tuple-element.41) | data formatting | bytes 524288 | tf_op jit(solution)/shard_map/slice | solution.py:75
  33.7 1.6 %select_subtract_fusion.1 = (f32[256,256]{1,0:T(8,128)S(1)}, f32[256,256]{1,0:T(8,128)S(1)}) fusion(f32[256,512]{1,0:T(8,128)} %collective-permute-done.2, s32[]{:T(128)S(6)} %select_n.255, f32[256,512]{1,0:T(8,128)S(1)} %get-tuple-element.37, pred[]{:T(512)S(6)} %eq.54, f32[256,256]{1,0:T(8,128)S(1)} %fusion.40, f32[3,256,256]{2,1,0:T(8,128)S(1)} %get-tuple-element.32), kind=kOutput, calls=%fused_computation.86 | convolution fusion | flops 201588736 | bytes 2099200 | tf_op jit(solution)/shard_map/dot_general | solution.py:12
  35.3 8.6 %collective-permute-done.3 = f32[264,256]{0,1:T(8,128)} collective-permute-done((f32[264,256]{0,1:T(8,128)}, f32[264,256]{0,1:T(8,128)}, u32[]{:S(2)}, u32[]{:S(2)}) %collective-permute-start.3) | collective-permute-done | bytes 270368 | tf_op jit(solution)/shard_map/ppermute | solution.py:85
  43.9 1.0 %slice_reduce_fusion.2 = f32[256]{0:T(256)S(1)} fusion(f32[264,256]{0,1:T(8,128)} %collective-permute-done.3), kind=kLoop, calls=%fused_computation.110 | loop fusion | bytes 2048 | tf_op jit(solution)/shard_map/slice | solution.py:90
  44.9 1.4 %fusion.36 = f32[256,256]{1,0:T(8,128)S(1)} fusion(f32[256,256]{1,0:T(8,128)S(1)} %get-tuple-element.20, f32[1,256,256]{1,2,0:T(8,128)S(1)} %copy.33, f32[264,256]{0,1:T(8,128)} %collective-permute-done.3, pred[]{:T(512)S(6)} %eq.62, pred[]{:T(512)S(6)} %eq.58), kind=kOutput, calls=%fused_computation.67 | convolution fusion | flops 201588736 | bytes 1048578 | tf_op jit(solution)/shard_map/dot_general | solution.py:12
  46.3 5.0 %collective-permute-done.4 = f32[256,256]{1,0:T(8,128)S(1)} collective-permute-done((f32[256,256]{1,0:T(8,128)S(1)}, f32[256,256]{1,0:T(8,128)S(1)}, u32[]{:S(2)}, u32[]{:S(2)}) %collective-permute-start.4) | collective-permute-done | bytes 262176 | tf_op jit(solution)/shard_map/ppermute | solution.py:123
  51.3 1.6 %subtract_select_fusion.2 = (f32[256,256]{1,0:T(8,128)S(1)}, f32[256,256]{1,0:T(8,128)S(1)}) fusion(f32[256,256]{1,0:T(8,128)S(1)} %get-tuple-element.20, pred[]{:T(512)S(6)} %eq.58, f32[256,256]{1,0:T(8,128)S(1)} %fusion.36, f32[256,256]{1,0:T(8,128)S(1)} %collective-permute-done.4, f32[264,256]{0,1:T(8,128)} %collective-permute-done.3, ...), kind=kOutput, calls=%fused_computation.32 | convolution fusion | flops 201916416 | bytes 1837568 | tf_op jit(solution)/shard_map/dot_general | solution.py:12
  53.0 1.0 %slice_reduce_fusion = f32[256]{0:T(256)S(1)} fusion(f32[264,256]{0,1:T(8,128)} %collective-permute-done.6), kind=kLoop, calls=%fused_computation.106 | loop fusion | bytes 2048 | tf_op jit(solution)/shard_map/slice | solution.py:90
  54.0 4.0 %collective-permute-start.7 = (f32[256,256]{1,0:T(8,128)S(1)}, f32[256,256]{1,0:T(8,128)S(1)}, u32[]{:S(2)}, u32[]{:S(2)}) collective-permute-start(f32[256,256]{1,0:T(8,128)S(1)} %get-tuple-element.24), channel_id=1, source_target_pairs={{0,8},{8,0},{2,10},{10,2},{16,24},{24,16},{18,26},{26,18},{1,9},{9... | collective-permute-start | bytes 786440 | tf_op jit(solution)/shard_map/ppermute | solution.py:123
  58.8 3.6 %collective-permute-done.7 = f32[256,256]{1,0:T(8,128)S(1)} collective-permute-done((f32[256,256]{1,0:T(8,128)S(1)}, f32[256,256]{1,0:T(8,128)S(1)}, u32[]{:S(2)}, u32[]{:S(2)}) %collective-permute-start.7) | collective-permute-done | bytes 262176 | tf_op jit(solution)/shard_map/ppermute | solution.py:123
  62.4 0.6 subtract_select_fusion.1
  63.0 5.5 %collective-permute-start.8 = (f32[256,256]{1,0:T(8,128)S(1)}, f32[256,256]{1,0:T(8,128)S(1)}, u32[]{:S(2)}, u32[]{:S(2)}) collective-permute-start(f32[256,256]{1,0:T(8,128)S(1)} %get-tuple-element.47), channel_id=1, source_target_pairs={{0,16},{16,0},{2,18},{18,2},{1,17},{17,1},{3,19},{19,3}} | collective-permute-start | bytes 786440 | tf_op jit(solution)/shard_map/ppermute | solution.py:123
  68.5 1.3 %fusion.30 = f32[256,256]{1,0:T(8,128)S(1)} fusion(f32[256,256]{1,0:T(8,128)S(1)} %get-tuple-element.47, f32[1,256,256]{1,2,0:T(8,128)S(1)} %copy.33, f32[264,256]{0,1:T(8,128)} %collective-permute-done.6, pred[]{:T(512)S(6)} %eq.56, pred[]{:T(512)S(6)} %eq.64), kind=kOutput, calls=%fused_computation.63 | convolution fusion | flops 201588736 | bytes 1048578 | tf_op jit(solution)/shard_map/dot_general | solution.py:12
  70.3 2.6 %collective-permute-done.8 = f32[256,256]{1,0:T(8,128)S(1)} collective-permute-done((f32[256,256]{1,0:T(8,128)S(1)}, f32[256,256]{1,0:T(8,128)S(1)}, u32[]{:S(2)}, u32[]{:S(2)}) %collective-permute-start.8) | collective-permute-done | bytes 262176 | tf_op jit(solution)/shard_map/ppermute | solution.py:123
  72.9 1.6 %fusion.20 = f32[256,256]{1,0:T(8,128)S(1)} fusion(f32[256,256]{1,0:T(8,128)S(1)} %collective-permute-done.8, f32[264,256]{0,1:T(8,128)} %collective-permute-done.6, f32[256]{0:T(256)S(1)} %slice_reduce_fusion, pred[]{:T(512)S(6)} %eq.64, pred[]{:T(512)S(6)} %eq.56, f32[3,256,256]{2,1,0:T(8,128)S(1)} %get-tuple-element.31), kind=kOutput, calls=%fused_computation.50 | convolution fusion | flops 201719808 | bytes 1049602 | tf_op jit(solution)/shard_map/dot_general | solution.py:12
  74.8 1.4 %broadcast_select_fusion.4 = (f32[256,256]{1,0:T(8,128)S(1)}, f32[256,256]{1,0:T(8,128)S(1)}) fusion(f32[256,256]{1,0:T(8,128)S(1)} %fusion.10, pred[]{:T(512)S(6)} %eq.54, f32[256,256]{1,0:T(8,128)S(1)} %fusion.40, f32[256,256]{1,0:T(8,128)S(1)} %get-tuple-element.44, f32[3,256,256]{2,1,0:T(8,128)S(1)} %get-tuple-element.32, ...), kind=kOutput, calls=%fused_computation.132 | convolution fusion | flops 201588736 | bytes 2097157 | tf_op jit(solution)/shard_map/dot_general | solution.py:8
  76.3 1.5 %collective-permute-done.9 = f32[256,256]{1,0:T(8,128)S(1)} collective-permute-done((f32[256,256]{1,0:T(8,128)S(1)}, f32[256,256]{1,0:T(8,128)S(1)}, u32[]{:S(2)}, u32[]{:S(2)}) %collective-permute-start.9) | collective-permute-done | bytes 262176 | tf_op jit(solution)/shard_map/ppermute | solution.py:133
  77.9 1.1 %pad_maximum_fusion = f32[512,512]{1,0:T(8,128)} fusion(f32[256,512]{1,0:T(8,128)S(1)} %get-tuple-element.38, f32[256,256]{1,0:T(8,128)S(1)} %get-tuple-element.40, f32[256,256]{1,0:T(8,128)S(1)} %get-tuple-element.39), kind=kLoop, calls=%fused_computation.18 | loop fusion | flops 524288 | bytes 2097152 | tf_op jit(solution)/shard_map/concatenate | solution.py:135
  (30 shorter events, 4.4 us)
Async XLA Ops:
  0.0 2.8 %copy-start.1 = (f32[256,128]{1,0:T(8,128)S(1)}, f32[256,128]{1,0:T(8,128)}, u32[]{:S(2)}) copy-start(f32[256,128]{1,0:T(8,128)} %param.9) | copy-start | bytes 393220
  2.9 17.8 %collective-permute-start = (f32[1280,128]{1,0:T(8,128)S(1)}, f32[1280,128]{1,0:T(8,128)S(1)}, u32[]{:S(2)}, u32[]{:S(2)}) collective-permute-start(f32[1280,128]{1,0:T(8,128)S(1)} %constant_dynamic-update-slice_fusion), channel_id=1, source_target_pairs={{0,1},{1,0},{2,3},{3,2},{4,5},{5,4},{6,7},{7,6},{8,9},{9,8},{10,11... | collective-permute-start | bytes 1966088 | tf_op jit(solution)/shard_map/ppermute | solution.py:34
  20.6 1.2 %copy-start = (f32[512,512]{1,0:T(8,128)S(1)}, f32[512,512]{1,0:T(8,128)}, u32[]{:S(2)}) copy-start(f32[512,512]{1,0:T(8,128)} %param.5) | copy-start | bytes 3145732
  23.6 2.5 %collective-permute-start.1 = (f32[3,256,256]{2,1,0:T(8,128)S(1)}, f32[3,256,256]{2,1,0:T(8,128)S(1)}, u32[]{:S(2)}, u32[]{:S(2)}) collective-permute-start(f32[3,256,256]{2,1,0:T(8,128)S(1)} %pad_maximum_fusion.1), channel_id=1, source_target_pairs={{0,2},{2,0},{4,6},{6,4},{8,10},{10,8},{12,14},{14,12},{16,18},{18,... | collective-permute-start | bytes 2359304 | tf_op jit(solution)/shard_map/ppermute | solution.py:69
  25.5 7.0 %collective-permute-start.2 = (f32[256,512]{1,0:T(8,128)S(1)}, f32[256,512]{1,0:T(8,128)}, u32[]{:S(2)}, u32[]{:S(2)}) collective-permute-start(f32[256,512]{1,0:T(8,128)S(1)} %get-tuple-element.37), channel_id=1, source_target_pairs={{0,2},{2,0},{4,6},{6,4},{8,10},{10,8},{12,14},{14,12},{16,18},{18,... | collective-permute-start | bytes 1572872 | tf_op jit(solution)/shard_map/ppermute | solution.py:94
  28.1 24.8 %collective-permute-start.6 = (f32[264,256]{0,1:T(8,128)}, f32[264,256]{0,1:T(8,128)}, u32[]{:S(2)}, u32[]{:S(2)}) collective-permute-start(f32[264,256]{0,1:T(8,128)} %pad_maximum_fusion.2), channel_id=1, source_target_pairs={{16,0},{18,2},{17,1},{19,3}} | collective-permute-start | bytes 811016 | tf_op jit(solution)/shard_map/ppermute | solution.py:85
  29.3 23.5 %collective-permute-start.5 = (f32[264,256]{0,1:T(8,128)}, f32[264,256]{0,1:T(8,128)S(1)}, u32[]{:S(2)}, u32[]{:S(2)}) collective-permute-start(f32[264,256]{0,1:T(8,128)} %pad_maximum_fusion.2), channel_id=1, source_target_pairs={{8,0},{10,2},{24,16},{26,18},{9,1},{11,3},{25,17},{27,19}} | collective-permute-start | bytes 811016 | tf_op jit(solution)/shard_map/ppermute | solution.py:85
  30.6 13.3 %collective-permute-start.3 = (f32[264,256]{0,1:T(8,128)}, f32[264,256]{0,1:T(8,128)}, u32[]{:S(2)}, u32[]{:S(2)}) collective-permute-start(f32[264,256]{0,1:T(8,128)} %pad_maximum_fusion.2), channel_id=1, source_target_pairs={{4,0},{6,2},{12,8},{14,10},{20,16},{22,18},{28,24},{30,26},{5,1},{... | collective-permute-start | bytes 811016 | tf_op jit(solution)/shard_map/ppermute | solution.py:85
  43.9 7.4 %collective-permute-start.4 = (f32[256,256]{1,0:T(8,128)S(1)}, f32[256,256]{1,0:T(8,128)S(1)}, u32[]{:S(2)}, u32[]{:S(2)}) collective-permute-start(f32[256,256]{1,0:T(8,128)S(1)} %get-tuple-element.20), channel_id=1, source_target_pairs={{0,4},{4,0},{2,6},{6,2},{8,12},{12,8},{10,14},{14,10},{16,20},{20,... | collective-permute-start | bytes 786440 | tf_op jit(solution)/shard_map/ppermute | solution.py:123
  54.0 8.4 %collective-permute-start.7 = (f32[256,256]{1,0:T(8,128)S(1)}, f32[256,256]{1,0:T(8,128)S(1)}, u32[]{:S(2)}, u32[]{:S(2)}) collective-permute-start(f32[256,256]{1,0:T(8,128)S(1)} %get-tuple-element.24), channel_id=1, source_target_pairs={{0,8},{8,0},{2,10},{10,2},{16,24},{24,16},{18,26},{26,18},{1,9},{9... | collective-permute-start | bytes 786440 | tf_op jit(solution)/shard_map/ppermute | solution.py:123
  63.0 9.9 %collective-permute-start.8 = (f32[256,256]{1,0:T(8,128)S(1)}, f32[256,256]{1,0:T(8,128)S(1)}, u32[]{:S(2)}, u32[]{:S(2)}) collective-permute-start(f32[256,256]{1,0:T(8,128)S(1)} %get-tuple-element.47), channel_id=1, source_target_pairs={{0,16},{16,0},{2,18},{18,2},{1,17},{17,1},{3,19},{19,3}} | collective-permute-start | bytes 786440 | tf_op jit(solution)/shard_map/ppermute | solution.py:123
  76.2 1.6 %collective-permute-start.9 = (f32[256,256]{1,0:T(8,128)S(1)}, f32[256,256]{1,0:T(8,128)S(1)}, u32[]{:S(2)}, u32[]{:S(2)}) collective-permute-start(f32[256,256]{1,0:T(8,128)S(1)} %get-tuple-element.49), channel_id=1, source_target_pairs={{0,2},{2,0},{4,6},{6,4},{8,10},{10,8},{12,14},{14,12},{16,18},{18,... | collective-permute-start | bytes 786440 | tf_op jit(solution)/shard_map/ppermute | solution.py:133

commit v5 on v4

--- a/solution.py
+++ b/solution.py
@@ -44,17 +44,13 @@
     rows = leaf_v.shape[0]
     width = leaf_t.shape[0]
 
-    gathered = col_gather(jnp.concatenate([leaf_v, leaf_t, tree_v, tree_t], axis=0))
-    leaf_full = gathered[:rows]
-    leaf_tri = gathered[rows:rows + width]
-    tree_full = gathered[rows + width:rows + 2 * width]
-    tree_tri = gathered[rows + 2 * width:]
-
-    leaf_vectors = unit_lower(leaf_full)
-    leaf_factor = jnp.triu(leaf_tri)
-    leaf_w = product_left_t(leaf_factor, product_left_t(leaf_vectors, slab))
-    leafed = slab - product(leaf_vectors, leaf_w)
-    current = leafed[:width]
+    tree_gathered = col_gather(jnp.concatenate([tree_v, tree_t], axis=0))
+    tree_gathered, leaf_v, leaf_t = lax.optimization_barrier((tree_gathered, leaf_v, leaf_t))
+    leaf_gathered = col_gather(jnp.concatenate([leaf_v, leaf_t], axis=0))
+    leaf_full = leaf_gathered[:rows]
+    leaf_tri = leaf_gathered[rows:]
+    tree_full = tree_gathered[:width]
+    tree_tri = tree_gathered[width:]
 
     tree_vectors = jnp.triu(tree_full)
     tree_factor = jnp.triu(tree_tri)
@@ -90,6 +86,13 @@
         their_m = jnp.where(row_ids < col_ids, square.T, jnp.where(row_ids == col_ids, got[width:width + 1], 0.0))
         return their_s, their_m
 
+    leaf_full, leaf_tri, partner_factors[0] = lax.optimization_barrier((leaf_full, leaf_tri, partner_factors[0]))
+    leaf_vectors = unit_lower(leaf_full)
+    leaf_factor = jnp.triu(leaf_tri)
+    leaf_w = product_left_t(leaf_factor, product_left_t(leaf_vectors, slab))
+    leafed = slab - product(leaf_vectors, leaf_w)
+    current = leafed[:width]
+
     is_lower = core == 0
     received = lax.ppermute(current, "row", swap)
     own_h = lax.dynamic_slice(current, (0, core * half), (width, half))
@@ -104,8 +107,6 @@
     zeros = jnp.zeros_like(tree_factor)
     result = chain
     for level in range(1, levels):
-        if level == 1:
-            chain, partner_factors[0] = lax.optimization_barrier((chain, partner_factors[0]))
         if level == 2:
             chain, rest = lax.optimization_barrier((chain, partner_factors[1:]))
             partner_factors[1:] = rest

time: 79.5 us -> 94.7 us (1.19)
  local copies, waits for them, and re-layouts: 8.06 us -> 18.5 us
  matrix products: 14.9 us -> 19.2 us
  starting transfers between devices: 17.1 us -> 14 us
  other arithmetic: 2.52 us -> 4.8 us
  waiting for transfers between devices: 36 us -> 37 us
    ppermute x1 -> x2, waiting for transfers between devices: 14.7 us -> 10.5 us  [col_gather(): by_shift.append(lax.ppermute(part, 'col', perm))]
    ppermute x3, starting transfers between devices: 9.5 us -> 5.31 us  [on_device(): received = lax.ppermute(chain, 'row', pairs)]
    dot_general x10, matrix products: 10.9 us -> 13.6 us  [product_left_t(): lax.dot_general(left, right, (((0,), (0,)), ((), ())), precision=lax.Prec...]
    ppermute x3, waiting for transfers between devices: 8.61 us -> 11.3 us  [on_device(): partner_factors.append(lax.ppermute(packed, 'row', pairs))]
    ppermute x3, waiting for transfers between devices: 11.2 us -> 13.7 us  [on_device(): received = lax.ppermute(chain, 'row', pairs)]
    optimization_barrier x0 -> x4, local copies, waits for them, and re-layouts: none -> 2.41 us  [on_device(): early, received = lax.optimization_barrier((early, received))]
    select_n x1, other arithmetic: 0.14 us -> 2.17 us  [on_device(): odd3 = jnp.where(core == 1, own3, mate3)]
    unnamed x7 -> x33, local copies, waits for them, and re-layouts: 3.8 us -> 5.78 us
  transfers between devices with their start and end apart: 10 -> 11, of which waited for: 6 -> 8; matrix products, arithmetic and copies ran while one was open for 17% -> 27% of each run, Pallas kernels for 0% -> 0%
where the time goes in v5:
time: 94.7 us; the launch traced here: 94 us
  waiting for transfers between devices  37 us (39%)
  matrix products  19.2 us (20%)
  local copies, waits for them, and re-layouts  18.5 us (20%)
  starting transfers between devices  14 us (15%)
  other arithmetic  4.8 us (5%)
    ppermute x3, waiting for transfers between devices, on_device(): received = lax.ppermute(chain, 'row', pairs)  13.7 us
    dot_general x10, matrix products, product_left_t(): lax.dot_general(left, right, (((0,), (0,)), ((), ())), precision=lax.Prec...  13.6 us
    ppermute x3, waiting for transfers between devices, on_device(): partner_factors.append(lax.ppermute(packed, 'row', pairs))  11.3 us
    ppermute x2, waiting for transfers between devices, col_gather(): by_shift.append(lax.ppermute(part, 'col', perm))  10.5 us
    unnamed x33, local copies, waits for them, and re-layouts  5.78 us
    dot_general x6, matrix products, product(): jnp.dot(left, right, precision=lax.Precision.HIGHEST, preferred_element_t...  5.66 us
    ppermute x3, starting transfers between devices, on_device(): received = lax.ppermute(chain, 'row', pairs)  5.31 us
    ppermute x2, starting transfers between devices, col_gather(): by_shift.append(lax.ppermute(part, 'col', perm))  4.77 us
  transfers between devices with their start and end apart: 11, of which 8 were waited for; matrix products, arithmetic and copies ran while one was open for 27% of the time, Pallas kernels for 0%

profile of v5, /device:TPU:0, one launch (start us, length us, event | category | flops | bytes accessed | tf_op | source)
XLA Modules:
  0.0 94.0 jit_solution(18312193694085893641)
XLA Ops:
  1.0 3.0 %collective-permute-start = (f32[512,128]{1,0:T(8,128)S(1)}, f32[512,128]{1,0:T(8,128)S(1)}, u32[]{:S(2)}, u32[]{:S(2)}) collective-permute-start(f32[512,128]{1,0:T(8,128)S(1)} %constant_dynamic-update-slice_fusion), channel_id=1, source_target_pairs={{0,1},{1,0},{2,3},{3,2},{4,5},{5,4},{6,7},{7,6},{8,9},{9,8},{10,11... | collective-permute-start | bytes 786440 | tf_op jit(solution)/shard_map/ppermute | solution.py:34
  4.0 6.3 %collective-permute-done = f32[512,128]{1,0:T(8,128)S(1)} collective-permute-done((f32[512,128]{1,0:T(8,128)S(1)}, f32[512,128]{1,0:T(8,128)S(1)}, u32[]{:S(2)}, u32[]{:S(2)}) %collective-permute-start) | collective-permute-done | bytes 262176 | tf_op jit(solution)/shard_map/ppermute | solution.py:34
  12.8 1.7 %constant_dynamic-update-slice_fusion.3 = f32[768,128]{1,0:T(8,128)} fusion(f32[512,128]{1,0:T(8,128)} %param.6), kind=kLoop, calls=%fused_computation.149 | loop fusion | bytes 524288
  15.1 1.7 %collective-permute-start.1 = (f32[768,128]{1,0:T(8,128)}, f32[768,128]{1,0:T(8,128)}, u32[]{:S(2)}, u32[]{:S(2)}) collective-permute-start(f32[768,128]{1,0:T(8,128)} %constant_dynamic-update-slice_fusion.2), channel_id=1, source_target_pairs={{0,1},{1,0},{2,3},{3,2},{4,5},{5,4},{6,7},{7,6},{8,9},{9,8},{10,11... | collective-permute-start | bytes 1179656 | tf_op jit(solution)/shard_map/ppermute | solution.py:34
  16.9 2.2 %broadcast_select_fusion = (f32[3,256,256]{2,1,0:T(8,128)}, f32[3,256,256]{2,1,0:T(8,128)S(1)}) fusion(f32[3,256,256]{2,1,0:T(8,128)} %collective-permute-done.2, pred[]{:T(512)S(6)} %eq.63, f32[1,256,256]{2,1,0:T(8,128)S(1)} %convolution_bitcast_fusion, f32[1,256,256]{2,1,0:T(8,128)S(1)} %copy-done.3, f32[1,256,256]{2,1,0:T(8,128)S(1)} %get-tuple-element.49, ...), kind=kLoop, calls=%fused_computation.33 | loop fusion | flops 786432 | bytes 3145730 | tf_op jit(solution)/shard_map/jit(_where)/select_n | solution.py:66
  20.9 1.3 %collective-permute-start.3 = (f32[264,256]{0,1:T(8,128)}, f32[264,256]{0,1:T(8,128)S(1)}, u32[]{:S(2)}, u32[]{:S(2)}) collective-permute-start(f32[264,256]{0,1:T(8,128)} %pad_maximum_fusion.3), channel_id=1, source_target_pairs={{4,0},{6,2},{12,8},{14,10},{20,16},{22,18},{28,24},{30,26},{5,1},{... | collective-permute-start | bytes 811016 | tf_op jit(solution)/shard_map/ppermute | solution.py:81
  22.2 4.2 %collective-permute-done.1 = f32[768,128]{1,0:T(8,128)} collective-permute-done((f32[768,128]{1,0:T(8,128)}, f32[768,128]{1,0:T(8,128)}, u32[]{:S(2)}, u32[]{:S(2)}) %collective-permute-start.1) | collective-permute-done | bytes 393248 | tf_op jit(solution)/shard_map/ppermute | solution.py:34
  26.3 1.2 %fusion.5 = (f32[768,128]{1,0:T(8,128)S(1)}, f32[768,128]{1,0:T(8,128)S(1)}) fusion(s32[]{:T(128)S(6)} %select_n.257, f32[1,768,128]{2,1,0:T(8,128)} %bitcast.4, f32[1,768,128]{2,1,0:T(8,128)} %bitcast.5, s32[]{:T(128)S(6)} %select_n.255), kind=kLoop, calls=%fused_computation.26 | loop fusion | flops 196608 | bytes 1572872 | tf_op jit(solution)/shard_map/squeeze | solution.py:36
  27.6 6.0 %collective-permute-done.3 = f32[264,256]{0,1:T(8,128)S(1)} collective-permute-done((f32[264,256]{0,1:T(8,128)}, f32[264,256]{0,1:T(8,128)S(1)}, u32[]{:S(2)}, u32[]{:S(2)}) %collective-permute-start.3) | collective-permute-done | bytes 270368 | tf_op jit(solution)/shard_map/ppermute | solution.py:81
  35.4 1.1 %convolution_subtract_fusion = f32[512,512]{0,1:T(8,128)S(1)} fusion(f32[512,512]{0,1:T(8,128)S(1)} %copy.32, f32[256,512]{1,0:T(8,128)S(1)} %fusion.48, f32[512,256]{1,0:T(8,128)S(1)} %fusion.3), kind=kOutput, calls=%fused_computation | convolution fusion | flops 806223872 | bytes 3145728 | tf_op jit(solution)/shard_map/dot_general | solution.py:8
  38.2 1.3 %collective-permute-start.7 = (f32[264,256]{0,1:T(8,128)}, f32[264,256]{0,1:T(8,128)}, u32[]{:S(2)}, u32[]{:S(2)}) collective-permute-start(f32[264,256]{0,1:T(8,128)} %pad_maximum_fusion.3), channel_id=1, source_target_pairs={{16,0},{18,2},{17,1},{19,3}} | collective-permute-start | bytes 811016 | tf_op jit(solution)/shard_map/ppermute | solution.py:81
  39.4 1.3 %collective-permute-start.6 = (f32[264,256]{0,1:T(8,128)}, f32[264,256]{0,1:T(8,128)}, u32[]{:S(2)}, u32[]{:S(2)}) collective-permute-start(f32[264,256]{0,1:T(8,128)} %pad_maximum_fusion.3), channel_id=1, source_target_pairs={{8,0},{10,2},{24,16},{26,18},{9,1},{11,3},{25,17},{27,19}} | collective-permute-start | bytes 811016 | tf_op jit(solution)/shard_map/ppermute | solution.py:81
  41.7 2.1 %select_subtract_fusion.1 = (f32[256,256]{0,1:T(8,128)S(1)}, f32[256,256]{0,1:T(8,128)}) fusion(f32[256,512]{0,1:T(8,128)} %collective-permute-done.4, s32[]{:T(128)S(6)} %select_n.267, f32[256,512]{0,1:T(8,128)S(1)} %get-tuple-element.41, pred[]{:T(512)S(6)} %eq.56, f32[256,256]{0,1:T(8,128)S(1)} %copy.34, f32[3,256,256]{2,1,0:T(8,128)S(1)} %copy-done.1), kind=kOutput, calls=%fused_computation.81 | convolution fusion | flops 201588736 | bytes 2099200 | tf_op jit(solution)/shard_map/dot_general | solution.py:12
  43.9 1.1 %fusion.42 = f32[256,256]{1,0:T(8,128)} fusion(f32[256,256]{0,1:T(8,128)S(1)} %get-tuple-element.53, f32[256,256]{0,1:T(8,128)S(1)} %copy.36, f32[264,256]{0,1:T(8,128)S(1)} %collective-permute-done.3, pred[]{:T(512)S(6)} %eq.64, pred[]{:T(512)S(6)} %eq.60), kind=kOutput, calls=%fused_computation.76 | convolution fusion | flops 201588736 | bytes 1048578 | tf_op jit(solution)/shard_map/dot_general | solution.py:12
  45.1 7.6 %collective-permute-done.5 = f32[256,256]{0,1:T(8,128)} collective-permute-done((f32[256,256]{0,1:T(8,128)S(1)}, f32[256,256]{0,1:T(8,128)}, u32[]{:S(2)}, u32[]{:S(2)}) %collective-permute-start.5) | collective-permute-done | bytes 262176 | tf_op jit(solution)/shard_map/ppermute | solution.py:124
  52.6 1.1 %copy.40 = f32[256,256]{0,1:T(8,128)S(1)} copy(f32[256,256]{1,0:T(8,128)} %fusion.42) | data formatting | bytes 524288 | tf_op jit(solution)/shard_map/optimization_barrier | solution.py:126
  53.7 2.2 %subtract_select_fusion.2 = (f32[256,256]{0,1:T(8,128)S(1)}, f32[256,256]{0,1:T(8,128)}) fusion(f32[256,256]{0,1:T(8,128)S(1)} %get-tuple-element.53, pred[]{:T(512)S(6)} %eq.60, f32[256,256]{0,1:T(8,128)S(1)} %copy.40, f32[256,256]{0,1:T(8,128)} %collective-permute-done.5, f32[264,256]{0,1:T(8,128)} %copy-done.5, f32[256]{0:T(256)S(1)} %slice_reduce_fusion.2, ...), kind=kOutput, calls=%fused_computation.32 | convolution fusion | flops 201916416 | bytes 1837568 | tf_op jit(solution)/shard_map/dot_general | solution.py:12
  55.9 5.3 %collective-permute-done.6 = f32[264,256]{0,1:T(8,128)} collective-permute-done((f32[264,256]{0,1:T(8,128)}, f32[264,256]{0,1:T(8,128)}, u32[]{:S(2)}, u32[]{:S(2)}) %collective-permute-start.6) | collective-permute-done | bytes 270368 | tf_op jit(solution)/shard_map/ppermute | solution.py:81
  62.2 1.9 %collective-permute-start.8 = (f32[256,256]{0,1:T(8,128)S(1)}, f32[256,256]{0,1:T(8,128)}, u32[]{:S(2)}, u32[]{:S(2)}) collective-permute-start(f32[256,256]{0,1:T(8,128)S(1)} %get-tuple-element.32), channel_id=1, source_target_pairs={{0,8},{8,0},{2,10},{10,2},{16,24},{24,16},{18,26},{26,18},{1,9},{9... | collective-permute-start | bytes 786440 | tf_op jit(solution)/shard_map/ppermute | solution.py:124
  64.1 2.1 %fusion.36 = f32[256,256]{1,0:T(8,128)} fusion(f32[256,256]{0,1:T(8,128)S(1)} %get-tuple-element.32, f32[256,256]{0,1:T(8,128)S(1)} %copy.36, f32[264,256]{0,1:T(8,128)} %collective-permute-done.6, pred[]{:T(512)S(6)} %eq.65, pred[]{:T(512)S(6)} %eq.59), kind=kOutput, calls=%fused_computation.69 | convolution fusion | flops 201588736 | bytes 1048578 | tf_op jit(solution)/shard_map/dot_general | solution.py:12
  67.2 1.7 %slice.77 = f32[256,256]{0,1:T(8,128)} slice(f32[264,256]{0,1:T(8,128)} %collective-permute-done.7), slice={[0:256], [0:256]} | slice | bytes 524288 | tf_op jit(solution)/shard_map/slice | solution.py:84
  68.9 1.8 %copy.49 = f32[256,256]{1,0:T(8,128)} copy(f32[256,256]{0,1:T(8,128)} %slice.77) | data formatting | bytes 524288 | tf_op jit(solution)/shard_map/slice | solution.py:84
  70.8 1.1 %fusion = f32[256,256]{0,1:T(8,128)} fusion(f32[256,256]{0,1:T(8,128)S(1)} %get-tuple-element.53, f32[3,256,256]{2,1,0:T(8,128)S(1)} %get-tuple-element.40, pred[]{:T(512)S(6)} %eq.64, f32[256,256]{0,1:T(8,128)S(1)} %copy.40, f32[256,256]{0,1:T(8,128)S(1)} %copy-done.6), kind=kOutput, calls=%fused_computation.2 | convolution fusion | flops 201523200 | bytes 1310721 | tf_op jit(solution)/shard_map/dot_general | solution.py:8
  72.5 1.1 %copy.47 = f32[256,256]{0,1:T(8,128)S(1)} copy(f32[256,256]{1,0:T(8,128)} %fusion.36) | data formatting | bytes 524288 | tf_op jit(solution)/shard_map/optimization_barrier | solution.py:126
  73.6 1.5 %subtract_select_fusion.1 = (f32[256,256]{0,1:T(8,128)S(1)}, f32[256,256]{0,1:T(8,128)S(1)}) fusion(f32[256,256]{0,1:T(8,128)S(1)} %get-tuple-element.32, pred[]{:T(512)S(6)} %eq.59, f32[256,256]{0,1:T(8,128)S(1)} %copy.47, f32[256,256]{0,1:T(8,128)} %collective-permute-done.8, f32[264,256]{0,1:T(8,128)} %collective-permute-done.6, ...), kind=kOutput, calls=%fused_computation.31 | convolution fusion | flops 201916416 | bytes 1837568 | tf_op jit(solution)/shard_map/dot_general | solution.py:12
  75.1 3.4 %collective-permute-start.9 = (f32[256,256]{0,1:T(8,128)S(1)}, f32[256,256]{0,1:T(8,128)}, u32[]{:S(2)}, u32[]{:S(2)}) collective-permute-start(f32[256,256]{0,1:T(8,128)S(1)} %get-tuple-element.57), channel_id=1, source_target_pairs={{0,16},{16,0},{2,18},{18,2},{1,17},{17,1},{3,19},{19,3}} | collective-permute-start | bytes 786440 | tf_op jit(solution)/shard_map/ppermute | solution.py:124
  79.2 1.2 %fusion.1 = f32[256,256]{0,1:T(8,128)} fusion(f32[256,256]{0,1:T(8,128)S(1)} %copy-done.8, f32[256,256]{0,1:T(8,128)S(1)} %get-tuple-element.32, f32[3,256,256]{2,1,0:T(8,128)S(1)} %get-tuple-element.40, pred[]{:T(512)S(6)} %eq.65, f32[256,256]{0,1:T(8,128)S(1)} %copy.47, f32[256,256]{0,1:T(8,128)S(1)} %get-tuple-element.58), kind=kOutput, calls=%fused_computation.4 | convolution fusion | flops 201523200 | bytes 1572865 | tf_op jit(solution)/shard_map/dot_general | solution.py:8
  80.3 5.5 %collective-permute-done.9 = f32[256,256]{0,1:T(8,128)} collective-permute-done((f32[256,256]{0,1:T(8,128)S(1)}, f32[256,256]{0,1:T(8,128)}, u32[]{:S(2)}, u32[]{:S(2)}) %collective-permute-start.9) | collective-permute-done | bytes 262176 | tf_op jit(solution)/shard_map/ppermute | solution.py:124
  86.0 1.5 %fusion.16 = f32[256,256]{0,1:T(8,128)S(1)} fusion(f32[256,256]{0,1:T(8,128)} %collective-permute-done.9, f32[256]{0:T(256)S(1)} %slice_reduce_fusion, pred[]{:T(512)S(6)} %eq.66, pred[]{:T(512)S(6)} %eq.58, f32[264,256]{0,1:T(8,128)} %collective-permute-done.7, f32[3,256,256]{2,1,0:T(8,128)S(1)} %get-tuple-element.40), kind=kOutput, calls=%fused_computation.49 | convolution fusion | flops 201719808 | bytes 1049602 | tf_op jit(solution)/shard_map/dot_general | solution.py:12
  88.5 1.4 %broadcast_select_fusion.4 = (f32[256,256]{0,1:T(8,128)S(1)}, f32[256,256]{0,1:T(8,128)S(1)}) fusion(f32[256,256]{0,1:T(8,128)S(1)} %fusion.9, pred[]{:T(512)S(6)} %eq.56, f32[256,256]{0,1:T(8,128)S(1)} %copy.34, f32[256,256]{0,1:T(8,128)S(1)} %copy-done.11, f32[3,256,256]{2,1,0:T(8,128)S(1)} %copy-done.1, f32[256,512]{0,1:T(8,128)S(1)} %get-tuple-element.41, ...), kind=kOutput, calls=%fused_computation.141 | convolution fusion | flops 201588736 | bytes 2097157 | tf_op jit(solution)/shard_map/dot_general | solution.py:8
  89.9 1.5 %collective-permute-done.10 = f32[256,256]{0,1:T(8,128)S(1)} collective-permute-done((f32[256,256]{0,1:T(8,128)S(1)}, f32[256,256]{0,1:T(8,128)S(1)}, u32[]{:S(2)}, u32[]{:S(2)}) %collective-permute-start.10) | collective-permute-done | bytes 262176 | tf_op jit(solution)/shard_map/ppermute | solution.py:134
  92.6 1.3 %copy.55 = f32[512,512]{1,0:T(8,128)} copy(f32[512,512]{0,1:T(8,128)S(1)} %pad_maximum_fusion) | data formatting | bytes 2097152 | tf_op jit(solution)/shard_map/concatenate | solution.py:136
  (72 shorter events, 15.9 us)
Async XLA Ops:
  0.0 1.0 %copy-start.13 = (f32[256,128]{1,0:T(8,128)S(1)}, f32[256,128]{1,0:T(8,128)}, u32[]{:S(2)}) copy-start(f32[256,128]{1,0:T(8,128)} %param.9) | copy-start | bytes 393220
  1.0 9.3 %collective-permute-start = (f32[512,128]{1,0:T(8,128)S(1)}, f32[512,128]{1,0:T(8,128)S(1)}, u32[]{:S(2)}, u32[]{:S(2)}) collective-permute-start(f32[512,128]{1,0:T(8,128)S(1)} %constant_dynamic-update-slice_fusion), channel_id=1, source_target_pairs={{0,1},{1,0},{2,3},{3,2},{4,5},{5,4},{6,7},{7,6},{8,9},{9,8},{10,11... | collective-permute-start | bytes 786440 | tf_op jit(solution)/shard_map/ppermute | solution.py:34
  11.1 0.7 copy-start.2
  11.1 1.3 %copy-start = (f32[512,512]{1,0:T(8,128)S(1)}, f32[512,512]{1,0:T(8,128)}, u32[]{:S(2)}) copy-start(f32[512,512]{1,0:T(8,128)} %param.5) | copy-start | bytes 3145732
  11.8 5.1 %collective-permute-start.2 = (f32[3,256,256]{2,1,0:T(8,128)S(1)}, f32[3,256,256]{2,1,0:T(8,128)}, u32[]{:S(2)}, u32[]{:S(2)}) collective-permute-start(f32[3,256,256]{2,1,0:T(8,128)S(1)} %pad_maximum_fusion.1), channel_id=1, source_target_pairs={{0,2},{2,0},{4,6},{6,4},{8,10},{10,8},{12,14},{14,12},{16,18},{18,... | collective-permute-start | bytes 2359304 | tf_op jit(solution)/shard_map/ppermute | solution.py:65
  12.7 1.7 %copy-start.14 = (f32[256,128]{1,0:T(8,128)S(1)}, f32[256,128]{1,0:T(8,128)}, u32[]{:S(2)}) copy-start(f32[256,128]{1,0:T(8,128)} %param.7) | copy-start | bytes 393220
  14.5 2.4 %copy-start.3 = (f32[1,256,256]{2,1,0:T(8,128)S(1)}, f32[1,256,256]{2,1,0:T(8,128)}, u32[]{:S(2)}) copy-start(f32[1,256,256]{2,1,0:T(8,128)} %copy-done.2) | copy-start | bytes 786436
  15.1 11.2 %collective-permute-start.1 = (f32[768,128]{1,0:T(8,128)}, f32[768,128]{1,0:T(8,128)}, u32[]{:S(2)}, u32[]{:S(2)}) collective-permute-start(f32[768,128]{1,0:T(8,128)} %constant_dynamic-update-slice_fusion.2), channel_id=1, source_target_pairs={{0,1},{1,0},{2,3},{3,2},{4,5},{5,4},{6,7},{7,6},{8,9},{9,8},{10,11... | collective-permute-start | bytes 1179656 | tf_op jit(solution)/shard_map/ppermute | solution.py:34
  20.9 12.7 %collective-permute-start.3 = (f32[264,256]{0,1:T(8,128)}, f32[264,256]{0,1:T(8,128)S(1)}, u32[]{:S(2)}, u32[]{:S(2)}) collective-permute-start(f32[264,256]{0,1:T(8,128)} %pad_maximum_fusion.3), channel_id=1, source_target_pairs={{4,0},{6,2},{12,8},{14,10},{20,16},{22,18},{28,24},{30,26},{5,1},{... | collective-permute-start | bytes 811016 | tf_op jit(solution)/shard_map/ppermute | solution.py:81
  33.6 10.3 %copy-start.5 = (f32[264,256]{0,1:T(8,128)}, f32[264,256]{0,1:T(8,128)S(1)}, u32[]{:S(2)}) copy-start(f32[264,256]{0,1:T(8,128)S(1)} %collective-permute-done.3) | copy-start | bytes 811012
  36.5 4.3 %copy-start.10 = (f32[256,256]{1,0:T(8,128)S(1)}, f32[256,256]{1,0:T(8,128)}, u32[]{:S(2)}) copy-start(f32[256,256]{1,0:T(8,128)} %get-tuple-element.45) | copy-start | bytes 786436
  37.4 3.5 %copy-start.1 = (f32[3,256,256]{2,1,0:T(8,128)S(1)}, f32[3,256,256]{2,1,0:T(8,128)}, u32[]{:S(2)}) copy-start(f32[3,256,256]{2,1,0:T(8,128)} %get-tuple-element.39) | copy-start | bytes 2359300
  37.4 4.1 %collective-permute-start.4 = (f32[256,512]{0,1:T(8,128)S(1)}, f32[256,512]{0,1:T(8,128)}, u32[]{:S(2)}, u32[]{:S(2)}) collective-permute-start(f32[256,512]{0,1:T(8,128)S(1)} %get-tuple-element.41), channel_id=1, source_target_pairs={{0,2},{2,0},{4,6},{6,4},{8,10},{10,8},{12,14},{14,12},{16,18},{18,... | collective-permute-start | bytes 1572872 | tf_op jit(solution)/shard_map/ppermute | solution.py:97
  38.2 17.7 %collective-permute-start.7 = (f32[264,256]{0,1:T(8,128)}, f32[264,256]{0,1:T(8,128)}, u32[]{:S(2)}, u32[]{:S(2)}) collective-permute-start(f32[264,256]{0,1:T(8,128)} %pad_maximum_fusion.3), channel_id=1, source_target_pairs={{16,0},{18,2},{17,1},{19,3}} | collective-permute-start | bytes 811016 | tf_op jit(solution)/shard_map/ppermute | solution.py:81
  39.4 21.8 %collective-permute-start.6 = (f32[264,256]{0,1:T(8,128)}, f32[264,256]{0,1:T(8,128)}, u32[]{:S(2)}, u32[]{:S(2)}) collective-permute-start(f32[264,256]{0,1:T(8,128)} %pad_maximum_fusion.3), channel_id=1, source_target_pairs={{8,0},{10,2},{24,16},{26,18},{9,1},{11,3},{25,17},{27,19}} | collective-permute-start | bytes 811016 | tf_op jit(solution)/shard_map/ppermute | solution.py:81
  43.8 8.8 %collective-permute-start.5 = (f32[256,256]{0,1:T(8,128)S(1)}, f32[256,256]{0,1:T(8,128)}, u32[]{:S(2)}, u32[]{:S(2)}) collective-permute-start(f32[256,256]{0,1:T(8,128)S(1)} %get-tuple-element.53), channel_id=1, source_target_pairs={{0,4},{4,0},{2,6},{6,2},{8,12},{12,8},{10,14},{14,10},{16,20},{20,... | collective-permute-start | bytes 786440 | tf_op jit(solution)/shard_map/ppermute | solution.py:124
  62.2 10.3 %collective-permute-start.8 = (f32[256,256]{0,1:T(8,128)S(1)}, f32[256,256]{0,1:T(8,128)}, u32[]{:S(2)}, u32[]{:S(2)}) collective-permute-start(f32[256,256]{0,1:T(8,128)S(1)} %get-tuple-element.32), channel_id=1, source_target_pairs={{0,8},{8,0},{2,10},{10,2},{16,24},{24,16},{18,26},{26,18},{1,9},{9... | collective-permute-start | bytes 786440 | tf_op jit(solution)/shard_map/ppermute | solution.py:124
  68.9 1.8 %copy-start.6 = (f32[256,256]{0,1:T(8,128)S(1)}, f32[256,256]{0,1:T(8,128)}, u32[]{:S(2)}) copy-start(f32[256,256]{0,1:T(8,128)} %get-tuple-element.56) | copy-start | bytes 786436
  73.6 5.0 %copy-start.7 = (f32[256,256]{1,0:T(8,128)S(1)}, f32[256,256]{1,0:T(8,128)}, u32[]{:S(2)}) copy-start(f32[256,256]{1,0:T(8,128)} %copy.49) | copy-start | bytes 786436
  73.6 5.0 %copy-start.12 = (pred[256,256]{1,0:T(32,128)(4,1)S(1)}, pred[256,256]{1,0:T(32,128)(4,1)}, u32[]{:S(2)}) copy-start(pred[256,256]{1,0:T(32,128)(4,1)} %copy.48) | copy-start | bytes 196612
  75.1 4.0 %copy-start.8 = (f32[256,256]{0,1:T(8,128)S(1)}, f32[256,256]{0,1:T(8,128)}, u32[]{:S(2)}) copy-start(f32[256,256]{0,1:T(8,128)} %fusion) | copy-start | bytes 786436
  75.1 10.7 %collective-permute-start.9 = (f32[256,256]{0,1:T(8,128)S(1)}, f32[256,256]{0,1:T(8,128)}, u32[]{:S(2)}, u32[]{:S(2)}) collective-permute-start(f32[256,256]{0,1:T(8,128)S(1)} %get-tuple-element.57), channel_id=1, source_target_pairs={{0,16},{16,0},{2,18},{18,2},{1,17},{17,1},{3,19},{19,3}} | collective-permute-start | bytes 786440 | tf_op jit(solution)/shard_map/ppermute | solution.py:124
  86.0 1.5 %copy-start.9 = (f32[256,256]{0,1:T(8,128)S(1)}, f32[256,256]{0,1:T(8,128)}, u32[]{:S(2)}) copy-start(f32[256,256]{0,1:T(8,128)} %fusion.1) | copy-start | bytes 786436
  87.5 1.0 %copy-start.11 = (f32[256,256]{0,1:T(8,128)S(1)}, f32[256,256]{0,1:T(8,128)}, u32[]{:S(2)}) copy-start(f32[256,256]{0,1:T(8,128)} %get-tuple-element.54) | copy-start | bytes 786436
  89.9 1.6 %collective-permute-start.10 = (f32[256,256]{0,1:T(8,128)S(1)}, f32[256,256]{0,1:T(8,128)S(1)}, u32[]{:S(2)}, u32[]{:S(2)}) collective-permute-start(f32[256,256]{0,1:T(8,128)S(1)} %get-tuple-element.59), channel_id=1, source_target_pairs={{0,2},{2,0},{4,6},{6,4},{8,10},{10,8},{12,14},{14,12},{16,18},{18,... | collective-permute-start | bytes 786440 | tf_op jit(solution)/shard_map/ppermute | solution.py:134
  91.5 1.0 %copy-start.4 = (f32[256,512]{0,1:T(8,128)S(1)}, f32[256,512]{0,1:T(8,128)}, u32[]{:S(2)}) copy-start(f32[256,512]{0,1:T(8,128)} %get-tuple-element.42) | copy-start | bytes 1572868

commit v6 on v4

--- a/solution.py
+++ b/solution.py
@@ -70,12 +70,20 @@
     odd3 = jnp.where(core == 1, own3, mate3)
     even3 = jnp.where(core == 0, own3, mate3)
 
-    row_ids = lax.broadcasted_iota(jnp.int32, tree_factor.shape, 0)
-    col_ids = lax.broadcasted_iota(jnp.int32, tree_factor.shape, 1)
-    even_s, even_m = even3[1], even3[2]
-    packed = jnp.where(row_ids <= col_ids, even_s, even_m.T)
-    diag_m = jnp.sum(jnp.where(row_ids == col_ids, even_m, 0.0), axis=0, keepdims=True)
-    packed = jnp.concatenate([packed, jnp.broadcast_to(diag_m, (8, width))], axis=0)
+    hw = width // 2
+    sub_r = lax.broadcasted_iota(jnp.int32, (hw, hw), 0)
+    sub_c = lax.broadcasted_iota(jnp.int32, (hw, hw), 1)
+    even_s = even3[1]
+    corner = even_s[hw:, hw:]
+    folded = jnp.where(sub_r <= sub_c, even_s[:hw, :hw], corner.T)
+    corner_diag = jnp.sum(jnp.where(sub_r == sub_c, corner, 0.0), axis=0, keepdims=True)
+    packed = jnp.concatenate(
+        [
+            jnp.concatenate([folded, even_s[:hw, hw:]], axis=1),
+            jnp.broadcast_to(jnp.concatenate([corner_diag, jnp.zeros_like(corner_diag)], axis=1), (8, width)),
+        ],
+        axis=0,
+    )
     partner_factors = []
     for level in range(1, levels):
         step = 1 << level
@@ -85,10 +93,12 @@
         partner_factors.append(lax.ppermute(packed, "row", pairs))
 
     def unpack(got):
-        square = got[:width]
-        their_s = jnp.where(row_ids <= col_ids, square, 0.0)
-        their_m = jnp.where(row_ids < col_ids, square.T, jnp.where(row_ids == col_ids, got[width:width + 1], 0.0))
-        return their_s, their_m
+        square = got[:hw, :hw]
+        top_left = jnp.where(sub_r <= sub_c, square, 0.0)
+        bottom_right = jnp.where(sub_r < sub_c, square.T, jnp.where(sub_r == sub_c, got[hw:hw + 1, :hw], 0.0))
+        top = jnp.concatenate([top_left, got[:hw, hw:]], axis=1)
+        bottom = jnp.concatenate([jnp.zeros_like(bottom_right), bottom_right], axis=1)
+        return jnp.concatenate([top, bottom], axis=0)
 
     is_lower = core == 0
     received = lax.ppermute(current, "row", swap)
@@ -113,19 +123,17 @@
         phase = base % (2 * step)
         is_lower = phase == 0
         is_upper = phase == step
-        their = unpack(partner_factors[level - 1])
-        first = jnp.where(is_lower, their[0], jnp.where(is_upper, even3[2], zeros))
-        second = jnp.where(is_lower, their[1], jnp.where(is_upper, even3[1], zeros))
+        their_s = unpack(partner_factors[level - 1])
+        first = jnp.where(is_lower, their_s, jnp.where(is_upper, even3[2], zeros))
         pairs = []
         for i in range(0, n_row, 2 * step):
             for c in range(2):
                 pairs += [(i + c, i + step + c), (i + step + c, i + c)]
-        received = lax.ppermute(chain, "row", pairs)
         early = product_left_t(first, chain)
-        early, received = lax.optimization_barrier((early, received))
-        update = early + product_left_t(second, received)
+        received = lax.ppermute(jnp.where(is_upper, early, chain), "row", pairs)
+        update = product_left_t(even3[1], received) + early
         result = jnp.where(is_upper, chain - product(even3[0], update), result)
-        chain = jnp.where(is_lower, chain - update, chain)
+        chain = jnp.where(is_lower, chain - early - received, chain)
     base_out = jnp.where(base == 0, chain, result)
 
     keep = jnp.where(core == 0, base_out, level0_out)

time: 79.5 us -> 77.6 us (0.976)
  starting transfers between devices: 17.1 us -> 11.8 us
  waiting for transfers between devices: 36 us -> 39.4 us
  matrix products: 14.9 us -> 13 us
  other arithmetic: 2.52 us -> 3.65 us
    ppermute x3, starting transfers between devices: 9.5 us -> 4.22 us  [on_device(): received = lax.ppermute(jnp.where(is_upper, early, chain), 'row', pairs)]
    slice x5 -> x1, local copies, waits for them, and re-layouts: 3.95 us -> 0.01 us  [on_device(): corner = even_s[hw:, hw:]]
    ppermute x3, waiting for transfers between devices: 11.2 us -> 14.9 us  [on_device(): received = lax.ppermute(jnp.where(is_upper, early, chain), 'row', pairs)]
    select_n x1 -> x9, other arithmetic: 0.03 us -> 1.81 us  [the longest x2 1.58 us: unpack(): jnp.where(sub_r < sub_c, square.T, jnp.where(sub_r == sub_c, got[hw:hw +...]
    dot_general x10, matrix products: 10.9 us -> 9.2 us  [product_left_t(): lax.dot_general(left, right, (((0,), (0,)), ((), ())), precision=lax.Prec...]
    unnamed x7 -> x29, local copies, waits for them, and re-layouts: 3.8 us -> 5.39 us
    transpose x0 -> x2, local copies, waits for them, and re-layouts: none -> 0.82 us  [unpack(): bottom_right = jnp.where(sub_r < sub_c, square.T, jnp.where(sub_r == sub_...]
  transfers between devices with their start and end apart: 10 -> 10, of which waited for: 6 -> 8; matrix products, arithmetic and copies ran while one was open for 17% -> 14% of each run, Pallas kernels for 0% -> 0%
where the time goes in v6:
time: 77.6 us; the launch traced here: 77.2 us
  waiting for transfers between devices  39.4 us (51%)
  matrix products  13 us (17%)
  starting transfers between devices  11.8 us (15%)
  local copies, waits for them, and re-layouts  8.79 us (11%)
  other arithmetic  3.65 us (5%)
    ppermute x3, waiting for transfers between devices, on_device(): received = lax.ppermute(jnp.where(is_upper, early, chain), 'row', pairs)  14.9 us
    ppermute x1, waiting for transfers between devices, col_gather(): by_shift.append(lax.ppermute(part, 'col', perm))  14.7 us
    dot_general x10, matrix products, product_left_t(): lax.dot_general(left, right, (((0,), (0,)), ((), ())), precision=lax.Prec...  9.2 us
    ppermute x3, waiting for transfers between devices, on_device(): partner_factors.append(lax.ppermute(packed, 'row', pairs))  8.24 us
    unnamed x29, local copies, waits for them, and re-layouts  5.39 us
    ppermute x3, starting transfers between devices, on_device(): received = lax.ppermute(jnp.where(is_upper, early, chain), 'row', pairs)  4.22 us
    ppermute x3, starting transfers between devices, on_device(): partner_factors.append(lax.ppermute(packed, 'row', pairs))  3.86 us
    dot_general x6, matrix products, product(): jnp.dot(left, right, precision=lax.Precision.HIGHEST, preferred_element_t...  3.83 us
  transfers between devices with their start and end apart: 10, of which 8 were waited for; matrix products, arithmetic and copies ran while one was open for 14% of the time, Pallas kernels for 0%

profile of v6, /device:TPU:0, one launch (start us, length us, event | category | flops | bytes accessed | tf_op | source)
XLA Modules:
  0.0 77.2 jit_solution(1636215585523642695)
XLA Ops:
  0.0 1.0 %constant_dynamic-update-slice_fusion.3 = f32[1280,128]{1,0:T(8,128)S(1)} fusion(f32[512,128]{1,0:T(8,128)} %param.6), kind=kLoop, calls=%fused_computation.138 | loop fusion | bytes 524288
  1.0 0.9 %constant_dynamic-update-slice_fusion.2 = f32[1280,128]{1,0:T(8,128)S(1)} fusion(f32[1280,128]{1,0:T(8,128)S(1)} %constant_dynamic-update-slice_fusion.3, f32[256,128]{1,0:T(8,128)} %param.7), kind=kLoop, calls=%fused_computation.137 | loop fusion | bytes 262144
  1.9 0.9 %constant_dynamic-update-slice_fusion.1 = f32[1280,128]{1,0:T(8,128)S(1)} fusion(f32[1280,128]{1,0:T(8,128)S(1)} %constant_dynamic-update-slice_fusion.2, f32[256,128]{1,0:T(8,128)} %param.8), kind=kLoop, calls=%fused_computation.136 | loop fusion | bytes 262144
  2.9 3.0 %collective-permute-start = (f32[1280,128]{1,0:T(8,128)S(1)}, f32[1280,128]{1,0:T(8,128)S(1)}, u32[]{:S(2)}, u32[]{:S(2)}) collective-permute-start(f32[1280,128]{1,0:T(8,128)S(1)} %constant_dynamic-update-slice_fusion), channel_id=1, source_target_pairs={{0,1},{1,0},{2,3},{3,2},{4,5},{5,4},{6,7},{7,6},{8,9},{9,8},{10,11... | collective-permute-start | bytes 1966088 | tf_op jit(solution)/shard_map/ppermute | solution.py:34
  5.9 14.7 %collective-permute-done = f32[1280,128]{1,0:T(8,128)S(1)} collective-permute-done((f32[1280,128]{1,0:T(8,128)S(1)}, f32[1280,128]{1,0:T(8,128)S(1)}, u32[]{:S(2)}, u32[]{:S(2)}) %collective-permute-start) | collective-permute-done | bytes 655392 | tf_op jit(solution)/shard_map/ppermute | solution.py:34
  20.9 1.0 %copy-done = f32[512,512]{1,0:T(8,128)S(1)} copy-done((f32[512,512]{1,0:T(8,128)S(1)}, f32[512,512]{1,0:T(8,128)}, u32[]{:S(2)}) %copy-start) | copy-done | bytes 1048600
  21.9 1.1 %fusion.99 = f32[256,512]{1,0:T(8,128)S(1)} fusion(f32[512,512]{1,0:T(8,128)S(1)} %copy-done, f32[1280,128]{1,0:T(8,128)S(1)} %get-tuple-element.24, f32[1280,128]{1,0:T(8,128)S(1)} %get-tuple-element.23), kind=kOutput, calls=%fused_computation.156 | convolution fusion | flops 806092800 | bytes 2883584 | tf_op jit(solution)/shard_map/dot_general | solution.py:12
  23.6 0.7 fusion.14
  24.4 1.1 %convolution_subtract_fusion = f32[512,512]{1,0:T(8,128)S(1)} fusion(f32[512,512]{1,0:T(8,128)S(1)} %copy-done, f32[256,512]{1,0:T(8,128)S(1)} %fusion.14, f32[1280,128]{1,0:T(8,128)S(1)} %get-tuple-element.24, f32[1280,128]{1,0:T(8,128)S(1)} %get-tuple-element.23), kind=kOutput, calls=%fused_computation.10 | convolution fusion | flops 806354944 | bytes 3932160 | tf_op jit(solution)/shard_map/dot_general | solution.py:8
  25.4 0.9 %fusion.103 = (f32[256,512]{1,0:T(8,128)S(1)}, f32[256,512]{1,0:T(8,128)}) fusion(f32[512,512]{1,0:T(8,128)S(1)} %convolution_subtract_fusion), kind=kLoop, calls=%fused_computation.158 | loop fusion | bytes 2097152 | tf_op jit(solution)/shard_map/slice | solution.py:57
  27.3 1.3 %collective-permute-start.3 = (f32[136,256]{1,0:T(8,128)S(1)}, f32[136,256]{1,0:T(8,128)S(1)}, u32[]{:S(2)}, u32[]{:S(2)}) collective-permute-start(f32[136,256]{1,0:T(8,128)S(1)} %pad_maximum_fusion.3), channel_id=1, source_target_pairs={{4,0},{6,2},{12,8},{14,10},{20,16},{22,18},{28,24},{30,26},{5,1},{... | collective-permute-start | bytes 417800 | tf_op jit(solution)/shard_map/ppermute | solution.py:93
  29.2 1.3 %select_subtract_fusion.1 = (f32[256,256]{1,0:T(8,128)S(1)}, f32[256,256]{1,0:T(8,128)}) fusion(f32[256,512]{1,0:T(8,128)S(1)} %collective-permute-done.2, s32[]{:T(128)S(6)} %select_n.258, f32[256,512]{1,0:T(8,128)S(1)} %get-tuple-element.25, pred[]{:T(512)S(6)} %eq.54, f32[256,256]{1,0:T(8,128)S(1)} %fusion.44, f32[3,256,256]{2,1,0:T(8,128)S(1)} %get-tuple-element.20), kind=kOutput, calls=%fused_computation.82 | convolution fusion | flops 201588736 | bytes 2099200 | tf_op jit(solution)/shard_map/dot_general | solution.py:12
  30.5 4.2 %collective-permute-done.3 = f32[136,256]{1,0:T(8,128)S(1)} collective-permute-done((f32[136,256]{1,0:T(8,128)S(1)}, f32[136,256]{1,0:T(8,128)S(1)}, u32[]{:S(2)}, u32[]{:S(2)}) %collective-permute-start.3) | collective-permute-done | bytes 139296 | tf_op jit(solution)/shard_map/ppermute | solution.py:93
  35.0 0.6 broadcast_select_fusion.4
  35.9 0.7 copy.12
  36.6 1.3 %collective-permute-start.6 = (f32[136,256]{1,0:T(8,128)S(1)}, f32[136,256]{1,0:T(8,128)S(1)}, u32[]{:S(2)}, u32[]{:S(2)}) collective-permute-start(f32[136,256]{1,0:T(8,128)S(1)} %pad_maximum_fusion.3), channel_id=1, source_target_pairs={{16,0},{18,2},{17,1},{19,3}} | collective-permute-start | bytes 417800 | tf_op jit(solution)/shard_map/ppermute | solution.py:93
  37.9 1.3 %collective-permute-start.5 = (f32[136,256]{1,0:T(8,128)S(1)}, f32[136,256]{1,0:T(8,128)S(1)}, u32[]{:S(2)}, u32[]{:S(2)}) collective-permute-start(f32[136,256]{1,0:T(8,128)S(1)} %pad_maximum_fusion.3), channel_id=1, source_target_pairs={{8,0},{10,2},{24,16},{26,18},{9,1},{11,3},{25,17},{27,19}} | collective-permute-start | bytes 417800 | tf_op jit(solution)/shard_map/ppermute | solution.py:93
  39.2 3.9 %collective-permute-done.4 = f32[256,256]{1,0:T(8,128)S(1)} collective-permute-done((f32[256,256]{1,0:T(8,128)S(1)}, f32[256,256]{1,0:T(8,128)S(1)}, u32[]{:S(2)}, u32[]{:S(2)}) %collective-permute-start.4) | collective-permute-done | bytes 262176 | tf_op jit(solution)/shard_map/ppermute | solution.py:133
  43.1 1.4 %collective-permute-done.6 = f32[136,256]{1,0:T(8,128)S(1)} collective-permute-done((f32[136,256]{1,0:T(8,128)S(1)}, f32[136,256]{1,0:T(8,128)S(1)}, u32[]{:S(2)}, u32[]{:S(2)}) %collective-permute-start.6) | collective-permute-done | bytes 139296 | tf_op jit(solution)/shard_map/ppermute | solution.py:93
  44.5 2.6 %collective-permute-done.5 = f32[136,256]{1,0:T(8,128)S(1)} collective-permute-done((f32[136,256]{1,0:T(8,128)S(1)}, f32[136,256]{1,0:T(8,128)S(1)}, u32[]{:S(2)}, u32[]{:S(2)}) %collective-permute-start.5) | collective-permute-done | bytes 139296 | tf_op jit(solution)/shard_map/ppermute | solution.py:93
  47.7 0.7 copy.18
  48.5 1.5 %select_select_fusion.1 = (f32[128,128]{1,0:T(8,128)}, f32[128,128]{1,0:T(8,128)S(1)}) fusion(pred[128,128]{1,0:T(8,128)(4,1)} %copy.12, f32[128,128]{1,0:T(8,128)} %copy.18, pred[128,128]{1,0:T(8,128)(4,1)S(1)} %copy.11, f32[128]{0:T(128)} %get-tuple-element.50, f32[128,128]{1,0:T(8,128)S(1)} %copy.13, f32[128]{0:T(128)} %get-tuple-element.51), kind=kLoop, calls=%fused_computation.124 | loop fusion | flops 65536 | bytes 295936 | tf_op jit(solution)/shard_map/jit(_where)/select_n | solution.py:98
  50.8 1.9 %collective-permute-start.7 = (f32[256,256]{1,0:T(8,128)S(1)}, f32[256,256]{1,0:T(8,128)S(1)}, u32[]{:S(2)}, u32[]{:S(2)}) collective-permute-start(f32[256,256]{1,0:T(8,128)S(1)} %broadcast_select_fusion.3), channel_id=1, source_target_pairs={{0,8},{8,0},{2,10},{10,2},{16,24},{24,16},{18,26},{26,18},{1,9},{9... | collective-permute-start | bytes 786440 | tf_op jit(solution)/shard_map/ppermute | solution.py:133
  52.8 1.5 %convolution_add_fusion = f32[256,256]{1,0:T(8,128)S(1)} fusion(f32[256,256]{1,0:T(8,128)S(1)} %get-tuple-element.44, f32[256,256]{1,0:T(8,128)} %copy-done.7, f32[3,256,256]{2,1,0:T(8,128)S(1)} %get-tuple-element.19), kind=kOutput, calls=%fused_computation.13 | convolution fusion | flops 201392128 | bytes 1048576 | tf_op jit(solution)/shard_map/dot_general | solution.py:12
  54.3 1.1 %fusion = f32[256,256]{1,0:T(8,128)} fusion(f32[256,256]{1,0:T(8,128)S(1)} %get-tuple-element.14, f32[256,256]{1,0:T(8,128)S(1)} %convolution_add_fusion, f32[3,256,256]{2,1,0:T(8,128)S(1)} %get-tuple-element.19, pred[]{:T(512)S(6)} %eq.62), kind=kOutput, calls=%fused_computation.12 | convolution fusion | flops 201457664 | bytes 1048577 | tf_op jit(solution)/shard_map/dot_general | solution.py:8
  55.4 5.3 %collective-permute-done.7 = f32[256,256]{1,0:T(8,128)S(1)} collective-permute-done((f32[256,256]{1,0:T(8,128)S(1)}, f32[256,256]{1,0:T(8,128)S(1)}, u32[]{:S(2)}, u32[]{:S(2)}) %collective-permute-start.7) | collective-permute-done | bytes 262176 | tf_op jit(solution)/shard_map/ppermute | solution.py:133
  60.8 0.6 copy-done.8
  62.2 2.2 %collective-permute-start.8 = (f32[256,256]{1,0:T(8,128)S(1)}, f32[256,256]{1,0:T(8,128)S(1)}, u32[]{:S(2)}, u32[]{:S(2)}) collective-permute-start(f32[256,256]{1,0:T(8,128)S(1)} %broadcast_select_fusion.2), channel_id=1, source_target_pairs={{0,16},{16,0},{2,18},{18,2},{1,17},{17,1},{3,19},{19,3}} | collective-permute-start | bytes 786440 | tf_op jit(solution)/shard_map/ppermute | solution.py:133
  64.4 1.5 %convolution_add_fusion.1 = f32[256,256]{0,1:T(8,128)S(1)} fusion(f32[256,256]{0,1:T(8,128)S(1)} %fusion.22, f32[256,256]{1,0:T(8,128)} %copy-done.8, f32[3,256,256]{2,1,0:T(8,128)S(1)} %get-tuple-element.19), kind=kOutput, calls=%fused_computation.16 | convolution fusion | flops 201392128 | bytes 1048576 | tf_op jit(solution)/shard_map/dot_general | solution.py:12
  66.4 5.8 %collective-permute-done.8 = f32[256,256]{1,0:T(8,128)S(1)} collective-permute-done((f32[256,256]{1,0:T(8,128)S(1)}, f32[256,256]{1,0:T(8,128)S(1)}, u32[]{:S(2)}, u32[]{:S(2)}) %collective-permute-start.8) | collective-permute-done | bytes 262176 | tf_op jit(solution)/shard_map/ppermute | solution.py:133
  74.5 1.5 %collective-permute-done.9 = f32[256,256]{1,0:T(8,128)S(1)} collective-permute-done((f32[256,256]{1,0:T(8,128)S(1)}, f32[256,256]{1,0:T(8,128)S(1)}, u32[]{:S(2)}, u32[]{:S(2)}) %collective-permute-start.9) | collective-permute-done | bytes 262176 | tf_op jit(solution)/shard_map/ppermute | solution.py:141
  76.1 1.1 %pad_maximum_fusion = f32[512,512]{1,0:T(8,128)} fusion(f32[256,512]{1,0:T(8,128)S(1)} %copy-done.3, f32[256,256]{1,0:T(8,128)S(1)} %get-tuple-element.28, f32[256,256]{1,0:T(8,128)S(1)} %get-tuple-element.27), kind=kLoop, calls=%fused_computation.21 | loop fusion | flops 524288 | bytes 2097152 | tf_op jit(solution)/shard_map/concatenate | solution.py:143
  (67 shorter events, 7.9 us)
Async XLA Ops:
  0.0 2.8 %copy-start.11 = (f32[256,128]{1,0:T(8,128)S(1)}, f32[256,128]{1,0:T(8,128)}, u32[]{:S(2)}) copy-start(f32[256,128]{1,0:T(8,128)} %param.9) | copy-start | bytes 393220
  2.9 17.8 %collective-permute-start = (f32[1280,128]{1,0:T(8,128)S(1)}, f32[1280,128]{1,0:T(8,128)S(1)}, u32[]{:S(2)}, u32[]{:S(2)}) collective-permute-start(f32[1280,128]{1,0:T(8,128)S(1)} %constant_dynamic-update-slice_fusion), channel_id=1, source_target_pairs={{0,1},{1,0},{2,3},{3,2},{4,5},{5,4},{6,7},{7,6},{8,9},{9,8},{10,11... | collective-permute-start | bytes 1966088 | tf_op jit(solution)/shard_map/ppermute | solution.py:34
  20.6 1.2 %copy-start = (f32[512,512]{1,0:T(8,128)S(1)}, f32[512,512]{1,0:T(8,128)}, u32[]{:S(2)}) copy-start(f32[512,512]{1,0:T(8,128)} %param.5) | copy-start | bytes 3145732
  23.6 3.2 %collective-permute-start.1 = (f32[3,256,256]{2,1,0:T(8,128)S(1)}, f32[3,256,256]{2,1,0:T(8,128)S(1)}, u32[]{:S(2)}, u32[]{:S(2)}) collective-permute-start(f32[3,256,256]{2,1,0:T(8,128)S(1)} %pad_maximum_fusion.1), channel_id=1, source_target_pairs={{0,2},{2,0},{4,6},{6,4},{8,10},{10,8},{12,14},{14,12},{16,18},{18,... | collective-permute-start | bytes 2359304 | tf_op jit(solution)/shard_map/ppermute | solution.py:69
  26.3 2.9 %collective-permute-start.2 = (f32[256,512]{1,0:T(8,128)S(1)}, f32[256,512]{1,0:T(8,128)S(1)}, u32[]{:S(2)}, u32[]{:S(2)}) collective-permute-start(f32[256,512]{1,0:T(8,128)S(1)} %get-tuple-element.25), channel_id=1, source_target_pairs={{0,2},{2,0},{4,6},{6,4},{8,10},{10,8},{12,14},{14,12},{16,18},{18,... | collective-permute-start | bytes 1572872 | tf_op jit(solution)/shard_map/ppermute | solution.py:104
  27.3 7.5 %collective-permute-start.3 = (f32[136,256]{1,0:T(8,128)S(1)}, f32[136,256]{1,0:T(8,128)S(1)}, u32[]{:S(2)}, u32[]{:S(2)}) collective-permute-start(f32[136,256]{1,0:T(8,128)S(1)} %pad_maximum_fusion.3), channel_id=1, source_target_pairs={{4,0},{6,2},{12,8},{14,10},{20,16},{22,18},{28,24},{30,26},{5,1},{... | collective-permute-start | bytes 417800 | tf_op jit(solution)/shard_map/ppermute | solution.py:93
  29.2 5.6 %copy-start.1 = (f32[256,256]{1,0:T(8,128)}, f32[256,256]{1,0:T(8,128)S(1)}, u32[]{:S(2)}) copy-start(f32[256,256]{1,0:T(8,128)S(1)} %fusion.44) | copy-start | bytes 786436
  29.2 5.6 %copy-start.4 = (f32[256,512]{1,0:T(8,128)}, f32[256,512]{1,0:T(8,128)S(1)}, u32[]{:S(2)}) copy-start(f32[256,512]{1,0:T(8,128)S(1)} %collective-permute-done.2) | copy-start | bytes 1572868
  35.6 7.4 %collective-permute-start.4 = (f32[256,256]{1,0:T(8,128)S(1)}, f32[256,256]{1,0:T(8,128)S(1)}, u32[]{:S(2)}, u32[]{:S(2)}) collective-permute-start(f32[256,256]{1,0:T(8,128)S(1)} %get-tuple-element.43), channel_id=1, source_target_pairs={{0,4},{4,0},{2,6},{6,2},{8,12},{12,8},{10,14},{14,10},{16,20},{20,... | collective-permute-start | bytes 786440 | tf_op jit(solution)/shard_map/ppermute | solution.py:133
  36.6 7.9 %collective-permute-start.6 = (f32[136,256]{1,0:T(8,128)S(1)}, f32[136,256]{1,0:T(8,128)S(1)}, u32[]{:S(2)}, u32[]{:S(2)}) collective-permute-start(f32[136,256]{1,0:T(8,128)S(1)} %pad_maximum_fusion.3), channel_id=1, source_target_pairs={{16,0},{18,2},{17,1},{19,3}} | collective-permute-start | bytes 417800 | tf_op jit(solution)/shard_map/ppermute | solution.py:93
  37.9 9.2 %collective-permute-start.5 = (f32[136,256]{1,0:T(8,128)S(1)}, f32[136,256]{1,0:T(8,128)S(1)}, u32[]{:S(2)}, u32[]{:S(2)}) collective-permute-start(f32[136,256]{1,0:T(8,128)S(1)} %pad_maximum_fusion.3), channel_id=1, source_target_pairs={{8,0},{10,2},{24,16},{26,18},{9,1},{11,3},{25,17},{27,19}} | collective-permute-start | bytes 417800 | tf_op jit(solution)/shard_map/ppermute | solution.py:93
  43.0 7.0 %copy-start.7 = (f32[256,256]{1,0:T(8,128)}, f32[256,256]{1,0:T(8,128)S(1)}, u32[]{:S(2)}) copy-start(f32[256,256]{1,0:T(8,128)S(1)} %collective-permute-done.4) | copy-start | bytes 786436
  50.8 9.9 %collective-permute-start.7 = (f32[256,256]{1,0:T(8,128)S(1)}, f32[256,256]{1,0:T(8,128)S(1)}, u32[]{:S(2)}, u32[]{:S(2)}) collective-permute-start(f32[256,256]{1,0:T(8,128)S(1)} %broadcast_select_fusion.3), channel_id=1, source_target_pairs={{0,8},{8,0},{2,10},{10,2},{16,24},{24,16},{18,26},{26,18},{1,9},{9... | collective-permute-start | bytes 786440 | tf_op jit(solution)/shard_map/ppermute | solution.py:133
  54.3 7.1 %copy-start.10 = (f32[128,128]{1,0:T(8,128)S(1)}, f32[128,128]{1,0:T(8,128)}, u32[]{:S(2)}) copy-start(f32[128,128]{1,0:T(8,128)} %get-tuple-element.39) | copy-start | bytes 196612
  60.7 0.7 copy-start.8
  62.2 3.9 %copy-start.6 = (f32[256,256]{1,0:T(8,128)S(1)}, f32[256,256]{1,0:T(8,128)}, u32[]{:S(2)}) copy-start(f32[256,256]{1,0:T(8,128)} %fusion) | copy-start | bytes 786436
  62.2 10.0 %collective-permute-start.8 = (f32[256,256]{1,0:T(8,128)S(1)}, f32[256,256]{1,0:T(8,128)S(1)}, u32[]{:S(2)}, u32[]{:S(2)}) collective-permute-start(f32[256,256]{1,0:T(8,128)S(1)} %broadcast_select_fusion.2), channel_id=1, source_target_pairs={{0,16},{16,0},{2,18},{18,2},{1,17},{17,1},{3,19},{19,3}} | collective-permute-start | bytes 786440 | tf_op jit(solution)/shard_map/ppermute | solution.py:133
  72.8 1.0 %copy-start.2 = (f32[256,256]{1,0:T(8,128)S(1)}, f32[256,256]{1,0:T(8,128)}, u32[]{:S(2)}) copy-start(f32[256,256]{1,0:T(8,128)} %copy-done.1) | copy-start | bytes 786436
  72.8 1.1 %copy-start.5 = (f32[256,512]{1,0:T(8,128)S(1)}, f32[256,512]{1,0:T(8,128)}, u32[]{:S(2)}) copy-start(f32[256,512]{1,0:T(8,128)} %copy-done.4) | copy-start | bytes 1572868
  72.8 1.2 %copy-start.9 = (f32[256,256]{1,0:T(8,128)S(1)}, f32[256,256]{1,0:T(8,128)}, u32[]{:S(2)}) copy-start(f32[256,256]{1,0:T(8,128)} %get-tuple-element.42) | copy-start | bytes 786436
  74.4 1.7 %copy-start.3 = (f32[256,512]{1,0:T(8,128)S(1)}, f32[256,512]{1,0:T(8,128)}, u32[]{:S(2)}) copy-start(f32[256,512]{1,0:T(8,128)} %get-tuple-element.26) | copy-start | bytes 1572868
  74.5 1.6 %collective-permute-start.9 = (f32[256,256]{1,0:T(8,128)S(1)}, f32[256,256]{1,0:T(8,128)S(1)}, u32[]{:S(2)}, u32[]{:S(2)}) collective-permute-start(f32[256,256]{1,0:T(8,128)S(1)} %get-tuple-element.45), channel_id=1, source_target_pairs={{0,2},{2,0},{4,6},{6,4},{8,10},{10,8},{12,14},{14,12},{16,18},{18,... | collective-permute-start | bytes 786440 | tf_op jit(solution)/shard_map/ppermute | solution.py:141

commit v7 on v6

--- a/solution.py
+++ b/solution.py
@@ -5,7 +5,7 @@
 
 
 def product(left, right):
-    return jnp.dot(left, right, precision=lax.Precision.HIGHEST, preferred_element_type=jnp.float32)
+    return jnp.dot(left, right, precision=lax.Precision.HIGH, preferred_element_type=jnp.float32)
 
 
 def product_left_t(left, right):
@@ -13,7 +13,7 @@
         left,
         right,
         (((0,), (0,)), ((), ())),
-        precision=lax.Precision.HIGHEST,
+        precision=lax.Precision.HIGH,
         preferred_element_type=jnp.float32,
     )
 

time: 77.6 us -> 75.3 us (0.970)
  matrix products: 13 us -> 9.78 us
  waiting for transfers between devices: 39.4 us -> 40.5 us
    dot_general x10, matrix products: 9.2 us -> 6.88 us  [product_left_t(): lax.dot_general(left, right, (((0,), (0,)), ((), ())), precision=lax.Prec...]
    dot_general x6, matrix products: 3.83 us -> 2.91 us  [product(): jnp.dot(left, right, precision=lax.Precision.HIGH, preferred_element_type...]
  transfers between devices with their start and end apart: 10 -> 10, of which waited for: 8 -> 8; matrix products, arithmetic and copies ran while one was open for 14% -> 12% of each run, Pallas kernels for 0% -> 0%
where the time goes in v7:
time: 75.3 us; the launch traced here: 74.9 us
  waiting for transfers between devices  40.5 us (54%)
  starting transfers between devices  11.6 us (15%)
  matrix products  9.78 us (13%)
  local copies, waits for them, and re-layouts  8.85 us (12%)
  other arithmetic  3.65 us (5%)
    ppermute x3, waiting for transfers between devices, on_device(): received = lax.ppermute(jnp.where(is_upper, early, chain), 'row', pairs)  15.6 us
    ppermute x1, waiting for transfers between devices, col_gather(): by_shift.append(lax.ppermute(part, 'col', perm))  14.7 us
    ppermute x3, waiting for transfers between devices, on_device(): partner_factors.append(lax.ppermute(packed, 'row', pairs))  8.65 us
    dot_general x10, matrix products, product_left_t(): lax.dot_general(left, right, (((0,), (0,)), ((), ())), precision=lax.Prec...  6.88 us
    unnamed x29, local copies, waits for them, and re-layouts  5.45 us
    ppermute x3, starting transfers between devices, on_device(): received = lax.ppermute(jnp.where(is_upper, early, chain), 'row', pairs)  4.04 us
    ppermute x3, starting transfers between devices, on_device(): partner_factors.append(lax.ppermute(packed, 'row', pairs))  3.86 us
    ppermute x1, starting transfers between devices, col_gather(): by_shift.append(lax.ppermute(part, 'col', perm))  3.03 us
  transfers between devices with their start and end apart: 10, of which 8 were waited for; matrix products, arithmetic and copies ran while one was open for 12% of the time, Pallas kernels for 0%

profile of v7, /device:TPU:0, one launch (start us, length us, event | category | flops | bytes accessed | tf_op | source)
XLA Modules:
  0.0 74.9 jit_solution(4200166214036353086)
XLA Ops:
  0.0 1.0 %constant_dynamic-update-slice_fusion.3 = f32[1280,128]{1,0:T(8,128)S(1)} fusion(f32[512,128]{1,0:T(8,128)} %param.6), kind=kLoop, calls=%fused_computation.138 | loop fusion | bytes 524288
  1.0 0.9 %constant_dynamic-update-slice_fusion.2 = f32[1280,128]{1,0:T(8,128)S(1)} fusion(f32[1280,128]{1,0:T(8,128)S(1)} %constant_dynamic-update-slice_fusion.3, f32[256,128]{1,0:T(8,128)} %param.7), kind=kLoop, calls=%fused_computation.137 | loop fusion | bytes 262144
  1.9 0.9 %constant_dynamic-update-slice_fusion.1 = f32[1280,128]{1,0:T(8,128)S(1)} fusion(f32[1280,128]{1,0:T(8,128)S(1)} %constant_dynamic-update-slice_fusion.2, f32[256,128]{1,0:T(8,128)} %param.8), kind=kLoop, calls=%fused_computation.136 | loop fusion | bytes 262144
  2.9 3.0 %collective-permute-start = (f32[1280,128]{1,0:T(8,128)S(1)}, f32[1280,128]{1,0:T(8,128)S(1)}, u32[]{:S(2)}, u32[]{:S(2)}) collective-permute-start(f32[1280,128]{1,0:T(8,128)S(1)} %constant_dynamic-update-slice_fusion), channel_id=1, source_target_pairs={{0,1},{1,0},{2,3},{3,2},{4,5},{5,4},{6,7},{7,6},{8,9},{9,8},{10,11... | collective-permute-start | bytes 1966088 | tf_op jit(solution)/shard_map/ppermute | solution.py:34
  5.9 14.7 %collective-permute-done = f32[1280,128]{1,0:T(8,128)S(1)} collective-permute-done((f32[1280,128]{1,0:T(8,128)S(1)}, f32[1280,128]{1,0:T(8,128)S(1)}, u32[]{:S(2)}, u32[]{:S(2)}) %collective-permute-start) | collective-permute-done | bytes 655392 | tf_op jit(solution)/shard_map/ppermute | solution.py:34
  20.9 1.0 %copy-done = f32[512,512]{1,0:T(8,128)S(1)} copy-done((f32[512,512]{1,0:T(8,128)S(1)}, f32[512,512]{1,0:T(8,128)}, u32[]{:S(2)}) %copy-start) | copy-done | bytes 1048600
  21.9 0.7 fusion.99
  23.6 0.6 convolution_subtract_fusion
  24.2 0.9 %fusion.103 = (f32[256,512]{1,0:T(8,128)S(1)}, f32[256,512]{1,0:T(8,128)}) fusion(f32[512,512]{1,0:T(8,128)S(1)} %convolution_subtract_fusion), kind=kLoop, calls=%fused_computation.158 | loop fusion | bytes 2097152 | tf_op jit(solution)/shard_map/slice | solution.py:57
  26.0 1.3 %collective-permute-start.3 = (f32[136,256]{1,0:T(8,128)S(1)}, f32[136,256]{1,0:T(8,128)S(1)}, u32[]{:S(2)}, u32[]{:S(2)}) collective-permute-start(f32[136,256]{1,0:T(8,128)S(1)} %pad_maximum_fusion.3), channel_id=1, source_target_pairs={{4,0},{6,2},{12,8},{14,10},{20,16},{22,18},{28,24},{30,26},{5,1},{... | collective-permute-start | bytes 417800 | tf_op jit(solution)/shard_map/ppermute | solution.py:93
  27.8 1.1 %select_subtract_fusion.1 = (f32[256,256]{1,0:T(8,128)S(1)}, f32[256,256]{1,0:T(8,128)}) fusion(f32[256,512]{1,0:T(8,128)S(1)} %collective-permute-done.2, s32[]{:T(128)S(6)} %select_n.258, f32[256,512]{1,0:T(8,128)S(1)} %get-tuple-element.25, pred[]{:T(512)S(6)} %eq.54, f32[256,256]{1,0:T(8,128)S(1)} %fusion.44, f32[3,256,256]{2,1,0:T(8,128)S(1)} %get-tuple-element.20), kind=kOutput, calls=%fused_computation.82 | convolution fusion | flops 100925440 | bytes 2099200 | tf_op jit(solution)/shard_map/dot_general | solution.py:12
  28.9 4.6 %collective-permute-done.3 = f32[136,256]{1,0:T(8,128)S(1)} collective-permute-done((f32[136,256]{1,0:T(8,128)S(1)}, f32[136,256]{1,0:T(8,128)S(1)}, u32[]{:S(2)}, u32[]{:S(2)}) %collective-permute-start.3) | collective-permute-done | bytes 139296 | tf_op jit(solution)/shard_map/ppermute | solution.py:93
  34.4 0.7 copy.12
  35.2 1.3 %collective-permute-start.6 = (f32[136,256]{1,0:T(8,128)S(1)}, f32[136,256]{1,0:T(8,128)S(1)}, u32[]{:S(2)}, u32[]{:S(2)}) collective-permute-start(f32[136,256]{1,0:T(8,128)S(1)} %pad_maximum_fusion.3), channel_id=1, source_target_pairs={{16,0},{18,2},{17,1},{19,3}} | collective-permute-start | bytes 417800 | tf_op jit(solution)/shard_map/ppermute | solution.py:93
  36.4 1.3 %collective-permute-start.5 = (f32[136,256]{1,0:T(8,128)S(1)}, f32[136,256]{1,0:T(8,128)S(1)}, u32[]{:S(2)}, u32[]{:S(2)}) collective-permute-start(f32[136,256]{1,0:T(8,128)S(1)} %pad_maximum_fusion.3), channel_id=1, source_target_pairs={{8,0},{10,2},{24,16},{26,18},{9,1},{11,3},{25,17},{27,19}} | collective-permute-start | bytes 417800 | tf_op jit(solution)/shard_map/ppermute | solution.py:93
  37.7 3.9 %collective-permute-done.4 = f32[256,256]{1,0:T(8,128)S(1)} collective-permute-done((f32[256,256]{1,0:T(8,128)S(1)}, f32[256,256]{1,0:T(8,128)S(1)}, u32[]{:S(2)}, u32[]{:S(2)}) %collective-permute-start.4) | collective-permute-done | bytes 262176 | tf_op jit(solution)/shard_map/ppermute | solution.py:133
  41.7 1.4 %collective-permute-done.6 = f32[136,256]{1,0:T(8,128)S(1)} collective-permute-done((f32[136,256]{1,0:T(8,128)S(1)}, f32[136,256]{1,0:T(8,128)S(1)}, u32[]{:S(2)}, u32[]{:S(2)}) %collective-permute-start.6) | collective-permute-done | bytes 139296 | tf_op jit(solution)/shard_map/ppermute | solution.py:93
  43.0 2.6 %collective-permute-done.5 = f32[136,256]{1,0:T(8,128)S(1)} collective-permute-done((f32[136,256]{1,0:T(8,128)S(1)}, f32[136,256]{1,0:T(8,128)S(1)}, u32[]{:S(2)}, u32[]{:S(2)}) %collective-permute-start.5) | collective-permute-done | bytes 139296 | tf_op jit(solution)/shard_map/ppermute | solution.py:93
  45.7 0.6 slice_bitcast_fusion.13
  46.3 0.7 copy.18
  47.1 1.5 %select_select_fusion.1 = (f32[128,128]{1,0:T(8,128)}, f32[128,128]{1,0:T(8,128)S(1)}) fusion(pred[128,128]{1,0:T(8,128)(4,1)} %copy.12, f32[128,128]{1,0:T(8,128)} %copy.18, pred[128,128]{1,0:T(8,128)(4,1)S(1)} %copy.11, f32[128]{0:T(128)} %get-tuple-element.50, f32[128,128]{1,0:T(8,128)S(1)} %copy.13, f32[128]{0:T(128)} %get-tuple-element.51), kind=kLoop, calls=%fused_computation.124 | loop fusion | flops 65536 | bytes 295936 | tf_op jit(solution)/shard_map/jit(_where)/select_n | solution.py:98
  49.2 1.9 %collective-permute-start.7 = (f32[256,256]{1,0:T(8,128)S(1)}, f32[256,256]{1,0:T(8,128)S(1)}, u32[]{:S(2)}, u32[]{:S(2)}) collective-permute-start(f32[256,256]{1,0:T(8,128)S(1)} %broadcast_select_fusion.3), channel_id=1, source_target_pairs={{0,8},{8,0},{2,10},{10,2},{16,24},{24,16},{18,26},{26,18},{1,9},{9... | collective-permute-start | bytes 786440 | tf_op jit(solution)/shard_map/ppermute | solution.py:133
  51.1 1.3 %convolution_add_fusion = f32[256,256]{1,0:T(8,128)S(1)} fusion(f32[256,256]{1,0:T(8,128)S(1)} %get-tuple-element.44, f32[256,256]{1,0:T(8,128)} %copy-done.7, f32[3,256,256]{2,1,0:T(8,128)S(1)} %get-tuple-element.19), kind=kOutput, calls=%fused_computation.13 | convolution fusion | flops 100728832 | bytes 1048576 | tf_op jit(solution)/shard_map/dot_general | solution.py:12
  52.5 1.0 %fusion = f32[256,256]{1,0:T(8,128)} fusion(f32[256,256]{1,0:T(8,128)S(1)} %get-tuple-element.14, f32[256,256]{1,0:T(8,128)S(1)} %convolution_add_fusion, f32[3,256,256]{2,1,0:T(8,128)S(1)} %get-tuple-element.19, pred[]{:T(512)S(6)} %eq.62), kind=kOutput, calls=%fused_computation.12 | convolution fusion | flops 100794368 | bytes 1048577 | tf_op jit(solution)/shard_map/dot_general | solution.py:8
  53.5 5.5 %collective-permute-done.7 = f32[256,256]{1,0:T(8,128)S(1)} collective-permute-done((f32[256,256]{1,0:T(8,128)S(1)}, f32[256,256]{1,0:T(8,128)S(1)}, u32[]{:S(2)}, u32[]{:S(2)}) %collective-permute-start.7) | collective-permute-done | bytes 262176 | tf_op jit(solution)/shard_map/ppermute | solution.py:133
  59.1 0.6 copy-done.8
  60.3 2.1 %collective-permute-start.8 = (f32[256,256]{1,0:T(8,128)S(1)}, f32[256,256]{1,0:T(8,128)S(1)}, u32[]{:S(2)}, u32[]{:S(2)}) collective-permute-start(f32[256,256]{1,0:T(8,128)S(1)} %broadcast_select_fusion.2), channel_id=1, source_target_pairs={{0,16},{16,0},{2,18},{18,2},{1,17},{17,1},{3,19},{19,3}} | collective-permute-start | bytes 786440 | tf_op jit(solution)/shard_map/ppermute | solution.py:133
  62.3 1.3 %convolution_add_fusion.1 = f32[256,256]{0,1:T(8,128)S(1)} fusion(f32[256,256]{0,1:T(8,128)S(1)} %fusion.22, f32[256,256]{1,0:T(8,128)} %copy-done.8, f32[3,256,256]{2,1,0:T(8,128)S(1)} %get-tuple-element.19), kind=kOutput, calls=%fused_computation.16 | convolution fusion | flops 100728832 | bytes 1048576 | tf_op jit(solution)/shard_map/dot_general | solution.py:12
  64.1 6.2 %collective-permute-done.8 = f32[256,256]{1,0:T(8,128)S(1)} collective-permute-done((f32[256,256]{1,0:T(8,128)S(1)}, f32[256,256]{1,0:T(8,128)S(1)}, u32[]{:S(2)}, u32[]{:S(2)}) %collective-permute-start.8) | collective-permute-done | bytes 262176 | tf_op jit(solution)/shard_map/ppermute | solution.py:133
  71.0 0.6 copy-done.2
  72.2 1.5 %collective-permute-done.9 = f32[256,256]{1,0:T(8,128)S(1)} collective-permute-done((f32[256,256]{1,0:T(8,128)S(1)}, f32[256,256]{1,0:T(8,128)S(1)}, u32[]{:S(2)}, u32[]{:S(2)}) %collective-permute-start.9) | collective-permute-done | bytes 262176 | tf_op jit(solution)/shard_map/ppermute | solution.py:141
  73.8 1.1 %pad_maximum_fusion = f32[512,512]{1,0:T(8,128)} fusion(f32[256,512]{1,0:T(8,128)S(1)} %copy-done.3, f32[256,256]{1,0:T(8,128)S(1)} %get-tuple-element.28, f32[256,256]{1,0:T(8,128)S(1)} %get-tuple-element.27), kind=kLoop, calls=%fused_computation.21 | loop fusion | flops 524288 | bytes 2097152 | tf_op jit(solution)/shard_map/concatenate | solution.py:143
  (67 shorter events, 6.5 us)
Async XLA Ops:
  0.0 2.8 %copy-start.11 = (f32[256,128]{1,0:T(8,128)S(1)}, f32[256,128]{1,0:T(8,128)}, u32[]{:S(2)}) copy-start(f32[256,128]{1,0:T(8,128)} %param.9) | copy-start | bytes 393220
  2.9 17.8 %collective-permute-start = (f32[1280,128]{1,0:T(8,128)S(1)}, f32[1280,128]{1,0:T(8,128)S(1)}, u32[]{:S(2)}, u32[]{:S(2)}) collective-permute-start(f32[1280,128]{1,0:T(8,128)S(1)} %constant_dynamic-update-slice_fusion), channel_id=1, source_target_pairs={{0,1},{1,0},{2,3},{3,2},{4,5},{5,4},{6,7},{7,6},{8,9},{9,8},{10,11... | collective-permute-start | bytes 1966088 | tf_op jit(solution)/shard_map/ppermute | solution.py:34
  20.6 1.2 %copy-start = (f32[512,512]{1,0:T(8,128)S(1)}, f32[512,512]{1,0:T(8,128)}, u32[]{:S(2)}) copy-start(f32[512,512]{1,0:T(8,128)} %param.5) | copy-start | bytes 3145732
  23.0 2.6 %collective-permute-start.1 = (f32[3,256,256]{2,1,0:T(8,128)S(1)}, f32[3,256,256]{2,1,0:T(8,128)S(1)}, u32[]{:S(2)}, u32[]{:S(2)}) collective-permute-start(f32[3,256,256]{2,1,0:T(8,128)S(1)} %pad_maximum_fusion.1), channel_id=1, source_target_pairs={{0,2},{2,0},{4,6},{6,4},{8,10},{10,8},{12,14},{14,12},{16,18},{18,... | collective-permute-start | bytes 2359304 | tf_op jit(solution)/shard_map/ppermute | solution.py:69
  25.1 2.7 %collective-permute-start.2 = (f32[256,512]{1,0:T(8,128)S(1)}, f32[256,512]{1,0:T(8,128)S(1)}, u32[]{:S(2)}, u32[]{:S(2)}) collective-permute-start(f32[256,512]{1,0:T(8,128)S(1)} %get-tuple-element.25), channel_id=1, source_target_pairs={{0,2},{2,0},{4,6},{6,4},{8,10},{10,8},{12,14},{14,12},{16,18},{18,... | collective-permute-start | bytes 1572872 | tf_op jit(solution)/shard_map/ppermute | solution.py:104
  26.0 7.5 %collective-permute-start.3 = (f32[136,256]{1,0:T(8,128)S(1)}, f32[136,256]{1,0:T(8,128)S(1)}, u32[]{:S(2)}, u32[]{:S(2)}) collective-permute-start(f32[136,256]{1,0:T(8,128)S(1)} %pad_maximum_fusion.3), channel_id=1, source_target_pairs={{4,0},{6,2},{12,8},{14,10},{20,16},{22,18},{28,24},{30,26},{5,1},{... | collective-permute-start | bytes 417800 | tf_op jit(solution)/shard_map/ppermute | solution.py:93
  27.7 5.8 %copy-start.1 = (f32[256,256]{1,0:T(8,128)}, f32[256,256]{1,0:T(8,128)S(1)}, u32[]{:S(2)}) copy-start(f32[256,256]{1,0:T(8,128)S(1)} %fusion.44) | copy-start | bytes 786436
  27.8 5.8 %copy-start.4 = (f32[256,512]{1,0:T(8,128)}, f32[256,512]{1,0:T(8,128)S(1)}, u32[]{:S(2)}) copy-start(f32[256,512]{1,0:T(8,128)S(1)} %collective-permute-done.2) | copy-start | bytes 1572868
  34.2 7.4 %collective-permute-start.4 = (f32[256,256]{1,0:T(8,128)S(1)}, f32[256,256]{1,0:T(8,128)S(1)}, u32[]{:S(2)}, u32[]{:S(2)}) collective-permute-start(f32[256,256]{1,0:T(8,128)S(1)} %get-tuple-element.43), channel_id=1, source_target_pairs={{0,4},{4,0},{2,6},{6,2},{8,12},{12,8},{10,14},{14,10},{16,20},{20,... | collective-permute-start | bytes 786440 | tf_op jit(solution)/shard_map/ppermute | solution.py:133
  35.2 7.9 %collective-permute-start.6 = (f32[136,256]{1,0:T(8,128)S(1)}, f32[136,256]{1,0:T(8,128)S(1)}, u32[]{:S(2)}, u32[]{:S(2)}) collective-permute-start(f32[136,256]{1,0:T(8,128)S(1)} %pad_maximum_fusion.3), channel_id=1, source_target_pairs={{16,0},{18,2},{17,1},{19,3}} | collective-permute-start | bytes 417800 | tf_op jit(solution)/shard_map/ppermute | solution.py:93
  36.4 9.2 %collective-permute-start.5 = (f32[136,256]{1,0:T(8,128)S(1)}, f32[136,256]{1,0:T(8,128)S(1)}, u32[]{:S(2)}, u32[]{:S(2)}) collective-permute-start(f32[136,256]{1,0:T(8,128)S(1)} %pad_maximum_fusion.3), channel_id=1, source_target_pairs={{8,0},{10,2},{24,16},{26,18},{9,1},{11,3},{25,17},{27,19}} | collective-permute-start | bytes 417800 | tf_op jit(solution)/shard_map/ppermute | solution.py:93
  41.6 7.0 %copy-start.7 = (f32[256,256]{1,0:T(8,128)}, f32[256,256]{1,0:T(8,128)S(1)}, u32[]{:S(2)}) copy-start(f32[256,256]{1,0:T(8,128)S(1)} %collective-permute-done.4) | copy-start | bytes 786436
  49.2 9.8 %collective-permute-start.7 = (f32[256,256]{1,0:T(8,128)S(1)}, f32[256,256]{1,0:T(8,128)S(1)}, u32[]{:S(2)}, u32[]{:S(2)}) collective-permute-start(f32[256,256]{1,0:T(8,128)S(1)} %broadcast_select_fusion.3), channel_id=1, source_target_pairs={{0,8},{8,0},{2,10},{10,2},{16,24},{24,16},{18,26},{26,18},{1,9},{9... | collective-permute-start | bytes 786440 | tf_op jit(solution)/shard_map/ppermute | solution.py:133
  52.5 7.2 %copy-start.10 = (f32[128,128]{1,0:T(8,128)S(1)}, f32[128,128]{1,0:T(8,128)}, u32[]{:S(2)}) copy-start(f32[128,128]{1,0:T(8,128)} %get-tuple-element.39) | copy-start | bytes 196612
  59.0 0.7 copy-start.8
  60.2 3.5 %copy-start.6 = (f32[256,256]{1,0:T(8,128)S(1)}, f32[256,256]{1,0:T(8,128)}, u32[]{:S(2)}) copy-start(f32[256,256]{1,0:T(8,128)} %fusion) | copy-start | bytes 786436
  60.3 9.9 %collective-permute-start.8 = (f32[256,256]{1,0:T(8,128)S(1)}, f32[256,256]{1,0:T(8,128)S(1)}, u32[]{:S(2)}, u32[]{:S(2)}) collective-permute-start(f32[256,256]{1,0:T(8,128)S(1)} %broadcast_select_fusion.2), channel_id=1, source_target_pairs={{0,16},{16,0},{2,18},{18,2},{1,17},{17,1},{3,19},{19,3}} | collective-permute-start | bytes 786440 | tf_op jit(solution)/shard_map/ppermute | solution.py:133
  70.6 1.0 %copy-start.2 = (f32[256,256]{1,0:T(8,128)S(1)}, f32[256,256]{1,0:T(8,128)}, u32[]{:S(2)}) copy-start(f32[256,256]{1,0:T(8,128)} %copy-done.1) | copy-start | bytes 786436
  70.6 1.1 %copy-start.5 = (f32[256,512]{1,0:T(8,128)S(1)}, f32[256,512]{1,0:T(8,128)}, u32[]{:S(2)}) copy-start(f32[256,512]{1,0:T(8,128)} %copy-done.4) | copy-start | bytes 1572868
  70.6 1.2 %copy-start.9 = (f32[256,256]{1,0:T(8,128)S(1)}, f32[256,256]{1,0:T(8,128)}, u32[]{:S(2)}) copy-start(f32[256,256]{1,0:T(8,128)} %get-tuple-element.42) | copy-start | bytes 786436
  72.1 1.7 %copy-start.3 = (f32[256,512]{1,0:T(8,128)S(1)}, f32[256,512]{1,0:T(8,128)}, u32[]{:S(2)}) copy-start(f32[256,512]{1,0:T(8,128)} %get-tuple-element.26) | copy-start | bytes 1572868
  72.1 1.6 %collective-permute-start.9 = (f32[256,256]{1,0:T(8,128)S(1)}, f32[256,256]{1,0:T(8,128)S(1)}, u32[]{:S(2)}, u32[]{:S(2)}) collective-permute-start(f32[256,256]{1,0:T(8,128)S(1)} %get-tuple-element.45), channel_id=1, source_target_pairs={{0,2},{2,0},{4,6},{6,4},{8,10},{10,8},{12,14},{14,12},{16,18},{18,... | collective-permute-start | bytes 786440 | tf_op jit(solution)/shard_map/ppermute | solution.py:141

commit v8 on v7

--- a/solution.py
+++ b/solution.py
@@ -104,7 +104,7 @@
     received = lax.ppermute(current, "row", swap)
     own_h = lax.dynamic_slice(current, (0, core * half), (width, half))
     early = product_left_t(jnp.where(is_lower, odd3[1], odd3[2]), own_h)
-    early, received = lax.optimization_barrier((early, received))
+    early, received, partner_factors[0] = lax.optimization_barrier((early, received, partner_factors[0]))
     recv_h = lax.dynamic_slice(received, (0, core * half), (width, half))
     update = early + product_left_t(jnp.where(is_lower, odd3[2], odd3[1]), recv_h)
     upper_h = jnp.where(is_lower, recv_h, own_h)
@@ -114,26 +114,24 @@
     zeros = jnp.zeros_like(tree_factor)
     result = chain
     for level in range(1, levels):
-        if level == 1:
-            chain, partner_factors[0] = lax.optimization_barrier((chain, partner_factors[0]))
-        if level == 2:
-            chain, rest = lax.optimization_barrier((chain, partner_factors[1:]))
-            partner_factors[1:] = rest
         step = 1 << level
         phase = base % (2 * step)
         is_lower = phase == 0
         is_upper = phase == step
-        their_s = unpack(partner_factors[level - 1])
-        first = jnp.where(is_lower, their_s, jnp.where(is_upper, even3[2], zeros))
         pairs = []
         for i in range(0, n_row, 2 * step):
             for c in range(2):
                 pairs += [(i + c, i + step + c), (i + step + c, i + c)]
-        early = product_left_t(first, chain)
-        received = lax.ppermute(jnp.where(is_upper, early, chain), "row", pairs)
-        update = product_left_t(even3[1], received) + early
+        q = product_left_t(jnp.where(is_upper, even3[2], zeros), chain)
+        received = lax.ppermute(jnp.where(is_upper, q, chain), "row", pairs)
+        if level == 1:
+            received, rest = lax.optimization_barrier((received, partner_factors[1:]))
+            partner_factors[1:] = rest
+        their_s = unpack(partner_factors[level - 1])
+        own_part = product_left_t(jnp.where(is_lower, their_s, zeros), chain)
+        update = product_left_t(even3[1], received) + q
         result = jnp.where(is_upper, chain - product(even3[0], update), result)
-        chain = jnp.where(is_lower, chain - early - received, chain)
+        chain = jnp.where(is_lower, chain - own_part - received, chain)
     base_out = jnp.where(base == 0, chain, result)
 
     keep = jnp.where(core == 0, base_out, level0_out)

time: 75.3 us -> 80.5 us (1.069)
  waiting for transfers between devices: 40.5 us -> 25 us
  matrix products: 9.78 us -> 15.7 us
  other arithmetic: 3.65 us -> 9.56 us
  local copies, waits for them, and re-layouts: 8.85 us -> 13.1 us
  starting transfers between devices: 11.6 us -> 15.7 us
    ppermute x3, waiting for transfers between devices: 15.6 us -> 5.5 us  [on_device(): received = lax.ppermute(jnp.where(is_upper, q, chain), 'row', pairs)]
    ppermute x3, waiting for transfers between devices: 8.65 us -> 2.83 us  [on_device(): partner_factors.append(lax.ppermute(packed, 'row', pairs))]
    dot_general x10 -> x13, matrix products: 6.88 us -> 12.2 us  [product_left_t(): lax.dot_general(left, right, (((0,), (0,)), ((), ())), precision=lax.Prec...]
    select_n x2 -> x3, other arithmetic: 0.04 us -> 4.55 us  [unpack(): top_left = jnp.where(sub_r <= sub_c, square, 0.0)]
    ppermute x3, starting transfers between devices: 4.04 us -> 8.1 us  [on_device(): received = lax.ppermute(jnp.where(is_upper, q, chain), 'row', pairs)]
    transpose x2, local copies, waits for them, and re-layouts: 0.82 us -> 3.12 us  [unpack(): bottom_right = jnp.where(sub_r < sub_c, square.T, jnp.where(sub_r == sub_...]
    select_n x0 -> x1, local copies, waits for them, and re-layouts: none -> 1.55 us  [unpack(): top_left = jnp.where(sub_r <= sub_c, square, 0.0)]
    select_n x2 -> x3, other arithmetic: 1.58 us -> 2.6 us  [unpack(): jnp.where(sub_r < sub_c, square.T, jnp.where(sub_r == sub_c, got[hw:hw +...]
  transfers between devices with their start and end apart: 10 -> 10, of which waited for: 8 -> 6; matrix products, arithmetic and copies ran while one was open for 12% -> 24% of each run, Pallas kernels for 0% -> 0%
where the time goes in v8:
time: 80.5 us; the launch traced here: 79.5 us
  waiting for transfers between devices  25 us (31%)
  starting transfers between devices  15.7 us (20%)
  matrix products  15.7 us (20%)
  local copies, waits for them, and re-layouts  13.1 us (16%)
  other arithmetic  9.56 us (12%)
    ppermute x1, waiting for transfers between devices, col_gather(): by_shift.append(lax.ppermute(part, 'col', perm))  14.6 us
    dot_general x13, matrix products, product_left_t(): lax.dot_general(left, right, (((0,), (0,)), ((), ())), precision=lax.Prec...  12.2 us
    ppermute x3, starting transfers between devices, on_device(): received = lax.ppermute(jnp.where(is_upper, q, chain), 'row', pairs)  8.1 us
    ppermute x3, waiting for transfers between devices, on_device(): received = lax.ppermute(jnp.where(is_upper, q, chain), 'row', pairs)  5.5 us
    unnamed x26, local copies, waits for them, and re-layouts  4.8 us
    select_n x3, other arithmetic, unpack(): top_left = jnp.where(sub_r <= sub_c, square, 0.0)  4.55 us
    ppermute x3, starting transfers between devices, on_device(): partner_factors.append(lax.ppermute(packed, 'row', pairs))  3.86 us
    dot_general x6, matrix products, product(): jnp.dot(left, right, precision=lax.Precision.HIGH, preferred_element_type...  3.46 us
  transfers between devices with their start and end apart: 10, of which 6 were waited for; matrix products, arithmetic and copies ran while one was open for 24% of the time, Pallas kernels for 0%

profile of v8, /device:TPU:0, one launch (start us, length us, event | category | flops | bytes accessed | tf_op | source)
XLA Modules:
  0.0 79.5 jit_solution(2185738756621220071)
XLA Ops:
  0.0 1.0 %constant_dynamic-update-slice_fusion.3 = f32[1280,128]{1,0:T(8,128)S(1)} fusion(f32[512,128]{1,0:T(8,128)} %param.6), kind=kLoop, calls=%fused_computation.147 | loop fusion | bytes 524288
  1.0 0.9 %constant_dynamic-update-slice_fusion.2 = f32[1280,128]{1,0:T(8,128)S(1)} fusion(f32[1280,128]{1,0:T(8,128)S(1)} %constant_dynamic-update-slice_fusion.3, f32[256,128]{1,0:T(8,128)} %param.7), kind=kLoop, calls=%fused_computation.146 | loop fusion | bytes 262144
  1.9 0.9 %constant_dynamic-update-slice_fusion.1 = f32[1280,128]{1,0:T(8,128)S(1)} fusion(f32[1280,128]{1,0:T(8,128)S(1)} %constant_dynamic-update-slice_fusion.2, f32[256,128]{1,0:T(8,128)} %param.8), kind=kLoop, calls=%fused_computation.145 | loop fusion | bytes 262144
  2.9 3.0 %collective-permute-start = (f32[1280,128]{1,0:T(8,128)S(1)}, f32[1280,128]{1,0:T(8,128)S(1)}, u32[]{:S(2)}, u32[]{:S(2)}) collective-permute-start(f32[1280,128]{1,0:T(8,128)S(1)} %constant_dynamic-update-slice_fusion), channel_id=1, source_target_pairs={{0,1},{1,0},{2,3},{3,2},{4,5},{5,4},{6,7},{7,6},{8,9},{9,8},{10,11... | collective-permute-start | bytes 1966088 | tf_op jit(solution)/shard_map/ppermute | solution.py:34
  6.1 14.6 %collective-permute-done = f32[1280,128]{1,0:T(8,128)S(1)} collective-permute-done((f32[1280,128]{1,0:T(8,128)S(1)}, f32[1280,128]{1,0:T(8,128)S(1)}, u32[]{:S(2)}, u32[]{:S(2)}) %collective-permute-start) | collective-permute-done | bytes 655392 | tf_op jit(solution)/shard_map/ppermute | solution.py:34
  26.7 1.3 %collective-permute-start.3 = (f32[136,256]{1,0:T(8,128)}, f32[136,256]{1,0:T(8,128)S(1)}, u32[]{:S(2)}, u32[]{:S(2)}) collective-permute-start(f32[136,256]{1,0:T(8,128)} %pad_maximum_fusion.3), channel_id=1, source_target_pairs={{4,0},{6,2},{12,8},{14,10},{20,16},{22,18},{28,24},{30,26},{5,1},{... | collective-permute-start | bytes 417800 | tf_op jit(solution)/shard_map/ppermute | solution.py:93
  28.0 1.3 %collective-permute-start.5 = (f32[136,256]{1,0:T(8,128)}, f32[136,256]{1,0:T(8,128)}, u32[]{:S(2)}, u32[]{:S(2)}) collective-permute-start(f32[136,256]{1,0:T(8,128)} %pad_maximum_fusion.3), channel_id=1, source_target_pairs={{8,0},{10,2},{24,16},{26,18},{9,1},{11,3},{25,17},{27,19}} | collective-permute-start | bytes 417800 | tf_op jit(solution)/shard_map/ppermute | solution.py:93
  29.3 1.3 %collective-permute-start.6 = (f32[136,256]{1,0:T(8,128)}, f32[136,256]{1,0:T(8,128)}, u32[]{:S(2)}, u32[]{:S(2)}) collective-permute-start(f32[136,256]{1,0:T(8,128)} %pad_maximum_fusion.3), channel_id=1, source_target_pairs={{16,0},{18,2},{17,1},{19,3}} | collective-permute-start | bytes 417800 | tf_op jit(solution)/shard_map/ppermute | solution.py:93
  31.7 2.8 %collective-permute-done.3 = f32[136,256]{1,0:T(8,128)S(1)} collective-permute-done((f32[136,256]{1,0:T(8,128)}, f32[136,256]{1,0:T(8,128)S(1)}, u32[]{:S(2)}, u32[]{:S(2)}) %collective-permute-start.3) | collective-permute-done | bytes 139296 | tf_op jit(solution)/shard_map/ppermute | solution.py:93
  34.5 2.0 %select_subtract_fusion.1 = (f32[256,256]{1,0:T(8,128)S(1)}, f32[256,256]{1,0:T(8,128)}) fusion(f32[256,512]{1,0:T(8,128)} %copy-done.1, s32[]{:T(128)S(6)} %select_n.258, f32[256,512]{1,0:T(8,128)S(1)} %get-tuple-element.23, pred[]{:T(512)S(6)} %eq.54, f32[256,256]{1,0:T(8,128)S(1)} %fusion.49, f32[3,256,256]{1,2,0:T(8,128)S(1)} %get-tuple-element.18), kind=kOutput, calls=%fused_computation.87 | convolution fusion | flops 100925440 | bytes 2099200 | tf_op jit(solution)/shard_map/dot_general | solution.py:12
  36.6 1.0 %broadcast_select_fusion.4 = (f32[256,256]{1,0:T(8,128)}, f32[256,256]{1,0:T(8,128)S(1)}) fusion(f32[256,256]{1,0:T(8,128)S(1)} %get-tuple-element.35, pred[]{:T(512)S(6)} %eq.62, f32[3,256,256]{1,2,0:T(8,128)S(1)} %get-tuple-element.17), kind=kOutput, calls=%fused_computation.120 | convolution fusion | flops 100794368 | bytes 1311744 | tf_op jit(solution)/shard_map/dot_general | solution.py:12
  38.4 1.5 %slice_select_fusion.1 = f32[128,128]{0,1:T(8,128)} fusion(pred[128,128]{0,1:T(8,128)(4,1)} %copy-done.9, f32[136,256]{0,1:T(8,128)} %copy.16), kind=kLoop, calls=%fused_computation.139 | loop fusion | flops 16384 | bytes 147456 | tf_op jit(solution)/shard_map/jit(_where)/select_n | solution.py:97
  40.5 1.6 %copy.19 = f32[128,128]{1,0:T(8,128)} copy(f32[128,128]{0,1:T(8,128)} %slice_select_fusion.1) | data formatting | bytes 131072 | tf_op jit(solution)/shard_map/jit(_where)/select_n | solution.py:97
  42.1 0.9 %bitcast_select_fusion = f32[128,128]{1,0:T(8,128)S(1)} fusion(f32[136,256]{0,1:T(8,128)} %copy.16, f32[128]{0:T(128)S(1)} %slice_bitcast_fusion.13), kind=kLoop, calls=%fused_computation.132 | loop fusion | flops 65536 | bytes 131584 | tf_op jit(solution)/shard_map/jit(_where)/select_n | solution.py:98
  43.0 2.5 %collective-permute-done.4 = f32[256,256]{1,0:T(8,128)} collective-permute-done((f32[256,256]{1,0:T(8,128)}, f32[256,256]{1,0:T(8,128)}, u32[]{:S(2)}, u32[]{:S(2)}) %collective-permute-start.4) | collective-permute-done | bytes 262176 | tf_op jit(solution)/shard_map/ppermute | solution.py:126
  45.5 1.5 %slice_select_fusion.3 = (f32[128,128]{1,0:T(8,128)S(1)}, f32[128,128]{0,1:T(8,128)}, f32[128,128]{1,0:T(8,128)S(1)}) fusion(f32[136,256]{1,0:T(8,128)} %collective-permute-done.5), kind=kLoop, calls=%fused_computation.143 | loop fusion | flops 32768 | bytes 327680 | tf_op jit(solution)/shard_map/jit(_where)/select_n | solution.py:97
  47.7 1.5 %slice_select_fusion.2 = (f32[128,128]{1,0:T(8,128)}, f32[128,128]{0,1:T(8,128)}, f32[128,128]{1,0:T(8,128)}) fusion(f32[136,256]{1,0:T(8,128)} %collective-permute-done.6), kind=kLoop, calls=%fused_computation.141 | loop fusion | flops 32768 | bytes 327680 | tf_op jit(solution)/shard_map/jit(_where)/select_n | solution.py:97
  49.9 1.9 %convolution_add_fusion = f32[256,256]{1,0:T(8,128)} fusion(f32[256,256]{1,0:T(8,128)S(1)} %get-tuple-element.38, f32[256,256]{1,0:T(8,128)} %collective-permute-done.4, f32[3,256,256]{1,2,0:T(8,128)S(1)} %get-tuple-element.17), kind=kOutput, calls=%fused_computation.22 | convolution fusion | flops 100728832 | bytes 1048576 | tf_op jit(solution)/shard_map/dot_general | solution.py:12
  51.9 1.3 %fusion.1 = f32[256,256]{1,0:T(8,128)S(1)} fusion(f32[256,256]{1,0:T(8,128)S(1)} %get-tuple-element.35, f32[256,256]{1,0:T(8,128)} %collective-permute-done.4, f32[128,128]{1,0:T(8,128)S(1)} %bitcast_select_fusion, f32[128,128]{1,0:T(8,128)S(1)} %copy-done.5, f32[128,128]{1,0:T(8,128)S(1)} %copy-done.6, pred[]{:T(512)S(6)} %eq.58), kind=kOutput, calls=%fused_computation.15 | convolution fusion | flops 101187584 | bytes 983041 | tf_op jit(solution)/shard_map/dot_general | solution.py:12
  53.2 1.1 %broadcast_select_fusion.3 = (f32[256,256]{1,0:T(8,128)}, f32[256,256]{1,0:T(8,128)}) fusion(f32[256,256]{1,0:T(8,128)S(1)} %fusion.1, pred[]{:T(512)S(6)} %eq.63, f32[3,256,256]{1,2,0:T(8,128)S(1)} %get-tuple-element.17), kind=kOutput, calls=%fused_computation.118 | convolution fusion | flops 100794368 | bytes 1311744 | tf_op jit(solution)/shard_map/dot_general | solution.py:12
  54.3 3.6 %collective-permute-start.7 = (f32[256,256]{1,0:T(8,128)}, f32[256,256]{1,0:T(8,128)}, u32[]{:S(2)}, u32[]{:S(2)}) collective-permute-start(f32[256,256]{1,0:T(8,128)} %get-tuple-element.39), channel_id=1, source_target_pairs={{0,8},{8,0},{2,10},{10,2},{16,24},{24,16},{18,26},{26,18},{1,9},{9... | collective-permute-start | bytes 786440 | tf_op jit(solution)/shard_map/ppermute | solution.py:126
  57.9 1.6 %copy.21 = f32[128,128]{1,0:T(8,128)} copy(f32[128,128]{0,1:T(8,128)} %get-tuple-element.33) | data formatting | bytes 131072 | tf_op jit(solution)/shard_map/transpose | solution.py:98
  59.5 1.6 %copy.23 = f32[128,128]{1,0:T(8,128)} copy(f32[128,128]{0,1:T(8,128)} %get-tuple-element.30) | data formatting | bytes 131072 | tf_op jit(solution)/shard_map/transpose | solution.py:98
  61.0 0.9 %select_select_fusion.1 = f32[128,128]{1,0:T(8,128)S(1)} fusion(f32[128,128]{1,0:T(8,128)} %copy.21, f32[128]{0:T(128)S(1)} %slice_bitcast_fusion.12), kind=kLoop, calls=%fused_computation.134 | loop fusion | flops 65536 | bytes 131584 | tf_op jit(solution)/shard_map/jit(_where)/select_n | solution.py:98
  61.9 0.9 %select_select_fusion = f32[128,128]{1,0:T(8,128)S(1)} fusion(f32[128,128]{1,0:T(8,128)} %copy.23, f32[128]{0:T(128)S(1)} %slice_bitcast_fusion.11), kind=kLoop, calls=%fused_computation.133 | loop fusion | flops 65536 | bytes 131584 | tf_op jit(solution)/shard_map/jit(_where)/select_n | solution.py:98
  62.7 1.3 %fusion.6 = f32[256,256]{1,0:T(8,128)S(1)} fusion(f32[256,256]{1,0:T(8,128)S(1)} %get-tuple-element.35, f32[256,256]{1,0:T(8,128)} %convolution_add_fusion, f32[3,256,256]{1,2,0:T(8,128)S(1)} %get-tuple-element.17, pred[]{:T(512)S(6)} %eq.62), kind=kOutput, calls=%fused_computation.21 | convolution fusion | flops 100794368 | bytes 1048577 | tf_op jit(solution)/shard_map/dot_general | solution.py:8
  64.1 1.4 %fusion.3 = f32[256,256]{1,0:T(8,128)S(1)} fusion(f32[256,256]{1,0:T(8,128)S(1)} %fusion.1, f32[256,256]{1,0:T(8,128)} %collective-permute-done.7, f32[128,128]{1,0:T(8,128)S(1)} %select_select_fusion.1, f32[128,128]{1,0:T(8,128)S(1)} %get-tuple-element.34, f32[128,128]{1,0:T(8,128)S(1)} %get-tuple-element.32, pred[]{:T(512)S(6)} %eq.57), kind=kOutput, calls=%fused_computation.17 | convolution fusion | flops 101187584 | bytes 983041 | tf_op jit(solution)/shard_map/dot_general | solution.py:12
  65.8 4.5 %collective-permute-start.8 = (f32[256,256]{1,0:T(8,128)S(1)}, f32[256,256]{1,0:T(8,128)S(1)}, u32[]{:S(2)}, u32[]{:S(2)}) collective-permute-start(f32[256,256]{1,0:T(8,128)S(1)} %get-tuple-element.41), channel_id=1, source_target_pairs={{0,16},{16,0},{2,18},{18,2},{1,17},{17,1},{3,19},{19,3}} | collective-permute-start | bytes 786440 | tf_op jit(solution)/shard_map/ppermute | solution.py:126
  70.3 1.2 %convolution_add_fusion.1 = f32[256,256]{1,0:T(8,128)S(1)} fusion(f32[256,256]{1,0:T(8,128)S(1)} %copy-done.3, f32[256,256]{1,0:T(8,128)} %collective-permute-done.7, f32[3,256,256]{1,2,0:T(8,128)S(1)} %get-tuple-element.17), kind=kOutput, calls=%fused_computation.25 | convolution fusion | flops 100728832 | bytes 1048576 | tf_op jit(solution)/shard_map/dot_general | solution.py:12
  71.9 3.0 %collective-permute-done.8 = f32[256,256]{1,0:T(8,128)S(1)} collective-permute-done((f32[256,256]{1,0:T(8,128)S(1)}, f32[256,256]{1,0:T(8,128)S(1)}, u32[]{:S(2)}, u32[]{:S(2)}) %collective-permute-start.8) | collective-permute-done | bytes 262176 | tf_op jit(solution)/shard_map/ppermute | solution.py:126
  76.8 1.5 %collective-permute-done.9 = f32[256,256]{1,0:T(8,128)S(1)} collective-permute-done((f32[256,256]{1,0:T(8,128)S(1)}, f32[256,256]{1,0:T(8,128)S(1)}, u32[]{:S(2)}, u32[]{:S(2)}) %collective-permute-start.9) | collective-permute-done | bytes 262176 | tf_op jit(solution)/shard_map/ppermute | solution.py:139
  78.4 1.1 %pad_maximum_fusion = f32[512,512]{1,0:T(8,128)} fusion(f32[256,512]{1,0:T(8,128)S(1)} %get-tuple-element.24, f32[256,256]{1,0:T(8,128)S(1)} %get-tuple-element.26, f32[256,256]{1,0:T(8,128)S(1)} %get-tuple-element.25), kind=kLoop, calls=%fused_computation.31 | loop fusion | flops 524288 | bytes 2097152 | tf_op jit(solution)/shard_map/concatenate | solution.py:141
  (69 shorter events, 12.6 us)
Async XLA Ops:
  0.0 2.8 %copy-start.10 = (f32[256,128]{1,0:T(8,128)S(1)}, f32[256,128]{1,0:T(8,128)}, u32[]{:S(2)}) copy-start(f32[256,128]{1,0:T(8,128)} %param.9) | copy-start | bytes 393220
  2.9 17.8 %collective-permute-start = (f32[1280,128]{1,0:T(8,128)S(1)}, f32[1280,128]{1,0:T(8,128)S(1)}, u32[]{:S(2)}, u32[]{:S(2)}) collective-permute-start(f32[1280,128]{1,0:T(8,128)S(1)} %constant_dynamic-update-slice_fusion), channel_id=1, source_target_pairs={{0,1},{1,0},{2,3},{3,2},{4,5},{5,4},{6,7},{7,6},{8,9},{9,8},{10,11... | collective-permute-start | bytes 1966088 | tf_op jit(solution)/shard_map/ppermute | solution.py:34
  6.0 19.8 %copy-start.9 = (pred[128,128]{0,1:T(8,128)(4,1)}, pred[128,128]{0,1:T(8,128)(4,1)S(1)}, u32[]{:S(2)}) copy-start(pred[128,128]{0,1:T(8,128)(4,1)S(1)} %copy.13) | copy-start | bytes 49156
  20.9 1.2 %copy-start = (f32[512,512]{1,0:T(8,128)S(1)}, f32[512,512]{1,0:T(8,128)}, u32[]{:S(2)}) copy-start(f32[512,512]{1,0:T(8,128)} %param.5) | copy-start | bytes 3145732
  23.2 2.4 %collective-permute-start.1 = (f32[3,256,256]{1,2,0:T(8,128)S(1)}, f32[3,256,256]{1,2,0:T(8,128)S(1)}, u32[]{:S(2)}, u32[]{:S(2)}) collective-permute-start(f32[3,256,256]{1,2,0:T(8,128)S(1)} %pad_maximum_fusion.1), channel_id=1, source_target_pairs={{0,2},{2,0},{4,6},{6,4},{8,10},{10,8},{12,14},{14,12},{16,18},{18,... | collective-permute-start | bytes 2359304 | tf_op jit(solution)/shard_map/ppermute | solution.py:69
  24.4 6.6 %collective-permute-start.2 = (f32[256,512]{1,0:T(8,128)S(1)}, f32[256,512]{1,0:T(8,128)S(1)}, u32[]{:S(2)}, u32[]{:S(2)}) collective-permute-start(f32[256,512]{1,0:T(8,128)S(1)} %get-tuple-element.23), channel_id=1, source_target_pairs={{0,2},{2,0},{4,6},{6,4},{8,10},{10,8},{12,14},{14,12},{16,18},{18,... | collective-permute-start | bytes 1572872 | tf_op jit(solution)/shard_map/ppermute | solution.py:104
  26.7 7.8 %collective-permute-start.3 = (f32[136,256]{1,0:T(8,128)}, f32[136,256]{1,0:T(8,128)S(1)}, u32[]{:S(2)}, u32[]{:S(2)}) collective-permute-start(f32[136,256]{1,0:T(8,128)} %pad_maximum_fusion.3), channel_id=1, source_target_pairs={{4,0},{6,2},{12,8},{14,10},{20,16},{22,18},{28,24},{30,26},{5,1},{... | collective-permute-start | bytes 417800 | tf_op jit(solution)/shard_map/ppermute | solution.py:93
  28.0 15.0 %collective-permute-start.5 = (f32[136,256]{1,0:T(8,128)}, f32[136,256]{1,0:T(8,128)}, u32[]{:S(2)}, u32[]{:S(2)}) collective-permute-start(f32[136,256]{1,0:T(8,128)} %pad_maximum_fusion.3), channel_id=1, source_target_pairs={{8,0},{10,2},{24,16},{26,18},{9,1},{11,3},{25,17},{27,19}} | collective-permute-start | bytes 417800 | tf_op jit(solution)/shard_map/ppermute | solution.py:93
  29.3 13.7 %collective-permute-start.6 = (f32[136,256]{1,0:T(8,128)}, f32[136,256]{1,0:T(8,128)}, u32[]{:S(2)}, u32[]{:S(2)}) collective-permute-start(f32[136,256]{1,0:T(8,128)} %pad_maximum_fusion.3), channel_id=1, source_target_pairs={{16,0},{18,2},{17,1},{19,3}} | collective-permute-start | bytes 417800 | tf_op jit(solution)/shard_map/ppermute | solution.py:93
  30.9 0.8 %copy-start.1 = (f32[256,512]{1,0:T(8,128)}, f32[256,512]{1,0:T(8,128)S(1)}, u32[]{:S(2)}) copy-start(f32[256,512]{1,0:T(8,128)S(1)} %collective-permute-done.2) | copy-start | bytes 1572868
  37.6 7.9 %collective-permute-start.4 = (f32[256,256]{1,0:T(8,128)}, f32[256,256]{1,0:T(8,128)}, u32[]{:S(2)}, u32[]{:S(2)}) collective-permute-start(f32[256,256]{1,0:T(8,128)} %get-tuple-element.37), channel_id=1, source_target_pairs={{0,4},{4,0},{2,6},{6,2},{8,12},{12,8},{10,14},{14,10},{16,20},{20,... | collective-permute-start | bytes 786440 | tf_op jit(solution)/shard_map/ppermute | solution.py:126
  42.1 9.8 %copy-start.5 = (f32[128,128]{1,0:T(8,128)S(1)}, f32[128,128]{1,0:T(8,128)}, u32[]{:S(2)}) copy-start(f32[128,128]{1,0:T(8,128)} %slice.93) | copy-start | bytes 196612
  42.1 9.8 %copy-start.6 = (f32[128,128]{1,0:T(8,128)S(1)}, f32[128,128]{1,0:T(8,128)}, u32[]{:S(2)}) copy-start(f32[128,128]{1,0:T(8,128)} %copy.19) | copy-start | bytes 196612
  54.3 9.8 %collective-permute-start.7 = (f32[256,256]{1,0:T(8,128)}, f32[256,256]{1,0:T(8,128)}, u32[]{:S(2)}, u32[]{:S(2)}) collective-permute-start(f32[256,256]{1,0:T(8,128)} %get-tuple-element.39), channel_id=1, source_target_pairs={{0,8},{8,0},{2,10},{10,2},{16,24},{24,16},{18,26},{26,18},{1,9},{9... | collective-permute-start | bytes 786440 | tf_op jit(solution)/shard_map/ppermute | solution.py:126
  64.1 6.2 %copy-start.3 = (f32[256,256]{1,0:T(8,128)S(1)}, f32[256,256]{1,0:T(8,128)}, u32[]{:S(2)}) copy-start(f32[256,256]{1,0:T(8,128)} %get-tuple-element.40) | copy-start | bytes 786436
  65.8 9.2 %collective-permute-start.8 = (f32[256,256]{1,0:T(8,128)S(1)}, f32[256,256]{1,0:T(8,128)S(1)}, u32[]{:S(2)}, u32[]{:S(2)}) collective-permute-start(f32[256,256]{1,0:T(8,128)S(1)} %get-tuple-element.41), channel_id=1, source_target_pairs={{0,16},{16,0},{2,18},{18,2},{1,17},{17,1},{3,19},{19,3}} | collective-permute-start | bytes 786440 | tf_op jit(solution)/shard_map/ppermute | solution.py:126
  74.9 0.8 %copy-start.7 = (f32[128,128]{1,0:T(8,128)S(1)}, f32[128,128]{1,0:T(8,128)}, u32[]{:S(2)}) copy-start(f32[128,128]{1,0:T(8,128)} %get-tuple-element.29) | copy-start | bytes 196612
  74.9 0.9 %copy-start.8 = (f32[128,128]{1,0:T(8,128)S(1)}, f32[128,128]{1,0:T(8,128)}, u32[]{:S(2)}) copy-start(f32[128,128]{1,0:T(8,128)} %get-tuple-element.31) | copy-start | bytes 196612
  75.2 1.1 %copy-start.2 = (f32[256,512]{1,0:T(8,128)S(1)}, f32[256,512]{1,0:T(8,128)}, u32[]{:S(2)}) copy-start(f32[256,512]{1,0:T(8,128)} %copy-done.1) | copy-start | bytes 1572868
  75.2 1.1 %copy-start.4 = (f32[256,256]{1,0:T(8,128)S(1)}, f32[256,256]{1,0:T(8,128)}, u32[]{:S(2)}) copy-start(f32[256,256]{1,0:T(8,128)} %get-tuple-element.36) | copy-start | bytes 786436
  76.7 1.6 %collective-permute-start.9 = (f32[256,256]{1,0:T(8,128)S(1)}, f32[256,256]{1,0:T(8,128)S(1)}, u32[]{:S(2)}, u32[]{:S(2)}) collective-permute-start(f32[256,256]{1,0:T(8,128)S(1)} %get-tuple-element.43), channel_id=1, source_target_pairs={{0,2},{2,0},{4,6},{6,4},{8,10},{10,8},{12,14},{14,12},{16,18},{18,... | collective-permute-start | bytes 786440 | tf_op jit(solution)/shard_map/ppermute | solution.py:139

commit v9 on v8

--- a/solution.py
+++ b/solution.py
@@ -70,20 +70,7 @@
     odd3 = jnp.where(core == 1, own3, mate3)
     even3 = jnp.where(core == 0, own3, mate3)
 
-    hw = width // 2
-    sub_r = lax.broadcasted_iota(jnp.int32, (hw, hw), 0)
-    sub_c = lax.broadcasted_iota(jnp.int32, (hw, hw), 1)
-    even_s = even3[1]
-    corner = even_s[hw:, hw:]
-    folded = jnp.where(sub_r <= sub_c, even_s[:hw, :hw], corner.T)
-    corner_diag = jnp.sum(jnp.where(sub_r == sub_c, corner, 0.0), axis=0, keepdims=True)
-    packed = jnp.concatenate(
-        [
-            jnp.concatenate([folded, even_s[:hw, hw:]], axis=1),
-            jnp.broadcast_to(jnp.concatenate([corner_diag, jnp.zeros_like(corner_diag)], axis=1), (8, width)),
-        ],
-        axis=0,
-    )
+    packed = even3[1]
     partner_factors = []
     for level in range(1, levels):
         step = 1 << level
@@ -91,14 +78,6 @@
         for i in range(0, n_row, 2 * step):
             pairs += [(i + step, i), (i + step + 1, i + 1)]
         partner_factors.append(lax.ppermute(packed, "row", pairs))
-
-    def unpack(got):
-        square = got[:hw, :hw]
-        top_left = jnp.where(sub_r <= sub_c, square, 0.0)
-        bottom_right = jnp.where(sub_r < sub_c, square.T, jnp.where(sub_r == sub_c, got[hw:hw + 1, :hw], 0.0))
-        top = jnp.concatenate([top_left, got[:hw, hw:]], axis=1)
-        bottom = jnp.concatenate([jnp.zeros_like(bottom_right), bottom_right], axis=1)
-        return jnp.concatenate([top, bottom], axis=0)
 
     is_lower = core == 0
     received = lax.ppermute(current, "row", swap)
@@ -127,7 +106,7 @@
         if level == 1:
             received, rest = lax.optimization_barrier((received, partner_factors[1:]))
             partner_factors[1:] = rest
-        their_s = unpack(partner_factors[level - 1])
+        their_s = partner_factors[level - 1]
         own_part = product_left_t(jnp.where(is_lower, their_s, zeros), chain)
         update = product_left_t(even3[1], received) + q
         result = jnp.where(is_upper, chain - product(even3[0], update), result)

time: 80.5 us -> 75.8 us (0.942)
  waiting for transfers between devices: 25 us -> 38 us
  local copies, waits for them, and re-layouts: 13.1 us -> 4.6 us
  other arithmetic: 9.56 us -> 1.68 us
  matrix products: 15.7 us -> 14.8 us
    select_n x7 -> x0, other arithmetic: 7.17 us -> none  [the longest x3 4.55 us: unpack(): top_left = jnp.where(sub_r <= sub_c, square, 0.0)]
    ppermute x3, waiting for transfers between devices: 2.83 us -> 9.94 us  [on_device(): partner_factors.append(lax.ppermute(packed, 'row', pairs))]
    ppermute x3, waiting for transfers between devices: 5.5 us -> 11.3 us  [on_device(): received = lax.ppermute(jnp.where(is_upper, q, chain), 'row', pairs)]
    transpose x2 -> x0, local copies, waits for them, and re-layouts: 3.12 us -> none  [unpack(): bottom_right = jnp.where(sub_r < sub_c, square.T, jnp.where(sub_r == sub_...]
    select_n x1 -> x0, local copies, waits for them, and re-layouts: 1.55 us -> none  [unpack(): top_left = jnp.where(sub_r <= sub_c, square, 0.0)]
    broadcast_in_dim x4 -> x0, local copies, waits for them, and re-layouts: 1.36 us -> none  [the longest x3 1.35 us: unpack(): jnp.where(sub_r == sub_c, got[hw:hw + 1, :hw], 0.0)]
    unnamed x26 -> x9, local copies, waits for them, and re-layouts: 4.8 us -> 3.81 us
    optimization_barrier x1 -> x0, local copies, waits for them, and re-layouts: 0.85 us -> none  [on_device(): lax.optimization_barrier((early, received, partner_factors[0]))]
  transfers between devices with their start and end apart: 10 -> 10, of which waited for: 6 -> 8; matrix products, arithmetic and copies ran while one was open for 24% -> 11% of each run, Pallas kernels for 0% -> 0%
where the time goes in v9:
time: 75.8 us; the launch traced here: 75.3 us
  waiting for transfers between devices  38 us (50%)
  starting transfers between devices  16 us (21%)
  matrix products  14.8 us (20%)
  local copies, waits for them, and re-layouts  4.6 us (6%)
  other arithmetic  1.68 us (2%)
    ppermute x1, waiting for transfers between devices, col_gather(): by_shift.append(lax.ppermute(part, 'col', perm))  14.7 us
    dot_general x13, matrix products, product_left_t(): lax.dot_general(left, right, (((0,), (0,)), ((), ())), precision=lax.Prec...  11.8 us
    ppermute x3, waiting for transfers between devices, on_device(): received = lax.ppermute(jnp.where(is_upper, q, chain), 'row', pairs)  11.3 us
    ppermute x3, waiting for transfers between devices, on_device(): partner_factors.append(lax.ppermute(packed, 'row', pairs))  9.94 us
    ppermute x3, starting transfers between devices, on_device(): received = lax.ppermute(jnp.where(is_upper, q, chain), 'row', pairs)  8.36 us
    ppermute x3, starting transfers between devices, on_device(): partner_factors.append(lax.ppermute(packed, 'row', pairs))  3.86 us
    unnamed x9, local copies, waits for them, and re-layouts  3.81 us
    ppermute x1, starting transfers between devices, col_gather(): by_shift.append(lax.ppermute(part, 'col', perm))  3.03 us
  transfers between devices with their start and end apart: 10, of which 8 were waited for; matrix products, arithmetic and copies ran while one was open for 11% of the time, Pallas kernels for 0%

profile of v9, /device:TPU:0, one launch (start us, length us, event | category | flops | bytes accessed | tf_op | source)
XLA Modules:
  0.0 75.3 jit_solution(17353081610324057047)
XLA Ops:
  0.0 1.0 %constant_dynamic-update-slice_fusion.3 = f32[1280,128]{1,0:T(8,128)S(1)} fusion(f32[512,128]{1,0:T(8,128)} %param.6), kind=kLoop, calls=%fused_computation.112 | loop fusion | bytes 524288
  1.0 0.9 %constant_dynamic-update-slice_fusion.2 = f32[1280,128]{1,0:T(8,128)S(1)} fusion(f32[1280,128]{1,0:T(8,128)S(1)} %constant_dynamic-update-slice_fusion.3, f32[256,128]{1,0:T(8,128)} %param.7), kind=kLoop, calls=%fused_computation.111 | loop fusion | bytes 262144
  1.9 0.9 %constant_dynamic-update-slice_fusion.1 = f32[1280,128]{1,0:T(8,128)S(1)} fusion(f32[1280,128]{1,0:T(8,128)S(1)} %constant_dynamic-update-slice_fusion.2, f32[256,128]{1,0:T(8,128)} %param.8), kind=kLoop, calls=%fused_computation.110 | loop fusion | bytes 262144
  2.9 3.0 %collective-permute-start = (f32[1280,128]{1,0:T(8,128)S(1)}, f32[1280,128]{1,0:T(8,128)S(1)}, u32[]{:S(2)}, u32[]{:S(2)}) collective-permute-start(f32[1280,128]{1,0:T(8,128)S(1)} %constant_dynamic-update-slice_fusion), channel_id=1, source_target_pairs={{0,1},{1,0},{2,3},{3,2},{4,5},{5,4},{6,7},{7,6},{8,9},{9,8},{10,11... | collective-permute-start | bytes 1966088 | tf_op jit(solution)/shard_map/ppermute | solution.py:34
  5.9 14.7 %collective-permute-done = f32[1280,128]{1,0:T(8,128)S(1)} collective-permute-done((f32[1280,128]{1,0:T(8,128)S(1)}, f32[1280,128]{1,0:T(8,128)S(1)}, u32[]{:S(2)}, u32[]{:S(2)}) %collective-permute-start) | collective-permute-done | bytes 655392 | tf_op jit(solution)/shard_map/ppermute | solution.py:34
  20.9 1.0 %copy-done = f32[512,512]{1,0:T(8,128)S(1)} copy-done((f32[512,512]{1,0:T(8,128)S(1)}, f32[512,512]{1,0:T(8,128)}, u32[]{:S(2)}) %copy-start) | copy-done | bytes 1048600
  21.9 0.7 fusion.82
  23.1 0.5 fusion.21
  23.6 0.6 convolution_subtract_fusion
  24.3 0.6 collective-permute-start.2
  24.9 0.5 collective-permute-done.1
  25.5 0.7 slice_bitcast_fusion.3
  26.2 1.3 %collective-permute-start.3 = (f32[256,256]{1,0:T(8,128)}, f32[256,256]{1,0:T(8,128)}, u32[]{:S(2)}, u32[]{:S(2)}) collective-permute-start(f32[256,256]{1,0:T(8,128)} %slice_bitcast_fusion.3), channel_id=1, source_target_pairs={{4,0},{6,2},{12,8},{14,10},{20,16},{22,18},{28,24},{30,26},{5,1},{... | collective-permute-start | bytes 786440 | tf_op jit(solution)/shard_map/ppermute | solution.py:80
  27.6 1.3 %collective-permute-start.5 = (f32[256,256]{1,0:T(8,128)}, f32[256,256]{1,0:T(8,128)}, u32[]{:S(2)}, u32[]{:S(2)}) collective-permute-start(f32[256,256]{1,0:T(8,128)} %slice_bitcast_fusion.3), channel_id=1, source_target_pairs={{8,0},{10,2},{24,16},{26,18},{9,1},{11,3},{25,17},{27,19}} | collective-permute-start | bytes 786440 | tf_op jit(solution)/shard_map/ppermute | solution.py:80
  28.9 1.3 %collective-permute-start.6 = (f32[256,256]{1,0:T(8,128)}, f32[256,256]{1,0:T(8,128)}, u32[]{:S(2)}, u32[]{:S(2)}) collective-permute-start(f32[256,256]{1,0:T(8,128)} %slice_bitcast_fusion.3), channel_id=1, source_target_pairs={{16,0},{18,2},{17,1},{19,3}} | collective-permute-start | bytes 786440 | tf_op jit(solution)/shard_map/ppermute | solution.py:80
  30.2 0.4 fusion.33
  30.6 6.2 %collective-permute-done.3 = f32[256,256]{1,0:T(8,128)} collective-permute-done((f32[256,256]{1,0:T(8,128)}, f32[256,256]{1,0:T(8,128)}, u32[]{:S(2)}, u32[]{:S(2)}) %collective-permute-start.3) | collective-permute-done | bytes 262176 | tf_op jit(solution)/shard_map/ppermute | solution.py:80
  36.8 2.1 %select_subtract_fusion.1 = (f32[256,256]{1,0:T(8,128)S(1)}, f32[256,256]{1,0:T(8,128)}) fusion(f32[256,512]{1,0:T(8,128)} %collective-permute-done.2, s32[]{:T(128)S(6)} %select_n.222, f32[256,512]{1,0:T(8,128)S(1)} %get-tuple-element.23, pred[]{:T(512)S(6)} %eq.42, f32[256,256]{1,0:T(8,128)S(1)} %fusion.33, f32[3,256,256]{2,1,0:T(8,128)S(1)} %get-tuple-element.18), kind=kOutput, calls=%fused_computation.73 | convolution fusion | flops 100925440 | bytes 2099200 | tf_op jit(solution)/shard_map/dot_general | solution.py:12
  38.9 1.1 %broadcast_select_fusion.4 = (f32[256,256]{1,0:T(8,128)}, f32[256,256]{1,0:T(8,128)S(1)}) fusion(f32[256,256]{1,0:T(8,128)S(1)} %get-tuple-element.27, pred[]{:T(512)S(6)} %eq.49, f32[3,256,256]{2,1,0:T(8,128)S(1)} %get-tuple-element.17), kind=kOutput, calls=%fused_computation.98 | convolution fusion | flops 100794368 | bytes 1311744 | tf_op jit(solution)/shard_map/dot_general | solution.py:12
  40.0 3.7 %collective-permute-done.5 = f32[256,256]{1,0:T(8,128)} collective-permute-done((f32[256,256]{1,0:T(8,128)}, f32[256,256]{1,0:T(8,128)}, u32[]{:S(2)}, u32[]{:S(2)}) %collective-permute-start.5) | collective-permute-done | bytes 262176 | tf_op jit(solution)/shard_map/ppermute | solution.py:80
  43.7 4.2 %collective-permute-done.4 = f32[256,256]{1,0:T(8,128)} collective-permute-done((f32[256,256]{1,0:T(8,128)}, f32[256,256]{1,0:T(8,128)}, u32[]{:S(2)}, u32[]{:S(2)}) %collective-permute-start.4) | collective-permute-done | bytes 262176 | tf_op jit(solution)/shard_map/ppermute | solution.py:105
  47.9 1.4 %fusion.1 = f32[256,256]{1,0:T(8,128)S(1)} fusion(f32[256,256]{1,0:T(8,128)S(1)} %get-tuple-element.27, f32[256,256]{1,0:T(8,128)} %collective-permute-done.4, f32[256,256]{1,0:T(8,128)} %collective-permute-done.3, pred[]{:T(512)S(6)} %eq.46), kind=kOutput, calls=%fused_computation.15 | convolution fusion | flops 100925440 | bytes 1048577 | tf_op jit(solution)/shard_map/dot_general | solution.py:12
  49.7 3.7 %collective-permute-start.7 = (f32[256,256]{1,0:T(8,128)S(1)}, f32[256,256]{1,0:T(8,128)S(1)}, u32[]{:S(2)}, u32[]{:S(2)}) collective-permute-start(f32[256,256]{1,0:T(8,128)S(1)} %get-tuple-element.31), channel_id=1, source_target_pairs={{0,8},{8,0},{2,10},{10,2},{16,24},{24,16},{18,26},{26,18},{1,9},{9... | collective-permute-start | bytes 786440 | tf_op jit(solution)/shard_map/ppermute | solution.py:105
  53.4 1.3 %convolution_add_fusion = f32[256,256]{1,0:T(8,128)S(1)} fusion(f32[256,256]{1,0:T(8,128)S(1)} %get-tuple-element.30, f32[256,256]{1,0:T(8,128)} %collective-permute-done.4, f32[3,256,256]{2,1,0:T(8,128)S(1)} %get-tuple-element.17), kind=kOutput, calls=%fused_computation.22 | convolution fusion | flops 100728832 | bytes 1048576 | tf_op jit(solution)/shard_map/dot_general | solution.py:12
  55.1 3.3 %collective-permute-done.7 = f32[256,256]{1,0:T(8,128)S(1)} collective-permute-done((f32[256,256]{1,0:T(8,128)S(1)}, f32[256,256]{1,0:T(8,128)S(1)}, u32[]{:S(2)}, u32[]{:S(2)}) %collective-permute-start.7) | collective-permute-done | bytes 262176 | tf_op jit(solution)/shard_map/ppermute | solution.py:105
  58.3 1.3 %fusion.3 = f32[256,256]{1,0:T(8,128)S(1)} fusion(f32[256,256]{1,0:T(8,128)S(1)} %fusion.1, f32[256,256]{1,0:T(8,128)S(1)} %collective-permute-done.7, f32[256,256]{1,0:T(8,128)} %collective-permute-done.5, pred[]{:T(512)S(6)} %eq.45), kind=kOutput, calls=%fused_computation.17 | convolution fusion | flops 100925440 | bytes 1048577 | tf_op jit(solution)/shard_map/dot_general | solution.py:12
  60.1 4.7 %collective-permute-start.8 = (f32[256,256]{1,0:T(8,128)S(1)}, f32[256,256]{1,0:T(8,128)S(1)}, u32[]{:S(2)}, u32[]{:S(2)}) collective-permute-start(f32[256,256]{1,0:T(8,128)S(1)} %get-tuple-element.33), channel_id=1, source_target_pairs={{0,16},{16,0},{2,18},{18,2},{1,17},{17,1},{3,19},{19,3}} | collective-permute-start | bytes 786440 | tf_op jit(solution)/shard_map/ppermute | solution.py:105
  65.4 3.8 %collective-permute-done.8 = f32[256,256]{1,0:T(8,128)S(1)} collective-permute-done((f32[256,256]{1,0:T(8,128)S(1)}, f32[256,256]{1,0:T(8,128)S(1)}, u32[]{:S(2)}, u32[]{:S(2)}) %collective-permute-start.8) | collective-permute-done | bytes 262176 | tf_op jit(solution)/shard_map/ppermute | solution.py:105
  69.9 1.4 %fusion.9 = f32[256,256]{1,0:T(8,128)S(1)} fusion(f32[256,256]{1,0:T(8,128)S(1)} %fusion.8, f32[256,256]{1,0:T(8,128)S(1)} %fusion.3, f32[256,256]{1,0:T(8,128)S(1)} %collective-permute-done.8, f32[256,256]{1,0:T(8,128)} %collective-permute-done.6, pred[]{:T(512)S(6)} %eq.44, pred[]{:T(512)S(6)} %eq.43), kind=kOutput, calls=%fused_computation.30 | convolution fusion | flops 100990976 | bytes 1310722 | tf_op jit(solution)/shard_map/dot_general | solution.py:12
  71.3 1.3 %broadcast_select_fusion.7 = (f32[256,256]{1,0:T(8,128)S(1)}, f32[256,256]{1,0:T(8,128)S(1)}) fusion(f32[256,256]{1,0:T(8,128)S(1)} %fusion.9, pred[]{:T(512)S(6)} %eq.42, f32[256,256]{1,0:T(8,128)S(1)} %fusion.33, f32[256,256]{1,0:T(8,128)S(1)} %copy-done.1, f32[3,256,256]{2,1,0:T(8,128)S(1)} %get-tuple-element.18, f32[256,512]{1,0:T(8,128)S(1)} %get-tuple-element.23, ...), kind=kOutput, calls=%fused_computation.106 | convolution fusion | flops 100925440 | bytes 2097157 | tf_op jit(solution)/shard_map/dot_general | solution.py:8
  72.7 1.5 %collective-permute-done.9 = f32[256,256]{1,0:T(8,128)S(1)} collective-permute-done((f32[256,256]{1,0:T(8,128)S(1)}, f32[256,256]{1,0:T(8,128)S(1)}, u32[]{:S(2)}, u32[]{:S(2)}) %collective-permute-start.9) | collective-permute-done | bytes 262176 | tf_op jit(solution)/shard_map/ppermute | solution.py:118
  74.2 1.1 %pad_maximum_fusion = f32[512,512]{1,0:T(8,128)} fusion(f32[256,512]{1,0:T(8,128)S(1)} %get-tuple-element.24, f32[256,256]{1,0:T(8,128)S(1)} %get-tuple-element.26, f32[256,256]{1,0:T(8,128)S(1)} %get-tuple-element.25), kind=kLoop, calls=%fused_computation.31 | loop fusion | flops 524288 | bytes 2097152 | tf_op jit(solution)/shard_map/concatenate | solution.py:120
  (26 shorter events, 3.6 us)
Async XLA Ops:
  0.0 2.8 %copy-start.2 = (f32[256,128]{1,0:T(8,128)S(1)}, f32[256,128]{1,0:T(8,128)}, u32[]{:S(2)}) copy-start(f32[256,128]{1,0:T(8,128)} %param.9) | copy-start | bytes 393220
  2.9 17.8 %collective-permute-start = (f32[1280,128]{1,0:T(8,128)S(1)}, f32[1280,128]{1,0:T(8,128)S(1)}, u32[]{:S(2)}, u32[]{:S(2)}) collective-permute-start(f32[1280,128]{1,0:T(8,128)S(1)} %constant_dynamic-update-slice_fusion), channel_id=1, source_target_pairs={{0,1},{1,0},{2,3},{3,2},{4,5},{5,4},{6,7},{7,6},{8,9},{9,8},{10,11... | collective-permute-start | bytes 1966088 | tf_op jit(solution)/shard_map/ppermute | solution.py:34
  20.6 1.2 %copy-start = (f32[512,512]{1,0:T(8,128)S(1)}, f32[512,512]{1,0:T(8,128)}, u32[]{:S(2)}) copy-start(f32[512,512]{1,0:T(8,128)} %param.5) | copy-start | bytes 3145732
  23.0 2.4 %collective-permute-start.1 = (f32[3,256,256]{2,1,0:T(8,128)S(1)}, f32[3,256,256]{2,1,0:T(8,128)S(1)}, u32[]{:S(2)}, u32[]{:S(2)}) collective-permute-start(f32[3,256,256]{2,1,0:T(8,128)S(1)} %pad_maximum_fusion.1), channel_id=1, source_target_pairs={{0,2},{2,0},{4,6},{6,4},{8,10},{10,8},{12,14},{14,12},{16,18},{18,... | collective-permute-start | bytes 2359304 | tf_op jit(solution)/shard_map/ppermute | solution.py:69
  24.3 6.3 %collective-permute-start.2 = (f32[256,512]{1,0:T(8,128)S(1)}, f32[256,512]{1,0:T(8,128)}, u32[]{:S(2)}, u32[]{:S(2)}) collective-permute-start(f32[256,512]{1,0:T(8,128)S(1)} %get-tuple-element.23), channel_id=1, source_target_pairs={{0,2},{2,0},{4,6},{6,4},{8,10},{10,8},{12,14},{14,12},{16,18},{18,... | collective-permute-start | bytes 1572872 | tf_op jit(solution)/shard_map/ppermute | solution.py:83
  26.2 10.5 %collective-permute-start.3 = (f32[256,256]{1,0:T(8,128)}, f32[256,256]{1,0:T(8,128)}, u32[]{:S(2)}, u32[]{:S(2)}) collective-permute-start(f32[256,256]{1,0:T(8,128)} %slice_bitcast_fusion.3), channel_id=1, source_target_pairs={{4,0},{6,2},{12,8},{14,10},{20,16},{22,18},{28,24},{30,26},{5,1},{... | collective-permute-start | bytes 786440 | tf_op jit(solution)/shard_map/ppermute | solution.py:80
  27.6 16.2 %collective-permute-start.5 = (f32[256,256]{1,0:T(8,128)}, f32[256,256]{1,0:T(8,128)}, u32[]{:S(2)}, u32[]{:S(2)}) collective-permute-start(f32[256,256]{1,0:T(8,128)} %slice_bitcast_fusion.3), channel_id=1, source_target_pairs={{8,0},{10,2},{24,16},{26,18},{9,1},{11,3},{25,17},{27,19}} | collective-permute-start | bytes 786440 | tf_op jit(solution)/shard_map/ppermute | solution.py:80
  28.9 14.9 %collective-permute-start.6 = (f32[256,256]{1,0:T(8,128)}, f32[256,256]{1,0:T(8,128)}, u32[]{:S(2)}, u32[]{:S(2)}) collective-permute-start(f32[256,256]{1,0:T(8,128)} %slice_bitcast_fusion.3), channel_id=1, source_target_pairs={{16,0},{18,2},{17,1},{19,3}} | collective-permute-start | bytes 786440 | tf_op jit(solution)/shard_map/ppermute | solution.py:80
  40.0 7.9 %collective-permute-start.4 = (f32[256,256]{1,0:T(8,128)}, f32[256,256]{1,0:T(8,128)}, u32[]{:S(2)}, u32[]{:S(2)}) collective-permute-start(f32[256,256]{1,0:T(8,128)} %get-tuple-element.29), channel_id=1, source_target_pairs={{0,4},{4,0},{2,6},{6,2},{8,12},{12,8},{10,14},{14,10},{16,20},{20,... | collective-permute-start | bytes 786440 | tf_op jit(solution)/shard_map/ppermute | solution.py:105
  49.7 8.6 %collective-permute-start.7 = (f32[256,256]{1,0:T(8,128)S(1)}, f32[256,256]{1,0:T(8,128)S(1)}, u32[]{:S(2)}, u32[]{:S(2)}) collective-permute-start(f32[256,256]{1,0:T(8,128)S(1)} %get-tuple-element.31), channel_id=1, source_target_pairs={{0,8},{8,0},{2,10},{10,2},{16,24},{24,16},{18,26},{26,18},{1,9},{9... | collective-permute-start | bytes 786440 | tf_op jit(solution)/shard_map/ppermute | solution.py:105
  60.1 9.2 %collective-permute-start.8 = (f32[256,256]{1,0:T(8,128)S(1)}, f32[256,256]{1,0:T(8,128)S(1)}, u32[]{:S(2)}, u32[]{:S(2)}) collective-permute-start(f32[256,256]{1,0:T(8,128)S(1)} %get-tuple-element.33), channel_id=1, source_target_pairs={{0,16},{16,0},{2,18},{18,2},{1,17},{17,1},{3,19},{19,3}} | collective-permute-start | bytes 786440 | tf_op jit(solution)/shard_map/ppermute | solution.py:105
  69.6 1.7 %copy-start.1 = (f32[256,256]{1,0:T(8,128)S(1)}, f32[256,256]{1,0:T(8,128)}, u32[]{:S(2)}) copy-start(f32[256,256]{1,0:T(8,128)} %get-tuple-element.28) | copy-start | bytes 786436
  72.6 1.6 %collective-permute-start.9 = (f32[256,256]{1,0:T(8,128)S(1)}, f32[256,256]{1,0:T(8,128)S(1)}, u32[]{:S(2)}, u32[]{:S(2)}) collective-permute-start(f32[256,256]{1,0:T(8,128)S(1)} %get-tuple-element.35), channel_id=1, source_target_pairs={{0,2},{2,0},{4,6},{6,4},{8,10},{10,8},{12,14},{14,12},{16,18},{18,... | collective-permute-start | bytes 786440 | tf_op jit(solution)/shard_map/ppermute | solution.py:118

commit v10 on v9

--- a/solution.py
+++ b/solution.py
@@ -77,6 +77,8 @@
         pairs = []
         for i in range(0, n_row, 2 * step):
             pairs += [(i + step, i), (i + step + 1, i + 1)]
+        if level == 2:
+            partner_factors[0], packed = lax.optimization_barrier((partner_factors[0], packed))
         partner_factors.append(lax.ppermute(packed, "row", pairs))
 
     is_lower = core == 0
@@ -109,7 +111,17 @@
         their_s = partner_factors[level - 1]
         own_part = product_left_t(jnp.where(is_lower, their_s, zeros), chain)
         update = product_left_t(even3[1], received) + q
-        result = jnp.where(is_upper, chain - product(even3[0], update), result)
+        if level == levels - 1:
+            result = lax.cond(
+                is_upper,
+                lambda c, u, r: c - product(even3[0], u),
+                lambda c, u, r: r,
+                chain,
+                update,
+                result,
+            )
+        else:
+            result = jnp.where(is_upper, chain - product(even3[0], update), result)
         chain = jnp.where(is_lower, chain - own_part - received, chain)
     base_out = jnp.where(base == 0, chain, result)
 

time: 75.8 us -> 82.4 us (1.087)
  waiting for transfers between devices: 38 us -> 49.1 us
  starting transfers between devices: 16 us -> 12.4 us
  matrix products: 14.8 us -> 12.6 us
  local copies, waits for them, and re-layouts: 4.6 us -> 5.69 us
    ppermute x3, waiting for transfers between devices: 9.94 us -> 18.8 us  [on_device(): partner_factors.append(lax.ppermute(packed, 'row', pairs))]
    ppermute x3, starting transfers between devices: 8.36 us -> 4.92 us  [on_device(): received = lax.ppermute(jnp.where(is_upper, q, chain), 'row', pairs)]
    ppermute x3, waiting for transfers between devices: 11.3 us -> 14 us  [on_device(): received = lax.ppermute(jnp.where(is_upper, q, chain), 'row', pairs)]
    dot_general x13, matrix products: 11.8 us -> 9.93 us  [product_left_t(): lax.dot_general(left, right, (((0,), (0,)), ((), ())), precision=lax.Prec...]
    dot_general x6 -> x5, matrix products: 3 us -> 2.69 us  [product(): jnp.dot(left, right, precision=lax.Precision.HIGH, preferred_element_type...]
    unnamed x9 -> x13, local copies, waits for them, and re-layouts: 3.81 us -> 4.11 us
  transfers between devices with their start and end apart: 10 -> 10, of which waited for: 8 -> 7; matrix products, arithmetic and copies ran while one was open for 11% -> 9% of each run, Pallas kernels for 0% -> 0%
where the time goes in v10:
time: 82.4 us; the launch traced here: 82 us
  waiting for transfers between devices  49.1 us (60%)
  matrix products  12.6 us (15%)
  starting transfers between devices  12.4 us (15%)
  local copies, waits for them, and re-layouts  5.69 us (7%)
  other arithmetic  1.75 us (2%)
    ppermute x3, waiting for transfers between devices, on_device(): partner_factors.append(lax.ppermute(packed, 'row', pairs))  18.8 us
    ppermute x1, waiting for transfers between devices, col_gather(): by_shift.append(lax.ppermute(part, 'col', perm))  14.7 us
    ppermute x3, waiting for transfers between devices, on_device(): received = lax.ppermute(jnp.where(is_upper, q, chain), 'row', pairs)  14 us
    dot_general x13, matrix products, product_left_t(): lax.dot_general(left, right, (((0,), (0,)), ((), ())), precision=lax.Prec...  9.93 us
    ppermute x3, starting transfers between devices, on_device(): received = lax.ppermute(jnp.where(is_upper, q, chain), 'row', pairs)  4.92 us
    unnamed x13, local copies, waits for them, and re-layouts  4.11 us
    ppermute x3, starting transfers between devices, on_device(): partner_factors.append(lax.ppermute(packed, 'row', pairs))  3.85 us
    ppermute x1, starting transfers between devices, col_gather(): by_shift.append(lax.ppermute(part, 'col', perm))  3.03 us
  transfers between devices with their start and end apart: 10, of which 7 were waited for; matrix products, arithmetic and copies ran while one was open for 9% of the time, Pallas kernels for 0%

profile of v10, /device:TPU:0, one launch (start us, length us, event | category | flops | bytes accessed | tf_op | source)
XLA Modules:
  0.0 82.0 jit_solution(7318750533256325111)
XLA Ops:
  0.0 1.0 %constant_dynamic-update-slice_fusion.3 = f32[1280,128]{1,0:T(8,128)S(1)} fusion(f32[512,128]{1,0:T(8,128)} %param.8), kind=kLoop, calls=%fused_computation.114 | loop fusion | bytes 524288
  1.0 0.9 %constant_dynamic-update-slice_fusion.2 = f32[1280,128]{1,0:T(8,128)S(1)} fusion(f32[1280,128]{1,0:T(8,128)S(1)} %constant_dynamic-update-slice_fusion.3, f32[256,128]{1,0:T(8,128)} %param.9), kind=kLoop, calls=%fused_computation.113 | loop fusion | bytes 262144
  1.9 0.9 %constant_dynamic-update-slice_fusion.1 = f32[1280,128]{1,0:T(8,128)S(1)} fusion(f32[1280,128]{1,0:T(8,128)S(1)} %constant_dynamic-update-slice_fusion.2, f32[256,128]{1,0:T(8,128)} %param.10), kind=kLoop, calls=%fused_computation.112 | loop fusion | bytes 262144
  2.9 3.0 %collective-permute-start = (f32[1280,128]{1,0:T(8,128)S(1)}, f32[1280,128]{1,0:T(8,128)S(1)}, u32[]{:S(2)}, u32[]{:S(2)}) collective-permute-start(f32[1280,128]{1,0:T(8,128)S(1)} %constant_dynamic-update-slice_fusion), channel_id=1, source_target_pairs={{0,1},{1,0},{2,3},{3,2},{4,5},{5,4},{6,7},{7,6},{8,9},{9,8},{10,11... | collective-permute-start | bytes 1966088 | tf_op jit(solution)/shard_map/ppermute | solution.py:34
  5.9 14.7 %collective-permute-done = f32[1280,128]{1,0:T(8,128)S(1)} collective-permute-done((f32[1280,128]{1,0:T(8,128)S(1)}, f32[1280,128]{1,0:T(8,128)S(1)}, u32[]{:S(2)}, u32[]{:S(2)}) %collective-permute-start) | collective-permute-done | bytes 655392 | tf_op jit(solution)/shard_map/ppermute | solution.py:34
  20.9 1.0 %copy-done = f32[512,512]{1,0:T(8,128)S(1)} copy-done((f32[512,512]{1,0:T(8,128)S(1)}, f32[512,512]{1,0:T(8,128)}, u32[]{:S(2)}) %copy-start) | copy-done | bytes 1048600
  21.9 0.7 fusion.87
  23.1 0.5 fusion.23
  23.6 0.6 convolution_subtract_fusion
  24.2 0.9 %fusion.91 = (f32[256,512]{1,0:T(8,128)S(1)}, f32[256,512]{1,0:T(8,128)}) fusion(f32[512,512]{1,0:T(8,128)S(1)} %convolution_subtract_fusion), kind=kLoop, calls=%fused_computation.129 | loop fusion | bytes 2097152 | tf_op jit(solution)/shard_map/slice | solution.py:57
  25.1 0.5 collective-permute-start.2
  25.7 0.7 slice_bitcast_fusion.3
  26.4 1.3 %collective-permute-start.3 = (f32[256,256]{1,0:T(8,128)}, f32[256,256]{1,0:T(8,128)S(1)}, u32[]{:S(2)}, u32[]{:S(2)}) collective-permute-start(f32[256,256]{1,0:T(8,128)} %slice_bitcast_fusion.3), channel_id=1, source_target_pairs={{4,0},{6,2},{12,8},{14,10},{20,16},{22,18},{28,24},{30,26},{5,1},{... | collective-permute-start | bytes 786440 | tf_op jit(solution)/shard_map/ppermute | solution.py:82
  27.8 0.4 fusion.35
  28.2 8.6 %collective-permute-done.3 = f32[256,256]{1,0:T(8,128)S(1)} collective-permute-done((f32[256,256]{1,0:T(8,128)}, f32[256,256]{1,0:T(8,128)S(1)}, u32[]{:S(2)}, u32[]{:S(2)}) %collective-permute-start.3) | collective-permute-done | bytes 262176 | tf_op jit(solution)/shard_map/ppermute | solution.py:82
  36.8 1.3 %collective-permute-start.6 = (f32[256,256]{1,0:T(8,128)}, f32[256,256]{1,0:T(8,128)}, u32[]{:S(2)}, u32[]{:S(2)}) collective-permute-start(f32[256,256]{1,0:T(8,128)} %slice_bitcast_fusion.3), channel_id=1, source_target_pairs={{16,0},{18,2},{17,1},{19,3}} | collective-permute-start | bytes 786440 | tf_op jit(solution)/shard_map/ppermute | solution.py:82
  38.0 1.3 %collective-permute-start.5 = (f32[256,256]{1,0:T(8,128)}, f32[256,256]{1,0:T(8,128)}, u32[]{:S(2)}, u32[]{:S(2)}) collective-permute-start(f32[256,256]{1,0:T(8,128)} %slice_bitcast_fusion.3), channel_id=1, source_target_pairs={{8,0},{10,2},{24,16},{26,18},{9,1},{11,3},{25,17},{27,19}} | collective-permute-start | bytes 786440 | tf_op jit(solution)/shard_map/ppermute | solution.py:82
  39.4 2.1 %select_subtract_fusion.1 = (f32[256,256]{1,0:T(8,128)S(1)}, f32[256,256]{1,0:T(8,128)}) fusion(f32[256,512]{1,0:T(8,128)} %collective-permute-done.2, s32[]{:T(128)S(6)} %select_n.226, f32[256,512]{1,0:T(8,128)S(1)} %get-tuple-element.73, pred[]{:T(512)S(6)} %eq.42, f32[256,256]{1,0:T(8,128)S(1)} %fusion.35, f32[3,256,256]{2,1,0:T(8,128)S(1)} %get-tuple-element.68), kind=kOutput, calls=%fused_computation.73 | convolution fusion | flops 100925440 | bytes 2099200 | tf_op jit(solution)/shard_map/dot_general | solution.py:12
  41.5 1.1 %broadcast_select_fusion.4 = (f32[256,256]{1,0:T(8,128)}, f32[256,256]{1,0:T(8,128)S(1)}) fusion(f32[256,256]{1,0:T(8,128)S(1)} %get-tuple-element.77, pred[]{:T(512)} %eq.49, f32[3,256,256]{2,1,0:T(8,128)S(1)} %get-tuple-element.67), kind=kOutput, calls=%fused_computation.100 | convolution fusion | flops 100794368 | bytes 1311744 | tf_op jit(solution)/shard_map/dot_general | solution.py:12
  42.6 4.7 %collective-permute-done.6 = f32[256,256]{1,0:T(8,128)} collective-permute-done((f32[256,256]{1,0:T(8,128)}, f32[256,256]{1,0:T(8,128)}, u32[]{:S(2)}, u32[]{:S(2)}) %collective-permute-start.6) | collective-permute-done | bytes 262176 | tf_op jit(solution)/shard_map/ppermute | solution.py:82
  47.3 5.5 %collective-permute-done.5 = f32[256,256]{1,0:T(8,128)} collective-permute-done((f32[256,256]{1,0:T(8,128)}, f32[256,256]{1,0:T(8,128)}, u32[]{:S(2)}, u32[]{:S(2)}) %collective-permute-start.5) | collective-permute-done | bytes 262176 | tf_op jit(solution)/shard_map/ppermute | solution.py:82
  53.2 0.4 broadcast_select_fusion.3
  53.6 2.4 %collective-permute-start.7 = (f32[256,256]{1,0:T(8,128)S(1)}, f32[256,256]{1,0:T(8,128)S(1)}, u32[]{:S(2)}, u32[]{:S(2)}) collective-permute-start(f32[256,256]{1,0:T(8,128)S(1)} %get-tuple-element.81), channel_id=1, source_target_pairs={{0,8},{8,0},{2,10},{10,2},{16,24},{24,16},{18,26},{26,18},{1,9},{9... | collective-permute-start | bytes 786440 | tf_op jit(solution)/shard_map/ppermute | solution.py:107
  56.7 7.0 %collective-permute-done.7 = f32[256,256]{1,0:T(8,128)S(1)} collective-permute-done((f32[256,256]{1,0:T(8,128)S(1)}, f32[256,256]{1,0:T(8,128)S(1)}, u32[]{:S(2)}, u32[]{:S(2)}) %collective-permute-start.7) | collective-permute-done | bytes 262176 | tf_op jit(solution)/shard_map/ppermute | solution.py:107
  63.8 1.3 %fusion.8 = f32[256,256]{1,0:T(8,128)S(1)} fusion(f32[256,256]{1,0:T(8,128)S(1)} %fusion.6, f32[256,256]{1,0:T(8,128)S(1)} %collective-permute-done.7, f32[256,256]{1,0:T(8,128)} %collective-permute-done.5, pred[]{:T(512)S(6)} %eq.45), kind=kOutput, calls=%fused_computation.24 | convolution fusion | flops 100925440 | bytes 1048577 | tf_op jit(solution)/shard_map/dot_general | solution.py:12
  65.5 2.5 %collective-permute-start.8 = (f32[256,256]{1,0:T(8,128)S(1)}, f32[256,256]{1,0:T(8,128)S(1)}, u32[]{:S(2)}, u32[]{:S(2)}) collective-permute-start(f32[256,256]{1,0:T(8,128)S(1)} %get-tuple-element.83), channel_id=1, source_target_pairs={{0,16},{16,0},{2,18},{18,2},{1,17},{17,1},{3,19},{19,3}} | collective-permute-start | bytes 786440 | tf_op jit(solution)/shard_map/ppermute | solution.py:107
  68.0 0.4 convolution_add_fusion.1
  68.7 7.0 %collective-permute-done.8 = f32[256,256]{1,0:T(8,128)S(1)} collective-permute-done((f32[256,256]{1,0:T(8,128)S(1)}, f32[256,256]{1,0:T(8,128)S(1)}, u32[]{:S(2)}, u32[]{:S(2)}) %collective-permute-start.8) | collective-permute-done | bytes 262176 | tf_op jit(solution)/shard_map/ppermute | solution.py:107
  76.5 1.5 %fusion.11 = f32[256,256]{1,0:T(8,128)S(1)} fusion(f32[256,256]{1,0:T(8,128)S(1)} %get-tuple-element.87, f32[256,256]{1,0:T(8,128)S(1)} %fusion.8, f32[256,256]{1,0:T(8,128)} %copy-done.2, f32[256,256]{1,0:T(8,128)} %collective-permute-done.6, pred[]{:T(512)S(6)} %eq.44, pred[]{:T(512)S(6)} %eq.43), kind=kOutput, calls=%fused_computation.30 | convolution fusion | flops 100990976 | bytes 1310722 | tf_op jit(solution)/shard_map/dot_general | solution.py:12
  78.0 1.2 %broadcast_select_fusion.7 = (f32[256,256]{1,0:T(8,128)S(1)}, f32[256,256]{1,0:T(8,128)S(1)}) fusion(f32[256,256]{1,0:T(8,128)S(1)} %fusion.11, pred[]{:T(512)S(6)} %eq.42, f32[256,256]{1,0:T(8,128)S(1)} %fusion.35, f32[256,256]{1,0:T(8,128)S(1)} %copy-done.3, f32[3,256,256]{2,1,0:T(8,128)S(1)} %get-tuple-element.68, ...), kind=kOutput, calls=%fused_computation.108 | convolution fusion | flops 100925440 | bytes 2097157 | tf_op jit(solution)/shard_map/dot_general | solution.py:8
  79.3 1.5 %collective-permute-done.9 = f32[256,256]{1,0:T(8,128)S(1)} collective-permute-done((f32[256,256]{1,0:T(8,128)S(1)}, f32[256,256]{1,0:T(8,128)S(1)}, u32[]{:S(2)}, u32[]{:S(2)}) %collective-permute-start.9) | collective-permute-done | bytes 262176 | tf_op jit(solution)/shard_map/ppermute | solution.py:130
  80.9 1.1 %pad_maximum_fusion = f32[512,512]{1,0:T(8,128)} fusion(f32[256,512]{1,0:T(8,128)S(1)} %copy-done.1, f32[256,256]{1,0:T(8,128)S(1)} %get-tuple-element.76, f32[256,256]{1,0:T(8,128)S(1)} %get-tuple-element.75), kind=kLoop, calls=%fused_computation.31 | loop fusion | flops 524288 | bytes 2097152 | tf_op jit(solution)/shard_map/concatenate | solution.py:132
  (31 shorter events, 3.6 us)
Async XLA Ops:
  0.0 2.8 %copy-start.4 = (f32[256,128]{1,0:T(8,128)S(1)}, f32[256,128]{1,0:T(8,128)}, u32[]{:S(2)}) copy-start(f32[256,128]{1,0:T(8,128)} %param.11) | copy-start | bytes 393220
  2.9 17.8 %collective-permute-start = (f32[1280,128]{1,0:T(8,128)S(1)}, f32[1280,128]{1,0:T(8,128)S(1)}, u32[]{:S(2)}, u32[]{:S(2)}) collective-permute-start(f32[1280,128]{1,0:T(8,128)S(1)} %constant_dynamic-update-slice_fusion), channel_id=1, source_target_pairs={{0,1},{1,0},{2,3},{3,2},{4,5},{5,4},{6,7},{7,6},{8,9},{9,8},{10,11... | collective-permute-start | bytes 1966088 | tf_op jit(solution)/shard_map/ppermute | solution.py:34
  20.6 1.2 %copy-start = (f32[512,512]{1,0:T(8,128)S(1)}, f32[512,512]{1,0:T(8,128)}, u32[]{:S(2)}) copy-start(f32[512,512]{1,0:T(8,128)} %param.7) | copy-start | bytes 3145732
  23.0 2.6 %collective-permute-start.1 = (f32[3,256,256]{2,1,0:T(8,128)S(1)}, f32[3,256,256]{2,1,0:T(8,128)S(1)}, u32[]{:S(2)}, u32[]{:S(2)}) collective-permute-start(f32[3,256,256]{2,1,0:T(8,128)S(1)} %pad_maximum_fusion.1), channel_id=1, source_target_pairs={{0,2},{2,0},{4,6},{6,4},{8,10},{10,8},{12,14},{14,12},{16,18},{18,... | collective-permute-start | bytes 2359304 | tf_op jit(solution)/shard_map/ppermute | solution.py:69
  25.1 14.3 %collective-permute-start.2 = (f32[256,512]{1,0:T(8,128)S(1)}, f32[256,512]{1,0:T(8,128)}, u32[]{:S(2)}, u32[]{:S(2)}) collective-permute-start(f32[256,512]{1,0:T(8,128)S(1)} %get-tuple-element.73), channel_id=1, source_target_pairs={{0,2},{2,0},{4,6},{6,4},{8,10},{10,8},{12,14},{14,12},{16,18},{18,... | collective-permute-start | bytes 1572872 | tf_op jit(solution)/shard_map/ppermute | solution.py:85
  26.4 10.3 %collective-permute-start.3 = (f32[256,256]{1,0:T(8,128)}, f32[256,256]{1,0:T(8,128)S(1)}, u32[]{:S(2)}, u32[]{:S(2)}) collective-permute-start(f32[256,256]{1,0:T(8,128)} %slice_bitcast_fusion.3), channel_id=1, source_target_pairs={{4,0},{6,2},{12,8},{14,10},{20,16},{22,18},{28,24},{30,26},{5,1},{... | collective-permute-start | bytes 786440 | tf_op jit(solution)/shard_map/ppermute | solution.py:82
  36.8 10.6 %collective-permute-start.6 = (f32[256,256]{1,0:T(8,128)}, f32[256,256]{1,0:T(8,128)}, u32[]{:S(2)}, u32[]{:S(2)}) collective-permute-start(f32[256,256]{1,0:T(8,128)} %slice_bitcast_fusion.3), channel_id=1, source_target_pairs={{16,0},{18,2},{17,1},{19,3}} | collective-permute-start | bytes 786440 | tf_op jit(solution)/shard_map/ppermute | solution.py:82
  38.0 14.8 %collective-permute-start.5 = (f32[256,256]{1,0:T(8,128)}, f32[256,256]{1,0:T(8,128)}, u32[]{:S(2)}, u32[]{:S(2)}) collective-permute-start(f32[256,256]{1,0:T(8,128)} %slice_bitcast_fusion.3), channel_id=1, source_target_pairs={{8,0},{10,2},{24,16},{26,18},{9,1},{11,3},{25,17},{27,19}} | collective-permute-start | bytes 786440 | tf_op jit(solution)/shard_map/ppermute | solution.py:82
  42.6 10.3 %collective-permute-start.4 = (f32[256,256]{1,0:T(8,128)}, f32[256,256]{1,0:T(8,128)S(1)}, u32[]{:S(2)}, u32[]{:S(2)}) collective-permute-start(f32[256,256]{1,0:T(8,128)} %get-tuple-element.79), channel_id=1, source_target_pairs={{0,4},{4,0},{2,6},{6,2},{8,12},{12,8},{10,14},{14,10},{16,20},{20,... | collective-permute-start | bytes 786440 | tf_op jit(solution)/shard_map/ppermute | solution.py:107
  53.6 10.1 %collective-permute-start.7 = (f32[256,256]{1,0:T(8,128)S(1)}, f32[256,256]{1,0:T(8,128)S(1)}, u32[]{:S(2)}, u32[]{:S(2)}) collective-permute-start(f32[256,256]{1,0:T(8,128)S(1)} %get-tuple-element.81), channel_id=1, source_target_pairs={{0,8},{8,0},{2,10},{10,2},{16,24},{24,16},{18,26},{26,18},{1,9},{9... | collective-permute-start | bytes 786440 | tf_op jit(solution)/shard_map/ppermute | solution.py:107
  65.5 10.2 %collective-permute-start.8 = (f32[256,256]{1,0:T(8,128)S(1)}, f32[256,256]{1,0:T(8,128)S(1)}, u32[]{:S(2)}, u32[]{:S(2)}) collective-permute-start(f32[256,256]{1,0:T(8,128)S(1)} %get-tuple-element.83), channel_id=1, source_target_pairs={{0,16},{16,0},{2,18},{18,2},{1,17},{17,1},{3,19},{19,3}} | collective-permute-start | bytes 786440 | tf_op jit(solution)/shard_map/ppermute | solution.py:107
  75.7 0.7 copy-start.2
  76.5 1.5 %copy-start.3 = (f32[256,256]{1,0:T(8,128)S(1)}, f32[256,256]{1,0:T(8,128)}, u32[]{:S(2)}) copy-start(f32[256,256]{1,0:T(8,128)} %get-tuple-element.78) | copy-start | bytes 786436
  79.2 1.7 %copy-start.1 = (f32[256,512]{1,0:T(8,128)S(1)}, f32[256,512]{1,0:T(8,128)}, u32[]{:S(2)}) copy-start(f32[256,512]{1,0:T(8,128)} %get-tuple-element.74) | copy-start | bytes 1572868
  79.2 1.6 %collective-permute-start.9 = (f32[256,256]{1,0:T(8,128)S(1)}, f32[256,256]{1,0:T(8,128)S(1)}, u32[]{:S(2)}, u32[]{:S(2)}) collective-permute-start(f32[256,256]{1,0:T(8,128)S(1)} %get-tuple-element.85), channel_id=1, source_target_pairs={{0,2},{2,0},{4,6},{6,4},{8,10},{10,8},{12,14},{14,12},{16,18},{18,... | collective-permute-start | bytes 786440 | tf_op jit(solution)/shard_map/ppermute | solution.py:130

commit v11 on v9

--- a/solution.py
+++ b/solution.py
@@ -70,14 +70,15 @@
     odd3 = jnp.where(core == 1, own3, mate3)
     even3 = jnp.where(core == 0, own3, mate3)
 
-    packed = even3[1]
+    hw = width // 2
+    half_s = jnp.where(core == 0, even3[1][:hw], even3[1][hw:])
     partner_factors = []
     for level in range(1, levels):
         step = 1 << level
         pairs = []
         for i in range(0, n_row, 2 * step):
             pairs += [(i + step, i), (i + step + 1, i + 1)]
-        partner_factors.append(lax.ppermute(packed, "row", pairs))
+        partner_factors.append(lax.ppermute(half_s, "row", pairs))
 
     is_lower = core == 0
     received = lax.ppermute(current, "row", swap)
@@ -106,8 +107,11 @@
         if level == 1:
             received, rest = lax.optimization_barrier((received, partner_factors[1:]))
             partner_factors[1:] = rest
-        their_s = partner_factors[level - 1]
-        own_part = product_left_t(jnp.where(is_lower, their_s, zeros), chain)
+        mine = partner_factors[level - 1]
+        mates = lax.ppermute(mine, "row", swap)
+        top_rows = jnp.where(is_lower & (core == 0), mine, jnp.where(is_lower, mates, 0.0))
+        bottom_rows = jnp.where(is_lower & (core == 0), mates, jnp.where(is_lower, mine, 0.0))
+        own_part = product_left_t(top_rows, chain[:hw]) + product_left_t(bottom_rows, chain[hw:])
         update = product_left_t(even3[1], received) + q
         result = jnp.where(is_upper, chain - product(even3[0], update), result)
         chain = jnp.where(is_lower, chain - own_part - received, chain)

time: 75.8 us -> 74.8 us (0.987)
  waiting for transfers between devices: 38 us -> 42.1 us
  starting transfers between devices: 16 us -> 13.1 us
  matrix products: 14.8 us -> 12.5 us
    ppermute x3, starting transfers between devices: 8.36 us -> 4.85 us  [on_device(): received = lax.ppermute(jnp.where(is_upper, q, chain), 'row', pairs)]
    ppermute x3 -> x6, waiting for transfers between devices: 9.94 us -> 13.2 us  [the longest x3 12.7 us: on_device(): partner_factors.append(lax.ppermute(half_s, 'row', pairs))]
    dot_general x13 -> x16, matrix products: 11.8 us -> 10.5 us  [product_left_t(): lax.dot_general(left, right, (((0,), (0,)), ((), ())), precision=lax.Prec...]
    dot_general x6, matrix products: 3 us -> 2.02 us  [product(): jnp.dot(left, right, precision=lax.Precision.HIGH, preferred_element_type...]
    ppermute x3, waiting for transfers between devices: 11.3 us -> 12.1 us  [on_device(): received = lax.ppermute(jnp.where(is_upper, q, chain), 'row', pairs)]
    unnamed x9 -> x15, local copies, waits for them, and re-layouts: 3.81 us -> 4.58 us
    ppermute x3 -> x6, starting transfers between devices: 3.86 us -> 4.5 us  [the longest x3 3.87 us: on_device(): partner_factors.append(lax.ppermute(half_s, 'row', pairs))]
  transfers between devices with their start and end apart: 10 -> 13, of which waited for: 8 -> 8; matrix products, arithmetic and copies ran while one was open for 11% -> 10% of each run, Pallas kernels for 0% -> 0%
where the time goes in v11:
time: 74.8 us; the launch traced here: 74.4 us
  waiting for transfers between devices  42.1 us (56%)
  starting transfers between devices  13.1 us (18%)
  matrix products  12.5 us (17%)
  local copies, waits for them, and re-layouts  4.66 us (6%)
  other arithmetic  1.7 us (2%)
    ppermute x1, waiting for transfers between devices, col_gather(): by_shift.append(lax.ppermute(part, 'col', perm))  14.7 us
    ppermute x3, waiting for transfers between devices, on_device(): partner_factors.append(lax.ppermute(half_s, 'row', pairs))  12.7 us
    ppermute x3, waiting for transfers between devices, on_device(): received = lax.ppermute(jnp.where(is_upper, q, chain), 'row', pairs)  12.1 us
    dot_general x16, matrix products, product_left_t(): lax.dot_general(left, right, (((0,), (0,)), ((), ())), precision=lax.Prec...  10.5 us
    ppermute x3, starting transfers between devices, on_device(): received = lax.ppermute(jnp.where(is_upper, q, chain), 'row', pairs)  4.85 us
    unnamed x15, local copies, waits for them, and re-layouts  4.58 us
    ppermute x3, starting transfers between devices, on_device(): partner_factors.append(lax.ppermute(half_s, 'row', pairs))  3.87 us
    ppermute x1, starting transfers between devices, col_gather(): by_shift.append(lax.ppermute(part, 'col', perm))  3.03 us
  transfers between devices with their start and end apart: 13, of which 8 were waited for; matrix products, arithmetic and copies ran while one was open for 10% of the time, Pallas kernels for 0%

profile of v11, /device:TPU:0, one launch (start us, length us, event | category | flops | bytes accessed | tf_op | source)
XLA Modules:
  0.0 74.4 jit_solution(15159673451451089491)
XLA Ops:
  0.0 1.0 %constant_dynamic-update-slice_fusion.3 = f32[1280,128]{1,0:T(8,128)S(1)} fusion(f32[512,128]{1,0:T(8,128)} %param.6), kind=kLoop, calls=%fused_computation.147 | loop fusion | bytes 524288
  1.0 0.9 %constant_dynamic-update-slice_fusion.2 = f32[1280,128]{1,0:T(8,128)S(1)} fusion(f32[1280,128]{1,0:T(8,128)S(1)} %constant_dynamic-update-slice_fusion.3, f32[256,128]{1,0:T(8,128)} %param.7), kind=kLoop, calls=%fused_computation.146 | loop fusion | bytes 262144
  1.9 0.9 %constant_dynamic-update-slice_fusion.1 = f32[1280,128]{1,0:T(8,128)S(1)} fusion(f32[1280,128]{1,0:T(8,128)S(1)} %constant_dynamic-update-slice_fusion.2, f32[256,128]{1,0:T(8,128)} %param.8), kind=kLoop, calls=%fused_computation.145 | loop fusion | bytes 262144
  2.9 3.0 %collective-permute-start = (f32[1280,128]{1,0:T(8,128)S(1)}, f32[1280,128]{1,0:T(8,128)S(1)}, u32[]{:S(2)}, u32[]{:S(2)}) collective-permute-start(f32[1280,128]{1,0:T(8,128)S(1)} %constant_dynamic-update-slice_fusion), channel_id=1, source_target_pairs={{0,1},{1,0},{2,3},{3,2},{4,5},{5,4},{6,7},{7,6},{8,9},{9,8},{10,11... | collective-permute-start | bytes 1966088 | tf_op jit(solution)/shard_map/ppermute | solution.py:34
  5.9 14.7 %collective-permute-done = f32[1280,128]{1,0:T(8,128)S(1)} collective-permute-done((f32[1280,128]{1,0:T(8,128)S(1)}, f32[1280,128]{1,0:T(8,128)S(1)}, u32[]{:S(2)}, u32[]{:S(2)}) %collective-permute-start) | collective-permute-done | bytes 655392 | tf_op jit(solution)/shard_map/ppermute | solution.py:34
  20.9 1.0 %copy-done = f32[512,512]{1,0:T(8,128)S(1)} copy-done((f32[512,512]{1,0:T(8,128)S(1)}, f32[512,512]{1,0:T(8,128)}, u32[]{:S(2)}) %copy-start) | copy-done | bytes 1048600
  21.9 0.7 fusion.119
  23.1 0.5 fusion.24
  23.6 0.6 convolution_subtract_fusion
  24.3 0.6 collective-permute-start.2
  24.8 0.5 collective-permute-done.1
  25.6 1.3 %collective-permute-start.3 = (f32[128,256]{1,0:T(8,128)S(1)}, f32[128,256]{1,0:T(8,128)S(1)}, u32[]{:S(2)}, u32[]{:S(2)}) collective-permute-start(f32[128,256]{1,0:T(8,128)S(1)} %fusion.61), channel_id=1, source_target_pairs={{4,0},{6,2},{12,8},{14,10},{20,16},{22,18},{28,24},{30,26},{5,1},{... | collective-permute-start | bytes 393224 | tf_op jit(solution)/shard_map/ppermute | solution.py:81
  26.9 0.4 fusion.36
  27.3 5.7 %collective-permute-done.3 = f32[128,256]{1,0:T(8,128)S(1)} collective-permute-done((f32[128,256]{1,0:T(8,128)S(1)}, f32[128,256]{1,0:T(8,128)S(1)}, u32[]{:S(2)}, u32[]{:S(2)}) %collective-permute-start.3) | collective-permute-done | bytes 131104 | tf_op jit(solution)/shard_map/ppermute | solution.py:81
  33.0 1.1 %select_subtract_fusion.1 = (f32[256,256]{1,0:T(8,128)S(1)}, f32[256,256]{1,0:T(8,128)}) fusion(f32[256,512]{1,0:T(8,128)S(1)} %collective-permute-done.2, s32[]{:T(128)S(6)} %select_n.283, f32[256,512]{1,0:T(8,128)S(1)} %get-tuple-element.23, pred[]{:T(512)S(6)} %eq.49, f32[256,256]{1,0:T(8,128)S(1)} %fusion.36, f32[3,256,256]{2,1,0:T(8,128)S(1)} %get-tuple-element.18), kind=kOutput, calls=%fused_computation.73 | convolution fusion | flops 100925440 | bytes 2099200 | tf_op jit(solution)/shard_map/dot_general | solution.py:12
  34.1 1.1 %broadcast_select_fusion.4 = (f32[256,256]{1,0:T(8,128)}, f32[256,256]{1,0:T(8,128)S(1)}) fusion(f32[256,256]{1,0:T(8,128)S(1)} %get-tuple-element.27, pred[]{:T(512)S(6)} %eq.56, f32[3,256,256]{2,1,0:T(8,128)S(1)} %get-tuple-element.17), kind=kOutput, calls=%fused_computation.118 | convolution fusion | flops 100794368 | bytes 1311744 | tf_op jit(solution)/shard_map/dot_general | solution.py:12
  35.2 1.3 %collective-permute-start.6 = (f32[128,256]{1,0:T(8,128)}, f32[128,256]{1,0:T(8,128)S(1)}, u32[]{:S(2)}, u32[]{:S(2)}) collective-permute-start(f32[128,256]{1,0:T(8,128)} %copy-done.5), channel_id=1, source_target_pairs={{8,0},{10,2},{24,16},{26,18},{9,1},{11,3},{25,17},{27,19}} | collective-permute-start | bytes 393224 | tf_op jit(solution)/shard_map/ppermute | solution.py:81
  36.5 1.3 %collective-permute-start.7 = (f32[128,256]{1,0:T(8,128)}, f32[128,256]{1,0:T(8,128)S(1)}, u32[]{:S(2)}, u32[]{:S(2)}) collective-permute-start(f32[128,256]{1,0:T(8,128)} %copy-done.5), channel_id=1, source_target_pairs={{16,0},{18,2},{17,1},{19,3}} | collective-permute-start | bytes 393224 | tf_op jit(solution)/shard_map/ppermute | solution.py:81
  37.8 1.2 %fusion.58 = f32[256,256]{1,0:T(8,128)S(1)} fusion(f32[256,256]{1,0:T(8,128)S(1)} %get-tuple-element.27, f32[128,256]{1,0:T(8,128)} %collective-permute-done.4, f32[128,256]{1,0:T(8,128)S(1)} %collective-permute-done.3, pred[]{:T(512)S(6)} %eq.53, pred[]{:T(512)S(6)} %and.45), kind=kOutput, calls=%fused_computation.91 | convolution fusion | flops 50397184 | bytes 655362 | tf_op jit(solution)/shard_map/dot_general | solution.py:12
  39.0 7.0 %collective-permute-done.6 = f32[128,256]{1,0:T(8,128)S(1)} collective-permute-done((f32[128,256]{1,0:T(8,128)}, f32[128,256]{1,0:T(8,128)S(1)}, u32[]{:S(2)}, u32[]{:S(2)}) %collective-permute-start.6) | collective-permute-done | bytes 131104 | tf_op jit(solution)/shard_map/ppermute | solution.py:81
  46.0 1.3 %convolution_add_fusion = f32[256,256]{1,0:T(8,128)S(1)} fusion(f32[256,256]{1,0:T(8,128)S(1)} %get-tuple-element.30, f32[256,256]{1,0:T(8,128)} %collective-permute-done.5, f32[3,256,256]{2,1,0:T(8,128)S(1)} %get-tuple-element.17), kind=kOutput, calls=%fused_computation.13 | convolution fusion | flops 100728832 | bytes 1048576 | tf_op jit(solution)/shard_map/dot_general | solution.py:12
  47.4 1.4 %fusion.11 = f32[256,256]{1,0:T(8,128)S(1)} fusion(f32[256,256]{1,0:T(8,128)S(1)} %get-tuple-element.27, f32[256,256]{1,0:T(8,128)} %collective-permute-done.5, f32[256,256]{1,0:T(8,128)S(1)} %fusion.58, f32[128,256]{1,0:T(8,128)S(1)} %collective-permute-done.3, f32[128,256]{1,0:T(8,128)} %collective-permute-done.4, pred[]{:T(512)S(6)} %eq.53, pred[]{:T(512)S(6)} %and.45), kind=kOutput, calls=%fused_computation.31 | convolution fusion | flops 50659328 | bytes 1443328 | tf_op jit(solution)/shard_map/dot_general | solution.py:12
  48.8 0.4 broadcast_select_fusion.3
  49.2 1.9 %collective-permute-start.9 = (f32[256,256]{1,0:T(8,128)S(1)}, f32[256,256]{1,0:T(8,128)S(1)}, u32[]{:S(2)}, u32[]{:S(2)}) collective-permute-start(f32[256,256]{1,0:T(8,128)S(1)} %get-tuple-element.31), channel_id=1, source_target_pairs={{0,8},{8,0},{2,10},{10,2},{16,24},{24,16},{18,26},{26,18},{1,9},{9... | collective-permute-start | bytes 786440 | tf_op jit(solution)/shard_map/ppermute | solution.py:106
  51.4 0.6 collective-permute-start.10
  52.0 0.5 collective-permute-done.8
  52.8 6.2 %collective-permute-done.9 = f32[256,256]{1,0:T(8,128)S(1)} collective-permute-done((f32[256,256]{1,0:T(8,128)S(1)}, f32[256,256]{1,0:T(8,128)S(1)}, u32[]{:S(2)}, u32[]{:S(2)}) %collective-permute-start.9) | collective-permute-done | bytes 262176 | tf_op jit(solution)/shard_map/ppermute | solution.py:106
  59.7 2.9 %collective-permute-start.11 = (f32[256,256]{1,0:T(8,128)S(1)}, f32[256,256]{1,0:T(8,128)S(1)}, u32[]{:S(2)}, u32[]{:S(2)}) collective-permute-start(f32[256,256]{1,0:T(8,128)S(1)} %get-tuple-element.33), channel_id=1, source_target_pairs={{0,16},{16,0},{2,18},{18,2},{1,17},{17,1},{3,19},{19,3}} | collective-permute-start | bytes 786440 | tf_op jit(solution)/shard_map/ppermute | solution.py:106
  63.7 5.9 %collective-permute-done.11 = f32[256,256]{1,0:T(8,128)S(1)} collective-permute-done((f32[256,256]{1,0:T(8,128)S(1)}, f32[256,256]{1,0:T(8,128)S(1)}, u32[]{:S(2)}, u32[]{:S(2)}) %collective-permute-start.11) | collective-permute-done | bytes 262176 | tf_op jit(solution)/shard_map/ppermute | solution.py:106
  70.6 0.7 copy-done.2
  71.7 1.5 %collective-permute-done.12 = f32[256,256]{1,0:T(8,128)S(1)} collective-permute-done((f32[256,256]{1,0:T(8,128)S(1)}, f32[256,256]{1,0:T(8,128)S(1)}, u32[]{:S(2)}, u32[]{:S(2)}) %collective-permute-start.12) | collective-permute-done | bytes 262176 | tf_op jit(solution)/shard_map/ppermute | solution.py:122
  73.3 1.1 %pad_maximum_fusion = f32[512,512]{1,0:T(8,128)} fusion(f32[256,512]{1,0:T(8,128)S(1)} %get-tuple-element.24, f32[256,256]{1,0:T(8,128)S(1)} %get-tuple-element.26, f32[256,256]{1,0:T(8,128)S(1)} %get-tuple-element.25), kind=kLoop, calls=%fused_computation.34 | loop fusion | flops 524288 | bytes 2097152 | tf_op jit(solution)/shard_map/concatenate | solution.py:124
  (41 shorter events, 4.9 us)
Async XLA Ops:
  0.0 2.8 %copy-start.4 = (f32[256,128]{1,0:T(8,128)S(1)}, f32[256,128]{1,0:T(8,128)}, u32[]{:S(2)}) copy-start(f32[256,128]{1,0:T(8,128)} %param.9) | copy-start | bytes 393220
  2.9 17.8 %collective-permute-start = (f32[1280,128]{1,0:T(8,128)S(1)}, f32[1280,128]{1,0:T(8,128)S(1)}, u32[]{:S(2)}, u32[]{:S(2)}) collective-permute-start(f32[1280,128]{1,0:T(8,128)S(1)} %constant_dynamic-update-slice_fusion), channel_id=1, source_target_pairs={{0,1},{1,0},{2,3},{3,2},{4,5},{5,4},{6,7},{7,6},{8,9},{9,8},{10,11... | collective-permute-start | bytes 1966088 | tf_op jit(solution)/shard_map/ppermute | solution.py:34
  20.6 1.2 %copy-start = (f32[512,512]{1,0:T(8,128)S(1)}, f32[512,512]{1,0:T(8,128)}, u32[]{:S(2)}) copy-start(f32[512,512]{1,0:T(8,128)} %param.5) | copy-start | bytes 3145732
  23.0 2.4 %collective-permute-start.1 = (f32[3,256,256]{2,1,0:T(8,128)S(1)}, f32[3,256,256]{2,1,0:T(8,128)S(1)}, u32[]{:S(2)}, u32[]{:S(2)}) collective-permute-start(f32[3,256,256]{2,1,0:T(8,128)S(1)} %pad_maximum_fusion.1), channel_id=1, source_target_pairs={{0,2},{2,0},{4,6},{6,4},{8,10},{10,8},{12,14},{14,12},{16,18},{18,... | collective-permute-start | bytes 2359304 | tf_op jit(solution)/shard_map/ppermute | solution.py:69
  24.3 3.0 %collective-permute-start.2 = (f32[256,512]{1,0:T(8,128)S(1)}, f32[256,512]{1,0:T(8,128)S(1)}, u32[]{:S(2)}, u32[]{:S(2)}) collective-permute-start(f32[256,512]{1,0:T(8,128)S(1)} %get-tuple-element.23), channel_id=1, source_target_pairs={{0,2},{2,0},{4,6},{6,4},{8,10},{10,8},{12,14},{14,12},{16,18},{18,... | collective-permute-start | bytes 1572872 | tf_op jit(solution)/shard_map/ppermute | solution.py:84
  25.5 7.4 %copy-start.5 = (f32[128,256]{1,0:T(8,128)}, f32[128,256]{1,0:T(8,128)S(1)}, u32[]{:S(2)}) copy-start(f32[128,256]{1,0:T(8,128)S(1)} %fusion.61) | copy-start | bytes 393220
  25.6 7.4 %collective-permute-start.3 = (f32[128,256]{1,0:T(8,128)S(1)}, f32[128,256]{1,0:T(8,128)S(1)}, u32[]{:S(2)}, u32[]{:S(2)}) collective-permute-start(f32[128,256]{1,0:T(8,128)S(1)} %fusion.61), channel_id=1, source_target_pairs={{4,0},{6,2},{12,8},{14,10},{20,16},{22,18},{28,24},{30,26},{5,1},{... | collective-permute-start | bytes 393224 | tf_op jit(solution)/shard_map/ppermute | solution.py:81
  27.3 7.9 %copy-start.1 = (f32[256,512]{1,0:T(8,128)}, f32[256,512]{1,0:T(8,128)S(1)}, u32[]{:S(2)}) copy-start(f32[256,512]{1,0:T(8,128)S(1)} %collective-permute-done.2) | copy-start | bytes 1572868
  33.0 4.8 %collective-permute-start.4 = (f32[128,256]{1,0:T(8,128)S(1)}, f32[128,256]{1,0:T(8,128)}, u32[]{:S(2)}, u32[]{:S(2)}) collective-permute-start(f32[128,256]{1,0:T(8,128)S(1)} %collective-permute-done.3), channel_id=1, source_target_pairs={{0,2},{2,0},{4,6},{6,4},{8,10},{10,8},{12,14},{14,12},{16,18},{18,... | collective-permute-start | bytes 393224 | tf_op jit(solution)/shard_map/ppermute | solution.py:111
  35.2 10.8 %collective-permute-start.5 = (f32[256,256]{1,0:T(8,128)}, f32[256,256]{1,0:T(8,128)}, u32[]{:S(2)}, u32[]{:S(2)}) collective-permute-start(f32[256,256]{1,0:T(8,128)} %get-tuple-element.29), channel_id=1, source_target_pairs={{0,4},{4,0},{2,6},{6,2},{8,12},{12,8},{10,14},{14,10},{16,20},{20,... | collective-permute-start | bytes 786440 | tf_op jit(solution)/shard_map/ppermute | solution.py:106
  35.2 10.8 %collective-permute-start.6 = (f32[128,256]{1,0:T(8,128)}, f32[128,256]{1,0:T(8,128)S(1)}, u32[]{:S(2)}, u32[]{:S(2)}) collective-permute-start(f32[128,256]{1,0:T(8,128)} %copy-done.5), channel_id=1, source_target_pairs={{8,0},{10,2},{24,16},{26,18},{9,1},{11,3},{25,17},{27,19}} | collective-permute-start | bytes 393224 | tf_op jit(solution)/shard_map/ppermute | solution.py:81
  36.5 9.5 %collective-permute-start.7 = (f32[128,256]{1,0:T(8,128)}, f32[128,256]{1,0:T(8,128)S(1)}, u32[]{:S(2)}, u32[]{:S(2)}) collective-permute-start(f32[128,256]{1,0:T(8,128)} %copy-done.5), channel_id=1, source_target_pairs={{16,0},{18,2},{17,1},{19,3}} | collective-permute-start | bytes 393224 | tf_op jit(solution)/shard_map/ppermute | solution.py:81
  49.2 9.8 %collective-permute-start.9 = (f32[256,256]{1,0:T(8,128)S(1)}, f32[256,256]{1,0:T(8,128)S(1)}, u32[]{:S(2)}, u32[]{:S(2)}) collective-permute-start(f32[256,256]{1,0:T(8,128)S(1)} %get-tuple-element.31), channel_id=1, source_target_pairs={{0,8},{8,0},{2,10},{10,2},{16,24},{24,16},{18,26},{26,18},{1,9},{9... | collective-permute-start | bytes 786440 | tf_op jit(solution)/shard_map/ppermute | solution.py:106
  51.1 1.4 %collective-permute-start.8 = (f32[128,256]{1,0:T(8,128)S(1)}, f32[128,256]{1,0:T(8,128)S(1)}, u32[]{:S(2)}, u32[]{:S(2)}) collective-permute-start(f32[128,256]{1,0:T(8,128)S(1)} %collective-permute-done.6), channel_id=1, source_target_pairs={{0,2},{2,0},{4,6},{6,4},{8,10},{10,8},{12,14},{14,12},{16,18},{18,... | collective-permute-start | bytes 393224 | tf_op jit(solution)/shard_map/ppermute | solution.py:111
  51.4 11.6 %collective-permute-start.10 = (f32[128,256]{1,0:T(8,128)S(1)}, f32[128,256]{1,0:T(8,128)S(1)}, u32[]{:S(2)}, u32[]{:S(2)}) collective-permute-start(f32[128,256]{1,0:T(8,128)S(1)} %collective-permute-done.7), channel_id=1, source_target_pairs={{0,2},{2,0},{4,6},{6,4},{8,10},{10,8},{12,14},{14,12},{16,18},{18,... | collective-permute-start | bytes 393224 | tf_op jit(solution)/shard_map/ppermute | solution.py:111
  59.7 9.9 %collective-permute-start.11 = (f32[256,256]{1,0:T(8,128)S(1)}, f32[256,256]{1,0:T(8,128)S(1)}, u32[]{:S(2)}, u32[]{:S(2)}) collective-permute-start(f32[256,256]{1,0:T(8,128)S(1)} %get-tuple-element.33), channel_id=1, source_target_pairs={{0,16},{16,0},{2,18},{18,2},{1,17},{17,1},{3,19},{19,3}} | collective-permute-start | bytes 786440 | tf_op jit(solution)/shard_map/ppermute | solution.py:106
  70.3 1.0 %copy-start.2 = (f32[256,512]{1,0:T(8,128)S(1)}, f32[256,512]{1,0:T(8,128)}, u32[]{:S(2)}) copy-start(f32[256,512]{1,0:T(8,128)} %copy-done.1) | copy-start | bytes 1572868
  70.3 1.1 %copy-start.3 = (f32[256,256]{1,0:T(8,128)S(1)}, f32[256,256]{1,0:T(8,128)}, u32[]{:S(2)}) copy-start(f32[256,256]{1,0:T(8,128)} %get-tuple-element.28) | copy-start | bytes 786436
  71.7 1.6 %collective-permute-start.12 = (f32[256,256]{1,0:T(8,128)S(1)}, f32[256,256]{1,0:T(8,128)S(1)}, u32[]{:S(2)}, u32[]{:S(2)}) collective-permute-start(f32[256,256]{1,0:T(8,128)S(1)} %get-tuple-element.35), channel_id=1, source_target_pairs={{0,2},{2,0},{4,6},{6,4},{8,10},{10,8},{12,14},{14,12},{16,18},{18,... | collective-permute-start | bytes 786440 | tf_op jit(solution)/shard_map/ppermute | solution.py:122

commit v12 on v11

--- a/solution.py
+++ b/solution.py
@@ -84,7 +84,7 @@
     received = lax.ppermute(current, "row", swap)
     own_h = lax.dynamic_slice(current, (0, core * half), (width, half))
     early = product_left_t(jnp.where(is_lower, odd3[1], odd3[2]), own_h)
-    early, received, partner_factors[0] = lax.optimization_barrier((early, received, partner_factors[0]))
+    early, received = lax.optimization_barrier((early, received))
     recv_h = lax.dynamic_slice(received, (0, core * half), (width, half))
     update = early + product_left_t(jnp.where(is_lower, odd3[2], odd3[1]), recv_h)
     upper_h = jnp.where(is_lower, recv_h, own_h)
@@ -104,10 +104,7 @@
                 pairs += [(i + c, i + step + c), (i + step + c, i + c)]
         q = product_left_t(jnp.where(is_upper, even3[2], zeros), chain)
         received = lax.ppermute(jnp.where(is_upper, q, chain), "row", pairs)
-        if level == 1:
-            received, rest = lax.optimization_barrier((received, partner_factors[1:]))
-            partner_factors[1:] = rest
-        mine = partner_factors[level - 1]
+        received, mine = lax.optimization_barrier((received, partner_factors[level - 1]))
         mates = lax.ppermute(mine, "row", swap)
         top_rows = jnp.where(is_lower & (core == 0), mine, jnp.where(is_lower, mates, 0.0))
         bottom_rows = jnp.where(is_lower & (core == 0), mates, jnp.where(is_lower, mine, 0.0))

time: 74.8 us -> 83.7 us (1.12)
  matrix products: 12.5 us -> 16.4 us
  starting transfers between devices: 13.1 us -> 15.1 us
  waiting for transfers between devices: 42.1 us -> 43.9 us
  other arithmetic: 1.7 us -> 2.85 us
    ppermute x3, waiting for transfers between devices: 12.1 us -> 7.58 us  [on_device(): received = lax.ppermute(jnp.where(is_upper, q, chain), 'row', pairs)]
    ppermute x3, waiting for transfers between devices: 12.7 us -> 16.5 us  [on_device(): partner_factors.append(lax.ppermute(half_s, 'row', pairs))]
    dot_general x16, matrix products: 10.5 us -> 13.4 us  [product_left_t(): lax.dot_general(left, right, (((0,), (0,)), ((), ())), precision=lax.Prec...]
    ppermute x3, waiting for transfers between devices: 0.5 us -> 3.02 us  [on_device(): mates = lax.ppermute(mine, 'row', swap)]
    ppermute x3, starting transfers between devices: 4.85 us -> 7.34 us  [on_device(): received = lax.ppermute(jnp.where(is_upper, q, chain), 'row', pairs)]
    select_n x1, other arithmetic: 0.14 us -> 1.29 us  [on_device(): even3 = jnp.where(core == 0, own3, mate3)]
    dot_general x6, matrix products: 2.02 us -> 2.99 us  [product(): jnp.dot(left, right, precision=lax.Precision.HIGH, preferred_element_type...]
    unnamed x15 -> x17, local copies, waits for them, and re-layouts: 4.58 us -> 4.48 us
  transfers between devices with their start and end apart: 13 -> 13, of which waited for: 8 -> 9; matrix products, arithmetic and copies ran while one was open for 10% -> 11% of each run, Pallas kernels for 0% -> 0%
where the time goes in v12:
time: 83.7 us; the launch traced here: 83.2 us
  waiting for transfers between devices  43.9 us (52%)
  matrix products  16.4 us (20%)
  starting transfers between devices  15.1 us (18%)
  local copies, waits for them, and re-layouts  4.56 us (5%)
  other arithmetic  2.85 us (3%)
    ppermute x3, waiting for transfers between devices, on_device(): partner_factors.append(lax.ppermute(half_s, 'row', pairs))  16.5 us
    ppermute x1, waiting for transfers between devices, col_gather(): by_shift.append(lax.ppermute(part, 'col', perm))  14.7 us
    dot_general x16, matrix products, product_left_t(): lax.dot_general(left, right, (((0,), (0,)), ((), ())), precision=lax.Prec...  13.4 us
    ppermute x3, waiting for transfers between devices, on_device(): received = lax.ppermute(jnp.where(is_upper, q, chain), 'row', pairs)  7.58 us
    ppermute x3, starting transfers between devices, on_device(): received = lax.ppermute(jnp.where(is_upper, q, chain), 'row', pairs)  7.34 us
    unnamed x17, local copies, waits for them, and re-layouts  4.48 us
    ppermute x3, starting transfers between devices, on_device(): partner_factors.append(lax.ppermute(half_s, 'row', pairs))  3.88 us
    ppermute x1, starting transfers between devices, col_gather(): by_shift.append(lax.ppermute(part, 'col', perm))  3.03 us
  transfers between devices with their start and end apart: 13, of which 9 were waited for; matrix products, arithmetic and copies ran while one was open for 11% of the time, Pallas kernels for 0%

profile of v12, /device:TPU:0, one launch (start us, length us, event | category | flops | bytes accessed | tf_op | source)
XLA Modules:
  0.0 83.2 jit_solution(1466763986174429568)
XLA Ops:
  0.0 1.0 %constant_dynamic-update-slice_fusion.3 = f32[1280,128]{1,0:T(8,128)S(1)} fusion(f32[512,128]{1,0:T(8,128)} %param.6), kind=kLoop, calls=%fused_computation.147 | loop fusion | bytes 524288
  1.0 0.9 %constant_dynamic-update-slice_fusion.2 = f32[1280,128]{1,0:T(8,128)S(1)} fusion(f32[1280,128]{1,0:T(8,128)S(1)} %constant_dynamic-update-slice_fusion.3, f32[256,128]{1,0:T(8,128)} %param.7), kind=kLoop, calls=%fused_computation.146 | loop fusion | bytes 262144
  1.9 0.9 %constant_dynamic-update-slice_fusion.1 = f32[1280,128]{1,0:T(8,128)S(1)} fusion(f32[1280,128]{1,0:T(8,128)S(1)} %constant_dynamic-update-slice_fusion.2, f32[256,128]{1,0:T(8,128)} %param.8), kind=kLoop, calls=%fused_computation.145 | loop fusion | bytes 262144
  2.9 3.0 %collective-permute-start = (f32[1280,128]{1,0:T(8,128)S(1)}, f32[1280,128]{1,0:T(8,128)S(1)}, u32[]{:S(2)}, u32[]{:S(2)}) collective-permute-start(f32[1280,128]{1,0:T(8,128)S(1)} %constant_dynamic-update-slice_fusion), channel_id=1, source_target_pairs={{0,1},{1,0},{2,3},{3,2},{4,5},{5,4},{6,7},{7,6},{8,9},{9,8},{10,11... | collective-permute-start | bytes 1966088 | tf_op jit(solution)/shard_map/ppermute | solution.py:34
  5.9 14.7 %collective-permute-done = f32[1280,128]{1,0:T(8,128)S(1)} collective-permute-done((f32[1280,128]{1,0:T(8,128)S(1)}, f32[1280,128]{1,0:T(8,128)S(1)}, u32[]{:S(2)}, u32[]{:S(2)}) %collective-permute-start) | collective-permute-done | bytes 655392 | tf_op jit(solution)/shard_map/ppermute | solution.py:34
  20.9 1.0 %copy-done = f32[512,512]{1,0:T(8,128)S(1)} copy-done((f32[512,512]{1,0:T(8,128)S(1)}, f32[512,512]{1,0:T(8,128)}, u32[]{:S(2)}) %copy-start) | copy-done | bytes 1048600
  21.9 0.7 fusion.119
  24.9 0.7 collective-permute-done.1
  25.5 1.3 %broadcast_select_fusion = (f32[3,256,256]{2,1,0:T(8,128)S(1)}, f32[3,256,256]{2,1,0:T(8,128)S(1)}) fusion(f32[3,256,256]{2,1,0:T(8,128)} %collective-permute-done.1, pred[]{:T(512)S(6)} %eq.49, f32[1,256,256]{2,1,0:T(8,128)S(1)} %convolution_bitcast_fusion, f32[1,256,256]{2,1,0:T(8,128)S(1)} %bitcast.67, f32[1,256,256]{2,1,0:T(8,128)S(1)} %get-tuple-element.23, ...), kind=kLoop, calls=%fused_computation.45 | loop fusion | flops 786432 | bytes 3145730 | tf_op jit(solution)/shard_map/jit(_where)/select_n | solution.py:71
  27.2 2.1 %select_subtract_fusion.1 = (f32[256,256]{1,0:T(8,128)S(1)}, f32[256,256]{1,0:T(8,128)}) fusion(f32[256,512]{1,0:T(8,128)} %collective-permute-done.2, s32[]{:T(128)S(6)} %select_n.283, f32[256,512]{1,0:T(8,128)S(1)} %get-tuple-element.27, pred[]{:T(512)S(6)} %eq.49, f32[256,256]{1,0:T(8,128)S(1)} %fusion.36, f32[3,256,256]{2,1,0:T(8,128)S(1)} %get-tuple-element.22), kind=kOutput, calls=%fused_computation.73 | convolution fusion | flops 100925440 | bytes 2099200 | tf_op jit(solution)/shard_map/dot_general | solution.py:12
  29.3 1.1 %broadcast_select_fusion.4 = (f32[256,256]{1,0:T(8,128)S(1)}, f32[256,256]{1,0:T(8,128)}) fusion(f32[256,256]{1,0:T(8,128)S(1)} %get-tuple-element.31, pred[]{:T(512)S(6)} %eq.56, f32[3,256,256]{2,1,0:T(8,128)S(1)} %get-tuple-element.21), kind=kOutput, calls=%fused_computation.118 | convolution fusion | flops 100794368 | bytes 1311744 | tf_op jit(solution)/shard_map/dot_general | solution.py:12
  30.4 1.7 %collective-permute-start.3 = (f32[256,256]{1,0:T(8,128)S(1)}, f32[256,256]{1,0:T(8,128)}, u32[]{:S(2)}, u32[]{:S(2)}) collective-permute-start(f32[256,256]{1,0:T(8,128)S(1)} %get-tuple-element.33), channel_id=1, source_target_pairs={{0,4},{4,0},{2,6},{6,2},{8,12},{12,8},{10,14},{14,10},{16,20},{20,... | collective-permute-start | bytes 786440 | tf_op jit(solution)/shard_map/ppermute | solution.py:106
  32.2 1.3 %collective-permute-start.4 = (f32[128,256]{1,0:T(8,128)S(1)}, f32[128,256]{1,0:T(8,128)S(1)}, u32[]{:S(2)}, u32[]{:S(2)}) collective-permute-start(f32[128,256]{1,0:T(8,128)S(1)} %fusion.61), channel_id=1, source_target_pairs={{4,0},{6,2},{12,8},{14,10},{20,16},{22,18},{28,24},{30,26},{5,1},{... | collective-permute-start | bytes 393224 | tf_op jit(solution)/shard_map/ppermute | solution.py:81
  33.5 8.1 %collective-permute-done.4 = f32[128,256]{1,0:T(8,128)S(1)} collective-permute-done((f32[128,256]{1,0:T(8,128)S(1)}, f32[128,256]{1,0:T(8,128)S(1)}, u32[]{:S(2)}, u32[]{:S(2)}) %collective-permute-start.4) | collective-permute-done | bytes 131104 | tf_op jit(solution)/shard_map/ppermute | solution.py:81
  41.7 1.3 %collective-permute-done.5 = f32[128,256]{1,0:T(8,128)S(1)} collective-permute-done((f32[128,256]{1,0:T(8,128)S(1)}, f32[128,256]{1,0:T(8,128)S(1)}, u32[]{:S(2)}, u32[]{:S(2)}) %collective-permute-start.5) | collective-permute-done | bytes 131104 | tf_op jit(solution)/shard_map/ppermute | solution.py:108
  43.0 0.7 copy-done.3
  43.9 1.3 %fusion.11 = f32[256,256]{1,0:T(8,128)S(1)} fusion(f32[256,256]{1,0:T(8,128)S(1)} %get-tuple-element.31, f32[256,256]{1,0:T(8,128)} %collective-permute-done.3, f32[256,256]{1,0:T(8,128)S(1)} %fusion.58, f32[128,256]{1,0:T(8,128)S(1)} %collective-permute-done.4, f32[128,256]{1,0:T(8,128)} %copy-done.3, pred[]{:T(512)S(6)} %eq.53, pred[]{:T(512)S(6)} %and.45), kind=kOutput, calls=%fused_computation.31 | convolution fusion | flops 50659328 | bytes 1443328 | tf_op jit(solution)/shard_map/dot_general | solution.py:12
  45.3 1.2 %broadcast_select_fusion.3 = (f32[256,256]{1,0:T(8,128)}, f32[256,256]{1,0:T(8,128)}) fusion(f32[256,256]{1,0:T(8,128)S(1)} %fusion.11, pred[]{:T(512)S(6)} %eq.57, f32[3,256,256]{2,1,0:T(8,128)S(1)} %get-tuple-element.21), kind=kOutput, calls=%fused_computation.116 | convolution fusion | flops 100794368 | bytes 1311744 | tf_op jit(solution)/shard_map/dot_general | solution.py:12
  46.5 3.7 %collective-permute-start.6 = (f32[256,256]{1,0:T(8,128)}, f32[256,256]{1,0:T(8,128)}, u32[]{:S(2)}, u32[]{:S(2)}) collective-permute-start(f32[256,256]{1,0:T(8,128)} %get-tuple-element.35), channel_id=1, source_target_pairs={{0,8},{8,0},{2,10},{10,2},{16,24},{24,16},{18,26},{26,18},{1,9},{9... | collective-permute-start | bytes 786440 | tf_op jit(solution)/shard_map/ppermute | solution.py:106
  50.3 1.3 %collective-permute-start.7 = (f32[128,256]{1,0:T(8,128)S(1)}, f32[128,256]{1,0:T(8,128)S(1)}, u32[]{:S(2)}, u32[]{:S(2)}) collective-permute-start(f32[128,256]{1,0:T(8,128)S(1)} %copy-done.6), channel_id=1, source_target_pairs={{8,0},{10,2},{24,16},{26,18},{9,1},{11,3},{25,17},{27,19}} | collective-permute-start | bytes 393224 | tf_op jit(solution)/shard_map/ppermute | solution.py:81
  51.6 1.3 %collective-permute-start.10 = (f32[128,256]{1,0:T(8,128)S(1)}, f32[128,256]{1,0:T(8,128)S(1)}, u32[]{:S(2)}, u32[]{:S(2)}) collective-permute-start(f32[128,256]{1,0:T(8,128)S(1)} %copy-done.6), channel_id=1, source_target_pairs={{16,0},{18,2},{17,1},{19,3}} | collective-permute-start | bytes 393224 | tf_op jit(solution)/shard_map/ppermute | solution.py:81
  52.9 1.4 %convolution_add_fusion = f32[256,256]{1,0:T(8,128)S(1)} fusion(f32[256,256]{1,0:T(8,128)} %get-tuple-element.34, f32[256,256]{1,0:T(8,128)} %collective-permute-done.3, f32[3,256,256]{2,1,0:T(8,128)S(1)} %get-tuple-element.21), kind=kOutput, calls=%fused_computation.13 | convolution fusion | flops 100728832 | bytes 1048576 | tf_op jit(solution)/shard_map/dot_general | solution.py:12
  54.3 8.4 %collective-permute-done.7 = f32[128,256]{1,0:T(8,128)S(1)} collective-permute-done((f32[128,256]{1,0:T(8,128)S(1)}, f32[128,256]{1,0:T(8,128)S(1)}, u32[]{:S(2)}, u32[]{:S(2)}) %collective-permute-start.7) | collective-permute-done | bytes 131104 | tf_op jit(solution)/shard_map/ppermute | solution.py:81
  62.9 1.1 %collective-permute-done.8 = f32[128,256]{1,0:T(8,128)S(1)} collective-permute-done((f32[128,256]{1,0:T(8,128)S(1)}, f32[128,256]{1,0:T(8,128)S(1)}, u32[]{:S(2)}, u32[]{:S(2)}) %collective-permute-start.8) | collective-permute-done | bytes 131104 | tf_op jit(solution)/shard_map/ppermute | solution.py:108
  64.3 1.3 %fusion.8 = f32[256,256]{1,0:T(8,128)S(1)} fusion(f32[256,256]{1,0:T(8,128)S(1)} %fusion.11, f32[256,256]{1,0:T(8,128)} %collective-permute-done.6, f32[256,256]{1,0:T(8,128)S(1)} %fusion.55, f32[128,256]{1,0:T(8,128)S(1)} %collective-permute-done.7, f32[128,256]{1,0:T(8,128)S(1)} %collective-permute-done.8, pred[]{:T(512)S(6)} %eq.52, pred[]{:T(512)S(6)} %and.46), kind=kOutput, calls=%fused_computation.27 | convolution fusion | flops 50659328 | bytes 1443328 | tf_op jit(solution)/shard_map/dot_general | solution.py:12
  66.0 1.9 %collective-permute-start.9 = (f32[256,256]{1,0:T(8,128)S(1)}, f32[256,256]{1,0:T(8,128)S(1)}, u32[]{:S(2)}, u32[]{:S(2)}) collective-permute-start(f32[256,256]{1,0:T(8,128)S(1)} %get-tuple-element.37), channel_id=1, source_target_pairs={{0,16},{16,0},{2,18},{18,2},{1,17},{17,1},{3,19},{19,3}} | collective-permute-start | bytes 786440 | tf_op jit(solution)/shard_map/ppermute | solution.py:106
  68.0 1.3 %convolution_add_fusion.1 = f32[256,256]{1,0:T(8,128)S(1)} fusion(f32[256,256]{1,0:T(8,128)S(1)} %copy-done.1, f32[256,256]{1,0:T(8,128)} %collective-permute-done.6, f32[3,256,256]{2,1,0:T(8,128)S(1)} %get-tuple-element.21), kind=kOutput, calls=%fused_computation.16 | convolution fusion | flops 100728832 | bytes 1048576 | tf_op jit(solution)/shard_map/dot_general | solution.py:12
  69.6 7.6 %collective-permute-done.9 = f32[256,256]{1,0:T(8,128)S(1)} collective-permute-done((f32[256,256]{1,0:T(8,128)S(1)}, f32[256,256]{1,0:T(8,128)S(1)}, u32[]{:S(2)}, u32[]{:S(2)}) %collective-permute-start.9) | collective-permute-done | bytes 262176 | tf_op jit(solution)/shard_map/ppermute | solution.py:106
  77.9 0.6 collective-permute-done.11
  79.2 1.2 %broadcast_select_fusion.7 = (f32[256,256]{1,0:T(8,128)S(1)}, f32[256,256]{1,0:T(8,128)S(1)}) fusion(f32[256,256]{1,0:T(8,128)S(1)} %fusion.12, pred[]{:T(512)S(6)} %eq.49, f32[256,256]{1,0:T(8,128)S(1)} %fusion.36, f32[256,256]{1,0:T(8,128)S(1)} %copy-done.2, f32[3,256,256]{2,1,0:T(8,128)S(1)} %get-tuple-element.22, ...), kind=kOutput, calls=%fused_computation.123 | convolution fusion | flops 100925440 | bytes 2097157 | tf_op jit(solution)/shard_map/dot_general | solution.py:8
  80.7 1.4 %collective-permute-done.12 = f32[256,256]{1,0:T(8,128)S(1)} collective-permute-done((f32[256,256]{1,0:T(8,128)S(1)}, f32[256,256]{1,0:T(8,128)S(1)}, u32[]{:S(2)}, u32[]{:S(2)}) %collective-permute-start.12) | collective-permute-done | bytes 262176 | tf_op jit(solution)/shard_map/ppermute | solution.py:119
  82.1 1.1 %pad_maximum_fusion = f32[512,512]{1,0:T(8,128)} fusion(f32[256,512]{1,0:T(8,128)S(1)} %get-tuple-element.28, f32[256,256]{1,0:T(8,128)S(1)} %get-tuple-element.30, f32[256,256]{1,0:T(8,128)S(1)} %get-tuple-element.29), kind=kLoop, calls=%fused_computation.34 | loop fusion | flops 524288 | bytes 2097152 | tf_op jit(solution)/shard_map/concatenate | solution.py:121
  (43 shorter events, 6.1 us)
Async XLA Ops:
  0.0 2.8 %copy-start.4 = (f32[256,128]{1,0:T(8,128)S(1)}, f32[256,128]{1,0:T(8,128)}, u32[]{:S(2)}) copy-start(f32[256,128]{1,0:T(8,128)} %param.9) | copy-start | bytes 393220
  2.9 17.8 %collective-permute-start = (f32[1280,128]{1,0:T(8,128)S(1)}, f32[1280,128]{1,0:T(8,128)S(1)}, u32[]{:S(2)}, u32[]{:S(2)}) collective-permute-start(f32[1280,128]{1,0:T(8,128)S(1)} %constant_dynamic-update-slice_fusion), channel_id=1, source_target_pairs={{0,1},{1,0},{2,3},{3,2},{4,5},{5,4},{6,7},{7,6},{8,9},{9,8},{10,11... | collective-permute-start | bytes 1966088 | tf_op jit(solution)/shard_map/ppermute | solution.py:34
  20.6 1.2 %copy-start = (f32[512,512]{1,0:T(8,128)S(1)}, f32[512,512]{1,0:T(8,128)}, u32[]{:S(2)}) copy-start(f32[512,512]{1,0:T(8,128)} %param.5) | copy-start | bytes 3145732
  23.0 2.5 %collective-permute-start.1 = (f32[3,256,256]{2,1,0:T(8,128)S(1)}, f32[3,256,256]{2,1,0:T(8,128)}, u32[]{:S(2)}, u32[]{:S(2)}) collective-permute-start(f32[3,256,256]{2,1,0:T(8,128)S(1)} %pad_maximum_fusion.1), channel_id=1, source_target_pairs={{0,2},{2,0},{4,6},{6,4},{8,10},{10,8},{12,14},{14,12},{16,18},{18,... | collective-permute-start | bytes 2359304 | tf_op jit(solution)/shard_map/ppermute | solution.py:69
  24.3 2.9 %collective-permute-start.2 = (f32[256,512]{1,0:T(8,128)S(1)}, f32[256,512]{1,0:T(8,128)}, u32[]{:S(2)}, u32[]{:S(2)}) collective-permute-start(f32[256,512]{1,0:T(8,128)S(1)} %get-tuple-element.27), channel_id=1, source_target_pairs={{0,2},{2,0},{4,6},{6,4},{8,10},{10,8},{12,14},{14,12},{16,18},{18,... | collective-permute-start | bytes 1572872 | tf_op jit(solution)/shard_map/ppermute | solution.py:84
  30.4 11.2 %collective-permute-start.3 = (f32[256,256]{1,0:T(8,128)S(1)}, f32[256,256]{1,0:T(8,128)}, u32[]{:S(2)}, u32[]{:S(2)}) collective-permute-start(f32[256,256]{1,0:T(8,128)S(1)} %get-tuple-element.33), channel_id=1, source_target_pairs={{0,4},{4,0},{2,6},{6,2},{8,12},{12,8},{10,14},{14,10},{16,20},{20,... | collective-permute-start | bytes 786440 | tf_op jit(solution)/shard_map/ppermute | solution.py:106
  32.2 9.4 %copy-start.5 = (f32[128,256]{1,0:T(8,128)}, f32[128,256]{1,0:T(8,128)S(1)}, u32[]{:S(2)}) copy-start(f32[128,256]{1,0:T(8,128)S(1)} %fusion.61) | copy-start | bytes 393220
  32.2 9.4 %collective-permute-start.4 = (f32[128,256]{1,0:T(8,128)S(1)}, f32[128,256]{1,0:T(8,128)S(1)}, u32[]{:S(2)}, u32[]{:S(2)}) collective-permute-start(f32[128,256]{1,0:T(8,128)S(1)} %fusion.61), channel_id=1, source_target_pairs={{4,0},{6,2},{12,8},{14,10},{20,16},{22,18},{28,24},{30,26},{5,1},{... | collective-permute-start | bytes 393224 | tf_op jit(solution)/shard_map/ppermute | solution.py:81
  41.6 1.4 %collective-permute-start.5 = (f32[128,256]{1,0:T(8,128)S(1)}, f32[128,256]{1,0:T(8,128)S(1)}, u32[]{:S(2)}, u32[]{:S(2)}) collective-permute-start(f32[128,256]{1,0:T(8,128)S(1)} %collective-permute-done.4), channel_id=1, source_target_pairs={{0,2},{2,0},{4,6},{6,4},{8,10},{10,8},{12,14},{14,12},{16,18},{18,... | collective-permute-start | bytes 393224 | tf_op jit(solution)/shard_map/ppermute | solution.py:108
  43.0 0.7 copy-start.3
  45.3 5.0 %copy-start.6 = (f32[128,256]{1,0:T(8,128)S(1)}, f32[128,256]{1,0:T(8,128)}, u32[]{:S(2)}) copy-start(f32[128,256]{1,0:T(8,128)} %copy-done.5) | copy-start | bytes 393220
  46.5 16.1 %collective-permute-start.6 = (f32[256,256]{1,0:T(8,128)}, f32[256,256]{1,0:T(8,128)}, u32[]{:S(2)}, u32[]{:S(2)}) collective-permute-start(f32[256,256]{1,0:T(8,128)} %get-tuple-element.35), channel_id=1, source_target_pairs={{0,8},{8,0},{2,10},{10,2},{16,24},{24,16},{18,26},{26,18},{1,9},{9... | collective-permute-start | bytes 786440 | tf_op jit(solution)/shard_map/ppermute | solution.py:106
  50.3 12.4 %collective-permute-start.7 = (f32[128,256]{1,0:T(8,128)S(1)}, f32[128,256]{1,0:T(8,128)S(1)}, u32[]{:S(2)}, u32[]{:S(2)}) collective-permute-start(f32[128,256]{1,0:T(8,128)S(1)} %copy-done.6), channel_id=1, source_target_pairs={{8,0},{10,2},{24,16},{26,18},{9,1},{11,3},{25,17},{27,19}} | collective-permute-start | bytes 393224 | tf_op jit(solution)/shard_map/ppermute | solution.py:81
  51.6 18.1 %collective-permute-start.10 = (f32[128,256]{1,0:T(8,128)S(1)}, f32[128,256]{1,0:T(8,128)S(1)}, u32[]{:S(2)}, u32[]{:S(2)}) collective-permute-start(f32[128,256]{1,0:T(8,128)S(1)} %copy-done.6), channel_id=1, source_target_pairs={{16,0},{18,2},{17,1},{19,3}} | collective-permute-start | bytes 393224 | tf_op jit(solution)/shard_map/ppermute | solution.py:81
  62.6 1.3 %collective-permute-start.8 = (f32[128,256]{1,0:T(8,128)S(1)}, f32[128,256]{1,0:T(8,128)S(1)}, u32[]{:S(2)}, u32[]{:S(2)}) collective-permute-start(f32[128,256]{1,0:T(8,128)S(1)} %collective-permute-done.7), channel_id=1, source_target_pairs={{0,2},{2,0},{4,6},{6,4},{8,10},{10,8},{12,14},{14,12},{16,18},{18,... | collective-permute-start | bytes 393224 | tf_op jit(solution)/shard_map/ppermute | solution.py:108
  64.3 3.7 %copy-start.1 = (f32[256,256]{1,0:T(8,128)S(1)}, f32[256,256]{1,0:T(8,128)}, u32[]{:S(2)}) copy-start(f32[256,256]{1,0:T(8,128)} %get-tuple-element.36) | copy-start | bytes 786436
  66.0 11.2 %collective-permute-start.9 = (f32[256,256]{1,0:T(8,128)S(1)}, f32[256,256]{1,0:T(8,128)S(1)}, u32[]{:S(2)}, u32[]{:S(2)}) collective-permute-start(f32[256,256]{1,0:T(8,128)S(1)} %get-tuple-element.37), channel_id=1, source_target_pairs={{0,16},{16,0},{2,18},{18,2},{1,17},{17,1},{3,19},{19,3}} | collective-permute-start | bytes 786440 | tf_op jit(solution)/shard_map/ppermute | solution.py:106
  77.2 1.3 %collective-permute-start.11 = (f32[128,256]{1,0:T(8,128)S(1)}, f32[128,256]{1,0:T(8,128)S(1)}, u32[]{:S(2)}, u32[]{:S(2)}) collective-permute-start(f32[128,256]{1,0:T(8,128)S(1)} %collective-permute-done.10), channel_id=1, source_target_pairs={{0,2},{2,0},{4,6},{6,4},{8,10},{10,8},{12,14},{14,12},{16,18},{18,... | collective-permute-start | bytes 393224 | tf_op jit(solution)/shard_map/ppermute | solution.py:108
  77.9 1.3 %copy-start.2 = (f32[256,256]{1,0:T(8,128)S(1)}, f32[256,256]{1,0:T(8,128)}, u32[]{:S(2)}) copy-start(f32[256,256]{1,0:T(8,128)} %get-tuple-element.32) | copy-start | bytes 786436
  80.5 1.6 %collective-permute-start.12 = (f32[256,256]{1,0:T(8,128)S(1)}, f32[256,256]{1,0:T(8,128)S(1)}, u32[]{:S(2)}, u32[]{:S(2)}) collective-permute-start(f32[256,256]{1,0:T(8,128)S(1)} %get-tuple-element.39), channel_id=1, source_target_pairs={{0,2},{2,0},{4,6},{6,4},{8,10},{10,8},{12,14},{14,12},{16,18},{18,... | collective-permute-start | bytes 786440 | tf_op jit(solution)/shard_map/ppermute | solution.py:119

commit v13 on v11

--- a/solution.py
+++ b/solution.py
@@ -44,11 +44,10 @@
     rows = leaf_v.shape[0]
     width = leaf_t.shape[0]
 
-    gathered = col_gather(jnp.concatenate([leaf_v, leaf_t, tree_v, tree_t], axis=0))
-    leaf_full = gathered[:rows]
-    leaf_tri = gathered[rows:rows + width]
-    tree_full = gathered[rows + width:rows + 2 * width]
-    tree_tri = gathered[rows + 2 * width:]
+    leaf_full = col_gather(leaf_v)
+    leaf_tri = col_gather(leaf_t)
+    tree_full = col_gather(tree_v)
+    tree_tri = col_gather(tree_t)
 
     leaf_vectors = unit_lower(leaf_full)
     leaf_factor = jnp.triu(leaf_tri)

time: 74.8 us -> 71.5 us (0.956)
  local copies, waits for them, and re-layouts: 4.66 us -> 1.9 us
  waiting for transfers between devices: 42.1 us -> 40.1 us
  starting transfers between devices: 13.1 us -> 14.6 us
    unnamed x15 -> x18, local copies, waits for them, and re-layouts: 4.58 us -> 1.83 us
    ppermute x1 -> x4, starting transfers between devices: 3.03 us -> 5.06 us  [col_gather(): by_shift.append(lax.ppermute(part, 'col', perm))]
    ppermute x1 -> x4, waiting for transfers between devices: 14.7 us -> 12.9 us  [col_gather(): by_shift.append(lax.ppermute(part, 'col', perm))]
  transfers between devices with their start and end apart: 13 -> 16, of which waited for: 8 -> 8; matrix products, arithmetic and copies ran while one was open for 10% -> 12% of each run, Pallas kernels for 0% -> 0%
where the time goes in v13:
time: 71.5 us; the launch traced here: 71.2 us
  waiting for transfers between devices  40.1 us (56%)
  starting transfers between devices  14.6 us (20%)
  matrix products  12.5 us (17%)
  local copies, waits for them, and re-layouts  1.9 us (3%)
  other arithmetic  1.75 us (2%)
    ppermute x3, waiting for transfers between devices, on_device(): partner_factors.append(lax.ppermute(half_s, 'row', pairs))  13 us
    ppermute x4, waiting for transfers between devices, col_gather(): by_shift.append(lax.ppermute(part, 'col', perm))  12.9 us
    ppermute x3, waiting for transfers between devices, on_device(): received = lax.ppermute(jnp.where(is_upper, q, chain), 'row', pairs)  12.2 us
    dot_general x16, matrix products, product_left_t(): lax.dot_general(left, right, (((0,), (0,)), ((), ())), precision=lax.Prec...  10.4 us
    ppermute x4, starting transfers between devices, col_gather(): by_shift.append(lax.ppermute(part, 'col', perm))  5.06 us
    ppermute x3, starting transfers between devices, on_device(): received = lax.ppermute(jnp.where(is_upper, q, chain), 'row', pairs)  4.79 us
    ppermute x3, starting transfers between devices, on_device(): partner_factors.append(lax.ppermute(half_s, 'row', pairs))  3.86 us
    dot_general x6, matrix products, product(): jnp.dot(left, right, precision=lax.Precision.HIGH, preferred_element_type...  2.05 us
  transfers between devices with their start and end apart: 16, of which 8 were waited for; matrix products, arithmetic and copies ran while one was open for 12% of the time, Pallas kernels for 0%

profile of v13, /device:TPU:0, one launch (start us, length us, event | category | flops | bytes accessed | tf_op | source)
XLA Modules:
  0.0 71.2 jit_solution(9934580204558731589)
XLA Ops:
  0.0 3.0 %collective-permute-start.2 = (f32[256,128]{1,0:T(8,128)}, f32[256,128]{1,0:T(8,128)S(1)}, u32[]{:S(2)}, u32[]{:S(2)}) collective-permute-start(f32[256,128]{1,0:T(8,128)} %param.8), channel_id=1, source_target_pairs={{0,1},{1,0},{2,3},{3,2},{4,5},{5,4},{6,7},{7,6},{8,9},{9,8},{10,11... | collective-permute-start | bytes 393224 | tf_op jit(solution)/shard_map/ppermute | solution.py:34
  3.0 2.0 %collective-permute-start.1 = (f32[256,128]{1,0:T(8,128)}, f32[256,128]{1,0:T(8,128)S(1)}, u32[]{:S(2)}, u32[]{:S(2)}) collective-permute-start(f32[256,128]{1,0:T(8,128)} %param.7), channel_id=1, source_target_pairs={{0,1},{1,0},{2,3},{3,2},{4,5},{5,4},{6,7},{7,6},{8,9},{9,8},{10,11... | collective-permute-start | bytes 393224 | tf_op jit(solution)/shard_map/ppermute | solution.py:34
  5.1 2.5 %collective-permute-done.2 = f32[256,128]{1,0:T(8,128)S(1)} collective-permute-done((f32[256,128]{1,0:T(8,128)}, f32[256,128]{1,0:T(8,128)S(1)}, u32[]{:S(2)}, u32[]{:S(2)}) %collective-permute-start.2) | collective-permute-done | bytes 131104 | tf_op jit(solution)/shard_map/ppermute | solution.py:34
  7.6 10.3 %collective-permute-done.3 = f32[256,128]{1,0:T(8,128)S(1)} collective-permute-done((f32[256,128]{1,0:T(8,128)}, f32[256,128]{1,0:T(8,128)S(1)}, u32[]{:S(2)}, u32[]{:S(2)}) %collective-permute-start.3) | collective-permute-done | bytes 131104 | tf_op jit(solution)/shard_map/ppermute | solution.py:34
  18.7 0.7 %copy-done.8 = f32[256,128]{1,0:T(8,128)S(1)} copy-done((f32[256,128]{1,0:T(8,128)S(1)}, f32[256,128]{1,0:T(8,128)}, u32[]{:S(2)}) %copy-start.8) | copy-done | bytes 131096
  19.9 0.6 fusion.15
  20.5 0.5 fusion.22
  21.0 0.6 convolution_subtract_fusion
  22.0 1.3 %collective-permute-start.6 = (f32[128,256]{1,0:T(8,128)S(1)}, f32[128,256]{1,0:T(8,128)S(1)}, u32[]{:S(2)}, u32[]{:S(2)}) collective-permute-start(f32[128,256]{1,0:T(8,128)S(1)} %fusion.74), channel_id=1, source_target_pairs={{4,0},{6,2},{12,8},{14,10},{20,16},{22,18},{28,24},{30,26},{5,1},{... | collective-permute-start | bytes 393224 | tf_op jit(solution)/shard_map/ppermute | solution.py:80
  23.3 0.4 fusion.37
  23.8 6.0 %collective-permute-done.6 = f32[128,256]{1,0:T(8,128)S(1)} collective-permute-done((f32[128,256]{1,0:T(8,128)S(1)}, f32[128,256]{1,0:T(8,128)S(1)}, u32[]{:S(2)}, u32[]{:S(2)}) %collective-permute-start.6) | collective-permute-done | bytes 131104 | tf_op jit(solution)/shard_map/ppermute | solution.py:80
  29.8 1.1 %select_subtract_fusion.1 = (f32[256,256]{1,0:T(8,128)S(1)}, f32[256,256]{1,0:T(8,128)}) fusion(f32[256,512]{1,0:T(8,128)S(1)} %collective-permute-done.5, s32[]{:T(128)S(6)} %select_n.319, f32[256,512]{1,0:T(8,128)S(1)} %get-tuple-element.19, pred[]{:T(512)S(6)} %eq.55, f32[256,256]{1,0:T(8,128)S(1)} %fusion.37, f32[3,256,256]{2,1,0:T(8,128)S(1)} %get-tuple-element.18), kind=kOutput, calls=%fused_computation.84 | convolution fusion | flops 100925440 | bytes 2099200 | tf_op jit(solution)/shard_map/dot_general | solution.py:12
  30.9 1.1 %broadcast_select_fusion.4 = (f32[256,256]{1,0:T(8,128)}, f32[256,256]{1,0:T(8,128)S(1)}) fusion(f32[256,256]{1,0:T(8,128)S(1)} %get-tuple-element.33, pred[]{:T(512)S(6)} %eq.62, f32[3,256,256]{2,1,0:T(8,128)S(1)} %get-tuple-element.17), kind=kOutput, calls=%fused_computation.144 | convolution fusion | flops 100794368 | bytes 1311744 | tf_op jit(solution)/shard_map/dot_general | solution.py:12
  32.0 1.3 %collective-permute-start.9 = (f32[128,256]{1,0:T(8,128)}, f32[128,256]{1,0:T(8,128)S(1)}, u32[]{:S(2)}, u32[]{:S(2)}) collective-permute-start(f32[128,256]{1,0:T(8,128)} %copy-done.5), channel_id=1, source_target_pairs={{8,0},{10,2},{24,16},{26,18},{9,1},{11,3},{25,17},{27,19}} | collective-permute-start | bytes 393224 | tf_op jit(solution)/shard_map/ppermute | solution.py:80
  33.3 1.3 %collective-permute-start.10 = (f32[128,256]{1,0:T(8,128)}, f32[128,256]{1,0:T(8,128)S(1)}, u32[]{:S(2)}, u32[]{:S(2)}) collective-permute-start(f32[128,256]{1,0:T(8,128)} %copy-done.5), channel_id=1, source_target_pairs={{16,0},{18,2},{17,1},{19,3}} | collective-permute-start | bytes 393224 | tf_op jit(solution)/shard_map/ppermute | solution.py:80
  34.6 1.2 %fusion.71 = f32[256,256]{1,0:T(8,128)S(1)} fusion(f32[256,256]{1,0:T(8,128)S(1)} %get-tuple-element.33, f32[128,256]{1,0:T(8,128)} %collective-permute-done.7, f32[128,256]{1,0:T(8,128)S(1)} %collective-permute-done.6, pred[]{:T(512)S(6)} %eq.59, pred[]{:T(512)S(6)} %and.51), kind=kOutput, calls=%fused_computation.115 | convolution fusion | flops 50397184 | bytes 655362 | tf_op jit(solution)/shard_map/dot_general | solution.py:12
  35.8 7.0 %collective-permute-done.9 = f32[128,256]{1,0:T(8,128)S(1)} collective-permute-done((f32[128,256]{1,0:T(8,128)}, f32[128,256]{1,0:T(8,128)S(1)}, u32[]{:S(2)}, u32[]{:S(2)}) %collective-permute-start.9) | collective-permute-done | bytes 131104 | tf_op jit(solution)/shard_map/ppermute | solution.py:80
  42.8 1.3 %convolution_add_fusion = f32[256,256]{1,0:T(8,128)S(1)} fusion(f32[256,256]{1,0:T(8,128)S(1)} %get-tuple-element.36, f32[256,256]{1,0:T(8,128)} %collective-permute-done.8, f32[3,256,256]{2,1,0:T(8,128)S(1)} %get-tuple-element.17), kind=kOutput, calls=%fused_computation.3 | convolution fusion | flops 100728832 | bytes 1048576 | tf_op jit(solution)/shard_map/dot_general | solution.py:12
  44.2 1.4 %fusion.11 = f32[256,256]{1,0:T(8,128)S(1)} fusion(f32[256,256]{1,0:T(8,128)S(1)} %get-tuple-element.33, f32[256,256]{1,0:T(8,128)} %collective-permute-done.8, f32[256,256]{1,0:T(8,128)S(1)} %fusion.71, f32[128,256]{1,0:T(8,128)S(1)} %collective-permute-done.6, f32[128,256]{1,0:T(8,128)} %collective-permute-done.7, pred[]{:T(512)S(6)} %eq.59, pred[]{:T(512)S(6)} %and.51), kind=kOutput, calls=%fused_computation.21 | convolution fusion | flops 50659328 | bytes 1443328 | tf_op jit(solution)/shard_map/dot_general | solution.py:12
  45.5 0.4 broadcast_select_fusion.3
  45.9 1.9 %collective-permute-start.12 = (f32[256,256]{1,0:T(8,128)S(1)}, f32[256,256]{1,0:T(8,128)S(1)}, u32[]{:S(2)}, u32[]{:S(2)}) collective-permute-start(f32[256,256]{1,0:T(8,128)S(1)} %get-tuple-element.37), channel_id=1, source_target_pairs={{0,8},{8,0},{2,10},{10,2},{16,24},{24,16},{18,26},{26,18},{1,9},{9... | collective-permute-start | bytes 786440 | tf_op jit(solution)/shard_map/ppermute | solution.py:105
  48.2 0.6 collective-permute-start.13
  48.8 0.5 collective-permute-done.11
  49.6 6.2 %collective-permute-done.12 = f32[256,256]{1,0:T(8,128)S(1)} collective-permute-done((f32[256,256]{1,0:T(8,128)S(1)}, f32[256,256]{1,0:T(8,128)S(1)}, u32[]{:S(2)}, u32[]{:S(2)}) %collective-permute-start.12) | collective-permute-done | bytes 262176 | tf_op jit(solution)/shard_map/ppermute | solution.py:105
  56.1 0.4 broadcast_select_fusion.2
  56.5 2.9 %collective-permute-start.14 = (f32[256,256]{1,0:T(8,128)S(1)}, f32[256,256]{1,0:T(8,128)S(1)}, u32[]{:S(2)}, u32[]{:S(2)}) collective-permute-start(f32[256,256]{1,0:T(8,128)S(1)} %get-tuple-element.39), channel_id=1, source_target_pairs={{0,16},{16,0},{2,18},{18,2},{1,17},{17,1},{3,19},{19,3}} | collective-permute-start | bytes 786440 | tf_op jit(solution)/shard_map/ppermute | solution.py:105
  59.4 0.4 convolution_add_fusion.1
  60.4 6.0 %collective-permute-done.14 = f32[256,256]{1,0:T(8,128)S(1)} collective-permute-done((f32[256,256]{1,0:T(8,128)S(1)}, f32[256,256]{1,0:T(8,128)S(1)}, u32[]{:S(2)}, u32[]{:S(2)}) %collective-permute-start.14) | collective-permute-done | bytes 262176 | tf_op jit(solution)/shard_map/ppermute | solution.py:105
  66.4 0.4 convolution_add_fusion.2
  67.4 0.7 copy-done.2
  68.5 1.5 %collective-permute-done.15 = f32[256,256]{1,0:T(8,128)S(1)} collective-permute-done((f32[256,256]{1,0:T(8,128)S(1)}, f32[256,256]{1,0:T(8,128)S(1)}, u32[]{:S(2)}, u32[]{:S(2)}) %collective-permute-start.15) | collective-permute-done | bytes 262176 | tf_op jit(solution)/shard_map/ppermute | solution.py:121
  70.1 1.1 %pad_maximum_fusion = f32[512,512]{1,0:T(8,128)} fusion(f32[256,512]{1,0:T(8,128)S(1)} %get-tuple-element.20, f32[256,256]{1,0:T(8,128)S(1)} %get-tuple-element.22, f32[256,256]{1,0:T(8,128)S(1)} %get-tuple-element.21), kind=kLoop, calls=%fused_computation.24 | loop fusion | flops 524288 | bytes 2097152 | tf_op jit(solution)/shard_map/concatenate | solution.py:123
  (52 shorter events, 4.3 us)
Async XLA Ops:
  0.0 7.6 %copy-start.6 = (f32[256,128]{1,0:T(8,128)S(1)}, f32[256,128]{1,0:T(8,128)}, u32[]{:S(2)}) copy-start(f32[256,128]{1,0:T(8,128)} %param.8) | copy-start | bytes 393220
  0.0 7.6 %collective-permute-start.2 = (f32[256,128]{1,0:T(8,128)}, f32[256,128]{1,0:T(8,128)S(1)}, u32[]{:S(2)}, u32[]{:S(2)}) collective-permute-start(f32[256,128]{1,0:T(8,128)} %param.8), channel_id=1, source_target_pairs={{0,1},{1,0},{2,3},{3,2},{4,5},{5,4},{6,7},{7,6},{8,9},{9,8},{10,11... | collective-permute-start | bytes 393224 | tf_op jit(solution)/shard_map/ppermute | solution.py:34
  3.0 16.5 %collective-permute-start = (f32[512,128]{1,0:T(8,128)}, f32[512,128]{1,0:T(8,128)S(1)}, u32[]{:S(2)}, u32[]{:S(2)}) collective-permute-start(f32[512,128]{1,0:T(8,128)} %param.6), channel_id=1, source_target_pairs={{0,1},{1,0},{2,3},{3,2},{4,5},{5,4},{6,7},{7,6},{8,9},{9,8},{10,11... | collective-permute-start | bytes 786440 | tf_op jit(solution)/shard_map/ppermute | solution.py:34
  3.0 15.7 %collective-permute-start.1 = (f32[256,128]{1,0:T(8,128)}, f32[256,128]{1,0:T(8,128)S(1)}, u32[]{:S(2)}, u32[]{:S(2)}) collective-permute-start(f32[256,128]{1,0:T(8,128)} %param.7), channel_id=1, source_target_pairs={{0,1},{1,0},{2,3},{3,2},{4,5},{5,4},{6,7},{7,6},{8,9},{9,8},{10,11... | collective-permute-start | bytes 393224 | tf_op jit(solution)/shard_map/ppermute | solution.py:34
  5.0 13.0 %collective-permute-start.3 = (f32[256,128]{1,0:T(8,128)}, f32[256,128]{1,0:T(8,128)S(1)}, u32[]{:S(2)}, u32[]{:S(2)}) collective-permute-start(f32[256,128]{1,0:T(8,128)} %param.9), channel_id=1, source_target_pairs={{0,1},{1,0},{2,3},{3,2},{4,5},{5,4},{6,7},{7,6},{8,9},{9,8},{10,11... | collective-permute-start | bytes 393224 | tf_op jit(solution)/shard_map/ppermute | solution.py:34
  7.6 10.4 %copy-start.7 = (f32[256,128]{1,0:T(8,128)S(1)}, f32[256,128]{1,0:T(8,128)}, u32[]{:S(2)}) copy-start(f32[256,128]{1,0:T(8,128)} %param.9) | copy-start | bytes 393220
  18.5 0.9 %copy-start.8 = (f32[256,128]{1,0:T(8,128)S(1)}, f32[256,128]{1,0:T(8,128)}, u32[]{:S(2)}) copy-start(f32[256,128]{1,0:T(8,128)} %param.7) | copy-start | bytes 393220
  18.5 1.0 %copy-start.4 = (f32[512,128]{1,0:T(8,128)S(1)}, f32[512,128]{1,0:T(8,128)}, u32[]{:S(2)}) copy-start(f32[512,128]{1,0:T(8,128)} %param.6) | copy-start | bytes 786436
  18.6 1.3 %copy-start = (f32[512,512]{1,0:T(8,128)S(1)}, f32[512,512]{1,0:T(8,128)}, u32[]{:S(2)}) copy-start(f32[512,512]{1,0:T(8,128)} %param.5) | copy-start | bytes 3145732
  18.6 3.2 %collective-permute-start.4 = (f32[3,256,256]{2,1,0:T(8,128)S(1)}, f32[3,256,256]{2,1,0:T(8,128)S(1)}, u32[]{:S(2)}, u32[]{:S(2)}) collective-permute-start(f32[3,256,256]{2,1,0:T(8,128)S(1)} %pad_maximum_fusion.1), channel_id=1, source_target_pairs={{0,2},{2,0},{4,6},{6,4},{8,10},{10,8},{12,14},{14,12},{16,18},{18,... | collective-permute-start | bytes 2359304 | tf_op jit(solution)/shard_map/ppermute | solution.py:68
  21.7 2.0 %collective-permute-start.5 = (f32[256,512]{1,0:T(8,128)S(1)}, f32[256,512]{1,0:T(8,128)S(1)}, u32[]{:S(2)}, u32[]{:S(2)}) collective-permute-start(f32[256,512]{1,0:T(8,128)S(1)} %get-tuple-element.19), channel_id=1, source_target_pairs={{0,2},{2,0},{4,6},{6,4},{8,10},{10,8},{12,14},{14,12},{16,18},{18,... | collective-permute-start | bytes 1572872 | tf_op jit(solution)/shard_map/ppermute | solution.py:83
  22.0 1.7 %copy-start.5 = (f32[128,256]{1,0:T(8,128)}, f32[128,256]{1,0:T(8,128)S(1)}, u32[]{:S(2)}) copy-start(f32[128,256]{1,0:T(8,128)S(1)} %fusion.74) | copy-start | bytes 393220
  22.0 7.8 %collective-permute-start.6 = (f32[128,256]{1,0:T(8,128)S(1)}, f32[128,256]{1,0:T(8,128)S(1)}, u32[]{:S(2)}, u32[]{:S(2)}) collective-permute-start(f32[128,256]{1,0:T(8,128)S(1)} %fusion.74), channel_id=1, source_target_pairs={{4,0},{6,2},{12,8},{14,10},{20,16},{22,18},{28,24},{30,26},{5,1},{... | collective-permute-start | bytes 393224 | tf_op jit(solution)/shard_map/ppermute | solution.py:80
  23.8 7.1 %copy-start.1 = (f32[256,512]{1,0:T(8,128)}, f32[256,512]{1,0:T(8,128)S(1)}, u32[]{:S(2)}) copy-start(f32[256,512]{1,0:T(8,128)S(1)} %collective-permute-done.5) | copy-start | bytes 1572868
  29.8 4.8 %collective-permute-start.7 = (f32[128,256]{1,0:T(8,128)S(1)}, f32[128,256]{1,0:T(8,128)}, u32[]{:S(2)}, u32[]{:S(2)}) collective-permute-start(f32[128,256]{1,0:T(8,128)S(1)} %collective-permute-done.6), channel_id=1, source_target_pairs={{0,2},{2,0},{4,6},{6,4},{8,10},{10,8},{12,14},{14,12},{16,18},{18,... | collective-permute-start | bytes 393224 | tf_op jit(solution)/shard_map/ppermute | solution.py:110
  32.0 10.8 %collective-permute-start.8 = (f32[256,256]{1,0:T(8,128)}, f32[256,256]{1,0:T(8,128)}, u32[]{:S(2)}, u32[]{:S(2)}) collective-permute-start(f32[256,256]{1,0:T(8,128)} %get-tuple-element.35), channel_id=1, source_target_pairs={{0,4},{4,0},{2,6},{6,2},{8,12},{12,8},{10,14},{14,10},{16,20},{20,... | collective-permute-start | bytes 786440 | tf_op jit(solution)/shard_map/ppermute | solution.py:105
  32.0 10.8 %collective-permute-start.9 = (f32[128,256]{1,0:T(8,128)}, f32[128,256]{1,0:T(8,128)S(1)}, u32[]{:S(2)}, u32[]{:S(2)}) collective-permute-start(f32[128,256]{1,0:T(8,128)} %copy-done.5), channel_id=1, source_target_pairs={{8,0},{10,2},{24,16},{26,18},{9,1},{11,3},{25,17},{27,19}} | collective-permute-start | bytes 393224 | tf_op jit(solution)/shard_map/ppermute | solution.py:80
  33.3 9.5 %collective-permute-start.10 = (f32[128,256]{1,0:T(8,128)}, f32[128,256]{1,0:T(8,128)S(1)}, u32[]{:S(2)}, u32[]{:S(2)}) collective-permute-start(f32[128,256]{1,0:T(8,128)} %copy-done.5), channel_id=1, source_target_pairs={{16,0},{18,2},{17,1},{19,3}} | collective-permute-start | bytes 393224 | tf_op jit(solution)/shard_map/ppermute | solution.py:80
  45.9 9.8 %collective-permute-start.12 = (f32[256,256]{1,0:T(8,128)S(1)}, f32[256,256]{1,0:T(8,128)S(1)}, u32[]{:S(2)}, u32[]{:S(2)}) collective-permute-start(f32[256,256]{1,0:T(8,128)S(1)} %get-tuple-element.37), channel_id=1, source_target_pairs={{0,8},{8,0},{2,10},{10,2},{16,24},{24,16},{18,26},{26,18},{1,9},{9... | collective-permute-start | bytes 786440 | tf_op jit(solution)/shard_map/ppermute | solution.py:105
  47.9 1.4 %collective-permute-start.11 = (f32[128,256]{1,0:T(8,128)S(1)}, f32[128,256]{1,0:T(8,128)S(1)}, u32[]{:S(2)}, u32[]{:S(2)}) collective-permute-start(f32[128,256]{1,0:T(8,128)S(1)} %collective-permute-done.9), channel_id=1, source_target_pairs={{0,2},{2,0},{4,6},{6,4},{8,10},{10,8},{12,14},{14,12},{16,18},{18,... | collective-permute-start | bytes 393224 | tf_op jit(solution)/shard_map/ppermute | solution.py:110
  48.2 11.6 %collective-permute-start.13 = (f32[128,256]{1,0:T(8,128)S(1)}, f32[128,256]{1,0:T(8,128)S(1)}, u32[]{:S(2)}, u32[]{:S(2)}) collective-permute-start(f32[128,256]{1,0:T(8,128)S(1)} %collective-permute-done.10), channel_id=1, source_target_pairs={{0,2},{2,0},{4,6},{6,4},{8,10},{10,8},{12,14},{14,12},{16,18},{18,... | collective-permute-start | bytes 393224 | tf_op jit(solution)/shard_map/ppermute | solution.py:110
  56.5 9.9 %collective-permute-start.14 = (f32[256,256]{1,0:T(8,128)S(1)}, f32[256,256]{1,0:T(8,128)S(1)}, u32[]{:S(2)}, u32[]{:S(2)}) collective-permute-start(f32[256,256]{1,0:T(8,128)S(1)} %get-tuple-element.39), channel_id=1, source_target_pairs={{0,16},{16,0},{2,18},{18,2},{1,17},{17,1},{3,19},{19,3}} | collective-permute-start | bytes 786440 | tf_op jit(solution)/shard_map/ppermute | solution.py:105
  67.0 1.0 %copy-start.2 = (f32[256,512]{1,0:T(8,128)S(1)}, f32[256,512]{1,0:T(8,128)}, u32[]{:S(2)}) copy-start(f32[256,512]{1,0:T(8,128)} %copy-done.1) | copy-start | bytes 1572868
  67.1 1.1 %copy-start.3 = (f32[256,256]{1,0:T(8,128)S(1)}, f32[256,256]{1,0:T(8,128)}, u32[]{:S(2)}) copy-start(f32[256,256]{1,0:T(8,128)} %get-tuple-element.34) | copy-start | bytes 786436
  68.4 1.6 %collective-permute-start.15 = (f32[256,256]{1,0:T(8,128)S(1)}, f32[256,256]{1,0:T(8,128)S(1)}, u32[]{:S(2)}, u32[]{:S(2)}) collective-permute-start(f32[256,256]{1,0:T(8,128)S(1)} %get-tuple-element.41), channel_id=1, source_target_pairs={{0,2},{2,0},{4,6},{6,4},{8,10},{10,8},{12,14},{14,12},{16,18},{18,... | collective-permute-start | bytes 786440 | tf_op jit(solution)/shard_map/ppermute | solution.py:121

commit v14 on v13

--- a/solution.py
+++ b/solution.py
@@ -111,6 +111,7 @@
         top_rows = jnp.where(is_lower & (core == 0), mine, jnp.where(is_lower, mates, 0.0))
         bottom_rows = jnp.where(is_lower & (core == 0), mates, jnp.where(is_lower, mine, 0.0))
         own_part = product_left_t(top_rows, chain[:hw]) + product_left_t(bottom_rows, chain[hw:])
+        own_part, received = lax.optimization_barrier((own_part, received))
         update = product_left_t(even3[1], received) + q
         result = jnp.where(is_upper, chain - product(even3[0], update), result)
         chain = jnp.where(is_lower, chain - own_part - received, chain)

time: 71.5 us -> 68 us (0.951)
  starting transfers between devices: 14.6 us -> 19.2 us
  matrix products: 12.5 us -> 8.2 us
  waiting for transfers between devices: 40.1 us -> 37.3 us
  local copies, waits for them, and re-layouts: 1.9 us -> 0.82 us
    ppermute x3, waiting for transfers between devices: 13 us -> 6.07 us  [on_device(): partner_factors.append(lax.ppermute(half_s, 'row', pairs))]
    ppermute x3, waiting for transfers between devices: 12.2 us -> 17.9 us  [on_device(): received = lax.ppermute(jnp.where(is_upper, q, chain), 'row', pairs)]
    ppermute x3, starting transfers between devices: 4.79 us -> 9.52 us  [on_device(): received = lax.ppermute(jnp.where(is_upper, q, chain), 'row', pairs)]
    dot_general x16, matrix products: 10.4 us -> 6.14 us  [product_left_t(): lax.dot_general(left, right, (((0,), (0,)), ((), ())), precision=lax.Prec...]
    ppermute x4, waiting for transfers between devices: 12.9 us -> 11.4 us  [col_gather(): by_shift.append(lax.ppermute(part, 'col', perm))]
    unnamed x18 -> x10, local copies, waits for them, and re-layouts: 1.83 us -> 0.74 us
  transfers between devices with their start and end apart: 16 -> 16, of which waited for: 8 -> 9; matrix products, arithmetic and copies ran while one was open for 12% -> 11% of each run, Pallas kernels for 0% -> 0%
where the time goes in v14:
time: 68 us; the launch traced here: 67.8 us
  waiting for transfers between devices  37.3 us (55%)
  starting transfers between devices  19.2 us (28%)
  matrix products  8.2 us (12%)
  other arithmetic  1.85 us (3%)
  local copies, waits for them, and re-layouts  0.82 us (1%)
    ppermute x3, waiting for transfers between devices, on_device(): received = lax.ppermute(jnp.where(is_upper, q, chain), 'row', pairs)  17.9 us
    ppermute x4, waiting for transfers between devices, col_gather(): by_shift.append(lax.ppermute(part, 'col', perm))  11.4 us
    ppermute x3, starting transfers between devices, on_device(): received = lax.ppermute(jnp.where(is_upper, q, chain), 'row', pairs)  9.52 us
    dot_general x16, matrix products, product_left_t(): lax.dot_general(left, right, (((0,), (0,)), ((), ())), precision=lax.Prec...  6.14 us
    ppermute x3, waiting for transfers between devices, on_device(): partner_factors.append(lax.ppermute(half_s, 'row', pairs))  6.07 us
    ppermute x4, starting transfers between devices, col_gather(): by_shift.append(lax.ppermute(part, 'col', perm))  5.06 us
    ppermute x3, starting transfers between devices, on_device(): partner_factors.append(lax.ppermute(half_s, 'row', pairs))  3.88 us
    dot_general x6, matrix products, product(): jnp.dot(left, right, precision=lax.Precision.HIGH, preferred_element_type...  2.06 us
  transfers between devices with their start and end apart: 16, of which 9 were waited for; matrix products, arithmetic and copies ran while one was open for 11% of the time, Pallas kernels for 0%

profile of v14, /device:TPU:0, one launch (start us, length us, event | category | flops | bytes accessed | tf_op | source)
XLA Modules:
  0.0 67.8 jit_solution(12496464267726650644)
XLA Ops:
  0.0 3.0 %collective-permute-start.2 = (f32[256,128]{1,0:T(8,128)}, f32[256,128]{1,0:T(8,128)S(1)}, u32[]{:S(2)}, u32[]{:S(2)}) collective-permute-start(f32[256,128]{1,0:T(8,128)} %param.8), channel_id=1, source_target_pairs={{0,1},{1,0},{2,3},{3,2},{4,5},{5,4},{6,7},{7,6},{8,9},{9,8},{10,11... | collective-permute-start | bytes 393224 | tf_op jit(solution)/shard_map/ppermute | solution.py:34
  3.0 2.0 %collective-permute-start.3 = (f32[256,128]{1,0:T(8,128)}, f32[256,128]{1,0:T(8,128)S(1)}, u32[]{:S(2)}, u32[]{:S(2)}) collective-permute-start(f32[256,128]{1,0:T(8,128)} %param.9), channel_id=1, source_target_pairs={{0,1},{1,0},{2,3},{3,2},{4,5},{5,4},{6,7},{7,6},{8,9},{9,8},{10,11... | collective-permute-start | bytes 393224 | tf_op jit(solution)/shard_map/ppermute | solution.py:34
  5.1 2.5 %collective-permute-done.2 = f32[256,128]{1,0:T(8,128)S(1)} collective-permute-done((f32[256,128]{1,0:T(8,128)}, f32[256,128]{1,0:T(8,128)S(1)}, u32[]{:S(2)}, u32[]{:S(2)}) %collective-permute-start.2) | collective-permute-done | bytes 131104 | tf_op jit(solution)/shard_map/ppermute | solution.py:34
  7.6 5.6 %collective-permute-done.3 = f32[256,128]{1,0:T(8,128)S(1)} collective-permute-done((f32[256,128]{1,0:T(8,128)}, f32[256,128]{1,0:T(8,128)S(1)}, u32[]{:S(2)}, u32[]{:S(2)}) %collective-permute-start.3) | collective-permute-done | bytes 131104 | tf_op jit(solution)/shard_map/ppermute | solution.py:34
  13.4 0.3 convolution_bitcast_fusion
  13.9 0.7 %copy-done.4 = f32[256,128]{1,0:T(8,128)S(1)} copy-done((f32[256,128]{1,0:T(8,128)S(1)}, f32[256,128]{1,0:T(8,128)}, u32[]{:S(2)}) %copy-start.4) | copy-done | bytes 131096
  14.7 3.3 %collective-permute-done = f32[512,128]{1,0:T(8,128)S(1)} collective-permute-done((f32[512,128]{1,0:T(8,128)}, f32[512,128]{1,0:T(8,128)S(1)}, u32[]{:S(2)}, u32[]{:S(2)}) %collective-permute-start) | collective-permute-done | bytes 262176 | tf_op jit(solution)/shard_map/ppermute | solution.py:34
  18.1 0.6 fusion.5
  18.7 0.5 fusion.12
  19.2 0.6 convolution_subtract_fusion
  20.2 1.3 %collective-permute-start.10 = (f32[128,256]{1,0:T(8,128)S(1)}, f32[128,256]{1,0:T(8,128)S(1)}, u32[]{:S(2)}, u32[]{:S(2)}) collective-permute-start(f32[128,256]{1,0:T(8,128)S(1)} %fusion.64), channel_id=1, source_target_pairs={{16,0},{18,2},{17,1},{19,3}} | collective-permute-start | bytes 393224 | tf_op jit(solution)/shard_map/ppermute | solution.py:80
  21.5 1.3 %collective-permute-start.9 = (f32[128,256]{1,0:T(8,128)S(1)}, f32[128,256]{1,0:T(8,128)S(1)}, u32[]{:S(2)}, u32[]{:S(2)}) collective-permute-start(f32[128,256]{1,0:T(8,128)S(1)} %fusion.64), channel_id=1, source_target_pairs={{8,0},{10,2},{24,16},{26,18},{9,1},{11,3},{25,17},{27,19}} | collective-permute-start | bytes 393224 | tf_op jit(solution)/shard_map/ppermute | solution.py:80
  22.8 1.3 %collective-permute-start.6 = (f32[128,256]{1,0:T(8,128)S(1)}, f32[128,256]{1,0:T(8,128)S(1)}, u32[]{:S(2)}, u32[]{:S(2)}) collective-permute-start(f32[128,256]{1,0:T(8,128)S(1)} %fusion.64), channel_id=1, source_target_pairs={{4,0},{6,2},{12,8},{14,10},{20,16},{22,18},{28,24},{30,26},{5,1},{... | collective-permute-start | bytes 393224 | tf_op jit(solution)/shard_map/ppermute | solution.py:80
  24.1 0.4 fusion.27
  24.5 6.1 %collective-permute-done.6 = f32[128,256]{1,0:T(8,128)S(1)} collective-permute-done((f32[128,256]{1,0:T(8,128)S(1)}, f32[128,256]{1,0:T(8,128)S(1)}, u32[]{:S(2)}, u32[]{:S(2)}) %collective-permute-start.6) | collective-permute-done | bytes 131104 | tf_op jit(solution)/shard_map/ppermute | solution.py:80
  30.6 0.4 select_subtract_fusion.1
  31.0 0.4 broadcast_select_fusion.4
  31.5 0.5 collective-permute-done.7
  32.3 0.3 convolution_add_fusion.5
  32.6 7.6 %collective-permute-done.8 = f32[256,256]{1,0:T(8,128)S(1)} collective-permute-done((f32[256,256]{1,0:T(8,128)S(1)}, f32[256,256]{1,0:T(8,128)S(1)}, u32[]{:S(2)}, u32[]{:S(2)}) %collective-permute-start.8) | collective-permute-done | bytes 262176 | tf_op jit(solution)/shard_map/ppermute | solution.py:105
  40.3 0.4 convolution_add_fusion
  40.7 0.5 collective-permute-start.13
  41.2 0.4 broadcast_select_fusion.3
  41.6 4.3 %collective-permute-start.12 = (f32[256,256]{1,0:T(8,128)S(1)}, f32[256,256]{1,0:T(8,128)S(1)}, u32[]{:S(2)}, u32[]{:S(2)}) collective-permute-start(f32[256,256]{1,0:T(8,128)S(1)} %get-tuple-element.49), channel_id=1, source_target_pairs={{0,8},{8,0},{2,10},{10,2},{16,24},{24,16},{18,26},{26,18},{1,9},{9... | collective-permute-start | bytes 786440 | tf_op jit(solution)/shard_map/ppermute | solution.py:105
  46.9 5.6 %collective-permute-done.12 = f32[256,256]{1,0:T(8,128)S(1)} collective-permute-done((f32[256,256]{1,0:T(8,128)S(1)}, f32[256,256]{1,0:T(8,128)S(1)}, u32[]{:S(2)}, u32[]{:S(2)}) %collective-permute-start.12) | collective-permute-done | bytes 262176 | tf_op jit(solution)/shard_map/ppermute | solution.py:105
  52.5 0.4 broadcast_select_fusion.2
  52.9 5.2 %collective-permute-start.14 = (f32[256,256]{1,0:T(8,128)S(1)}, f32[256,256]{1,0:T(8,128)S(1)}, u32[]{:S(2)}, u32[]{:S(2)}) collective-permute-start(f32[256,256]{1,0:T(8,128)S(1)} %get-tuple-element.51), channel_id=1, source_target_pairs={{0,16},{16,0},{2,18},{18,2},{1,17},{17,1},{3,19},{19,3}} | collective-permute-start | bytes 786440 | tf_op jit(solution)/shard_map/ppermute | solution.py:105
  58.1 0.4 convolution_add_fusion.1
  59.4 4.7 %collective-permute-done.14 = f32[256,256]{1,0:T(8,128)S(1)} collective-permute-done((f32[256,256]{1,0:T(8,128)S(1)}, f32[256,256]{1,0:T(8,128)S(1)}, u32[]{:S(2)}, u32[]{:S(2)}) %collective-permute-start.14) | collective-permute-done | bytes 262176 | tf_op jit(solution)/shard_map/ppermute | solution.py:105
  64.1 0.4 convolution_add_fusion.2
  65.2 1.5 %collective-permute-done.15 = f32[256,256]{1,0:T(8,128)S(1)} collective-permute-done((f32[256,256]{1,0:T(8,128)S(1)}, f32[256,256]{1,0:T(8,128)S(1)}, u32[]{:S(2)}, u32[]{:S(2)}) %collective-permute-start.15) | collective-permute-done | bytes 262176 | tf_op jit(solution)/shard_map/ppermute | solution.py:122
  66.7 1.1 %pad_maximum_fusion = f32[512,512]{1,0:T(8,128)} fusion(f32[256,512]{1,0:T(8,128)S(1)} %get-tuple-element.32, f32[256,256]{1,0:T(8,128)S(1)} %get-tuple-element.34, f32[256,256]{1,0:T(8,128)S(1)} %get-tuple-element.33), kind=kLoop, calls=%fused_computation.14 | loop fusion | flops 524288 | bytes 2097152 | tf_op jit(solution)/shard_map/concatenate | solution.py:124
  (46 shorter events, 4.1 us)
Async XLA Ops:
  0.0 7.6 %copy-start.2 = (f32[256,128]{1,0:T(8,128)S(1)}, f32[256,128]{1,0:T(8,128)}, u32[]{:S(2)}) copy-start(f32[256,128]{1,0:T(8,128)} %param.8) | copy-start | bytes 393220
  0.0 7.6 %collective-permute-start.2 = (f32[256,128]{1,0:T(8,128)}, f32[256,128]{1,0:T(8,128)S(1)}, u32[]{:S(2)}, u32[]{:S(2)}) collective-permute-start(f32[256,128]{1,0:T(8,128)} %param.8), channel_id=1, source_target_pairs={{0,1},{1,0},{2,3},{3,2},{4,5},{5,4},{6,7},{7,6},{8,9},{9,8},{10,11... | collective-permute-start | bytes 393224 | tf_op jit(solution)/shard_map/ppermute | solution.py:34
  3.0 10.9 %collective-permute-start.1 = (f32[256,128]{1,0:T(8,128)}, f32[256,128]{1,0:T(8,128)S(1)}, u32[]{:S(2)}, u32[]{:S(2)}) collective-permute-start(f32[256,128]{1,0:T(8,128)} %param.7), channel_id=1, source_target_pairs={{0,1},{1,0},{2,3},{3,2},{4,5},{5,4},{6,7},{7,6},{8,9},{9,8},{10,11... | collective-permute-start | bytes 393224 | tf_op jit(solution)/shard_map/ppermute | solution.py:34
  3.0 10.2 %collective-permute-start.3 = (f32[256,128]{1,0:T(8,128)}, f32[256,128]{1,0:T(8,128)S(1)}, u32[]{:S(2)}, u32[]{:S(2)}) collective-permute-start(f32[256,128]{1,0:T(8,128)} %param.9), channel_id=1, source_target_pairs={{0,1},{1,0},{2,3},{3,2},{4,5},{5,4},{6,7},{7,6},{8,9},{9,8},{10,11... | collective-permute-start | bytes 393224 | tf_op jit(solution)/shard_map/ppermute | solution.py:34
  5.0 13.0 %collective-permute-start = (f32[512,128]{1,0:T(8,128)}, f32[512,128]{1,0:T(8,128)S(1)}, u32[]{:S(2)}, u32[]{:S(2)}) collective-permute-start(f32[512,128]{1,0:T(8,128)} %param.6), channel_id=1, source_target_pairs={{0,1},{1,0},{2,3},{3,2},{4,5},{5,4},{6,7},{7,6},{8,9},{9,8},{10,11... | collective-permute-start | bytes 786440 | tf_op jit(solution)/shard_map/ppermute | solution.py:34
  7.6 5.6 %copy-start.3 = (f32[256,128]{1,0:T(8,128)S(1)}, f32[256,128]{1,0:T(8,128)}, u32[]{:S(2)}) copy-start(f32[256,128]{1,0:T(8,128)} %param.9) | copy-start | bytes 393220
  13.7 0.9 %copy-start.4 = (f32[256,128]{1,0:T(8,128)S(1)}, f32[256,128]{1,0:T(8,128)}, u32[]{:S(2)}) copy-start(f32[256,128]{1,0:T(8,128)} %param.7) | copy-start | bytes 393220
  13.7 4.3 %copy-start.1 = (f32[512,128]{1,0:T(8,128)S(1)}, f32[512,128]{1,0:T(8,128)}, u32[]{:S(2)}) copy-start(f32[512,128]{1,0:T(8,128)} %param.6) | copy-start | bytes 786436
  13.8 4.3 %copy-start = (f32[512,512]{1,0:T(8,128)S(1)}, f32[512,512]{1,0:T(8,128)}, u32[]{:S(2)}) copy-start(f32[512,512]{1,0:T(8,128)} %param.5) | copy-start | bytes 3145732
  13.8 6.2 %collective-permute-start.4 = (f32[3,256,256]{2,1,0:T(8,128)S(1)}, f32[3,256,256]{2,1,0:T(8,128)S(1)}, u32[]{:S(2)}, u32[]{:S(2)}) collective-permute-start(f32[3,256,256]{2,1,0:T(8,128)S(1)} %pad_maximum_fusion.1), channel_id=1, source_target_pairs={{0,2},{2,0},{4,6},{6,4},{8,10},{10,8},{12,14},{14,12},{16,18},{18,... | collective-permute-start | bytes 2359304 | tf_op jit(solution)/shard_map/ppermute | solution.py:68
  19.9 4.6 %collective-permute-start.5 = (f32[256,512]{1,0:T(8,128)S(1)}, f32[256,512]{1,0:T(8,128)S(1)}, u32[]{:S(2)}, u32[]{:S(2)}) collective-permute-start(f32[256,512]{1,0:T(8,128)S(1)} %get-tuple-element.31), channel_id=1, source_target_pairs={{0,2},{2,0},{4,6},{6,4},{8,10},{10,8},{12,14},{14,12},{16,18},{18,... | collective-permute-start | bytes 1572872 | tf_op jit(solution)/shard_map/ppermute | solution.py:83
  20.2 12.4 %collective-permute-start.10 = (f32[128,256]{1,0:T(8,128)S(1)}, f32[128,256]{1,0:T(8,128)S(1)}, u32[]{:S(2)}, u32[]{:S(2)}) collective-permute-start(f32[128,256]{1,0:T(8,128)S(1)} %fusion.64), channel_id=1, source_target_pairs={{16,0},{18,2},{17,1},{19,3}} | collective-permute-start | bytes 393224 | tf_op jit(solution)/shard_map/ppermute | solution.py:80
  21.5 11.1 %collective-permute-start.9 = (f32[128,256]{1,0:T(8,128)S(1)}, f32[128,256]{1,0:T(8,128)S(1)}, u32[]{:S(2)}, u32[]{:S(2)}) collective-permute-start(f32[128,256]{1,0:T(8,128)S(1)} %fusion.64), channel_id=1, source_target_pairs={{8,0},{10,2},{24,16},{26,18},{9,1},{11,3},{25,17},{27,19}} | collective-permute-start | bytes 393224 | tf_op jit(solution)/shard_map/ppermute | solution.py:80
  22.8 7.8 %collective-permute-start.6 = (f32[128,256]{1,0:T(8,128)S(1)}, f32[128,256]{1,0:T(8,128)S(1)}, u32[]{:S(2)}, u32[]{:S(2)}) collective-permute-start(f32[128,256]{1,0:T(8,128)S(1)} %fusion.64), channel_id=1, source_target_pairs={{4,0},{6,2},{12,8},{14,10},{20,16},{22,18},{28,24},{30,26},{5,1},{... | collective-permute-start | bytes 393224 | tf_op jit(solution)/shard_map/ppermute | solution.py:80
  30.6 1.3 %collective-permute-start.7 = (f32[128,256]{1,0:T(8,128)S(1)}, f32[128,256]{1,0:T(8,128)S(1)}, u32[]{:S(2)}, u32[]{:S(2)}) collective-permute-start(f32[128,256]{1,0:T(8,128)S(1)} %collective-permute-done.6), channel_id=1, source_target_pairs={{0,2},{2,0},{4,6},{6,4},{8,10},{10,8},{12,14},{14,12},{16,18},{18,... | collective-permute-start | bytes 393224 | tf_op jit(solution)/shard_map/ppermute | solution.py:110
  31.4 8.8 %collective-permute-start.8 = (f32[256,256]{1,0:T(8,128)S(1)}, f32[256,256]{1,0:T(8,128)S(1)}, u32[]{:S(2)}, u32[]{:S(2)}) collective-permute-start(f32[256,256]{1,0:T(8,128)S(1)} %get-tuple-element.47), channel_id=1, source_target_pairs={{0,4},{4,0},{2,6},{6,2},{8,12},{12,8},{10,14},{14,10},{16,20},{20,... | collective-permute-start | bytes 786440 | tf_op jit(solution)/shard_map/ppermute | solution.py:105
  40.7 5.5 %collective-permute-start.11 = (f32[128,256]{1,0:T(8,128)S(1)}, f32[128,256]{1,0:T(8,128)S(1)}, u32[]{:S(2)}, u32[]{:S(2)}) collective-permute-start(f32[128,256]{1,0:T(8,128)S(1)} %collective-permute-done.9), channel_id=1, source_target_pairs={{0,2},{2,0},{4,6},{6,4},{8,10},{10,8},{12,14},{14,12},{16,18},{18,... | collective-permute-start | bytes 393224 | tf_op jit(solution)/shard_map/ppermute | solution.py:110
  40.7 17.8 %collective-permute-start.13 = (f32[128,256]{1,0:T(8,128)S(1)}, f32[128,256]{1,0:T(8,128)S(1)}, u32[]{:S(2)}, u32[]{:S(2)}) collective-permute-start(f32[128,256]{1,0:T(8,128)S(1)} %collective-permute-done.10), channel_id=1, source_target_pairs={{0,2},{2,0},{4,6},{6,4},{8,10},{10,8},{12,14},{14,12},{16,18},{18,... | collective-permute-start | bytes 393224 | tf_op jit(solution)/shard_map/ppermute | solution.py:110
  41.6 10.8 %collective-permute-start.12 = (f32[256,256]{1,0:T(8,128)S(1)}, f32[256,256]{1,0:T(8,128)S(1)}, u32[]{:S(2)}, u32[]{:S(2)}) collective-permute-start(f32[256,256]{1,0:T(8,128)S(1)} %get-tuple-element.49), channel_id=1, source_target_pairs={{0,8},{8,0},{2,10},{10,2},{16,24},{24,16},{18,26},{26,18},{1,9},{9... | collective-permute-start | bytes 786440 | tf_op jit(solution)/shard_map/ppermute | solution.py:105
  52.9 11.2 %collective-permute-start.14 = (f32[256,256]{1,0:T(8,128)S(1)}, f32[256,256]{1,0:T(8,128)S(1)}, u32[]{:S(2)}, u32[]{:S(2)}) collective-permute-start(f32[256,256]{1,0:T(8,128)S(1)} %get-tuple-element.51), channel_id=1, source_target_pairs={{0,16},{16,0},{2,18},{18,2},{1,17},{17,1},{3,19},{19,3}} | collective-permute-start | bytes 786440 | tf_op jit(solution)/shard_map/ppermute | solution.py:105
  65.1 1.6 %collective-permute-start.15 = (f32[256,256]{1,0:T(8,128)S(1)}, f32[256,256]{1,0:T(8,128)S(1)}, u32[]{:S(2)}, u32[]{:S(2)}) collective-permute-start(f32[256,256]{1,0:T(8,128)S(1)} %get-tuple-element.53), channel_id=1, source_target_pairs={{0,2},{2,0},{4,6},{6,4},{8,10},{10,8},{12,14},{14,12},{16,18},{18,... | collective-permute-start | bytes 786440 | tf_op jit(solution)/shard_map/ppermute | solution.py:122

commit v15 on v14

--- a/solution.py
+++ b/solution.py
@@ -49,12 +49,6 @@
     tree_full = col_gather(tree_v)
     tree_tri = col_gather(tree_t)
 
-    leaf_vectors = unit_lower(leaf_full)
-    leaf_factor = jnp.triu(leaf_tri)
-    leaf_w = product_left_t(leaf_factor, product_left_t(leaf_vectors, slab))
-    leafed = slab - product(leaf_vectors, leaf_w)
-    current = leafed[:width]
-
     tree_vectors = jnp.triu(tree_full)
     tree_factor = jnp.triu(tree_tri)
     tree_joint = product(tree_vectors, tree_factor)
@@ -70,7 +64,8 @@
     even3 = jnp.where(core == 0, own3, mate3)
 
     hw = width // 2
-    half_s = jnp.where(core == 0, even3[1][:hw], even3[1][hw:])
+    mate_s = lax.ppermute(tree_factor[hw:], "row", swap)
+    half_s = jnp.where(core == 0, tree_factor[:hw], mate_s)
     partner_factors = []
     for level in range(1, levels):
         step = 1 << level
@@ -79,11 +74,18 @@
             pairs += [(i + step, i), (i + step + 1, i + 1)]
         partner_factors.append(lax.ppermute(half_s, "row", pairs))
 
+    leaf_full, leaf_tri, partner_factors[0] = lax.optimization_barrier((leaf_full, leaf_tri, partner_factors[0]))
+    leaf_vectors = unit_lower(leaf_full)
+    leaf_factor = jnp.triu(leaf_tri)
+    leaf_w = product_left_t(leaf_factor, product_left_t(leaf_vectors, slab))
+    leafed = slab - product(leaf_vectors, leaf_w)
+    current = leafed[:width]
+
     is_lower = core == 0
     received = lax.ppermute(current, "row", swap)
     own_h = lax.dynamic_slice(current, (0, core * half), (width, half))
     early = product_left_t(jnp.where(is_lower, odd3[1], odd3[2]), own_h)
-    early, received, partner_factors[0] = lax.optimization_barrier((early, received, partner_factors[0]))
+    early, received = lax.optimization_barrier((early, received))
     recv_h = lax.dynamic_slice(received, (0, core * half), (width, half))
     update = early + product_left_t(jnp.where(is_lower, odd3[2], odd3[1]), recv_h)
     upper_h = jnp.where(is_lower, recv_h, own_h)

time: 68 us -> 66.3 us (0.975)
  waiting for transfers between devices: 37.3 us -> 32 us
  other arithmetic: 1.85 us -> 4.01 us
  starting transfers between devices: 19.2 us -> 20.5 us
    ppermute x3, waiting for transfers between devices: 17.9 us -> 12.8 us  [on_device(): received = lax.ppermute(jnp.where(is_upper, q, chain), 'row', pairs)]
    ppermute x3, waiting for transfers between devices: 6.07 us -> 8.92 us  [on_device(): partner_factors.append(lax.ppermute(half_s, 'row', pairs))]
    ppermute x4, waiting for transfers between devices: 11.4 us -> 8.68 us  [col_gather(): by_shift.append(lax.ppermute(part, 'col', perm))]
    select_n x1, other arithmetic: 0.19 us -> 1.29 us  [on_device(): even3 = jnp.where(core == 0, own3, mate3)]
    another operation x2, other arithmetic: 0.11 us -> 0.99 us  [col_gather(): stacked = jnp.stack(by_shift)]
  transfers between devices with their start and end apart: 16 -> 17, of which waited for: 9 -> 10; matrix products, arithmetic and copies ran while one was open for 11% -> 15% of each run, Pallas kernels for 0% -> 0%
where the time goes in v15:
time: 66.3 us; the launch traced here: 66 us
  waiting for transfers between devices  32 us (48%)
  starting transfers between devices  20.5 us (31%)
  matrix products  8.23 us (12%)
  other arithmetic  4.01 us (6%)
  local copies, waits for them, and re-layouts  0.85 us (1%)
    ppermute x3, waiting for transfers between devices, on_device(): received = lax.ppermute(jnp.where(is_upper, q, chain), 'row', pairs)  12.8 us
    ppermute x3, starting transfers between devices, on_device(): received = lax.ppermute(jnp.where(is_upper, q, chain), 'row', pairs)  10.1 us
    ppermute x3, waiting for transfers between devices, on_device(): partner_factors.append(lax.ppermute(half_s, 'row', pairs))  8.92 us
    ppermute x4, waiting for transfers between devices, col_gather(): by_shift.append(lax.ppermute(part, 'col', perm))  8.68 us
    dot_general x16, matrix products, product_left_t(): lax.dot_general(left, right, (((0,), (0,)), ((), ())), precision=lax.Prec...  6.16 us
    ppermute x4, starting transfers between devices, col_gather(): by_shift.append(lax.ppermute(part, 'col', perm))  5.04 us
    ppermute x3, starting transfers between devices, on_device(): partner_factors.append(lax.ppermute(half_s, 'row', pairs))  4.01 us
    dot_general x6, matrix products, product(): jnp.dot(left, right, precision=lax.Precision.HIGH, preferred_element_type...  2.08 us
  transfers between devices with their start and end apart: 17, of which 10 were waited for; matrix products, arithmetic and copies ran while one was open for 15% of the time, Pallas kernels for 0%

profile of v15, /device:TPU:0, one launch (start us, length us, event | category | flops | bytes accessed | tf_op | source)
XLA Modules:
  0.0 66.0 jit_solution(3405346275977332580)
XLA Ops:
  0.0 3.0 %collective-permute-start.2 = (f32[256,128]{1,0:T(8,128)}, f32[256,128]{1,0:T(8,128)S(1)}, u32[]{:S(2)}, u32[]{:S(2)}) collective-permute-start(f32[256,128]{1,0:T(8,128)} %param.9), channel_id=1, source_target_pairs={{0,1},{1,0},{2,3},{3,2},{4,5},{5,4},{6,7},{7,6},{8,9},{9,8},{10,11... | collective-permute-start | bytes 393224 | tf_op jit(solution)/shard_map/ppermute | solution.py:34
  3.0 2.0 %collective-permute-start.5 = (f32[256,128]{1,0:T(8,128)}, f32[256,128]{1,0:T(8,128)S(1)}, u32[]{:S(2)}, u32[]{:S(2)}) collective-permute-start(f32[256,128]{1,0:T(8,128)} %param.8), channel_id=1, source_target_pairs={{0,1},{1,0},{2,3},{3,2},{4,5},{5,4},{6,7},{7,6},{8,9},{9,8},{10,11... | collective-permute-start | bytes 393224 | tf_op jit(solution)/shard_map/ppermute | solution.py:34
  5.0 2.5 %collective-permute-done.2 = f32[256,128]{1,0:T(8,128)S(1)} collective-permute-done((f32[256,128]{1,0:T(8,128)}, f32[256,128]{1,0:T(8,128)S(1)}, u32[]{:S(2)}, u32[]{:S(2)}) %collective-permute-start.2) | collective-permute-done | bytes 131104 | tf_op jit(solution)/shard_map/ppermute | solution.py:34
  7.5 0.9 %fusion.44 = (f32[1,256,128]{2,1,0:T(8,128)S(1)}, f32[1,256,128]{2,1,0:T(8,128)S(1)}) fusion(s32[]{:T(128)S(6)} %select_n.310, f32[1,256,128]{2,1,0:T(8,128)} %bitcast.84, f32[1,256,128]{2,1,0:T(8,128)S(1)} %bitcast.89, s32[]{:T(128)S(6)} %select_n.312), kind=kLoop, calls=%fused_computation.94 | loop fusion | flops 65536 | bytes 524296 | tf_op jit(solution)/shard_map/stack | solution.py:35
  8.7 4.5 %collective-permute-done.5 = f32[256,128]{1,0:T(8,128)S(1)} collective-permute-done((f32[256,128]{1,0:T(8,128)}, f32[256,128]{1,0:T(8,128)S(1)}, u32[]{:S(2)}, u32[]{:S(2)}) %collective-permute-start.5) | collective-permute-done | bytes 131104 | tf_op jit(solution)/shard_map/ppermute | solution.py:34
  13.8 0.7 %copy-done.3 = f32[256,128]{1,0:T(8,128)S(1)} copy-done((f32[256,128]{1,0:T(8,128)S(1)}, f32[256,128]{1,0:T(8,128)}, u32[]{:S(2)}) %copy-start.3) | copy-done | bytes 131096
  14.7 1.4 %collective-permute-start.4 = (f32[128,256]{1,0:T(8,128)S(1)}, f32[128,256]{1,0:T(8,128)S(1)}, u32[]{:S(2)}, u32[]{:S(2)}) collective-permute-start(f32[128,256]{1,0:T(8,128)S(1)} %slice_select_fusion), channel_id=1, source_target_pairs={{4,0},{6,2},{12,8},{14,10},{20,16},{22,18},{28,24},{30,26},{5,1},{... | collective-permute-start | bytes 393224 | tf_op jit(solution)/shard_map/ppermute | solution.py:75
  16.1 1.8 %collective-permute-done = f32[512,128]{1,0:T(8,128)S(1)} collective-permute-done((f32[512,128]{1,0:T(8,128)}, f32[512,128]{1,0:T(8,128)S(1)}, u32[]{:S(2)}, u32[]{:S(2)}) %collective-permute-start) | collective-permute-done | bytes 262176 | tf_op jit(solution)/shard_map/ppermute | solution.py:34
  18.1 3.8 %collective-permute-done.4 = f32[128,256]{1,0:T(8,128)S(1)} collective-permute-done((f32[128,256]{1,0:T(8,128)S(1)}, f32[128,256]{1,0:T(8,128)S(1)}, u32[]{:S(2)}, u32[]{:S(2)}) %collective-permute-start.4) | collective-permute-done | bytes 131104 | tf_op jit(solution)/shard_map/ppermute | solution.py:75
  21.9 0.6 fusion.3
  22.5 0.5 fusion.26
  23.0 0.6 convolution_subtract_fusion
  23.9 1.3 %collective-permute-start.11 = (f32[128,256]{1,0:T(8,128)S(1)}, f32[128,256]{1,0:T(8,128)S(1)}, u32[]{:S(2)}, u32[]{:S(2)}) collective-permute-start(f32[128,256]{1,0:T(8,128)S(1)} %slice_select_fusion), channel_id=1, source_target_pairs={{16,0},{18,2},{17,1},{19,3}} | collective-permute-start | bytes 393224 | tf_op jit(solution)/shard_map/ppermute | solution.py:75
  25.2 1.3 %collective-permute-start.10 = (f32[128,256]{1,0:T(8,128)S(1)}, f32[128,256]{1,0:T(8,128)S(1)}, u32[]{:S(2)}, u32[]{:S(2)}) collective-permute-start(f32[128,256]{1,0:T(8,128)S(1)} %slice_select_fusion), channel_id=1, source_target_pairs={{8,0},{10,2},{24,16},{26,18},{9,1},{11,3},{25,17},{27,19}} | collective-permute-start | bytes 393224 | tf_op jit(solution)/shard_map/ppermute | solution.py:75
  26.5 0.5 collective-permute-start.8
  26.9 1.3 %broadcast_select_fusion = (f32[3,256,256]{2,1,0:T(8,128)S(1)}, f32[3,256,256]{2,1,0:T(8,128)S(1)}) fusion(f32[3,256,256]{2,1,0:T(8,128)} %collective-permute-done.6, pred[]{:T(512)S(6)} %eq.55, f32[1,256,256]{2,1,0:T(8,128)S(1)} %convolution_bitcast_fusion, f32[1,256,256]{2,1,0:T(8,128)S(1)} %get-tuple-element.48, f32[1,256,256]{2,1,0:T(8,128)S(1)} %get-tuple-element.47, ...), kind=kLoop, calls=%fused_computation.24 | loop fusion | flops 786432 | bytes 3145730 | tf_op jit(solution)/shard_map/jit(_where)/select_n | solution.py:64
  28.2 0.4 fusion.19
  28.7 0.4 select_subtract_fusion.1
  29.1 0.4 broadcast_select_fusion.4
  30.2 2.4 %collective-permute-done.11 = f32[128,256]{1,0:T(8,128)S(1)} collective-permute-done((f32[128,256]{1,0:T(8,128)S(1)}, f32[128,256]{1,0:T(8,128)S(1)}, u32[]{:S(2)}, u32[]{:S(2)}) %collective-permute-start.11) | collective-permute-done | bytes 131104 | tf_op jit(solution)/shard_map/ppermute | solution.py:75
  32.6 2.7 %collective-permute-done.10 = f32[128,256]{1,0:T(8,128)S(1)} collective-permute-done((f32[128,256]{1,0:T(8,128)S(1)}, f32[128,256]{1,0:T(8,128)S(1)}, u32[]{:S(2)}, u32[]{:S(2)}) %collective-permute-start.10) | collective-permute-done | bytes 131104 | tf_op jit(solution)/shard_map/ppermute | solution.py:75
  35.3 2.6 %collective-permute-done.9 = f32[256,256]{1,0:T(8,128)S(1)} collective-permute-done((f32[256,256]{1,0:T(8,128)S(1)}, f32[256,256]{1,0:T(8,128)S(1)}, u32[]{:S(2)}, u32[]{:S(2)}) %collective-permute-start.9) | collective-permute-done | bytes 262176 | tf_op jit(solution)/shard_map/ppermute | solution.py:107
  37.9 0.4 convolution_add_fusion
  38.4 0.5 collective-permute-start.14
  39.3 4.6 %collective-permute-start.13 = (f32[256,256]{1,0:T(8,128)S(1)}, f32[256,256]{1,0:T(8,128)S(1)}, u32[]{:S(2)}, u32[]{:S(2)}) collective-permute-start(f32[256,256]{1,0:T(8,128)S(1)} %get-tuple-element.53), channel_id=1, source_target_pairs={{0,8},{8,0},{2,10},{10,2},{16,24},{24,16},{18,26},{26,18},{1,9},{9... | collective-permute-start | bytes 786440 | tf_op jit(solution)/shard_map/ppermute | solution.py:107
  44.8 5.6 %collective-permute-done.13 = f32[256,256]{1,0:T(8,128)S(1)} collective-permute-done((f32[256,256]{1,0:T(8,128)S(1)}, f32[256,256]{1,0:T(8,128)S(1)}, u32[]{:S(2)}, u32[]{:S(2)}) %collective-permute-start.13) | collective-permute-done | bytes 262176 | tf_op jit(solution)/shard_map/ppermute | solution.py:107
  50.4 0.4 broadcast_select_fusion.2
  50.8 5.5 %collective-permute-start.15 = (f32[256,256]{1,0:T(8,128)S(1)}, f32[256,256]{1,0:T(8,128)S(1)}, u32[]{:S(2)}, u32[]{:S(2)}) collective-permute-start(f32[256,256]{1,0:T(8,128)S(1)} %get-tuple-element.55), channel_id=1, source_target_pairs={{0,16},{16,0},{2,18},{18,2},{1,17},{17,1},{3,19},{19,3}} | collective-permute-start | bytes 786440 | tf_op jit(solution)/shard_map/ppermute | solution.py:107
  56.3 0.4 convolution_add_fusion.1
  57.6 4.7 %collective-permute-done.15 = f32[256,256]{1,0:T(8,128)S(1)} collective-permute-done((f32[256,256]{1,0:T(8,128)S(1)}, f32[256,256]{1,0:T(8,128)S(1)}, u32[]{:S(2)}, u32[]{:S(2)}) %collective-permute-start.15) | collective-permute-done | bytes 262176 | tf_op jit(solution)/shard_map/ppermute | solution.py:107
  63.4 1.5 %collective-permute-done.16 = f32[256,256]{1,0:T(8,128)S(1)} collective-permute-done((f32[256,256]{1,0:T(8,128)S(1)}, f32[256,256]{1,0:T(8,128)S(1)}, u32[]{:S(2)}, u32[]{:S(2)}) %collective-permute-start.16) | collective-permute-done | bytes 262176 | tf_op jit(solution)/shard_map/ppermute | solution.py:124
  65.0 1.1 %pad_maximum_fusion = f32[512,512]{1,0:T(8,128)} fusion(f32[256,512]{1,0:T(8,128)S(1)} %get-tuple-element.36, f32[256,256]{1,0:T(8,128)S(1)} %get-tuple-element.38, f32[256,256]{1,0:T(8,128)S(1)} %get-tuple-element.37), kind=kLoop, calls=%fused_computation.14 | loop fusion | flops 524288 | bytes 2097152 | tf_op jit(solution)/shard_map/concatenate | solution.py:126
  (50 shorter events, 5.5 us)
Async XLA Ops:
  0.0 7.5 %collective-permute-start.2 = (f32[256,128]{1,0:T(8,128)}, f32[256,128]{1,0:T(8,128)S(1)}, u32[]{:S(2)}, u32[]{:S(2)}) collective-permute-start(f32[256,128]{1,0:T(8,128)} %param.9), channel_id=1, source_target_pairs={{0,1},{1,0},{2,3},{3,2},{4,5},{5,4},{6,7},{7,6},{8,9},{9,8},{10,11... | collective-permute-start | bytes 393224 | tf_op jit(solution)/shard_map/ppermute | solution.py:34
  3.0 10.9 %collective-permute-start.1 = (f32[256,128]{1,0:T(8,128)}, f32[256,128]{1,0:T(8,128)S(1)}, u32[]{:S(2)}, u32[]{:S(2)}) collective-permute-start(f32[256,128]{1,0:T(8,128)} %param.7), channel_id=1, source_target_pairs={{0,1},{1,0},{2,3},{3,2},{4,5},{5,4},{6,7},{7,6},{8,9},{9,8},{10,11... | collective-permute-start | bytes 393224 | tf_op jit(solution)/shard_map/ppermute | solution.py:34
  3.0 10.1 %collective-permute-start.5 = (f32[256,128]{1,0:T(8,128)}, f32[256,128]{1,0:T(8,128)S(1)}, u32[]{:S(2)}, u32[]{:S(2)}) collective-permute-start(f32[256,128]{1,0:T(8,128)} %param.8), channel_id=1, source_target_pairs={{0,1},{1,0},{2,3},{3,2},{4,5},{5,4},{6,7},{7,6},{8,9},{9,8},{10,11... | collective-permute-start | bytes 393224 | tf_op jit(solution)/shard_map/ppermute | solution.py:34
  5.0 12.9 %collective-permute-start = (f32[512,128]{1,0:T(8,128)}, f32[512,128]{1,0:T(8,128)S(1)}, u32[]{:S(2)}, u32[]{:S(2)}) collective-permute-start(f32[512,128]{1,0:T(8,128)} %param.6), channel_id=1, source_target_pairs={{0,1},{1,0},{2,3},{3,2},{4,5},{5,4},{6,7},{7,6},{8,9},{9,8},{10,11... | collective-permute-start | bytes 786440 | tf_op jit(solution)/shard_map/ppermute | solution.py:34
  8.6 4.6 %copy-start.2 = (f32[256,128]{1,0:T(8,128)S(1)}, f32[256,128]{1,0:T(8,128)}, u32[]{:S(2)}) copy-start(f32[256,128]{1,0:T(8,128)} %param.8) | copy-start | bytes 393220
  8.6 6.1 %collective-permute-start.3 = (f32[128,256]{1,0:T(8,128)S(1)}, f32[128,256]{1,0:T(8,128)S(1)}, u32[]{:S(2)}, u32[]{:S(2)}) collective-permute-start(f32[128,256]{1,0:T(8,128)S(1)} %slice.73), channel_id=1, source_target_pairs={{0,2},{2,0},{4,6},{6,4},{8,10},{10,8},{12,14},{14,12},{16,18},{18,... | collective-permute-start | bytes 393224 | tf_op jit(solution)/shard_map/ppermute | solution.py:67
  13.7 0.9 %copy-start.3 = (f32[256,128]{1,0:T(8,128)S(1)}, f32[256,128]{1,0:T(8,128)}, u32[]{:S(2)}) copy-start(f32[256,128]{1,0:T(8,128)} %param.7) | copy-start | bytes 393220
  13.7 13.2 %collective-permute-start.6 = (f32[3,256,256]{2,1,0:T(8,128)S(1)}, f32[3,256,256]{2,1,0:T(8,128)}, u32[]{:S(2)}, u32[]{:S(2)}) collective-permute-start(f32[3,256,256]{2,1,0:T(8,128)S(1)} %pad_maximum_fusion.1), channel_id=1, source_target_pairs={{0,2},{2,0},{4,6},{6,4},{8,10},{10,8},{12,14},{14,12},{16,18},{18,... | collective-permute-start | bytes 2359304 | tf_op jit(solution)/shard_map/ppermute | solution.py:62
  14.7 3.3 %copy-start.1 = (f32[512,128]{1,0:T(8,128)S(1)}, f32[512,128]{1,0:T(8,128)}, u32[]{:S(2)}) copy-start(f32[512,128]{1,0:T(8,128)} %param.6) | copy-start | bytes 786436
  14.7 7.2 %collective-permute-start.4 = (f32[128,256]{1,0:T(8,128)S(1)}, f32[128,256]{1,0:T(8,128)S(1)}, u32[]{:S(2)}, u32[]{:S(2)}) collective-permute-start(f32[128,256]{1,0:T(8,128)S(1)} %slice_select_fusion), channel_id=1, source_target_pairs={{4,0},{6,2},{12,8},{14,10},{20,16},{22,18},{28,24},{30,26},{5,1},{... | collective-permute-start | bytes 393224 | tf_op jit(solution)/shard_map/ppermute | solution.py:75
  17.9 4.0 %copy-start = (f32[512,512]{1,0:T(8,128)S(1)}, f32[512,512]{1,0:T(8,128)}, u32[]{:S(2)}) copy-start(f32[512,512]{1,0:T(8,128)} %param.5) | copy-start | bytes 3145732
  23.7 4.9 %collective-permute-start.7 = (f32[256,512]{1,0:T(8,128)S(1)}, f32[256,512]{1,0:T(8,128)S(1)}, u32[]{:S(2)}, u32[]{:S(2)}) collective-permute-start(f32[256,512]{1,0:T(8,128)S(1)} %get-tuple-element.35), channel_id=1, source_target_pairs={{0,2},{2,0},{4,6},{6,4},{8,10},{10,8},{12,14},{14,12},{16,18},{18,... | collective-permute-start | bytes 1572872 | tf_op jit(solution)/shard_map/ppermute | solution.py:85
  23.9 8.7 %collective-permute-start.11 = (f32[128,256]{1,0:T(8,128)S(1)}, f32[128,256]{1,0:T(8,128)S(1)}, u32[]{:S(2)}, u32[]{:S(2)}) collective-permute-start(f32[128,256]{1,0:T(8,128)S(1)} %slice_select_fusion), channel_id=1, source_target_pairs={{16,0},{18,2},{17,1},{19,3}} | collective-permute-start | bytes 393224 | tf_op jit(solution)/shard_map/ppermute | solution.py:75
  25.2 10.1 %collective-permute-start.10 = (f32[128,256]{1,0:T(8,128)S(1)}, f32[128,256]{1,0:T(8,128)S(1)}, u32[]{:S(2)}, u32[]{:S(2)}) collective-permute-start(f32[128,256]{1,0:T(8,128)S(1)} %slice_select_fusion), channel_id=1, source_target_pairs={{8,0},{10,2},{24,16},{26,18},{9,1},{11,3},{25,17},{27,19}} | collective-permute-start | bytes 393224 | tf_op jit(solution)/shard_map/ppermute | solution.py:75
  26.5 3.1 %collective-permute-start.8 = (f32[128,256]{1,0:T(8,128)S(1)}, f32[128,256]{1,0:T(8,128)S(1)}, u32[]{:S(2)}, u32[]{:S(2)}) collective-permute-start(f32[128,256]{1,0:T(8,128)S(1)} %collective-permute-done.4), channel_id=1, source_target_pairs={{0,2},{2,0},{4,6},{6,4},{8,10},{10,8},{12,14},{14,12},{16,18},{18,... | collective-permute-start | bytes 393224 | tf_op jit(solution)/shard_map/ppermute | solution.py:112
  29.5 8.4 %collective-permute-start.9 = (f32[256,256]{1,0:T(8,128)S(1)}, f32[256,256]{1,0:T(8,128)S(1)}, u32[]{:S(2)}, u32[]{:S(2)}) collective-permute-start(f32[256,256]{1,0:T(8,128)S(1)} %get-tuple-element.51), channel_id=1, source_target_pairs={{0,4},{4,0},{2,6},{6,2},{8,12},{12,8},{10,14},{14,10},{16,20},{20,... | collective-permute-start | bytes 786440 | tf_op jit(solution)/shard_map/ppermute | solution.py:107
  38.3 5.8 %collective-permute-start.12 = (f32[128,256]{1,0:T(8,128)S(1)}, f32[128,256]{1,0:T(8,128)S(1)}, u32[]{:S(2)}, u32[]{:S(2)}) collective-permute-start(f32[128,256]{1,0:T(8,128)S(1)} %collective-permute-done.10), channel_id=1, source_target_pairs={{0,2},{2,0},{4,6},{6,4},{8,10},{10,8},{12,14},{14,12},{16,18},{18,... | collective-permute-start | bytes 393224 | tf_op jit(solution)/shard_map/ppermute | solution.py:112
  38.4 18.3 %collective-permute-start.14 = (f32[128,256]{1,0:T(8,128)S(1)}, f32[128,256]{1,0:T(8,128)S(1)}, u32[]{:S(2)}, u32[]{:S(2)}) collective-permute-start(f32[128,256]{1,0:T(8,128)S(1)} %collective-permute-done.11), channel_id=1, source_target_pairs={{0,2},{2,0},{4,6},{6,4},{8,10},{10,8},{12,14},{14,12},{16,18},{18,... | collective-permute-start | bytes 393224 | tf_op jit(solution)/shard_map/ppermute | solution.py:112
  39.3 11.1 %collective-permute-start.13 = (f32[256,256]{1,0:T(8,128)S(1)}, f32[256,256]{1,0:T(8,128)S(1)}, u32[]{:S(2)}, u32[]{:S(2)}) collective-permute-start(f32[256,256]{1,0:T(8,128)S(1)} %get-tuple-element.53), channel_id=1, source_target_pairs={{0,8},{8,0},{2,10},{10,2},{16,24},{24,16},{18,26},{26,18},{1,9},{9... | collective-permute-start | bytes 786440 | tf_op jit(solution)/shard_map/ppermute | solution.py:107
  50.8 11.5 %collective-permute-start.15 = (f32[256,256]{1,0:T(8,128)S(1)}, f32[256,256]{1,0:T(8,128)S(1)}, u32[]{:S(2)}, u32[]{:S(2)}) collective-permute-start(f32[256,256]{1,0:T(8,128)S(1)} %get-tuple-element.55), channel_id=1, source_target_pairs={{0,16},{16,0},{2,18},{18,2},{1,17},{17,1},{3,19},{19,3}} | collective-permute-start | bytes 786440 | tf_op jit(solution)/shard_map/ppermute | solution.py:107
  63.3 1.6 %collective-permute-start.16 = (f32[256,256]{1,0:T(8,128)S(1)}, f32[256,256]{1,0:T(8,128)S(1)}, u32[]{:S(2)}, u32[]{:S(2)}) collective-permute-start(f32[256,256]{1,0:T(8,128)S(1)} %get-tuple-element.57), channel_id=1, source_target_pairs={{0,2},{2,0},{4,6},{6,4},{8,10},{10,8},{12,14},{14,12},{16,18},{18,... | collective-permute-start | bytes 786440 | tf_op jit(solution)/shard_map/ppermute | solution.py:124

commit v16 on v15

--- a/solution.py
+++ b/solution.py
@@ -106,10 +106,14 @@
         q = product_left_t(jnp.where(is_upper, even3[2], zeros), chain)
         received = lax.ppermute(jnp.where(is_upper, q, chain), "row", pairs)
         if level == 1:
+            mates_of = [lax.ppermute(partner_factors[0], "row", swap)]
             received, rest = lax.optimization_barrier((received, partner_factors[1:]))
             partner_factors[1:] = rest
+            if rest:
+                swapped_rest = lax.ppermute(jnp.stack(rest), "row", swap)
+                mates_of += [swapped_rest[k] for k in range(len(rest))]
         mine = partner_factors[level - 1]
-        mates = lax.ppermute(mine, "row", swap)
+        mates = mates_of[level - 1]
         top_rows = jnp.where(is_lower & (core == 0), mine, jnp.where(is_lower, mates, 0.0))
         bottom_rows = jnp.where(is_lower & (core == 0), mates, jnp.where(is_lower, mine, 0.0))
         own_part = product_left_t(top_rows, chain[:hw]) + product_left_t(bottom_rows, chain[hw:])

time: 66.3 us -> 67 us (1.011)
  waiting for transfers between devices: 32 us -> 33.1 us
    ppermute x3, waiting for transfers between devices: 12.8 us -> 14 us  [on_device(): received = lax.ppermute(jnp.where(is_upper, q, chain), 'row', pairs)]
  transfers between devices with their start and end apart: 17 -> 16, of which waited for: 10 -> 10; matrix products, arithmetic and copies ran while one was open for 15% -> 13% of each run, Pallas kernels for 0% -> 0%
where the time goes in v16:
time: 67 us; the launch traced here: 66.7 us
  waiting for transfers between devices  33.1 us (49%)
  starting transfers between devices  20 us (30%)
  matrix products  8.24 us (12%)
  other arithmetic  4.03 us (6%)
  local copies, waits for them, and re-layouts  0.85 us (1%)
    ppermute x3, waiting for transfers between devices, on_device(): received = lax.ppermute(jnp.where(is_upper, q, chain), 'row', pairs)  14 us
    ppermute x3, starting transfers between devices, on_device(): received = lax.ppermute(jnp.where(is_upper, q, chain), 'row', pairs)  10.1 us
    ppermute x3, waiting for transfers between devices, on_device(): partner_factors.append(lax.ppermute(half_s, 'row', pairs))  8.92 us
    ppermute x4, waiting for transfers between devices, col_gather(): by_shift.append(lax.ppermute(part, 'col', perm))  8.68 us
    dot_general x16, matrix products, product_left_t(): lax.dot_general(left, right, (((0,), (0,)), ((), ())), precision=lax.Prec...  6.16 us
    ppermute x4, starting transfers between devices, col_gather(): by_shift.append(lax.ppermute(part, 'col', perm))  5.04 us
    ppermute x3, starting transfers between devices, on_device(): partner_factors.append(lax.ppermute(half_s, 'row', pairs))  4.01 us
    dot_general x6, matrix products, product(): jnp.dot(left, right, precision=lax.Precision.HIGH, preferred_element_type...  2.08 us
  transfers between devices with their start and end apart: 16, of which 10 were waited for; matrix products, arithmetic and copies ran while one was open for 13% of the time, Pallas kernels for 0%

profile of v16, /device:TPU:0, one launch (start us, length us, event | category | flops | bytes accessed | tf_op | source)
XLA Modules:
  0.0 66.7 jit_solution(11174429578792843606)
XLA Ops:
  0.0 3.0 %collective-permute-start.2 = (f32[256,128]{1,0:T(8,128)}, f32[256,128]{1,0:T(8,128)S(1)}, u32[]{:S(2)}, u32[]{:S(2)}) collective-permute-start(f32[256,128]{1,0:T(8,128)} %param.9), channel_id=1, source_target_pairs={{0,1},{1,0},{2,3},{3,2},{4,5},{5,4},{6,7},{7,6},{8,9},{9,8},{10,11... | collective-permute-start | bytes 393224 | tf_op jit(solution)/shard_map/ppermute | solution.py:34
  3.0 2.0 %collective-permute-start.5 = (f32[256,128]{1,0:T(8,128)}, f32[256,128]{1,0:T(8,128)S(1)}, u32[]{:S(2)}, u32[]{:S(2)}) collective-permute-start(f32[256,128]{1,0:T(8,128)} %param.8), channel_id=1, source_target_pairs={{0,1},{1,0},{2,3},{3,2},{4,5},{5,4},{6,7},{7,6},{8,9},{9,8},{10,11... | collective-permute-start | bytes 393224 | tf_op jit(solution)/shard_map/ppermute | solution.py:34
  5.0 2.5 %collective-permute-done.2 = f32[256,128]{1,0:T(8,128)S(1)} collective-permute-done((f32[256,128]{1,0:T(8,128)}, f32[256,128]{1,0:T(8,128)S(1)}, u32[]{:S(2)}, u32[]{:S(2)}) %collective-permute-start.2) | collective-permute-done | bytes 131104 | tf_op jit(solution)/shard_map/ppermute | solution.py:34
  7.5 0.9 %fusion.44 = (f32[1,256,128]{2,1,0:T(8,128)S(1)}, f32[1,256,128]{2,1,0:T(8,128)S(1)}) fusion(s32[]{:T(128)S(6)} %select_n.310, f32[1,256,128]{2,1,0:T(8,128)} %bitcast.104, f32[1,256,128]{2,1,0:T(8,128)S(1)} %bitcast.109, s32[]{:T(128)S(6)} %select_n.312), kind=kLoop, calls=%fused_computation.95 | loop fusion | flops 65536 | bytes 524296 | tf_op jit(solution)/shard_map/stack | solution.py:35
  8.7 4.5 %collective-permute-done.5 = f32[256,128]{1,0:T(8,128)S(1)} collective-permute-done((f32[256,128]{1,0:T(8,128)}, f32[256,128]{1,0:T(8,128)S(1)}, u32[]{:S(2)}, u32[]{:S(2)}) %collective-permute-start.5) | collective-permute-done | bytes 131104 | tf_op jit(solution)/shard_map/ppermute | solution.py:34
  13.8 0.7 %copy-done.3 = f32[256,128]{1,0:T(8,128)S(1)} copy-done((f32[256,128]{1,0:T(8,128)S(1)}, f32[256,128]{1,0:T(8,128)}, u32[]{:S(2)}) %copy-start.3) | copy-done | bytes 131096
  14.7 1.4 %collective-permute-start.4 = (f32[128,256]{1,0:T(8,128)S(1)}, f32[128,256]{1,0:T(8,128)S(1)}, u32[]{:S(2)}, u32[]{:S(2)}) collective-permute-start(f32[128,256]{1,0:T(8,128)S(1)} %slice_select_fusion), channel_id=1, source_target_pairs={{4,0},{6,2},{12,8},{14,10},{20,16},{22,18},{28,24},{30,26},{5,1},{... | collective-permute-start | bytes 393224 | tf_op jit(solution)/shard_map/ppermute | solution.py:75
  16.1 1.8 %collective-permute-done = f32[512,128]{1,0:T(8,128)S(1)} collective-permute-done((f32[512,128]{1,0:T(8,128)}, f32[512,128]{1,0:T(8,128)S(1)}, u32[]{:S(2)}, u32[]{:S(2)}) %collective-permute-start) | collective-permute-done | bytes 262176 | tf_op jit(solution)/shard_map/ppermute | solution.py:34
  18.1 3.8 %collective-permute-done.4 = f32[128,256]{1,0:T(8,128)S(1)} collective-permute-done((f32[128,256]{1,0:T(8,128)S(1)}, f32[128,256]{1,0:T(8,128)S(1)}, u32[]{:S(2)}, u32[]{:S(2)}) %collective-permute-start.4) | collective-permute-done | bytes 131104 | tf_op jit(solution)/shard_map/ppermute | solution.py:75
  21.9 0.6 fusion.3
  22.5 0.5 fusion.26
  23.0 0.6 convolution_subtract_fusion
  23.9 1.3 %collective-permute-start.11 = (f32[128,256]{1,0:T(8,128)S(1)}, f32[128,256]{1,0:T(8,128)S(1)}, u32[]{:S(2)}, u32[]{:S(2)}) collective-permute-start(f32[128,256]{1,0:T(8,128)S(1)} %slice_select_fusion), channel_id=1, source_target_pairs={{16,0},{18,2},{17,1},{19,3}} | collective-permute-start | bytes 393224 | tf_op jit(solution)/shard_map/ppermute | solution.py:75
  25.2 1.3 %collective-permute-start.10 = (f32[128,256]{1,0:T(8,128)S(1)}, f32[128,256]{1,0:T(8,128)S(1)}, u32[]{:S(2)}, u32[]{:S(2)}) collective-permute-start(f32[128,256]{1,0:T(8,128)S(1)} %slice_select_fusion), channel_id=1, source_target_pairs={{8,0},{10,2},{24,16},{26,18},{9,1},{11,3},{25,17},{27,19}} | collective-permute-start | bytes 393224 | tf_op jit(solution)/shard_map/ppermute | solution.py:75
  26.5 0.5 collective-permute-start.8
  26.9 1.3 %broadcast_select_fusion = (f32[3,256,256]{2,1,0:T(8,128)S(1)}, f32[3,256,256]{2,1,0:T(8,128)S(1)}) fusion(f32[3,256,256]{2,1,0:T(8,128)} %collective-permute-done.6, pred[]{:T(512)S(6)} %eq.55, f32[1,256,256]{2,1,0:T(8,128)S(1)} %convolution_bitcast_fusion, f32[1,256,256]{2,1,0:T(8,128)S(1)} %get-tuple-element.48, f32[1,256,256]{2,1,0:T(8,128)S(1)} %get-tuple-element.47, ...), kind=kLoop, calls=%fused_computation.24 | loop fusion | flops 786432 | bytes 3145730 | tf_op jit(solution)/shard_map/jit(_where)/select_n | solution.py:64
  28.2 0.4 fusion.19
  28.7 0.4 select_subtract_fusion.1
  29.1 0.4 broadcast_select_fusion.4
  30.2 2.4 %collective-permute-done.11 = f32[128,256]{1,0:T(8,128)S(1)} collective-permute-done((f32[128,256]{1,0:T(8,128)S(1)}, f32[128,256]{1,0:T(8,128)S(1)}, u32[]{:S(2)}, u32[]{:S(2)}) %collective-permute-start.11) | collective-permute-done | bytes 131104 | tf_op jit(solution)/shard_map/ppermute | solution.py:75
  32.6 2.7 %collective-permute-done.10 = f32[128,256]{1,0:T(8,128)S(1)} collective-permute-done((f32[128,256]{1,0:T(8,128)S(1)}, f32[128,256]{1,0:T(8,128)S(1)}, u32[]{:S(2)}, u32[]{:S(2)}) %collective-permute-start.10) | collective-permute-done | bytes 131104 | tf_op jit(solution)/shard_map/ppermute | solution.py:75
  35.3 2.6 %collective-permute-done.9 = f32[256,256]{1,0:T(8,128)S(1)} collective-permute-done((f32[256,256]{1,0:T(8,128)S(1)}, f32[256,256]{1,0:T(8,128)S(1)}, u32[]{:S(2)}, u32[]{:S(2)}) %collective-permute-start.9) | collective-permute-done | bytes 262176 | tf_op jit(solution)/shard_map/ppermute | solution.py:107
  37.9 0.4 convolution_add_fusion
  38.4 0.4 broadcast_select_fusion.3
  38.8 4.6 %collective-permute-start.13 = (f32[256,256]{1,0:T(8,128)S(1)}, f32[256,256]{1,0:T(8,128)S(1)}, u32[]{:S(2)}, u32[]{:S(2)}) collective-permute-start(f32[256,256]{1,0:T(8,128)S(1)} %get-tuple-element.53), channel_id=1, source_target_pairs={{0,8},{8,0},{2,10},{10,2},{16,24},{24,16},{18,26},{26,18},{1,9},{9... | collective-permute-start | bytes 786440 | tf_op jit(solution)/shard_map/ppermute | solution.py:107
  44.3 6.0 %collective-permute-done.13 = f32[256,256]{1,0:T(8,128)S(1)} collective-permute-done((f32[256,256]{1,0:T(8,128)S(1)}, f32[256,256]{1,0:T(8,128)S(1)}, u32[]{:S(2)}, u32[]{:S(2)}) %collective-permute-start.13) | collective-permute-done | bytes 262176 | tf_op jit(solution)/shard_map/ppermute | solution.py:107
  50.4 0.4 convolution_add_fusion.1
  50.8 0.4 broadcast_select_fusion.2
  51.2 5.5 %collective-permute-start.14 = (f32[256,256]{1,0:T(8,128)S(1)}, f32[256,256]{1,0:T(8,128)S(1)}, u32[]{:S(2)}, u32[]{:S(2)}) collective-permute-start(f32[256,256]{1,0:T(8,128)S(1)} %get-tuple-element.55), channel_id=1, source_target_pairs={{0,16},{16,0},{2,18},{18,2},{1,17},{17,1},{3,19},{19,3}} | collective-permute-start | bytes 786440 | tf_op jit(solution)/shard_map/ppermute | solution.py:107
  57.6 5.4 %collective-permute-done.14 = f32[256,256]{1,0:T(8,128)S(1)} collective-permute-done((f32[256,256]{1,0:T(8,128)S(1)}, f32[256,256]{1,0:T(8,128)S(1)}, u32[]{:S(2)}, u32[]{:S(2)}) %collective-permute-start.14) | collective-permute-done | bytes 262176 | tf_op jit(solution)/shard_map/ppermute | solution.py:107
  64.1 1.5 %collective-permute-done.15 = f32[256,256]{1,0:T(8,128)S(1)} collective-permute-done((f32[256,256]{1,0:T(8,128)S(1)}, f32[256,256]{1,0:T(8,128)S(1)}, u32[]{:S(2)}, u32[]{:S(2)}) %collective-permute-start.15) | collective-permute-done | bytes 262176 | tf_op jit(solution)/shard_map/ppermute | solution.py:128
  65.7 1.1 %pad_maximum_fusion = f32[512,512]{1,0:T(8,128)} fusion(f32[256,512]{1,0:T(8,128)S(1)} %get-tuple-element.36, f32[256,256]{1,0:T(8,128)S(1)} %get-tuple-element.38, f32[256,256]{1,0:T(8,128)S(1)} %get-tuple-element.37), kind=kLoop, calls=%fused_computation.14 | loop fusion | flops 524288 | bytes 2097152 | tf_op jit(solution)/shard_map/concatenate | solution.py:130
  (49 shorter events, 5.1 us)
Async XLA Ops:
  0.0 7.5 %collective-permute-start.2 = (f32[256,128]{1,0:T(8,128)}, f32[256,128]{1,0:T(8,128)S(1)}, u32[]{:S(2)}, u32[]{:S(2)}) collective-permute-start(f32[256,128]{1,0:T(8,128)} %param.9), channel_id=1, source_target_pairs={{0,1},{1,0},{2,3},{3,2},{4,5},{5,4},{6,7},{7,6},{8,9},{9,8},{10,11... | collective-permute-start | bytes 393224 | tf_op jit(solution)/shard_map/ppermute | solution.py:34
  3.0 10.9 %collective-permute-start.1 = (f32[256,128]{1,0:T(8,128)}, f32[256,128]{1,0:T(8,128)S(1)}, u32[]{:S(2)}, u32[]{:S(2)}) collective-permute-start(f32[256,128]{1,0:T(8,128)} %param.7), channel_id=1, source_target_pairs={{0,1},{1,0},{2,3},{3,2},{4,5},{5,4},{6,7},{7,6},{8,9},{9,8},{10,11... | collective-permute-start | bytes 393224 | tf_op jit(solution)/shard_map/ppermute | solution.py:34
  3.0 10.1 %collective-permute-start.5 = (f32[256,128]{1,0:T(8,128)}, f32[256,128]{1,0:T(8,128)S(1)}, u32[]{:S(2)}, u32[]{:S(2)}) collective-permute-start(f32[256,128]{1,0:T(8,128)} %param.8), channel_id=1, source_target_pairs={{0,1},{1,0},{2,3},{3,2},{4,5},{5,4},{6,7},{7,6},{8,9},{9,8},{10,11... | collective-permute-start | bytes 393224 | tf_op jit(solution)/shard_map/ppermute | solution.py:34
  5.0 12.9 %collective-permute-start = (f32[512,128]{1,0:T(8,128)}, f32[512,128]{1,0:T(8,128)S(1)}, u32[]{:S(2)}, u32[]{:S(2)}) collective-permute-start(f32[512,128]{1,0:T(8,128)} %param.6), channel_id=1, source_target_pairs={{0,1},{1,0},{2,3},{3,2},{4,5},{5,4},{6,7},{7,6},{8,9},{9,8},{10,11... | collective-permute-start | bytes 786440 | tf_op jit(solution)/shard_map/ppermute | solution.py:34
  8.6 4.6 %copy-start.2 = (f32[256,128]{1,0:T(8,128)S(1)}, f32[256,128]{1,0:T(8,128)}, u32[]{:S(2)}) copy-start(f32[256,128]{1,0:T(8,128)} %param.8) | copy-start | bytes 393220
  8.6 6.1 %collective-permute-start.3 = (f32[128,256]{1,0:T(8,128)S(1)}, f32[128,256]{1,0:T(8,128)S(1)}, u32[]{:S(2)}, u32[]{:S(2)}) collective-permute-start(f32[128,256]{1,0:T(8,128)S(1)} %slice.81), channel_id=1, source_target_pairs={{0,2},{2,0},{4,6},{6,4},{8,10},{10,8},{12,14},{14,12},{16,18},{18,... | collective-permute-start | bytes 393224 | tf_op jit(solution)/shard_map/ppermute | solution.py:67
  13.7 0.9 %copy-start.3 = (f32[256,128]{1,0:T(8,128)S(1)}, f32[256,128]{1,0:T(8,128)}, u32[]{:S(2)}) copy-start(f32[256,128]{1,0:T(8,128)} %param.7) | copy-start | bytes 393220
  13.7 13.2 %collective-permute-start.6 = (f32[3,256,256]{2,1,0:T(8,128)S(1)}, f32[3,256,256]{2,1,0:T(8,128)}, u32[]{:S(2)}, u32[]{:S(2)}) collective-permute-start(f32[3,256,256]{2,1,0:T(8,128)S(1)} %pad_maximum_fusion.1), channel_id=1, source_target_pairs={{0,2},{2,0},{4,6},{6,4},{8,10},{10,8},{12,14},{14,12},{16,18},{18,... | collective-permute-start | bytes 2359304 | tf_op jit(solution)/shard_map/ppermute | solution.py:62
  14.7 3.3 %copy-start.1 = (f32[512,128]{1,0:T(8,128)S(1)}, f32[512,128]{1,0:T(8,128)}, u32[]{:S(2)}) copy-start(f32[512,128]{1,0:T(8,128)} %param.6) | copy-start | bytes 786436
  14.7 7.2 %collective-permute-start.4 = (f32[128,256]{1,0:T(8,128)S(1)}, f32[128,256]{1,0:T(8,128)S(1)}, u32[]{:S(2)}, u32[]{:S(2)}) collective-permute-start(f32[128,256]{1,0:T(8,128)S(1)} %slice_select_fusion), channel_id=1, source_target_pairs={{4,0},{6,2},{12,8},{14,10},{20,16},{22,18},{28,24},{30,26},{5,1},{... | collective-permute-start | bytes 393224 | tf_op jit(solution)/shard_map/ppermute | solution.py:75
  17.9 4.0 %copy-start = (f32[512,512]{1,0:T(8,128)S(1)}, f32[512,512]{1,0:T(8,128)}, u32[]{:S(2)}) copy-start(f32[512,512]{1,0:T(8,128)} %param.5) | copy-start | bytes 3145732
  23.7 4.9 %collective-permute-start.7 = (f32[256,512]{1,0:T(8,128)S(1)}, f32[256,512]{1,0:T(8,128)S(1)}, u32[]{:S(2)}, u32[]{:S(2)}) collective-permute-start(f32[256,512]{1,0:T(8,128)S(1)} %get-tuple-element.35), channel_id=1, source_target_pairs={{0,2},{2,0},{4,6},{6,4},{8,10},{10,8},{12,14},{14,12},{16,18},{18,... | collective-permute-start | bytes 1572872 | tf_op jit(solution)/shard_map/ppermute | solution.py:85
  23.9 8.7 %collective-permute-start.11 = (f32[128,256]{1,0:T(8,128)S(1)}, f32[128,256]{1,0:T(8,128)S(1)}, u32[]{:S(2)}, u32[]{:S(2)}) collective-permute-start(f32[128,256]{1,0:T(8,128)S(1)} %slice_select_fusion), channel_id=1, source_target_pairs={{16,0},{18,2},{17,1},{19,3}} | collective-permute-start | bytes 393224 | tf_op jit(solution)/shard_map/ppermute | solution.py:75
  25.2 10.1 %collective-permute-start.10 = (f32[128,256]{1,0:T(8,128)S(1)}, f32[128,256]{1,0:T(8,128)S(1)}, u32[]{:S(2)}, u32[]{:S(2)}) collective-permute-start(f32[128,256]{1,0:T(8,128)S(1)} %slice_select_fusion), channel_id=1, source_target_pairs={{8,0},{10,2},{24,16},{26,18},{9,1},{11,3},{25,17},{27,19}} | collective-permute-start | bytes 393224 | tf_op jit(solution)/shard_map/ppermute | solution.py:75
  26.5 3.1 %collective-permute-start.8 = (f32[128,256]{1,0:T(8,128)S(1)}, f32[128,256]{1,0:T(8,128)S(1)}, u32[]{:S(2)}, u32[]{:S(2)}) collective-permute-start(f32[128,256]{1,0:T(8,128)S(1)} %collective-permute-done.4), channel_id=1, source_target_pairs={{0,2},{2,0},{4,6},{6,4},{8,10},{10,8},{12,14},{14,12},{16,18},{18,... | collective-permute-start | bytes 393224 | tf_op jit(solution)/shard_map/ppermute | solution.py:109
  29.5 8.4 %collective-permute-start.9 = (f32[256,256]{1,0:T(8,128)S(1)}, f32[256,256]{1,0:T(8,128)S(1)}, u32[]{:S(2)}, u32[]{:S(2)}) collective-permute-start(f32[256,256]{1,0:T(8,128)S(1)} %get-tuple-element.51), channel_id=1, source_target_pairs={{0,4},{4,0},{2,6},{6,2},{8,12},{12,8},{10,14},{14,10},{16,20},{20,... | collective-permute-start | bytes 786440 | tf_op jit(solution)/shard_map/ppermute | solution.py:107
  38.3 5.3 %collective-permute-start.12 = (f32[2,128,256]{2,1,0:T(8,128)S(1)}, f32[2,128,256]{2,1,0:T(8,128)S(1)}, u32[]{:S(2)}, u32[]{:S(2)}) collective-permute-start(f32[2,128,256]{2,1,0:T(8,128)S(1)} %pad_maximum_fusion.4), channel_id=1, source_target_pairs={{0,2},{2,0},{4,6},{6,4},{8,10},{10,8},{12,14},{14,12},{16,18},{18,... | collective-permute-start | bytes 786440 | tf_op jit(solution)/shard_map/ppermute | solution.py:113
  38.8 11.5 %collective-permute-start.13 = (f32[256,256]{1,0:T(8,128)S(1)}, f32[256,256]{1,0:T(8,128)S(1)}, u32[]{:S(2)}, u32[]{:S(2)}) collective-permute-start(f32[256,256]{1,0:T(8,128)S(1)} %get-tuple-element.53), channel_id=1, source_target_pairs={{0,8},{8,0},{2,10},{10,2},{16,24},{24,16},{18,26},{26,18},{1,9},{9... | collective-permute-start | bytes 786440 | tf_op jit(solution)/shard_map/ppermute | solution.py:107
  51.2 11.8 %collective-permute-start.14 = (f32[256,256]{1,0:T(8,128)S(1)}, f32[256,256]{1,0:T(8,128)S(1)}, u32[]{:S(2)}, u32[]{:S(2)}) collective-permute-start(f32[256,256]{1,0:T(8,128)S(1)} %get-tuple-element.55), channel_id=1, source_target_pairs={{0,16},{16,0},{2,18},{18,2},{1,17},{17,1},{3,19},{19,3}} | collective-permute-start | bytes 786440 | tf_op jit(solution)/shard_map/ppermute | solution.py:107
  64.0 1.6 %collective-permute-start.15 = (f32[256,256]{1,0:T(8,128)S(1)}, f32[256,256]{1,0:T(8,128)S(1)}, u32[]{:S(2)}, u32[]{:S(2)}) collective-permute-start(f32[256,256]{1,0:T(8,128)S(1)} %get-tuple-element.57), channel_id=1, source_target_pairs={{0,2},{2,0},{4,6},{6,4},{8,10},{10,8},{12,14},{14,12},{16,18},{18,... | collective-permute-start | bytes 786440 | tf_op jit(solution)/shard_map/ppermute | solution.py:128

commit v17 on v15

--- a/solution.py
+++ b/solution.py
@@ -74,7 +74,7 @@
             pairs += [(i + step, i), (i + step + 1, i + 1)]
         partner_factors.append(lax.ppermute(half_s, "row", pairs))
 
-    leaf_full, leaf_tri, partner_factors[0] = lax.optimization_barrier((leaf_full, leaf_tri, partner_factors[0]))
+    leaf_full, leaf_tri, partner_factors = lax.optimization_barrier((leaf_full, leaf_tri, partner_factors))
     leaf_vectors = unit_lower(leaf_full)
     leaf_factor = jnp.triu(leaf_tri)
     leaf_w = product_left_t(leaf_factor, product_left_t(leaf_vectors, slab))
@@ -105,9 +105,6 @@
                 pairs += [(i + c, i + step + c), (i + step + c, i + c)]
         q = product_left_t(jnp.where(is_upper, even3[2], zeros), chain)
         received = lax.ppermute(jnp.where(is_upper, q, chain), "row", pairs)
-        if level == 1:
-            received, rest = lax.optimization_barrier((received, partner_factors[1:]))
-            partner_factors[1:] = rest
         mine = partner_factors[level - 1]
         mates = lax.ppermute(mine, "row", swap)
         top_rows = jnp.where(is_lower & (core == 0), mine, jnp.where(is_lower, mates, 0.0))

time: 66.3 us -> 64.1 us (0.967)
  starting transfers between devices: 20.5 us -> 18.7 us
    ppermute x3, waiting for transfers between devices: 12.8 us -> 16.4 us  [on_device(): received = lax.ppermute(jnp.where(is_upper, q, chain), 'row', pairs)]
    ppermute x3, waiting for transfers between devices: 8.92 us -> 6.65 us  [on_device(): partner_factors.append(lax.ppermute(half_s, 'row', pairs))]
    ppermute x4, waiting for transfers between devices: 8.68 us -> 6.92 us  [col_gather(): by_shift.append(lax.ppermute(part, 'col', perm))]
    ppermute x3, starting transfers between devices: 10.1 us -> 8.4 us  [on_device(): received = lax.ppermute(jnp.where(is_upper, q, chain), 'row', pairs)]
  transfers between devices with their start and end apart: 17 -> 17, of which waited for: 10 -> 8; matrix products, arithmetic and copies ran while one was open for 15% -> 16% of each run, Pallas kernels for 0% -> 0%
where the time goes in v17:
time: 64.1 us; the launch traced here: 63.8 us
  waiting for transfers between devices  31.5 us (49%)
  starting transfers between devices  18.7 us (29%)
  matrix products  8.25 us (13%)
  other arithmetic  4.02 us (6%)
  local copies, waits for them, and re-layouts  0.85 us (1%)
    ppermute x3, waiting for transfers between devices, on_device(): received = lax.ppermute(jnp.where(is_upper, q, chain), 'row', pairs)  16.4 us
    ppermute x3, starting transfers between devices, on_device(): received = lax.ppermute(jnp.where(is_upper, q, chain), 'row', pairs)  8.4 us
    ppermute x4, waiting for transfers between devices, col_gather(): by_shift.append(lax.ppermute(part, 'col', perm))  6.92 us
    ppermute x3, waiting for transfers between devices, on_device(): partner_factors.append(lax.ppermute(half_s, 'row', pairs))  6.65 us
    dot_general x16, matrix products, product_left_t(): lax.dot_general(left, right, (((0,), (0,)), ((), ())), precision=lax.Prec...  6.17 us
    ppermute x4, starting transfers between devices, col_gather(): by_shift.append(lax.ppermute(part, 'col', perm))  5.04 us
    ppermute x3, starting transfers between devices, on_device(): partner_factors.append(lax.ppermute(half_s, 'row', pairs))  4.01 us
    dot_general x6, matrix products, product(): jnp.dot(left, right, precision=lax.Precision.HIGH, preferred_element_type...  2.08 us
  transfers between devices with their start and end apart: 17, of which 8 were waited for; matrix products, arithmetic and copies ran while one was open for 16% of the time, Pallas kernels for 0%

profile of v17, /device:TPU:0, one launch (start us, length us, event | category | flops | bytes accessed | tf_op | source)
XLA Modules:
  0.0 63.8 jit_solution(5797398352314236749)
XLA Ops:
  0.0 3.0 %collective-permute-start.2 = (f32[256,128]{1,0:T(8,128)}, f32[256,128]{1,0:T(8,128)S(1)}, u32[]{:S(2)}, u32[]{:S(2)}) collective-permute-start(f32[256,128]{1,0:T(8,128)} %param.9), channel_id=1, source_target_pairs={{0,1},{1,0},{2,3},{3,2},{4,5},{5,4},{6,7},{7,6},{8,9},{9,8},{10,11... | collective-permute-start | bytes 393224 | tf_op jit(solution)/shard_map/ppermute | solution.py:34
  3.0 2.0 %collective-permute-start.7 = (f32[256,128]{1,0:T(8,128)}, f32[256,128]{1,0:T(8,128)S(1)}, u32[]{:S(2)}, u32[]{:S(2)}) collective-permute-start(f32[256,128]{1,0:T(8,128)} %param.8), channel_id=1, source_target_pairs={{0,1},{1,0},{2,3},{3,2},{4,5},{5,4},{6,7},{7,6},{8,9},{9,8},{10,11... | collective-permute-start | bytes 393224 | tf_op jit(solution)/shard_map/ppermute | solution.py:34
  5.0 2.5 %collective-permute-done.2 = f32[256,128]{1,0:T(8,128)S(1)} collective-permute-done((f32[256,128]{1,0:T(8,128)}, f32[256,128]{1,0:T(8,128)S(1)}, u32[]{:S(2)}, u32[]{:S(2)}) %collective-permute-start.2) | collective-permute-done | bytes 131104 | tf_op jit(solution)/shard_map/ppermute | solution.py:34
  7.5 0.9 %fusion.44 = (f32[1,256,128]{2,1,0:T(8,128)S(1)}, f32[1,256,128]{2,1,0:T(8,128)S(1)}) fusion(s32[]{:T(128)S(6)} %select_n.310, f32[1,256,128]{2,1,0:T(8,128)} %bitcast.84, f32[1,256,128]{2,1,0:T(8,128)S(1)} %bitcast.89, s32[]{:T(128)S(6)} %select_n.312), kind=kLoop, calls=%fused_computation.94 | loop fusion | flops 65536 | bytes 524296 | tf_op jit(solution)/shard_map/stack | solution.py:35
  8.7 4.5 %collective-permute-done.7 = f32[256,128]{1,0:T(8,128)S(1)} collective-permute-done((f32[256,128]{1,0:T(8,128)}, f32[256,128]{1,0:T(8,128)S(1)}, u32[]{:S(2)}, u32[]{:S(2)}) %collective-permute-start.7) | collective-permute-done | bytes 131104 | tf_op jit(solution)/shard_map/ppermute | solution.py:34
  13.3 0.4 convolution_bitcast_fusion
  13.8 0.7 %copy-done.3 = f32[256,128]{1,0:T(8,128)S(1)} copy-done((f32[256,128]{1,0:T(8,128)S(1)}, f32[256,128]{1,0:T(8,128)}, u32[]{:S(2)}) %copy-start.3) | copy-done | bytes 131096
  14.7 1.4 %collective-permute-start.6 = (f32[128,256]{1,0:T(8,128)S(1)}, f32[128,256]{1,0:T(8,128)S(1)}, u32[]{:S(2)}, u32[]{:S(2)}) collective-permute-start(f32[128,256]{1,0:T(8,128)S(1)} %slice_select_fusion), channel_id=1, source_target_pairs={{16,0},{18,2},{17,1},{19,3}} | collective-permute-start | bytes 393224 | tf_op jit(solution)/shard_map/ppermute | solution.py:75
  16.1 1.3 %collective-permute-start.5 = (f32[128,256]{1,0:T(8,128)S(1)}, f32[128,256]{1,0:T(8,128)S(1)}, u32[]{:S(2)}, u32[]{:S(2)}) collective-permute-start(f32[128,256]{1,0:T(8,128)S(1)} %slice_select_fusion), channel_id=1, source_target_pairs={{8,0},{10,2},{24,16},{26,18},{9,1},{11,3},{25,17},{27,19}} | collective-permute-start | bytes 393224 | tf_op jit(solution)/shard_map/ppermute | solution.py:75
  17.4 1.3 %collective-permute-start.4 = (f32[128,256]{1,0:T(8,128)S(1)}, f32[128,256]{1,0:T(8,128)S(1)}, u32[]{:S(2)}, u32[]{:S(2)}) collective-permute-start(f32[128,256]{1,0:T(8,128)S(1)} %slice_select_fusion), channel_id=1, source_target_pairs={{4,0},{6,2},{12,8},{14,10},{20,16},{22,18},{28,24},{30,26},{5,1},{... | collective-permute-start | bytes 393224 | tf_op jit(solution)/shard_map/ppermute | solution.py:75
  18.9 3.9 %collective-permute-done.6 = f32[128,256]{1,0:T(8,128)S(1)} collective-permute-done((f32[128,256]{1,0:T(8,128)S(1)}, f32[128,256]{1,0:T(8,128)S(1)}, u32[]{:S(2)}, u32[]{:S(2)}) %collective-permute-start.6) | collective-permute-done | bytes 131104 | tf_op jit(solution)/shard_map/ppermute | solution.py:75
  22.9 2.7 %collective-permute-done.5 = f32[128,256]{1,0:T(8,128)S(1)} collective-permute-done((f32[128,256]{1,0:T(8,128)S(1)}, f32[128,256]{1,0:T(8,128)S(1)}, u32[]{:S(2)}, u32[]{:S(2)}) %collective-permute-start.5) | collective-permute-done | bytes 131104 | tf_op jit(solution)/shard_map/ppermute | solution.py:75
  25.6 0.6 fusion.3
  26.2 0.5 fusion.26
  26.7 0.6 convolution_subtract_fusion
  27.6 0.4 collective-permute-start.10
  28.5 1.3 %broadcast_select_fusion = (f32[3,256,256]{2,1,0:T(8,128)S(1)}, f32[3,256,256]{2,1,0:T(8,128)S(1)}) fusion(f32[3,256,256]{2,1,0:T(8,128)} %collective-permute-done.8, pred[]{:T(512)S(6)} %eq.55, f32[1,256,256]{2,1,0:T(8,128)S(1)} %convolution_bitcast_fusion, f32[1,256,256]{2,1,0:T(8,128)S(1)} %get-tuple-element.46, f32[1,256,256]{2,1,0:T(8,128)S(1)} %get-tuple-element.45, ...), kind=kLoop, calls=%fused_computation.24 | loop fusion | flops 786432 | bytes 3145730 | tf_op jit(solution)/shard_map/jit(_where)/select_n | solution.py:64
  29.8 0.4 fusion.19
  30.2 0.4 select_subtract_fusion.1
  30.6 0.4 broadcast_select_fusion.4
  31.8 7.7 %collective-permute-done.11 = f32[256,256]{1,0:T(8,128)S(1)} collective-permute-done((f32[256,256]{1,0:T(8,128)S(1)}, f32[256,256]{1,0:T(8,128)S(1)}, u32[]{:S(2)}, u32[]{:S(2)}) %collective-permute-start.11) | collective-permute-done | bytes 262176 | tf_op jit(solution)/shard_map/ppermute | solution.py:107
  39.5 0.4 broadcast_select_fusion.3
  39.9 3.3 %collective-permute-start.13 = (f32[256,256]{1,0:T(8,128)S(1)}, f32[256,256]{1,0:T(8,128)S(1)}, u32[]{:S(2)}, u32[]{:S(2)}) collective-permute-start(f32[256,256]{1,0:T(8,128)S(1)} %get-tuple-element.51), channel_id=1, source_target_pairs={{0,8},{8,0},{2,10},{10,2},{16,24},{24,16},{18,26},{26,18},{1,9},{9... | collective-permute-start | bytes 786440 | tf_op jit(solution)/shard_map/ppermute | solution.py:107
  43.2 0.4 convolution_add_fusion
  44.5 4.9 %collective-permute-done.13 = f32[256,256]{1,0:T(8,128)S(1)} collective-permute-done((f32[256,256]{1,0:T(8,128)S(1)}, f32[256,256]{1,0:T(8,128)S(1)}, u32[]{:S(2)}, u32[]{:S(2)}) %collective-permute-start.13) | collective-permute-done | bytes 262176 | tf_op jit(solution)/shard_map/ppermute | solution.py:107
  49.4 0.4 broadcast_select_fusion.2
  49.8 5.1 %collective-permute-start.15 = (f32[256,256]{1,0:T(8,128)S(1)}, f32[256,256]{1,0:T(8,128)S(1)}, u32[]{:S(2)}, u32[]{:S(2)}) collective-permute-start(f32[256,256]{1,0:T(8,128)S(1)} %get-tuple-element.53), channel_id=1, source_target_pairs={{0,16},{16,0},{2,18},{18,2},{1,17},{17,1},{3,19},{19,3}} | collective-permute-start | bytes 786440 | tf_op jit(solution)/shard_map/ppermute | solution.py:107
  54.9 0.4 convolution_add_fusion.1
  56.3 3.8 %collective-permute-done.15 = f32[256,256]{1,0:T(8,128)S(1)} collective-permute-done((f32[256,256]{1,0:T(8,128)S(1)}, f32[256,256]{1,0:T(8,128)S(1)}, u32[]{:S(2)}, u32[]{:S(2)}) %collective-permute-start.15) | collective-permute-done | bytes 262176 | tf_op jit(solution)/shard_map/ppermute | solution.py:107
  60.1 0.4 convolution_add_fusion.2
  61.2 1.5 %collective-permute-done.16 = f32[256,256]{1,0:T(8,128)S(1)} collective-permute-done((f32[256,256]{1,0:T(8,128)S(1)}, f32[256,256]{1,0:T(8,128)S(1)}, u32[]{:S(2)}, u32[]{:S(2)}) %collective-permute-start.16) | collective-permute-done | bytes 262176 | tf_op jit(solution)/shard_map/ppermute | solution.py:121
  62.8 1.1 %pad_maximum_fusion = f32[512,512]{1,0:T(8,128)} fusion(f32[256,512]{1,0:T(8,128)S(1)} %get-tuple-element.34, f32[256,256]{1,0:T(8,128)S(1)} %get-tuple-element.36, f32[256,256]{1,0:T(8,128)S(1)} %get-tuple-element.35), kind=kLoop, calls=%fused_computation.14 | loop fusion | flops 524288 | bytes 2097152 | tf_op jit(solution)/shard_map/concatenate | solution.py:123
  (50 shorter events, 4.8 us)
Async XLA Ops:
  0.0 7.5 %collective-permute-start.2 = (f32[256,128]{1,0:T(8,128)}, f32[256,128]{1,0:T(8,128)S(1)}, u32[]{:S(2)}, u32[]{:S(2)}) collective-permute-start(f32[256,128]{1,0:T(8,128)} %param.9), channel_id=1, source_target_pairs={{0,1},{1,0},{2,3},{3,2},{4,5},{5,4},{6,7},{7,6},{8,9},{9,8},{10,11... | collective-permute-start | bytes 393224 | tf_op jit(solution)/shard_map/ppermute | solution.py:34
  3.0 10.9 %collective-permute-start.1 = (f32[256,128]{1,0:T(8,128)}, f32[256,128]{1,0:T(8,128)S(1)}, u32[]{:S(2)}, u32[]{:S(2)}) collective-permute-start(f32[256,128]{1,0:T(8,128)} %param.7), channel_id=1, source_target_pairs={{0,1},{1,0},{2,3},{3,2},{4,5},{5,4},{6,7},{7,6},{8,9},{9,8},{10,11... | collective-permute-start | bytes 393224 | tf_op jit(solution)/shard_map/ppermute | solution.py:34
  3.0 10.1 %collective-permute-start.7 = (f32[256,128]{1,0:T(8,128)}, f32[256,128]{1,0:T(8,128)S(1)}, u32[]{:S(2)}, u32[]{:S(2)}) collective-permute-start(f32[256,128]{1,0:T(8,128)} %param.8), channel_id=1, source_target_pairs={{0,1},{1,0},{2,3},{3,2},{4,5},{5,4},{6,7},{7,6},{8,9},{9,8},{10,11... | collective-permute-start | bytes 393224 | tf_op jit(solution)/shard_map/ppermute | solution.py:34
  5.0 13.7 %collective-permute-start = (f32[512,128]{1,0:T(8,128)}, f32[512,128]{1,0:T(8,128)S(1)}, u32[]{:S(2)}, u32[]{:S(2)}) collective-permute-start(f32[512,128]{1,0:T(8,128)} %param.6), channel_id=1, source_target_pairs={{0,1},{1,0},{2,3},{3,2},{4,5},{5,4},{6,7},{7,6},{8,9},{9,8},{10,11... | collective-permute-start | bytes 786440 | tf_op jit(solution)/shard_map/ppermute | solution.py:34
  8.6 4.6 %copy-start.2 = (f32[256,128]{1,0:T(8,128)S(1)}, f32[256,128]{1,0:T(8,128)}, u32[]{:S(2)}) copy-start(f32[256,128]{1,0:T(8,128)} %param.8) | copy-start | bytes 393220
  8.6 6.1 %collective-permute-start.3 = (f32[128,256]{1,0:T(8,128)S(1)}, f32[128,256]{1,0:T(8,128)S(1)}, u32[]{:S(2)}, u32[]{:S(2)}) collective-permute-start(f32[128,256]{1,0:T(8,128)S(1)} %slice.73), channel_id=1, source_target_pairs={{0,2},{2,0},{4,6},{6,4},{8,10},{10,8},{12,14},{14,12},{16,18},{18,... | collective-permute-start | bytes 393224 | tf_op jit(solution)/shard_map/ppermute | solution.py:67
  13.7 0.9 %copy-start.3 = (f32[256,128]{1,0:T(8,128)S(1)}, f32[256,128]{1,0:T(8,128)}, u32[]{:S(2)}) copy-start(f32[256,128]{1,0:T(8,128)} %param.7) | copy-start | bytes 393220
  13.7 14.8 %collective-permute-start.8 = (f32[3,256,256]{2,1,0:T(8,128)S(1)}, f32[3,256,256]{2,1,0:T(8,128)}, u32[]{:S(2)}, u32[]{:S(2)}) collective-permute-start(f32[3,256,256]{2,1,0:T(8,128)S(1)} %pad_maximum_fusion.1), channel_id=1, source_target_pairs={{0,2},{2,0},{4,6},{6,4},{8,10},{10,8},{12,14},{14,12},{16,18},{18,... | collective-permute-start | bytes 2359304 | tf_op jit(solution)/shard_map/ppermute | solution.py:62
  14.7 4.1 %copy-start.1 = (f32[512,128]{1,0:T(8,128)S(1)}, f32[512,128]{1,0:T(8,128)}, u32[]{:S(2)}) copy-start(f32[512,128]{1,0:T(8,128)} %param.6) | copy-start | bytes 786436
  14.7 8.2 %collective-permute-start.6 = (f32[128,256]{1,0:T(8,128)S(1)}, f32[128,256]{1,0:T(8,128)S(1)}, u32[]{:S(2)}, u32[]{:S(2)}) collective-permute-start(f32[128,256]{1,0:T(8,128)S(1)} %slice_select_fusion), channel_id=1, source_target_pairs={{16,0},{18,2},{17,1},{19,3}} | collective-permute-start | bytes 393224 | tf_op jit(solution)/shard_map/ppermute | solution.py:75
  16.1 9.5 %collective-permute-start.5 = (f32[128,256]{1,0:T(8,128)S(1)}, f32[128,256]{1,0:T(8,128)S(1)}, u32[]{:S(2)}, u32[]{:S(2)}) collective-permute-start(f32[128,256]{1,0:T(8,128)S(1)} %slice_select_fusion), channel_id=1, source_target_pairs={{8,0},{10,2},{24,16},{26,18},{9,1},{11,3},{25,17},{27,19}} | collective-permute-start | bytes 393224 | tf_op jit(solution)/shard_map/ppermute | solution.py:75
  17.4 8.2 %collective-permute-start.4 = (f32[128,256]{1,0:T(8,128)S(1)}, f32[128,256]{1,0:T(8,128)S(1)}, u32[]{:S(2)}, u32[]{:S(2)}) collective-permute-start(f32[128,256]{1,0:T(8,128)S(1)} %slice_select_fusion), channel_id=1, source_target_pairs={{4,0},{6,2},{12,8},{14,10},{20,16},{22,18},{28,24},{30,26},{5,1},{... | collective-permute-start | bytes 393224 | tf_op jit(solution)/shard_map/ppermute | solution.py:75
  18.8 6.8 %copy-start = (f32[512,512]{1,0:T(8,128)S(1)}, f32[512,512]{1,0:T(8,128)}, u32[]{:S(2)}) copy-start(f32[512,512]{1,0:T(8,128)} %param.5) | copy-start | bytes 3145732
  27.4 2.8 %collective-permute-start.9 = (f32[256,512]{1,0:T(8,128)S(1)}, f32[256,512]{1,0:T(8,128)S(1)}, u32[]{:S(2)}, u32[]{:S(2)}) collective-permute-start(f32[256,512]{1,0:T(8,128)S(1)} %get-tuple-element.33), channel_id=1, source_target_pairs={{0,2},{2,0},{4,6},{6,4},{8,10},{10,8},{12,14},{14,12},{16,18},{18,... | collective-permute-start | bytes 1572872 | tf_op jit(solution)/shard_map/ppermute | solution.py:85
  27.6 3.5 %collective-permute-start.10 = (f32[128,256]{1,0:T(8,128)S(1)}, f32[128,256]{1,0:T(8,128)S(1)}, u32[]{:S(2)}, u32[]{:S(2)}) collective-permute-start(f32[128,256]{1,0:T(8,128)S(1)} %collective-permute-done.4), channel_id=1, source_target_pairs={{0,2},{2,0},{4,6},{6,4},{8,10},{10,8},{12,14},{14,12},{16,18},{18,... | collective-permute-start | bytes 393224 | tf_op jit(solution)/shard_map/ppermute | solution.py:109
  28.0 15.6 %collective-permute-start.12 = (f32[128,256]{1,0:T(8,128)S(1)}, f32[128,256]{1,0:T(8,128)S(1)}, u32[]{:S(2)}, u32[]{:S(2)}) collective-permute-start(f32[128,256]{1,0:T(8,128)S(1)} %collective-permute-done.5), channel_id=1, source_target_pairs={{0,2},{2,0},{4,6},{6,4},{8,10},{10,8},{12,14},{14,12},{16,18},{18,... | collective-permute-start | bytes 393224 | tf_op jit(solution)/shard_map/ppermute | solution.py:109
  28.2 27.2 %collective-permute-start.14 = (f32[128,256]{1,0:T(8,128)S(1)}, f32[128,256]{1,0:T(8,128)S(1)}, u32[]{:S(2)}, u32[]{:S(2)}) collective-permute-start(f32[128,256]{1,0:T(8,128)S(1)} %collective-permute-done.6), channel_id=1, source_target_pairs={{0,2},{2,0},{4,6},{6,4},{8,10},{10,8},{12,14},{14,12},{16,18},{18,... | collective-permute-start | bytes 393224 | tf_op jit(solution)/shard_map/ppermute | solution.py:109
  31.0 8.4 %collective-permute-start.11 = (f32[256,256]{1,0:T(8,128)S(1)}, f32[256,256]{1,0:T(8,128)S(1)}, u32[]{:S(2)}, u32[]{:S(2)}) collective-permute-start(f32[256,256]{1,0:T(8,128)S(1)} %get-tuple-element.49), channel_id=1, source_target_pairs={{0,4},{4,0},{2,6},{6,2},{8,12},{12,8},{10,14},{14,10},{16,20},{20,... | collective-permute-start | bytes 786440 | tf_op jit(solution)/shard_map/ppermute | solution.py:107
  39.9 9.5 %collective-permute-start.13 = (f32[256,256]{1,0:T(8,128)S(1)}, f32[256,256]{1,0:T(8,128)S(1)}, u32[]{:S(2)}, u32[]{:S(2)}) collective-permute-start(f32[256,256]{1,0:T(8,128)S(1)} %get-tuple-element.51), channel_id=1, source_target_pairs={{0,8},{8,0},{2,10},{10,2},{16,24},{24,16},{18,26},{26,18},{1,9},{9... | collective-permute-start | bytes 786440 | tf_op jit(solution)/shard_map/ppermute | solution.py:107
  49.8 10.3 %collective-permute-start.15 = (f32[256,256]{1,0:T(8,128)S(1)}, f32[256,256]{1,0:T(8,128)S(1)}, u32[]{:S(2)}, u32[]{:S(2)}) collective-permute-start(f32[256,256]{1,0:T(8,128)S(1)} %get-tuple-element.53), channel_id=1, source_target_pairs={{0,16},{16,0},{2,18},{18,2},{1,17},{17,1},{3,19},{19,3}} | collective-permute-start | bytes 786440 | tf_op jit(solution)/shard_map/ppermute | solution.py:107
  61.1 1.6 %collective-permute-start.16 = (f32[256,256]{1,0:T(8,128)S(1)}, f32[256,256]{1,0:T(8,128)S(1)}, u32[]{:S(2)}, u32[]{:S(2)}) collective-permute-start(f32[256,256]{1,0:T(8,128)S(1)} %get-tuple-element.55), channel_id=1, source_target_pairs={{0,2},{2,0},{4,6},{6,4},{8,10},{10,8},{12,14},{14,12},{16,18},{18,... | collective-permute-start | bytes 786440 | tf_op jit(solution)/shard_map/ppermute | solution.py:121

commit v18 on v17

--- a/solution.py
+++ b/solution.py
@@ -64,15 +64,14 @@
     even3 = jnp.where(core == 0, own3, mate3)
 
     hw = width // 2
-    mate_s = lax.ppermute(tree_factor[hw:], "row", swap)
-    half_s = jnp.where(core == 0, tree_factor[:hw], mate_s)
     partner_factors = []
     for level in range(1, levels):
         step = 1 << level
-        pairs = []
-        for i in range(0, n_row, 2 * step):
-            pairs += [(i + step, i), (i + step + 1, i + 1)]
-        partner_factors.append(lax.ppermute(half_s, "row", pairs))
+        to_even = [(i + step, i) for i in range(0, n_row, 2 * step)]
+        to_odd = [(i + step, i + 1) for i in range(0, n_row, 2 * step)]
+        top_half = lax.ppermute(tree_factor[:hw], "row", to_even)
+        bottom_half = lax.ppermute(tree_factor[hw:], "row", to_odd)
+        partner_factors.append(jnp.where(core == 0, top_half, bottom_half))
 
     leaf_full, leaf_tri, partner_factors = lax.optimization_barrier((leaf_full, leaf_tri, partner_factors))
     leaf_vectors = unit_lower(leaf_full)

time: 64.1 us -> 65.5 us (1.022)
  waiting for transfers between devices: 31.5 us -> 35.3 us
  starting transfers between devices: 18.7 us -> 16.1 us
    ppermute x3, starting transfers between devices: 8.4 us -> 3.91 us  [on_device(): received = lax.ppermute(jnp.where(is_upper, q, chain), 'row', pairs)]
    ppermute x3, waiting for transfers between devices: 16.4 us -> 20.1 us  [on_device(): received = lax.ppermute(jnp.where(is_upper, q, chain), 'row', pairs)]
    ppermute x4 -> x6, waiting for transfers between devices: 6.66 us -> 8.99 us  [the longest x3 8.98 us: on_device(): top_half = lax.ppermute(tree_factor[:hw], 'row', to_even)]
    ppermute x4, waiting for transfers between devices: 6.92 us -> 4.71 us  [col_gather(): by_shift.append(lax.ppermute(part, 'col', perm))]
    ppermute x4 -> x6, starting transfers between devices: 4.08 us -> 5.98 us  [the longest x3 3.85 us: on_device(): top_half = lax.ppermute(tree_factor[:hw], 'row', to_even)]
  transfers between devices with their start and end apart: 17 -> 19, of which waited for: 8 -> 9; matrix products, arithmetic and copies ran while one was open for 16% -> 16% of each run, Pallas kernels for 0% -> 0%
where the time goes in v18:
time: 65.5 us; the launch traced here: 65.2 us
  waiting for transfers between devices  35.3 us (54%)
  starting transfers between devices  16.1 us (25%)
  matrix products  8.23 us (13%)
  other arithmetic  4.06 us (6%)
  local copies, waits for them, and re-layouts  0.91 us (1%)
    ppermute x3, waiting for transfers between devices, on_device(): received = lax.ppermute(jnp.where(is_upper, q, chain), 'row', pairs)  20.1 us
    ppermute x3, waiting for transfers between devices, on_device(): top_half = lax.ppermute(tree_factor[:hw], 'row', to_even)  8.98 us
    dot_general x16, matrix products, product_left_t(): lax.dot_general(left, right, (((0,), (0,)), ((), ())), precision=lax.Prec...  6.15 us
    ppermute x4, starting transfers between devices, col_gather(): by_shift.append(lax.ppermute(part, 'col', perm))  5.04 us
    ppermute x4, waiting for transfers between devices, col_gather(): by_shift.append(lax.ppermute(part, 'col', perm))  4.71 us
    ppermute x3, starting transfers between devices, on_device(): received = lax.ppermute(jnp.where(is_upper, q, chain), 'row', pairs)  3.91 us
    ppermute x3, starting transfers between devices, on_device(): top_half = lax.ppermute(tree_factor[:hw], 'row', to_even)  3.85 us
    ppermute x3, starting transfers between devices, on_device(): bottom_half = lax.ppermute(tree_factor[hw:], 'row', to_odd)  2.13 us
  transfers between devices with their start and end apart: 19, of which 9 were waited for; matrix products, arithmetic and copies ran while one was open for 16% of the time, Pallas kernels for 0%

profile of v18, /device:TPU:0, one launch (start us, length us, event | category | flops | bytes accessed | tf_op | source)
XLA Modules:
  0.0 65.2 jit_solution(2376421030133563652)
XLA Ops:
  0.0 3.0 %collective-permute-start.2 = (f32[256,128]{1,0:T(8,128)}, f32[256,128]{1,0:T(8,128)S(1)}, u32[]{:S(2)}, u32[]{:S(2)}) collective-permute-start(f32[256,128]{1,0:T(8,128)} %param.9), channel_id=1, source_target_pairs={{0,1},{1,0},{2,3},{3,2},{4,5},{5,4},{6,7},{7,6},{8,9},{9,8},{10,11... | collective-permute-start | bytes 393224 | tf_op jit(solution)/shard_map/ppermute | solution.py:34
  3.0 2.0 %collective-permute-start.9 = (f32[256,128]{1,0:T(8,128)}, f32[256,128]{1,0:T(8,128)S(1)}, u32[]{:S(2)}, u32[]{:S(2)}) collective-permute-start(f32[256,128]{1,0:T(8,128)} %param.8), channel_id=1, source_target_pairs={{0,1},{1,0},{2,3},{3,2},{4,5},{5,4},{6,7},{7,6},{8,9},{9,8},{10,11... | collective-permute-start | bytes 393224 | tf_op jit(solution)/shard_map/ppermute | solution.py:34
  5.0 2.5 %collective-permute-done.2 = f32[256,128]{1,0:T(8,128)S(1)} collective-permute-done((f32[256,128]{1,0:T(8,128)}, f32[256,128]{1,0:T(8,128)S(1)}, u32[]{:S(2)}, u32[]{:S(2)}) %collective-permute-start.2) | collective-permute-done | bytes 131104 | tf_op jit(solution)/shard_map/ppermute | solution.py:34
  7.5 0.9 %fusion.44 = (f32[1,256,128]{2,1,0:T(8,128)S(1)}, f32[1,256,128]{2,1,0:T(8,128)S(1)}) fusion(s32[]{:T(128)S(6)} %select_n.318, f32[1,256,128]{2,1,0:T(8,128)} %bitcast.84, f32[1,256,128]{2,1,0:T(8,128)S(1)} %bitcast.89, s32[]{:T(128)S(6)} %select_n.320), kind=kLoop, calls=%fused_computation.94 | loop fusion | flops 65536 | bytes 524296 | tf_op jit(solution)/shard_map/stack | solution.py:35
  8.6 0.8 %collective-permute-start.8 = (f32[128,256]{1,0:T(8,128)S(1)}, f32[128,256]{1,0:T(8,128)S(1)}, u32[]{:S(2)}, u32[]{:S(2)}) collective-permute-start(f32[128,256]{1,0:T(8,128)S(1)} %get-tuple-element.41), channel_id=1, source_target_pairs={{16,2},{17,3}} | collective-permute-start | bytes 393224 | tf_op jit(solution)/shard_map/ppermute | solution.py:73
  9.4 0.7 %collective-permute-start.6 = (f32[128,256]{1,0:T(8,128)S(1)}, f32[128,256]{1,0:T(8,128)S(1)}, u32[]{:S(2)}, u32[]{:S(2)}) collective-permute-start(f32[128,256]{1,0:T(8,128)S(1)} %get-tuple-element.41), channel_id=1, source_target_pairs={{8,2},{24,18},{9,3},{25,19}} | collective-permute-start | bytes 393224 | tf_op jit(solution)/shard_map/ppermute | solution.py:73
  10.3 0.7 %collective-permute-start.4 = (f32[128,256]{1,0:T(8,128)S(1)}, f32[128,256]{1,0:T(8,128)S(1)}, u32[]{:S(2)}, u32[]{:S(2)}) collective-permute-start(f32[128,256]{1,0:T(8,128)S(1)} %get-tuple-element.41), channel_id=1, source_target_pairs={{4,2},{12,10},{20,18},{28,26},{5,3},{13,11},{21,19},{29,27}} | collective-permute-start | bytes 393224 | tf_op jit(solution)/shard_map/ppermute | solution.py:73
  11.1 2.0 %collective-permute-done.9 = f32[256,128]{1,0:T(8,128)S(1)} collective-permute-done((f32[256,128]{1,0:T(8,128)}, f32[256,128]{1,0:T(8,128)S(1)}, u32[]{:S(2)}, u32[]{:S(2)}) %collective-permute-start.9) | collective-permute-done | bytes 131104 | tf_op jit(solution)/shard_map/ppermute | solution.py:34
  13.1 1.3 %collective-permute-start.7 = (f32[128,256]{1,0:T(8,128)S(1)}, f32[128,256]{1,0:T(8,128)S(1)}, u32[]{:S(2)}, u32[]{:S(2)}) collective-permute-start(f32[128,256]{1,0:T(8,128)S(1)} %get-tuple-element.42), channel_id=1, source_target_pairs={{16,0},{17,1}} | collective-permute-start | bytes 393224 | tf_op jit(solution)/shard_map/ppermute | solution.py:72
  15.0 1.3 %collective-permute-start.5 = (f32[128,256]{1,0:T(8,128)S(1)}, f32[128,256]{1,0:T(8,128)S(1)}, u32[]{:S(2)}, u32[]{:S(2)}) collective-permute-start(f32[128,256]{1,0:T(8,128)S(1)} %get-tuple-element.42), channel_id=1, source_target_pairs={{8,0},{24,16},{9,1},{25,17}} | collective-permute-start | bytes 393224 | tf_op jit(solution)/shard_map/ppermute | solution.py:72
  16.3 4.6 %collective-permute-done.7 = f32[128,256]{1,0:T(8,128)S(1)} collective-permute-done((f32[128,256]{1,0:T(8,128)S(1)}, f32[128,256]{1,0:T(8,128)S(1)}, u32[]{:S(2)}, u32[]{:S(2)}) %collective-permute-start.7) | collective-permute-done | bytes 131104 | tf_op jit(solution)/shard_map/ppermute | solution.py:72
  20.9 1.3 %collective-permute-start.3 = (f32[128,256]{1,0:T(8,128)S(1)}, f32[128,256]{1,0:T(8,128)S(1)}, u32[]{:S(2)}, u32[]{:S(2)}) collective-permute-start(f32[128,256]{1,0:T(8,128)S(1)} %get-tuple-element.42), channel_id=1, source_target_pairs={{4,0},{12,8},{20,16},{28,24},{5,1},{13,9},{21,17},{29,25}} | collective-permute-start | bytes 393224 | tf_op jit(solution)/shard_map/ppermute | solution.py:72
  22.4 0.8 %copy-done.1 = f32[512,128]{1,0:T(8,128)S(1)} copy-done((f32[512,128]{1,0:T(8,128)S(1)}, f32[512,128]{1,0:T(8,128)}, u32[]{:S(2)}) %copy-start.1) | copy-done | bytes 262168
  23.3 4.4 %collective-permute-done.3 = f32[128,256]{1,0:T(8,128)S(1)} collective-permute-done((f32[128,256]{1,0:T(8,128)S(1)}, f32[128,256]{1,0:T(8,128)S(1)}, u32[]{:S(2)}, u32[]{:S(2)}) %collective-permute-start.3) | collective-permute-done | bytes 131104 | tf_op jit(solution)/shard_map/ppermute | solution.py:72
  27.8 0.6 fusion.3
  28.4 0.5 fusion.26
  28.9 0.6 convolution_subtract_fusion
  29.8 0.4 collective-permute-start.12
  30.7 1.3 %broadcast_select_fusion = (f32[3,256,256]{2,1,0:T(8,128)S(1)}, f32[3,256,256]{2,1,0:T(8,128)S(1)}) fusion(f32[3,256,256]{2,1,0:T(8,128)} %collective-permute-done.10, pred[]{:T(512)S(6)} %eq.57, f32[1,256,256]{2,1,0:T(8,128)S(1)} %convolution_bitcast_fusion, f32[1,256,256]{2,1,0:T(8,128)S(1)} %get-tuple-element.48, ...), kind=kLoop, calls=%fused_computation.24 | loop fusion | flops 786432 | bytes 3145730 | tf_op jit(solution)/shard_map/jit(_where)/select_n | solution.py:64
  32.0 0.4 fusion.19
  32.4 0.4 select_subtract_fusion.1
  32.8 0.4 broadcast_select_fusion.4
  33.9 7.7 %collective-permute-done.13 = f32[256,256]{1,0:T(8,128)S(1)} collective-permute-done((f32[256,256]{1,0:T(8,128)S(1)}, f32[256,256]{1,0:T(8,128)S(1)}, u32[]{:S(2)}, u32[]{:S(2)}) %collective-permute-start.13) | collective-permute-done | bytes 262176 | tf_op jit(solution)/shard_map/ppermute | solution.py:106
  41.7 0.4 broadcast_select_fusion.3
  42.1 1.9 %collective-permute-start.15 = (f32[256,256]{1,0:T(8,128)S(1)}, f32[256,256]{1,0:T(8,128)S(1)}, u32[]{:S(2)}, u32[]{:S(2)}) collective-permute-start(f32[256,256]{1,0:T(8,128)S(1)} %get-tuple-element.53), channel_id=1, source_target_pairs={{0,8},{8,0},{2,10},{10,2},{16,24},{24,16},{18,26},{26,18},{1,9},{9... | collective-permute-start | bytes 786440 | tf_op jit(solution)/shard_map/ppermute | solution.py:106
  44.1 0.4 convolution_add_fusion
  45.4 6.2 %collective-permute-done.15 = f32[256,256]{1,0:T(8,128)S(1)} collective-permute-done((f32[256,256]{1,0:T(8,128)S(1)}, f32[256,256]{1,0:T(8,128)S(1)}, u32[]{:S(2)}, u32[]{:S(2)}) %collective-permute-start.15) | collective-permute-done | bytes 262176 | tf_op jit(solution)/shard_map/ppermute | solution.py:106
  52.0 1.9 %collective-permute-start.17 = (f32[256,256]{1,0:T(8,128)S(1)}, f32[256,256]{1,0:T(8,128)S(1)}, u32[]{:S(2)}, u32[]{:S(2)}) collective-permute-start(f32[256,256]{1,0:T(8,128)S(1)} %get-tuple-element.55), channel_id=1, source_target_pairs={{0,16},{16,0},{2,18},{18,2},{1,17},{17,1},{3,19},{19,3}} | collective-permute-start | bytes 786440 | tf_op jit(solution)/shard_map/ppermute | solution.py:106
  54.0 0.4 convolution_add_fusion.1
  55.3 6.2 %collective-permute-done.17 = f32[256,256]{1,0:T(8,128)S(1)} collective-permute-done((f32[256,256]{1,0:T(8,128)S(1)}, f32[256,256]{1,0:T(8,128)S(1)}, u32[]{:S(2)}, u32[]{:S(2)}) %collective-permute-start.17) | collective-permute-done | bytes 262176 | tf_op jit(solution)/shard_map/ppermute | solution.py:106
  62.5 1.5 %collective-permute-done.18 = f32[256,256]{1,0:T(8,128)S(1)} collective-permute-done((f32[256,256]{1,0:T(8,128)S(1)}, f32[256,256]{1,0:T(8,128)S(1)}, u32[]{:S(2)}, u32[]{:S(2)}) %collective-permute-start.18) | collective-permute-done | bytes 262176 | tf_op jit(solution)/shard_map/ppermute | solution.py:120
  64.1 1.1 %pad_maximum_fusion = f32[512,512]{1,0:T(8,128)} fusion(f32[256,512]{1,0:T(8,128)S(1)} %get-tuple-element.34, f32[256,256]{1,0:T(8,128)S(1)} %get-tuple-element.36, f32[256,256]{1,0:T(8,128)S(1)} %get-tuple-element.35), kind=kLoop, calls=%fused_computation.14 | loop fusion | flops 524288 | bytes 2097152 | tf_op jit(solution)/shard_map/concatenate | solution.py:122
  (56 shorter events, 6.2 us)
Async XLA Ops:
  0.0 7.5 %collective-permute-start.2 = (f32[256,128]{1,0:T(8,128)}, f32[256,128]{1,0:T(8,128)S(1)}, u32[]{:S(2)}, u32[]{:S(2)}) collective-permute-start(f32[256,128]{1,0:T(8,128)} %param.9), channel_id=1, source_target_pairs={{0,1},{1,0},{2,3},{3,2},{4,5},{5,4},{6,7},{7,6},{8,9},{9,8},{10,11... | collective-permute-start | bytes 393224 | tf_op jit(solution)/shard_map/ppermute | solution.py:34
  3.0 7.3 %collective-permute-start.1 = (f32[256,128]{1,0:T(8,128)}, f32[256,128]{1,0:T(8,128)S(1)}, u32[]{:S(2)}, u32[]{:S(2)}) collective-permute-start(f32[256,128]{1,0:T(8,128)} %param.7), channel_id=1, source_target_pairs={{0,1},{1,0},{2,3},{3,2},{4,5},{5,4},{6,7},{7,6},{8,9},{9,8},{10,11... | collective-permute-start | bytes 393224 | tf_op jit(solution)/shard_map/ppermute | solution.py:34
  3.0 10.1 %collective-permute-start.9 = (f32[256,128]{1,0:T(8,128)}, f32[256,128]{1,0:T(8,128)S(1)}, u32[]{:S(2)}, u32[]{:S(2)}) collective-permute-start(f32[256,128]{1,0:T(8,128)} %param.8), channel_id=1, source_target_pairs={{0,1},{1,0},{2,3},{3,2},{4,5},{5,4},{6,7},{7,6},{8,9},{9,8},{10,11... | collective-permute-start | bytes 393224 | tf_op jit(solution)/shard_map/ppermute | solution.py:34
  5.0 17.4 %collective-permute-start = (f32[512,128]{1,0:T(8,128)}, f32[512,128]{1,0:T(8,128)S(1)}, u32[]{:S(2)}, u32[]{:S(2)}) collective-permute-start(f32[512,128]{1,0:T(8,128)} %param.6), channel_id=1, source_target_pairs={{0,1},{1,0},{2,3},{3,2},{4,5},{5,4},{6,7},{7,6},{8,9},{9,8},{10,11... | collective-permute-start | bytes 786440 | tf_op jit(solution)/shard_map/ppermute | solution.py:34
  8.6 2.4 %copy-start.2 = (f32[256,128]{1,0:T(8,128)S(1)}, f32[256,128]{1,0:T(8,128)}, u32[]{:S(2)}) copy-start(f32[256,128]{1,0:T(8,128)} %param.7) | copy-start | bytes 393220
  8.6 6.4 %collective-permute-start.8 = (f32[128,256]{1,0:T(8,128)S(1)}, f32[128,256]{1,0:T(8,128)S(1)}, u32[]{:S(2)}, u32[]{:S(2)}) collective-permute-start(f32[128,256]{1,0:T(8,128)S(1)} %get-tuple-element.41), channel_id=1, source_target_pairs={{16,2},{17,3}} | collective-permute-start | bytes 393224 | tf_op jit(solution)/shard_map/ppermute | solution.py:73
  9.4 12.8 %collective-permute-start.6 = (f32[128,256]{1,0:T(8,128)S(1)}, f32[128,256]{1,0:T(8,128)S(1)}, u32[]{:S(2)}, u32[]{:S(2)}) collective-permute-start(f32[128,256]{1,0:T(8,128)S(1)} %get-tuple-element.41), channel_id=1, source_target_pairs={{8,2},{24,18},{9,3},{25,19}} | collective-permute-start | bytes 393224 | tf_op jit(solution)/shard_map/ppermute | solution.py:73
  10.3 13.0 %collective-permute-start.4 = (f32[128,256]{1,0:T(8,128)S(1)}, f32[128,256]{1,0:T(8,128)S(1)}, u32[]{:S(2)}, u32[]{:S(2)}) collective-permute-start(f32[128,256]{1,0:T(8,128)S(1)} %get-tuple-element.41), channel_id=1, source_target_pairs={{4,2},{12,10},{20,18},{28,26},{5,3},{13,11},{21,19},{29,27}} | collective-permute-start | bytes 393224 | tf_op jit(solution)/shard_map/ppermute | solution.py:73
  11.1 3.4 %copy-start.3 = (f32[256,128]{1,0:T(8,128)S(1)}, f32[256,128]{1,0:T(8,128)}, u32[]{:S(2)}) copy-start(f32[256,128]{1,0:T(8,128)} %param.8) | copy-start | bytes 393220
  13.1 7.8 %collective-permute-start.7 = (f32[128,256]{1,0:T(8,128)S(1)}, f32[128,256]{1,0:T(8,128)S(1)}, u32[]{:S(2)}, u32[]{:S(2)}) collective-permute-start(f32[128,256]{1,0:T(8,128)S(1)} %get-tuple-element.42), channel_id=1, source_target_pairs={{16,0},{17,1}} | collective-permute-start | bytes 393224 | tf_op jit(solution)/shard_map/ppermute | solution.py:72
  15.0 7.3 %collective-permute-start.5 = (f32[128,256]{1,0:T(8,128)S(1)}, f32[128,256]{1,0:T(8,128)S(1)}, u32[]{:S(2)}, u32[]{:S(2)}) collective-permute-start(f32[128,256]{1,0:T(8,128)S(1)} %get-tuple-element.42), channel_id=1, source_target_pairs={{8,0},{24,16},{9,1},{25,17}} | collective-permute-start | bytes 393224 | tf_op jit(solution)/shard_map/ppermute | solution.py:72
  20.9 6.8 %collective-permute-start.3 = (f32[128,256]{1,0:T(8,128)S(1)}, f32[128,256]{1,0:T(8,128)S(1)}, u32[]{:S(2)}, u32[]{:S(2)}) collective-permute-start(f32[128,256]{1,0:T(8,128)S(1)} %get-tuple-element.42), channel_id=1, source_target_pairs={{4,0},{12,8},{20,16},{28,24},{5,1},{13,9},{21,17},{29,25}} | collective-permute-start | bytes 393224 | tf_op jit(solution)/shard_map/ppermute | solution.py:72
  22.2 1.0 %copy-start.1 = (f32[512,128]{1,0:T(8,128)S(1)}, f32[512,128]{1,0:T(8,128)}, u32[]{:S(2)}) copy-start(f32[512,128]{1,0:T(8,128)} %param.6) | copy-start | bytes 786436
  22.2 8.5 %collective-permute-start.10 = (f32[3,256,256]{2,1,0:T(8,128)S(1)}, f32[3,256,256]{2,1,0:T(8,128)}, u32[]{:S(2)}, u32[]{:S(2)}) collective-permute-start(f32[3,256,256]{2,1,0:T(8,128)S(1)} %pad_maximum_fusion.1), channel_id=1, source_target_pairs={{0,2},{2,0},{4,6},{6,4},{8,10},{10,8},{12,14},{14,12},{16,18},{18,... | collective-permute-start | bytes 2359304 | tf_op jit(solution)/shard_map/ppermute | solution.py:62
  23.2 4.6 %copy-start = (f32[512,512]{1,0:T(8,128)S(1)}, f32[512,512]{1,0:T(8,128)}, u32[]{:S(2)}) copy-start(f32[512,512]{1,0:T(8,128)} %param.5) | copy-start | bytes 3145732
  29.6 2.8 %collective-permute-start.11 = (f32[256,512]{1,0:T(8,128)S(1)}, f32[256,512]{1,0:T(8,128)S(1)}, u32[]{:S(2)}, u32[]{:S(2)}) collective-permute-start(f32[256,512]{1,0:T(8,128)S(1)} %get-tuple-element.33), channel_id=1, source_target_pairs={{0,2},{2,0},{4,6},{6,4},{8,10},{10,8},{12,14},{14,12},{16,18},{18,... | collective-permute-start | bytes 1572872 | tf_op jit(solution)/shard_map/ppermute | solution.py:84
  29.8 3.5 %collective-permute-start.12 = (f32[128,256]{1,0:T(8,128)S(1)}, f32[128,256]{1,0:T(8,128)S(1)}, u32[]{:S(2)}, u32[]{:S(2)}) collective-permute-start(f32[128,256]{1,0:T(8,128)S(1)} %broadcast_select_fusion.11), channel_id=1, source_target_pairs={{0,2},{2,0},{4,6},{6,4},{8,10},{10,8},{12,14},{14,12},{16,18},{18,... | collective-permute-start | bytes 393224 | tf_op jit(solution)/shard_map/ppermute | solution.py:108
  30.2 14.3 %collective-permute-start.14 = (f32[128,256]{1,0:T(8,128)S(1)}, f32[128,256]{1,0:T(8,128)S(1)}, u32[]{:S(2)}, u32[]{:S(2)}) collective-permute-start(f32[128,256]{1,0:T(8,128)S(1)} %broadcast_select_fusion.10), channel_id=1, source_target_pairs={{0,2},{2,0},{4,6},{6,4},{8,10},{10,8},{12,14},{14,12},{16,18},{18,... | collective-permute-start | bytes 393224 | tf_op jit(solution)/shard_map/ppermute | solution.py:108
  30.3 24.0 %collective-permute-start.16 = (f32[128,256]{1,0:T(8,128)S(1)}, f32[128,256]{1,0:T(8,128)S(1)}, u32[]{:S(2)}, u32[]{:S(2)}) collective-permute-start(f32[128,256]{1,0:T(8,128)S(1)} %broadcast_select_fusion.9), channel_id=1, source_target_pairs={{0,2},{2,0},{4,6},{6,4},{8,10},{10,8},{12,14},{14,12},{16,18},{18,... | collective-permute-start | bytes 393224 | tf_op jit(solution)/shard_map/ppermute | solution.py:108
  33.2 8.4 %collective-permute-start.13 = (f32[256,256]{1,0:T(8,128)S(1)}, f32[256,256]{1,0:T(8,128)S(1)}, u32[]{:S(2)}, u32[]{:S(2)}) collective-permute-start(f32[256,256]{1,0:T(8,128)S(1)} %get-tuple-element.51), channel_id=1, source_target_pairs={{0,4},{4,0},{2,6},{6,2},{8,12},{12,8},{10,14},{14,10},{16,20},{20,... | collective-permute-start | bytes 786440 | tf_op jit(solution)/shard_map/ppermute | solution.py:106
  42.1 9.5 %collective-permute-start.15 = (f32[256,256]{1,0:T(8,128)S(1)}, f32[256,256]{1,0:T(8,128)S(1)}, u32[]{:S(2)}, u32[]{:S(2)}) collective-permute-start(f32[256,256]{1,0:T(8,128)S(1)} %get-tuple-element.53), channel_id=1, source_target_pairs={{0,8},{8,0},{2,10},{10,2},{16,24},{24,16},{18,26},{26,18},{1,9},{9... | collective-permute-start | bytes 786440 | tf_op jit(solution)/shard_map/ppermute | solution.py:106
  52.0 9.4 %collective-permute-start.17 = (f32[256,256]{1,0:T(8,128)S(1)}, f32[256,256]{1,0:T(8,128)S(1)}, u32[]{:S(2)}, u32[]{:S(2)}) collective-permute-start(f32[256,256]{1,0:T(8,128)S(1)} %get-tuple-element.55), channel_id=1, source_target_pairs={{0,16},{16,0},{2,18},{18,2},{1,17},{17,1},{3,19},{19,3}} | collective-permute-start | bytes 786440 | tf_op jit(solution)/shard_map/ppermute | solution.py:106
  62.4 1.6 %collective-permute-start.18 = (f32[256,256]{1,0:T(8,128)S(1)}, f32[256,256]{1,0:T(8,128)S(1)}, u32[]{:S(2)}, u32[]{:S(2)}) collective-permute-start(f32[256,256]{1,0:T(8,128)S(1)} %get-tuple-element.57), channel_id=1, source_target_pairs={{0,2},{2,0},{4,6},{6,4},{8,10},{10,8},{12,14},{14,12},{16,18},{18,... | collective-permute-start | bytes 786440 | tf_op jit(solution)/shard_map/ppermute | solution.py:120

commit v19 on v17

--- a/solution.py
+++ b/solution.py
@@ -44,10 +44,11 @@
     rows = leaf_v.shape[0]
     width = leaf_t.shape[0]
 
+    tree_tri = col_gather(tree_t)
+    tree_tri, leaf_v, leaf_t, tree_v = lax.optimization_barrier((tree_tri, leaf_v, leaf_t, tree_v))
     leaf_full = col_gather(leaf_v)
     leaf_tri = col_gather(leaf_t)
     tree_full = col_gather(tree_v)
-    tree_tri = col_gather(tree_t)
 
     tree_vectors = jnp.triu(tree_full)
     tree_factor = jnp.triu(tree_tri)

time: 64.1 us -> 62.8 us (0.980)
  waiting for transfers between devices: 31.5 us -> 27.8 us
  starting transfers between devices: 18.7 us -> 20 us
  local copies, waits for them, and re-layouts: 0.85 us -> 1.8 us
    ppermute x3, waiting for transfers between devices: 6.65 us -> 2.82 us  [on_device(): partner_factors.append(lax.ppermute(half_s, 'row', pairs))]
    ppermute x4, starting transfers between devices: 5.04 us -> 6.73 us  [col_gather(): by_shift.append(lax.ppermute(part, 'col', perm))]
    unnamed x8, local copies, waits for them, and re-layouts: 0.77 us -> 1.72 us
    squeeze x2 -> x3, other arithmetic: 0.17 us -> 1.11 us  [col_gather(): blocks = [stacked[(me - b) % n_col] for b in range(n_col)]]
    another operation x2 -> x1, other arithmetic: 0.99 us -> 0.07 us  [col_gather(): stacked = jnp.stack(by_shift)]
  transfers between devices with their start and end apart: 17 -> 17, of which waited for: 8 -> 9; matrix products, arithmetic and copies ran while one was open for 16% -> 15% of each run, Pallas kernels for 0% -> 0%
where the time goes in v19:
time: 62.8 us; the launch traced here: 62.5 us
  waiting for transfers between devices  27.8 us (44%)
  starting transfers between devices  20 us (32%)
  matrix products  8.26 us (13%)
  other arithmetic  4.13 us (7%)
  local copies, waits for them, and re-layouts  1.8 us (3%)
    ppermute x3, waiting for transfers between devices, on_device(): received = lax.ppermute(jnp.where(is_upper, q, chain), 'row', pairs)  16.3 us
    ppermute x3, starting transfers between devices, on_device(): received = lax.ppermute(jnp.where(is_upper, q, chain), 'row', pairs)  8.19 us
    ppermute x4, waiting for transfers between devices, col_gather(): by_shift.append(lax.ppermute(part, 'col', perm))  7.15 us
    ppermute x4, starting transfers between devices, col_gather(): by_shift.append(lax.ppermute(part, 'col', perm))  6.73 us
    dot_general x16, matrix products, product_left_t(): lax.dot_general(left, right, (((0,), (0,)), ((), ())), precision=lax.Prec...  6.17 us
    ppermute x3, starting transfers between devices, on_device(): partner_factors.append(lax.ppermute(half_s, 'row', pairs))  3.86 us
    ppermute x3, waiting for transfers between devices, on_device(): partner_factors.append(lax.ppermute(half_s, 'row', pairs))  2.82 us
    dot_general x6, matrix products, product(): jnp.dot(left, right, precision=lax.Precision.HIGH, preferred_element_type...  2.08 us
  transfers between devices with their start and end apart: 17, of which 9 were waited for; matrix products, arithmetic and copies ran while one was open for 15% of the time, Pallas kernels for 0%

profile of v19, /device:TPU:0, one launch (start us, length us, event | category | flops | bytes accessed | tf_op | source)
XLA Modules:
  0.0 62.5 jit_solution(13537989257952781281)
XLA Ops:
  0.0 3.0 %collective-permute-start = (f32[256,128]{1,0:T(8,128)}, f32[256,128]{1,0:T(8,128)S(1)}, u32[]{:S(2)}, u32[]{:S(2)}) collective-permute-start(f32[256,128]{1,0:T(8,128)} %param.9), channel_id=1, source_target_pairs={{0,1},{1,0},{2,3},{3,2},{4,5},{5,4},{6,7},{7,6},{8,9},{9,8},{10,11... | collective-permute-start | bytes 393224 | tf_op jit(solution)/shard_map/ppermute | solution.py:34
  3.0 3.7 %collective-permute-done = f32[256,128]{1,0:T(8,128)S(1)} collective-permute-done((f32[256,128]{1,0:T(8,128)}, f32[256,128]{1,0:T(8,128)S(1)}, u32[]{:S(2)}, u32[]{:S(2)}) %collective-permute-start) | collective-permute-done | bytes 131104 | tf_op jit(solution)/shard_map/ppermute | solution.py:34
  6.7 0.9 %fusion.51 = (f32[256,128]{1,0:T(8,128)S(1)}, f32[256,128]{1,0:T(8,128)S(1)}) fusion(s32[]{:T(128)S(6)} %select_n.301, f32[1,256,128]{2,1,0:T(8,128)} %bitcast.85, f32[1,256,128]{2,1,0:T(8,128)S(1)} %bitcast.88, s32[]{:T(128)S(6)} %select_n.303), kind=kLoop, calls=%fused_computation.100 | loop fusion | flops 65536 | bytes 524296 | tf_op jit(solution)/shard_map/squeeze | solution.py:36
  7.7 0.9 %copy-done.3 = f32[256,128]{1,0:T(8,128)S(1)} copy-done((f32[256,128]{1,0:T(8,128)S(1)}, f32[256,128]{1,0:T(8,128)}, u32[]{:S(2)}) %copy-start.3) | copy-done | bytes 131096
  8.5 1.7 %collective-permute-start.2 = (f32[256,128]{1,0:T(8,128)S(1)}, f32[256,128]{1,0:T(8,128)S(1)}, u32[]{:S(2)}, u32[]{:S(2)}) collective-permute-start(f32[256,128]{1,0:T(8,128)S(1)} %copy-done.3), channel_id=1, source_target_pairs={{0,1},{1,0},{2,3},{3,2},{4,5},{5,4},{6,7},{7,6},{8,9},{9,8},{10,11... | collective-permute-start | bytes 393224 | tf_op jit(solution)/shard_map/ppermute | solution.py:34
  10.8 0.8 %copy-done.1 = f32[512,128]{1,0:T(8,128)S(1)} copy-done((f32[512,128]{1,0:T(8,128)S(1)}, f32[512,128]{1,0:T(8,128)}, u32[]{:S(2)}) %copy-start.1) | copy-done | bytes 262168
  11.6 1.7 %collective-permute-start.1 = (f32[512,128]{1,0:T(8,128)S(1)}, f32[512,128]{1,0:T(8,128)S(1)}, u32[]{:S(2)}, u32[]{:S(2)}) collective-permute-start(f32[512,128]{1,0:T(8,128)S(1)} %copy-done.1), channel_id=1, source_target_pairs={{0,1},{1,0},{2,3},{3,2},{4,5},{5,4},{6,7},{7,6},{8,9},{9,8},{10,11... | collective-permute-start | bytes 786440 | tf_op jit(solution)/shard_map/ppermute | solution.py:34
  13.5 1.3 %collective-permute-start.6 = (f32[128,256]{1,0:T(8,128)S(1)}, f32[128,256]{1,0:T(8,128)S(1)}, u32[]{:S(2)}, u32[]{:S(2)}) collective-permute-start(f32[128,256]{1,0:T(8,128)S(1)} %slice_select_fusion), channel_id=1, source_target_pairs={{16,0},{18,2},{17,1},{19,3}} | collective-permute-start | bytes 393224 | tf_op jit(solution)/shard_map/ppermute | solution.py:76
  14.8 1.3 %collective-permute-start.5 = (f32[128,256]{1,0:T(8,128)S(1)}, f32[128,256]{1,0:T(8,128)S(1)}, u32[]{:S(2)}, u32[]{:S(2)}) collective-permute-start(f32[128,256]{1,0:T(8,128)S(1)} %slice_select_fusion), channel_id=1, source_target_pairs={{8,0},{10,2},{24,16},{26,18},{9,1},{11,3},{25,17},{27,19}} | collective-permute-start | bytes 393224 | tf_op jit(solution)/shard_map/ppermute | solution.py:76
  16.1 1.7 %collective-permute-done.7 = f32[256,128]{1,0:T(8,128)S(1)} collective-permute-done((f32[256,128]{1,0:T(8,128)S(1)}, f32[256,128]{1,0:T(8,128)S(1)}, u32[]{:S(2)}, u32[]{:S(2)}) %collective-permute-start.7) | collective-permute-done | bytes 131104 | tf_op jit(solution)/shard_map/ppermute | solution.py:34
  17.8 1.3 %collective-permute-start.4 = (f32[128,256]{1,0:T(8,128)S(1)}, f32[128,256]{1,0:T(8,128)S(1)}, u32[]{:S(2)}, u32[]{:S(2)}) collective-permute-start(f32[128,256]{1,0:T(8,128)S(1)} %slice_select_fusion), channel_id=1, source_target_pairs={{4,0},{6,2},{12,8},{14,10},{20,16},{22,18},{28,24},{30,26},{5,1},{... | collective-permute-start | bytes 393224 | tf_op jit(solution)/shard_map/ppermute | solution.py:76
  19.9 1.8 %collective-permute-done.1 = f32[512,128]{1,0:T(8,128)S(1)} collective-permute-done((f32[512,128]{1,0:T(8,128)S(1)}, f32[512,128]{1,0:T(8,128)S(1)}, u32[]{:S(2)}, u32[]{:S(2)}) %collective-permute-start.1) | collective-permute-done | bytes 262176 | tf_op jit(solution)/shard_map/ppermute | solution.py:34
  21.8 2.1 %collective-permute-done.5 = f32[128,256]{1,0:T(8,128)S(1)} collective-permute-done((f32[128,256]{1,0:T(8,128)S(1)}, f32[128,256]{1,0:T(8,128)S(1)}, u32[]{:S(2)}, u32[]{:S(2)}) %collective-permute-start.5) | collective-permute-done | bytes 131104 | tf_op jit(solution)/shard_map/ppermute | solution.py:76
  23.9 0.7 %collective-permute-done.4 = f32[128,256]{1,0:T(8,128)S(1)} collective-permute-done((f32[128,256]{1,0:T(8,128)S(1)}, f32[128,256]{1,0:T(8,128)S(1)}, u32[]{:S(2)}, u32[]{:S(2)}) %collective-permute-start.4) | collective-permute-done | bytes 131104 | tf_op jit(solution)/shard_map/ppermute | solution.py:76
  24.6 0.6 %fusion.3 = f32[256,512]{1,0:T(8,128)S(1)} fusion(f32[512,512]{1,0:T(8,128)S(1)} %copy-done, f32[512,256]{1,0:T(8,128)S(1)} %pad_maximum_fusion.2), kind=kOutput, calls=%fused_computation.26 | convolution fusion | flops 403308544 | bytes 2097152 | tf_op jit(solution)/shard_map/dot_general | solution.py:12
  25.3 0.5 fusion.26
  25.8 0.6 convolution_subtract_fusion
  26.6 0.4 collective-permute-start.10
  27.5 1.3 %broadcast_select_fusion = (f32[3,256,256]{2,1,0:T(8,128)S(1)}, f32[3,256,256]{2,1,0:T(8,128)S(1)}) fusion(f32[3,256,256]{2,1,0:T(8,128)} %collective-permute-done.8, pred[]{:T(512)S(6)} %eq.55, f32[1,256,256]{2,1,0:T(8,128)S(1)} %convolution_bitcast_fusion, f32[1,256,256]{2,1,0:T(8,128)S(1)} %fusion.138, f32[1,256,256]{2,1,0:T(8,128)S(1)} %maximum_select_fusion, ...), kind=kLoop, calls=%fused_computation.24 | loop fusion | flops 786432 | bytes 3145730 | tf_op jit(solution)/shard_map/jit(_where)/select_n | solution.py:65
  28.8 0.4 fusion.19
  29.2 0.4 select_subtract_fusion.1
  29.7 0.4 broadcast_select_fusion.4
  30.8 7.7 %collective-permute-done.11 = f32[256,256]{1,0:T(8,128)S(1)} collective-permute-done((f32[256,256]{1,0:T(8,128)S(1)}, f32[256,256]{1,0:T(8,128)S(1)}, u32[]{:S(2)}, u32[]{:S(2)}) %collective-permute-start.11) | collective-permute-done | bytes 262176 | tf_op jit(solution)/shard_map/ppermute | solution.py:108
  38.6 0.4 broadcast_select_fusion.3
  39.0 3.4 %collective-permute-start.13 = (f32[256,256]{1,0:T(8,128)S(1)}, f32[256,256]{1,0:T(8,128)S(1)}, u32[]{:S(2)}, u32[]{:S(2)}) collective-permute-start(f32[256,256]{1,0:T(8,128)S(1)} %get-tuple-element.57), channel_id=1, source_target_pairs={{0,8},{8,0},{2,10},{10,2},{16,24},{24,16},{18,26},{26,18},{1,9},{9... | collective-permute-start | bytes 786440 | tf_op jit(solution)/shard_map/ppermute | solution.py:108
  43.7 4.7 %collective-permute-done.13 = f32[256,256]{1,0:T(8,128)S(1)} collective-permute-done((f32[256,256]{1,0:T(8,128)S(1)}, f32[256,256]{1,0:T(8,128)S(1)}, u32[]{:S(2)}, u32[]{:S(2)}) %collective-permute-start.13) | collective-permute-done | bytes 262176 | tf_op jit(solution)/shard_map/ppermute | solution.py:108
  48.5 0.4 broadcast_select_fusion.2
  48.9 4.7 %collective-permute-start.15 = (f32[256,256]{1,0:T(8,128)S(1)}, f32[256,256]{1,0:T(8,128)S(1)}, u32[]{:S(2)}, u32[]{:S(2)}) collective-permute-start(f32[256,256]{1,0:T(8,128)S(1)} %get-tuple-element.59), channel_id=1, source_target_pairs={{0,16},{16,0},{2,18},{18,2},{1,17},{17,1},{3,19},{19,3}} | collective-permute-start | bytes 786440 | tf_op jit(solution)/shard_map/ppermute | solution.py:108
  53.6 0.4 convolution_add_fusion.1
  54.9 3.8 %collective-permute-done.15 = f32[256,256]{1,0:T(8,128)S(1)} collective-permute-done((f32[256,256]{1,0:T(8,128)S(1)}, f32[256,256]{1,0:T(8,128)S(1)}, u32[]{:S(2)}, u32[]{:S(2)}) %collective-permute-start.15) | collective-permute-done | bytes 262176 | tf_op jit(solution)/shard_map/ppermute | solution.py:108
  59.9 1.5 %collective-permute-done.16 = f32[256,256]{1,0:T(8,128)S(1)} collective-permute-done((f32[256,256]{1,0:T(8,128)S(1)}, f32[256,256]{1,0:T(8,128)S(1)}, u32[]{:S(2)}, u32[]{:S(2)}) %collective-permute-start.16) | collective-permute-done | bytes 262176 | tf_op jit(solution)/shard_map/ppermute | solution.py:122
  61.4 1.1 %pad_maximum_fusion = f32[512,512]{1,0:T(8,128)} fusion(f32[256,512]{1,0:T(8,128)S(1)} %get-tuple-element.42, f32[256,256]{1,0:T(8,128)S(1)} %get-tuple-element.44, f32[256,256]{1,0:T(8,128)S(1)} %get-tuple-element.43), kind=kLoop, calls=%fused_computation.14 | loop fusion | flops 524288 | bytes 2097152 | tf_op jit(solution)/shard_map/concatenate | solution.py:124
  (52 shorter events, 6.3 us)
Async XLA Ops:
  0.0 6.7 %collective-permute-start = (f32[256,128]{1,0:T(8,128)}, f32[256,128]{1,0:T(8,128)S(1)}, u32[]{:S(2)}, u32[]{:S(2)}) collective-permute-start(f32[256,128]{1,0:T(8,128)} %param.9), channel_id=1, source_target_pairs={{0,1},{1,0},{2,3},{3,2},{4,5},{5,4},{6,7},{7,6},{8,9},{9,8},{10,11... | collective-permute-start | bytes 393224 | tf_op jit(solution)/shard_map/ppermute | solution.py:34
  7.6 0.9 %copy-start.3 = (f32[256,128]{1,0:T(8,128)S(1)}, f32[256,128]{1,0:T(8,128)}, u32[]{:S(2)}) copy-start(f32[256,128]{1,0:T(8,128)} %param.7) | copy-start | bytes 393220
  7.6 2.6 %copy-start.2 = (f32[256,128]{1,0:T(8,128)S(1)}, f32[256,128]{1,0:T(8,128)}, u32[]{:S(2)}) copy-start(f32[256,128]{1,0:T(8,128)} %param.8) | copy-start | bytes 393220
  8.5 11.1 %collective-permute-start.2 = (f32[256,128]{1,0:T(8,128)S(1)}, f32[256,128]{1,0:T(8,128)S(1)}, u32[]{:S(2)}, u32[]{:S(2)}) collective-permute-start(f32[256,128]{1,0:T(8,128)S(1)} %copy-done.3), channel_id=1, source_target_pairs={{0,1},{1,0},{2,3},{3,2},{4,5},{5,4},{6,7},{7,6},{8,9},{9,8},{10,11... | collective-permute-start | bytes 393224 | tf_op jit(solution)/shard_map/ppermute | solution.py:34
  10.3 7.5 %collective-permute-start.7 = (f32[256,128]{1,0:T(8,128)S(1)}, f32[256,128]{1,0:T(8,128)S(1)}, u32[]{:S(2)}, u32[]{:S(2)}) collective-permute-start(f32[256,128]{1,0:T(8,128)S(1)} %copy-done.2), channel_id=1, source_target_pairs={{0,1},{1,0},{2,3},{3,2},{4,5},{5,4},{6,7},{7,6},{8,9},{9,8},{10,11... | collective-permute-start | bytes 393224 | tf_op jit(solution)/shard_map/ppermute | solution.py:34
  10.7 1.0 %copy-start.1 = (f32[512,128]{1,0:T(8,128)S(1)}, f32[512,128]{1,0:T(8,128)}, u32[]{:S(2)}) copy-start(f32[512,128]{1,0:T(8,128)} %param.6) | copy-start | bytes 786436
  10.7 2.8 %collective-permute-start.3 = (f32[128,256]{1,0:T(8,128)S(1)}, f32[128,256]{1,0:T(8,128)S(1)}, u32[]{:S(2)}, u32[]{:S(2)}) collective-permute-start(f32[128,256]{1,0:T(8,128)S(1)} %slice.73), channel_id=1, source_target_pairs={{0,2},{2,0},{4,6},{6,4},{8,10},{10,8},{12,14},{14,12},{16,18},{18,... | collective-permute-start | bytes 393224 | tf_op jit(solution)/shard_map/ppermute | solution.py:68
  11.6 10.0 %collective-permute-start.1 = (f32[512,128]{1,0:T(8,128)S(1)}, f32[512,128]{1,0:T(8,128)S(1)}, u32[]{:S(2)}, u32[]{:S(2)}) collective-permute-start(f32[512,128]{1,0:T(8,128)S(1)} %copy-done.1), channel_id=1, source_target_pairs={{0,1},{1,0},{2,3},{3,2},{4,5},{5,4},{6,7},{7,6},{8,9},{9,8},{10,11... | collective-permute-start | bytes 786440 | tf_op jit(solution)/shard_map/ppermute | solution.py:34
  13.5 8.3 %collective-permute-start.6 = (f32[128,256]{1,0:T(8,128)S(1)}, f32[128,256]{1,0:T(8,128)S(1)}, u32[]{:S(2)}, u32[]{:S(2)}) collective-permute-start(f32[128,256]{1,0:T(8,128)S(1)} %slice_select_fusion), channel_id=1, source_target_pairs={{16,0},{18,2},{17,1},{19,3}} | collective-permute-start | bytes 393224 | tf_op jit(solution)/shard_map/ppermute | solution.py:76
  14.8 9.1 %collective-permute-start.5 = (f32[128,256]{1,0:T(8,128)S(1)}, f32[128,256]{1,0:T(8,128)S(1)}, u32[]{:S(2)}, u32[]{:S(2)}) collective-permute-start(f32[128,256]{1,0:T(8,128)S(1)} %slice_select_fusion), channel_id=1, source_target_pairs={{8,0},{10,2},{24,16},{26,18},{9,1},{11,3},{25,17},{27,19}} | collective-permute-start | bytes 393224 | tf_op jit(solution)/shard_map/ppermute | solution.py:76
  17.8 6.8 %collective-permute-start.4 = (f32[128,256]{1,0:T(8,128)S(1)}, f32[128,256]{1,0:T(8,128)S(1)}, u32[]{:S(2)}, u32[]{:S(2)}) collective-permute-start(f32[128,256]{1,0:T(8,128)S(1)} %slice_select_fusion), channel_id=1, source_target_pairs={{4,0},{6,2},{12,8},{14,10},{20,16},{22,18},{28,24},{30,26},{5,1},{... | collective-permute-start | bytes 393224 | tf_op jit(solution)/shard_map/ppermute | solution.py:76
  19.7 7.9 %collective-permute-start.8 = (f32[3,256,256]{2,1,0:T(8,128)S(1)}, f32[3,256,256]{2,1,0:T(8,128)}, u32[]{:S(2)}, u32[]{:S(2)}) collective-permute-start(f32[3,256,256]{2,1,0:T(8,128)S(1)} %pad_maximum_fusion.1), channel_id=1, source_target_pairs={{0,2},{2,0},{4,6},{6,4},{8,10},{10,8},{12,14},{14,12},{16,18},{18,... | collective-permute-start | bytes 2359304 | tf_op jit(solution)/shard_map/ppermute | solution.py:63
  21.6 3.0 %copy-start = (f32[512,512]{1,0:T(8,128)S(1)}, f32[512,512]{1,0:T(8,128)}, u32[]{:S(2)}) copy-start(f32[512,512]{1,0:T(8,128)} %param.5) | copy-start | bytes 3145732
  26.4 2.8 %collective-permute-start.9 = (f32[256,512]{1,0:T(8,128)S(1)}, f32[256,512]{1,0:T(8,128)S(1)}, u32[]{:S(2)}, u32[]{:S(2)}) collective-permute-start(f32[256,512]{1,0:T(8,128)S(1)} %get-tuple-element.41), channel_id=1, source_target_pairs={{0,2},{2,0},{4,6},{6,4},{8,10},{10,8},{12,14},{14,12},{16,18},{18,... | collective-permute-start | bytes 1572872 | tf_op jit(solution)/shard_map/ppermute | solution.py:86
  26.6 3.5 %collective-permute-start.10 = (f32[128,256]{1,0:T(8,128)S(1)}, f32[128,256]{1,0:T(8,128)S(1)}, u32[]{:S(2)}, u32[]{:S(2)}) collective-permute-start(f32[128,256]{1,0:T(8,128)S(1)} %collective-permute-done.4), channel_id=1, source_target_pairs={{0,2},{2,0},{4,6},{6,4},{8,10},{10,8},{12,14},{14,12},{16,18},{18,... | collective-permute-start | bytes 393224 | tf_op jit(solution)/shard_map/ppermute | solution.py:110
  27.0 15.8 %collective-permute-start.12 = (f32[128,256]{1,0:T(8,128)S(1)}, f32[128,256]{1,0:T(8,128)S(1)}, u32[]{:S(2)}, u32[]{:S(2)}) collective-permute-start(f32[128,256]{1,0:T(8,128)S(1)} %collective-permute-done.5), channel_id=1, source_target_pairs={{0,2},{2,0},{4,6},{6,4},{8,10},{10,8},{12,14},{14,12},{16,18},{18,... | collective-permute-start | bytes 393224 | tf_op jit(solution)/shard_map/ppermute | solution.py:110
  27.2 26.8 %collective-permute-start.14 = (f32[128,256]{1,0:T(8,128)S(1)}, f32[128,256]{1,0:T(8,128)S(1)}, u32[]{:S(2)}, u32[]{:S(2)}) collective-permute-start(f32[128,256]{1,0:T(8,128)S(1)} %collective-permute-done.6), channel_id=1, source_target_pairs={{0,2},{2,0},{4,6},{6,4},{8,10},{10,8},{12,14},{14,12},{16,18},{18,... | collective-permute-start | bytes 393224 | tf_op jit(solution)/shard_map/ppermute | solution.py:110
  30.1 8.4 %collective-permute-start.11 = (f32[256,256]{1,0:T(8,128)S(1)}, f32[256,256]{1,0:T(8,128)S(1)}, u32[]{:S(2)}, u32[]{:S(2)}) collective-permute-start(f32[256,256]{1,0:T(8,128)S(1)} %get-tuple-element.55), channel_id=1, source_target_pairs={{0,4},{4,0},{2,6},{6,2},{8,12},{12,8},{10,14},{14,10},{16,20},{20,... | collective-permute-start | bytes 786440 | tf_op jit(solution)/shard_map/ppermute | solution.py:108
  39.0 9.5 %collective-permute-start.13 = (f32[256,256]{1,0:T(8,128)S(1)}, f32[256,256]{1,0:T(8,128)S(1)}, u32[]{:S(2)}, u32[]{:S(2)}) collective-permute-start(f32[256,256]{1,0:T(8,128)S(1)} %get-tuple-element.57), channel_id=1, source_target_pairs={{0,8},{8,0},{2,10},{10,2},{16,24},{24,16},{18,26},{26,18},{1,9},{9... | collective-permute-start | bytes 786440 | tf_op jit(solution)/shard_map/ppermute | solution.py:108
  48.9 9.9 %collective-permute-start.15 = (f32[256,256]{1,0:T(8,128)S(1)}, f32[256,256]{1,0:T(8,128)S(1)}, u32[]{:S(2)}, u32[]{:S(2)}) collective-permute-start(f32[256,256]{1,0:T(8,128)S(1)} %get-tuple-element.59), channel_id=1, source_target_pairs={{0,16},{16,0},{2,18},{18,2},{1,17},{17,1},{3,19},{19,3}} | collective-permute-start | bytes 786440 | tf_op jit(solution)/shard_map/ppermute | solution.py:108
  59.8 1.6 %collective-permute-start.16 = (f32[256,256]{1,0:T(8,128)S(1)}, f32[256,256]{1,0:T(8,128)S(1)}, u32[]{:S(2)}, u32[]{:S(2)}) collective-permute-start(f32[256,256]{1,0:T(8,128)S(1)} %get-tuple-element.61), channel_id=1, source_target_pairs={{0,2},{2,0},{4,6},{6,4},{8,10},{10,8},{12,14},{14,12},{16,18},{18,... | collective-permute-start | bytes 786440 | tf_op jit(solution)/shard_map/ppermute | solution.py:122

commit v20 on v19

--- a/solution.py
+++ b/solution.py
@@ -61,7 +61,6 @@
     half = cols // 2
     swap = [(p, p ^ 1) for p in range(n_row)]
     mate3 = lax.ppermute(own3, "row", swap)
-    odd3 = jnp.where(core == 1, own3, mate3)
     even3 = jnp.where(core == 0, own3, mate3)
 
     hw = width // 2
@@ -85,12 +84,12 @@
     is_lower = core == 0
     received = lax.ppermute(current, "row", swap)
     own_h = lax.dynamic_slice(current, (0, core * half), (width, half))
-    early = product_left_t(jnp.where(is_lower, odd3[1], odd3[2]), own_h)
+    early = product_left_t(jnp.where(is_lower, mate3[1], own3[2]), own_h)
     early, received = lax.optimization_barrier((early, received))
     recv_h = lax.dynamic_slice(received, (0, core * half), (width, half))
-    update = early + product_left_t(jnp.where(is_lower, odd3[2], odd3[1]), recv_h)
+    update = early + product_left_t(jnp.where(is_lower, mate3[2], own3[1]), recv_h)
     upper_h = jnp.where(is_lower, recv_h, own_h)
-    level0_out = upper_h - product(odd3[0], update)
+    level0_out = upper_h - product(jnp.where(is_lower, mate3[0], own3[0]), update)
     chain = jnp.where(is_lower, own_h, recv_h) - update
 
     zeros = jnp.zeros_like(tree_factor)

time: 62.8 us -> 64.4 us (1.025)
  matrix products: 8.26 us -> 10.3 us
    select_n x1, other arithmetic: 1.29 us -> 0.1 us  [on_device(): even3 = jnp.where(core == 0, own3, mate3)]
    dot_general x16, matrix products: 6.17 us -> 7.3 us  [product_left_t(): lax.dot_general(left, right, (((0,), (0,)), ((), ())), precision=lax.Prec...]
    dot_general x6, matrix products: 2.08 us -> 3.01 us  [product(): jnp.dot(left, right, precision=lax.Precision.HIGH, preferred_element_type...]
    another operation x2, other arithmetic: 0.15 us -> 1.03 us  [on_device(): own3 = jnp.stack([tree_vectors, tree_factor, tree_joint])]
    ppermute x4, waiting for transfers between devices: 7.15 us -> 6.42 us  [col_gather(): by_shift.append(lax.ppermute(part, 'col', perm))]
  transfers between devices with their start and end apart: 17 -> 17, of which waited for: 9 -> 10; matrix products, arithmetic and copies ran while one was open for 15% -> 16% of each run, Pallas kernels for 0% -> 0%
where the time goes in v20:
time: 64.4 us; the launch traced here: 64 us
  waiting for transfers between devices  27.7 us (43%)
  starting transfers between devices  19.9 us (31%)
  matrix products  10.3 us (16%)
  other arithmetic  3.81 us (6%)
  local copies, waits for them, and re-layouts  1.8 us (3%)
    ppermute x3, waiting for transfers between devices, on_device(): received = lax.ppermute(jnp.where(is_upper, q, chain), 'row', pairs)  16.3 us
    ppermute x3, starting transfers between devices, on_device(): received = lax.ppermute(jnp.where(is_upper, q, chain), 'row', pairs)  8.19 us
    dot_general x16, matrix products, product_left_t(): lax.dot_general(left, right, (((0,), (0,)), ((), ())), precision=lax.Prec...  7.3 us
    ppermute x4, starting transfers between devices, col_gather(): by_shift.append(lax.ppermute(part, 'col', perm))  6.73 us
    ppermute x4, waiting for transfers between devices, col_gather(): by_shift.append(lax.ppermute(part, 'col', perm))  6.42 us
    ppermute x3, starting transfers between devices, on_device(): partner_factors.append(lax.ppermute(half_s, 'row', pairs))  3.86 us
    dot_general x6, matrix products, product(): jnp.dot(left, right, precision=lax.Precision.HIGH, preferred_element_type...  3.01 us
    ppermute x3, waiting for transfers between devices, on_device(): partner_factors.append(lax.ppermute(half_s, 'row', pairs))  2.82 us
  transfers between devices with their start and end apart: 17, of which 10 were waited for; matrix products, arithmetic and copies ran while one was open for 16% of the time, Pallas kernels for 0%

profile of v20, /device:TPU:0, one launch (start us, length us, event | category | flops | bytes accessed | tf_op | source)
XLA Modules:
  0.0 64.0 jit_solution(10606039541118572891)
XLA Ops:
  0.0 3.0 %collective-permute-start = (f32[256,128]{1,0:T(8,128)}, f32[256,128]{1,0:T(8,128)S(1)}, u32[]{:S(2)}, u32[]{:S(2)}) collective-permute-start(f32[256,128]{1,0:T(8,128)} %param.9), channel_id=1, source_target_pairs={{0,1},{1,0},{2,3},{3,2},{4,5},{5,4},{6,7},{7,6},{8,9},{9,8},{10,11... | collective-permute-start | bytes 393224 | tf_op jit(solution)/shard_map/ppermute | solution.py:34
  3.0 3.7 %collective-permute-done = f32[256,128]{1,0:T(8,128)S(1)} collective-permute-done((f32[256,128]{1,0:T(8,128)}, f32[256,128]{1,0:T(8,128)S(1)}, u32[]{:S(2)}, u32[]{:S(2)}) %collective-permute-start) | collective-permute-done | bytes 131104 | tf_op jit(solution)/shard_map/ppermute | solution.py:34
  6.7 0.9 %fusion.50 = (f32[256,128]{1,0:T(8,128)S(1)}, f32[256,128]{1,0:T(8,128)S(1)}) fusion(s32[]{:T(128)S(6)} %select_n.291, f32[1,256,128]{2,1,0:T(8,128)} %bitcast.94, f32[1,256,128]{2,1,0:T(8,128)S(1)} %bitcast.97, s32[]{:T(128)S(6)} %select_n.293), kind=kLoop, calls=%fused_computation.94 | loop fusion | flops 65536 | bytes 524296 | tf_op jit(solution)/shard_map/squeeze | solution.py:36
  7.7 0.9 %copy-done.3 = f32[256,128]{1,0:T(8,128)S(1)} copy-done((f32[256,128]{1,0:T(8,128)S(1)}, f32[256,128]{1,0:T(8,128)}, u32[]{:S(2)}) %copy-start.3) | copy-done | bytes 131096
  8.5 1.7 %collective-permute-start.2 = (f32[256,128]{1,0:T(8,128)S(1)}, f32[256,128]{1,0:T(8,128)S(1)}, u32[]{:S(2)}, u32[]{:S(2)}) collective-permute-start(f32[256,128]{1,0:T(8,128)S(1)} %copy-done.3), channel_id=1, source_target_pairs={{0,1},{1,0},{2,3},{3,2},{4,5},{5,4},{6,7},{7,6},{8,9},{9,8},{10,11... | collective-permute-start | bytes 393224 | tf_op jit(solution)/shard_map/ppermute | solution.py:34
  10.8 0.8 %copy-done.1 = f32[512,128]{1,0:T(8,128)S(1)} copy-done((f32[512,128]{1,0:T(8,128)S(1)}, f32[512,128]{1,0:T(8,128)}, u32[]{:S(2)}) %copy-start.1) | copy-done | bytes 262168
  11.6 1.7 %collective-permute-start.1 = (f32[512,128]{1,0:T(8,128)S(1)}, f32[512,128]{1,0:T(8,128)S(1)}, u32[]{:S(2)}, u32[]{:S(2)}) collective-permute-start(f32[512,128]{1,0:T(8,128)S(1)} %copy-done.1), channel_id=1, source_target_pairs={{0,1},{1,0},{2,3},{3,2},{4,5},{5,4},{6,7},{7,6},{8,9},{9,8},{10,11... | collective-permute-start | bytes 786440 | tf_op jit(solution)/shard_map/ppermute | solution.py:34
  13.5 1.3 %collective-permute-start.6 = (f32[128,256]{1,0:T(8,128)S(1)}, f32[128,256]{1,0:T(8,128)S(1)}, u32[]{:S(2)}, u32[]{:S(2)}) collective-permute-start(f32[128,256]{1,0:T(8,128)S(1)} %slice_select_fusion), channel_id=1, source_target_pairs={{16,0},{18,2},{17,1},{19,3}} | collective-permute-start | bytes 393224 | tf_op jit(solution)/shard_map/ppermute | solution.py:75
  14.8 1.3 %collective-permute-start.5 = (f32[128,256]{1,0:T(8,128)S(1)}, f32[128,256]{1,0:T(8,128)S(1)}, u32[]{:S(2)}, u32[]{:S(2)}) collective-permute-start(f32[128,256]{1,0:T(8,128)S(1)} %slice_select_fusion), channel_id=1, source_target_pairs={{8,0},{10,2},{24,16},{26,18},{9,1},{11,3},{25,17},{27,19}} | collective-permute-start | bytes 393224 | tf_op jit(solution)/shard_map/ppermute | solution.py:75
  16.1 1.7 %collective-permute-done.7 = f32[256,128]{1,0:T(8,128)S(1)} collective-permute-done((f32[256,128]{1,0:T(8,128)S(1)}, f32[256,128]{1,0:T(8,128)S(1)}, u32[]{:S(2)}, u32[]{:S(2)}) %collective-permute-start.7) | collective-permute-done | bytes 131104 | tf_op jit(solution)/shard_map/ppermute | solution.py:34
  17.8 1.3 %collective-permute-start.4 = (f32[128,256]{1,0:T(8,128)S(1)}, f32[128,256]{1,0:T(8,128)S(1)}, u32[]{:S(2)}, u32[]{:S(2)}) collective-permute-start(f32[128,256]{1,0:T(8,128)S(1)} %slice_select_fusion), channel_id=1, source_target_pairs={{4,0},{6,2},{12,8},{14,10},{20,16},{22,18},{28,24},{30,26},{5,1},{... | collective-permute-start | bytes 393224 | tf_op jit(solution)/shard_map/ppermute | solution.py:75
  19.6 0.9 %pad_maximum_fusion.1 = f32[3,256,256]{2,1,0:T(8,128)} fusion(f32[1,256,256]{2,1,0:T(8,128)S(1)} %bitcast.86, f32[1,256,256]{2,1,0:T(8,128)S(1)} %fusion.140, f32[1,256,256]{2,1,0:T(8,128)S(1)} %maximum_select_fusion), kind=kLoop, calls=%fused_computation.14 | loop fusion | flops 393216 | bytes 1572864 | tf_op jit(solution)/shard_map/stack | solution.py:56
  20.6 1.1 %collective-permute-done.1 = f32[512,128]{1,0:T(8,128)S(1)} collective-permute-done((f32[512,128]{1,0:T(8,128)S(1)}, f32[512,128]{1,0:T(8,128)S(1)}, u32[]{:S(2)}, u32[]{:S(2)}) %collective-permute-start.1) | collective-permute-done | bytes 262176 | tf_op jit(solution)/shard_map/ppermute | solution.py:34
  21.8 2.1 %collective-permute-done.5 = f32[128,256]{1,0:T(8,128)S(1)} collective-permute-done((f32[128,256]{1,0:T(8,128)S(1)}, f32[128,256]{1,0:T(8,128)S(1)}, u32[]{:S(2)}, u32[]{:S(2)}) %collective-permute-start.5) | collective-permute-done | bytes 131104 | tf_op jit(solution)/shard_map/ppermute | solution.py:75
  23.9 0.7 %collective-permute-done.4 = f32[128,256]{1,0:T(8,128)S(1)} collective-permute-done((f32[128,256]{1,0:T(8,128)S(1)}, f32[128,256]{1,0:T(8,128)S(1)}, u32[]{:S(2)}, u32[]{:S(2)}) %collective-permute-start.4) | collective-permute-done | bytes 131104 | tf_op jit(solution)/shard_map/ppermute | solution.py:75
  24.6 0.6 fusion.3
  25.3 0.5 fusion.26
  25.8 0.6 convolution_subtract_fusion
  26.6 0.4 collective-permute-start.10
  27.5 0.4 fusion.15
  27.9 0.6 collective-permute-done.9
  28.7 1.5 %select_subtract_fusion.1 = (f32[256,256]{1,0:T(8,128)S(1)}, f32[256,256]{1,0:T(8,128)S(1)}) fusion(f32[256,512]{1,0:T(8,128)} %collective-permute-done.9, s32[]{:T(128)S(6)} %select_n.300, f32[256,512]{1,0:T(8,128)S(1)} %get-tuple-element.39, pred[]{:T(512)S(6)} %eq.52, f32[256,256]{1,0:T(8,128)S(1)} %fusion.15, f32[256,256]{1,0:T(8,128)S(1)} %fusion.32, ...), kind=kOutput, calls=%fused_computation.69 | convolution fusion | flops 100925440 | bytes 2099200 | tf_op jit(solution)/shard_map/dot_general | solution.py:12
  31.3 7.7 %collective-permute-done.11 = f32[256,256]{1,0:T(8,128)S(1)} collective-permute-done((f32[256,256]{1,0:T(8,128)S(1)}, f32[256,256]{1,0:T(8,128)S(1)}, u32[]{:S(2)}, u32[]{:S(2)}) %collective-permute-start.11) | collective-permute-done | bytes 262176 | tf_op jit(solution)/shard_map/ppermute | solution.py:107
  39.1 0.4 broadcast_select_fusion.2
  39.5 3.4 %collective-permute-start.13 = (f32[256,256]{1,0:T(8,128)S(1)}, f32[256,256]{1,0:T(8,128)S(1)}, u32[]{:S(2)}, u32[]{:S(2)}) collective-permute-start(f32[256,256]{1,0:T(8,128)S(1)} %get-tuple-element.55), channel_id=1, source_target_pairs={{0,8},{8,0},{2,10},{10,2},{16,24},{24,16},{18,26},{26,18},{1,9},{9... | collective-permute-start | bytes 786440 | tf_op jit(solution)/shard_map/ppermute | solution.py:107
  44.3 4.7 %collective-permute-done.13 = f32[256,256]{1,0:T(8,128)S(1)} collective-permute-done((f32[256,256]{1,0:T(8,128)S(1)}, f32[256,256]{1,0:T(8,128)S(1)}, u32[]{:S(2)}, u32[]{:S(2)}) %collective-permute-start.13) | collective-permute-done | bytes 262176 | tf_op jit(solution)/shard_map/ppermute | solution.py:107
  49.0 0.4 broadcast_select_fusion.1
  49.4 4.7 %collective-permute-start.15 = (f32[256,256]{1,0:T(8,128)S(1)}, f32[256,256]{1,0:T(8,128)S(1)}, u32[]{:S(2)}, u32[]{:S(2)}) collective-permute-start(f32[256,256]{1,0:T(8,128)S(1)} %get-tuple-element.57), channel_id=1, source_target_pairs={{0,16},{16,0},{2,18},{18,2},{1,17},{17,1},{3,19},{19,3}} | collective-permute-start | bytes 786440 | tf_op jit(solution)/shard_map/ppermute | solution.py:107
  55.5 3.8 %collective-permute-done.15 = f32[256,256]{1,0:T(8,128)S(1)} collective-permute-done((f32[256,256]{1,0:T(8,128)S(1)}, f32[256,256]{1,0:T(8,128)S(1)}, u32[]{:S(2)}, u32[]{:S(2)}) %collective-permute-start.15) | collective-permute-done | bytes 262176 | tf_op jit(solution)/shard_map/ppermute | solution.py:107
  60.0 1.3 %broadcast_select_fusion.5 = (f32[256,256]{1,0:T(8,128)S(1)}, f32[256,256]{1,0:T(8,128)S(1)}) fusion(f32[256,256]{1,0:T(8,128)S(1)} %select_select_fusion, pred[]{:T(512)S(6)} %eq.52, f32[256,256]{1,0:T(8,128)S(1)} %fusion.15, f32[256,256]{1,0:T(8,128)S(1)} %get-tuple-element.52, f32[3,256,256]{2,1,0:T(8,128)S(1)} %collective-permute-done.8, ...), kind=kOutput, calls=%fused_computation.133 | convolution fusion | flops 101187584 | bytes 2361856 | tf_op jit(solution)/shard_map/dot_general | solution.py:8
  61.4 1.5 %collective-permute-done.16 = f32[256,256]{1,0:T(8,128)S(1)} collective-permute-done((f32[256,256]{1,0:T(8,128)S(1)}, f32[256,256]{1,0:T(8,128)S(1)}, u32[]{:S(2)}, u32[]{:S(2)}) %collective-permute-start.16) | collective-permute-done | bytes 262176 | tf_op jit(solution)/shard_map/ppermute | solution.py:121
  63.0 1.1 %pad_maximum_fusion = f32[512,512]{1,0:T(8,128)} fusion(f32[256,512]{1,0:T(8,128)S(1)} %get-tuple-element.40, f32[256,256]{1,0:T(8,128)S(1)} %get-tuple-element.42, f32[256,256]{1,0:T(8,128)S(1)} %get-tuple-element.41), kind=kLoop, calls=%fused_computation.13 | loop fusion | flops 524288 | bytes 2097152 | tf_op jit(solution)/shard_map/concatenate | solution.py:123
  (52 shorter events, 6.7 us)
Async XLA Ops:
  0.0 6.7 %collective-permute-start = (f32[256,128]{1,0:T(8,128)}, f32[256,128]{1,0:T(8,128)S(1)}, u32[]{:S(2)}, u32[]{:S(2)}) collective-permute-start(f32[256,128]{1,0:T(8,128)} %param.9), channel_id=1, source_target_pairs={{0,1},{1,0},{2,3},{3,2},{4,5},{5,4},{6,7},{7,6},{8,9},{9,8},{10,11... | collective-permute-start | bytes 393224 | tf_op jit(solution)/shard_map/ppermute | solution.py:34
  7.6 0.9 %copy-start.3 = (f32[256,128]{1,0:T(8,128)S(1)}, f32[256,128]{1,0:T(8,128)}, u32[]{:S(2)}) copy-start(f32[256,128]{1,0:T(8,128)} %param.7) | copy-start | bytes 393220
  7.6 2.6 %copy-start.2 = (f32[256,128]{1,0:T(8,128)S(1)}, f32[256,128]{1,0:T(8,128)}, u32[]{:S(2)}) copy-start(f32[256,128]{1,0:T(8,128)} %param.8) | copy-start | bytes 393220
  8.5 12.0 %collective-permute-start.2 = (f32[256,128]{1,0:T(8,128)S(1)}, f32[256,128]{1,0:T(8,128)S(1)}, u32[]{:S(2)}, u32[]{:S(2)}) collective-permute-start(f32[256,128]{1,0:T(8,128)S(1)} %copy-done.3), channel_id=1, source_target_pairs={{0,1},{1,0},{2,3},{3,2},{4,5},{5,4},{6,7},{7,6},{8,9},{9,8},{10,11... | collective-permute-start | bytes 393224 | tf_op jit(solution)/shard_map/ppermute | solution.py:34
  10.3 7.5 %collective-permute-start.7 = (f32[256,128]{1,0:T(8,128)S(1)}, f32[256,128]{1,0:T(8,128)S(1)}, u32[]{:S(2)}, u32[]{:S(2)}) collective-permute-start(f32[256,128]{1,0:T(8,128)S(1)} %copy-done.2), channel_id=1, source_target_pairs={{0,1},{1,0},{2,3},{3,2},{4,5},{5,4},{6,7},{7,6},{8,9},{9,8},{10,11... | collective-permute-start | bytes 393224 | tf_op jit(solution)/shard_map/ppermute | solution.py:34
  10.7 1.0 %copy-start.1 = (f32[512,128]{1,0:T(8,128)S(1)}, f32[512,128]{1,0:T(8,128)}, u32[]{:S(2)}) copy-start(f32[512,128]{1,0:T(8,128)} %param.6) | copy-start | bytes 786436
  10.7 2.8 %collective-permute-start.3 = (f32[128,256]{1,0:T(8,128)S(1)}, f32[128,256]{1,0:T(8,128)S(1)}, u32[]{:S(2)}, u32[]{:S(2)}) collective-permute-start(f32[128,256]{1,0:T(8,128)S(1)} %slice.71), channel_id=1, source_target_pairs={{0,2},{2,0},{4,6},{6,4},{8,10},{10,8},{12,14},{14,12},{16,18},{18,... | collective-permute-start | bytes 393224 | tf_op jit(solution)/shard_map/ppermute | solution.py:67
  11.6 10.0 %collective-permute-start.1 = (f32[512,128]{1,0:T(8,128)S(1)}, f32[512,128]{1,0:T(8,128)S(1)}, u32[]{:S(2)}, u32[]{:S(2)}) collective-permute-start(f32[512,128]{1,0:T(8,128)S(1)} %copy-done.1), channel_id=1, source_target_pairs={{0,1},{1,0},{2,3},{3,2},{4,5},{5,4},{6,7},{7,6},{8,9},{9,8},{10,11... | collective-permute-start | bytes 786440 | tf_op jit(solution)/shard_map/ppermute | solution.py:34
  13.5 8.3 %collective-permute-start.6 = (f32[128,256]{1,0:T(8,128)S(1)}, f32[128,256]{1,0:T(8,128)S(1)}, u32[]{:S(2)}, u32[]{:S(2)}) collective-permute-start(f32[128,256]{1,0:T(8,128)S(1)} %slice_select_fusion), channel_id=1, source_target_pairs={{16,0},{18,2},{17,1},{19,3}} | collective-permute-start | bytes 393224 | tf_op jit(solution)/shard_map/ppermute | solution.py:75
  14.8 9.1 %collective-permute-start.5 = (f32[128,256]{1,0:T(8,128)S(1)}, f32[128,256]{1,0:T(8,128)S(1)}, u32[]{:S(2)}, u32[]{:S(2)}) collective-permute-start(f32[128,256]{1,0:T(8,128)S(1)} %slice_select_fusion), channel_id=1, source_target_pairs={{8,0},{10,2},{24,16},{26,18},{9,1},{11,3},{25,17},{27,19}} | collective-permute-start | bytes 393224 | tf_op jit(solution)/shard_map/ppermute | solution.py:75
  17.8 6.8 %collective-permute-start.4 = (f32[128,256]{1,0:T(8,128)S(1)}, f32[128,256]{1,0:T(8,128)S(1)}, u32[]{:S(2)}, u32[]{:S(2)}) collective-permute-start(f32[128,256]{1,0:T(8,128)S(1)} %slice_select_fusion), channel_id=1, source_target_pairs={{4,0},{6,2},{12,8},{14,10},{20,16},{22,18},{28,24},{30,26},{5,1},{... | collective-permute-start | bytes 393224 | tf_op jit(solution)/shard_map/ppermute | solution.py:75
  20.5 7.0 %collective-permute-start.8 = (f32[3,256,256]{2,1,0:T(8,128)}, f32[3,256,256]{2,1,0:T(8,128)S(1)}, u32[]{:S(2)}, u32[]{:S(2)}) collective-permute-start(f32[3,256,256]{2,1,0:T(8,128)} %pad_maximum_fusion.1), channel_id=1, source_target_pairs={{0,2},{2,0},{4,6},{6,4},{8,10},{10,8},{12,14},{14,12},{16,18},{18,... | collective-permute-start | bytes 2359304 | tf_op jit(solution)/shard_map/ppermute | solution.py:63
  21.6 3.0 %copy-start = (f32[512,512]{1,0:T(8,128)S(1)}, f32[512,512]{1,0:T(8,128)}, u32[]{:S(2)}) copy-start(f32[512,512]{1,0:T(8,128)} %param.5) | copy-start | bytes 3145732
  26.4 2.1 %collective-permute-start.9 = (f32[256,512]{1,0:T(8,128)S(1)}, f32[256,512]{1,0:T(8,128)}, u32[]{:S(2)}, u32[]{:S(2)}) collective-permute-start(f32[256,512]{1,0:T(8,128)S(1)} %get-tuple-element.39), channel_id=1, source_target_pairs={{0,2},{2,0},{4,6},{6,4},{8,10},{10,8},{12,14},{14,12},{16,18},{18,... | collective-permute-start | bytes 1572872 | tf_op jit(solution)/shard_map/ppermute | solution.py:85
  26.6 4.1 %collective-permute-start.10 = (f32[128,256]{1,0:T(8,128)S(1)}, f32[128,256]{1,0:T(8,128)S(1)}, u32[]{:S(2)}, u32[]{:S(2)}) collective-permute-start(f32[128,256]{1,0:T(8,128)S(1)} %collective-permute-done.4), channel_id=1, source_target_pairs={{0,2},{2,0},{4,6},{6,4},{8,10},{10,8},{12,14},{14,12},{16,18},{18,... | collective-permute-start | bytes 393224 | tf_op jit(solution)/shard_map/ppermute | solution.py:109
  27.0 16.3 %collective-permute-start.12 = (f32[128,256]{1,0:T(8,128)S(1)}, f32[128,256]{1,0:T(8,128)S(1)}, u32[]{:S(2)}, u32[]{:S(2)}) collective-permute-start(f32[128,256]{1,0:T(8,128)S(1)} %collective-permute-done.5), channel_id=1, source_target_pairs={{0,2},{2,0},{4,6},{6,4},{8,10},{10,8},{12,14},{14,12},{16,18},{18,... | collective-permute-start | bytes 393224 | tf_op jit(solution)/shard_map/ppermute | solution.py:109
  27.2 27.4 %collective-permute-start.14 = (f32[128,256]{1,0:T(8,128)S(1)}, f32[128,256]{1,0:T(8,128)S(1)}, u32[]{:S(2)}, u32[]{:S(2)}) collective-permute-start(f32[128,256]{1,0:T(8,128)S(1)} %collective-permute-done.6), channel_id=1, source_target_pairs={{0,2},{2,0},{4,6},{6,4},{8,10},{10,8},{12,14},{14,12},{16,18},{18,... | collective-permute-start | bytes 393224 | tf_op jit(solution)/shard_map/ppermute | solution.py:109
  30.6 8.5 %collective-permute-start.11 = (f32[256,256]{1,0:T(8,128)S(1)}, f32[256,256]{1,0:T(8,128)S(1)}, u32[]{:S(2)}, u32[]{:S(2)}) collective-permute-start(f32[256,256]{1,0:T(8,128)S(1)} %get-tuple-element.53), channel_id=1, source_target_pairs={{0,4},{4,0},{2,6},{6,2},{8,12},{12,8},{10,14},{14,10},{16,20},{20,... | collective-permute-start | bytes 786440 | tf_op jit(solution)/shard_map/ppermute | solution.py:107
  39.5 9.5 %collective-permute-start.13 = (f32[256,256]{1,0:T(8,128)S(1)}, f32[256,256]{1,0:T(8,128)S(1)}, u32[]{:S(2)}, u32[]{:S(2)}) collective-permute-start(f32[256,256]{1,0:T(8,128)S(1)} %get-tuple-element.55), channel_id=1, source_target_pairs={{0,8},{8,0},{2,10},{10,2},{16,24},{24,16},{18,26},{26,18},{1,9},{9... | collective-permute-start | bytes 786440 | tf_op jit(solution)/shard_map/ppermute | solution.py:107
  49.4 9.9 %collective-permute-start.15 = (f32[256,256]{1,0:T(8,128)S(1)}, f32[256,256]{1,0:T(8,128)S(1)}, u32[]{:S(2)}, u32[]{:S(2)}) collective-permute-start(f32[256,256]{1,0:T(8,128)S(1)} %get-tuple-element.57), channel_id=1, source_target_pairs={{0,16},{16,0},{2,18},{18,2},{1,17},{17,1},{3,19},{19,3}} | collective-permute-start | bytes 786440 | tf_op jit(solution)/shard_map/ppermute | solution.py:107
  61.3 1.6 %collective-permute-start.16 = (f32[256,256]{1,0:T(8,128)S(1)}, f32[256,256]{1,0:T(8,128)S(1)}, u32[]{:S(2)}, u32[]{:S(2)}) collective-permute-start(f32[256,256]{1,0:T(8,128)S(1)} %get-tuple-element.59), channel_id=1, source_target_pairs={{0,2},{2,0},{4,6},{6,4},{8,10},{10,8},{12,14},{14,12},{16,18},{18,... | collective-permute-start | bytes 786440 | tf_op jit(solution)/shard_map/ppermute | solution.py:121

commit v21 on v19

--- a/solution.py
+++ b/solution.py
@@ -75,12 +75,15 @@
             pairs += [(i + step, i), (i + step + 1, i + 1)]
         partner_factors.append(lax.ppermute(half_s, "row", pairs))
 
-    leaf_full, leaf_tri, partner_factors = lax.optimization_barrier((leaf_full, leaf_tri, partner_factors))
+    mates_of = [lax.ppermute(got, "row", swap) for got in partner_factors]
+    leaf_full, leaf_tri, partner_factors, mates_of = lax.optimization_barrier(
+        (leaf_full, leaf_tri, partner_factors, mates_of)
+    )
     leaf_vectors = unit_lower(leaf_full)
     leaf_factor = jnp.triu(leaf_tri)
     leaf_w = product_left_t(leaf_factor, product_left_t(leaf_vectors, slab))
-    leafed = slab - product(leaf_vectors, leaf_w)
-    current = leafed[:width]
+    current = slab[:width] - product(leaf_vectors[:width], leaf_w)
+    remainder = slab[width:] - product(leaf_vectors[width:], leaf_w)
 
     is_lower = core == 0
     received = lax.ppermute(current, "row", swap)
@@ -107,7 +110,7 @@
         q = product_left_t(jnp.where(is_upper, even3[2], zeros), chain)
         received = lax.ppermute(jnp.where(is_upper, q, chain), "row", pairs)
         mine = partner_factors[level - 1]
-        mates = lax.ppermute(mine, "row", swap)
+        mates = mates_of[level - 1]
         top_rows = jnp.where(is_lower & (core == 0), mine, jnp.where(is_lower, mates, 0.0))
         bottom_rows = jnp.where(is_lower & (core == 0), mates, jnp.where(is_lower, mine, 0.0))
         own_part = product_left_t(top_rows, chain[:hw]) + product_left_t(bottom_rows, chain[hw:])
@@ -121,7 +124,7 @@
     give = jnp.where(core == 0, level0_out, base_out)
     got = lax.ppermute(give, "row", swap)
     top = jnp.concatenate([jnp.where(core == 0, keep, got), jnp.where(core == 0, got, keep)], axis=1)
-    return jnp.concatenate([top, leafed[width:]], axis=0)
+    return jnp.concatenate([top, remainder], axis=0)
 
 
 def solution(mesh):

time: 62.8 us -> 67.2 us (1.070)
  matrix products: 8.26 us -> 12.2 us
  other arithmetic: 4.13 us -> 5.05 us
  waiting for transfers between devices: 27.8 us -> 26.9 us
    dot_general x16, matrix products: 6.17 us -> 9.02 us  [product_left_t(): lax.dot_general(left, right, (((0,), (0,)), ((), ())), precision=lax.Prec...]
    ppermute x4, waiting for transfers between devices: 7.15 us -> 5.37 us  [col_gather(): by_shift.append(lax.ppermute(part, 'col', perm))]
    ppermute x3, waiting for transfers between devices: 2.82 us -> 3.98 us  [on_device(): partner_factors.append(lax.ppermute(half_s, 'row', pairs))]
    dot_general x6 -> x7, matrix products: 2.08 us -> 3.19 us  [product(): jnp.dot(left, right, precision=lax.Precision.HIGH, preferred_element_type...]
    ppermute x3, starting transfers between devices: 0.93 us -> 0.01 us  [on_device(): mates_of = [lax.ppermute(got, 'row', swap) for got in partner_factors]]
    another operation x2, other arithmetic: 0.15 us -> 1.03 us  [on_device(): own3 = jnp.stack([tree_vectors, tree_factor, tree_joint])]
    ppermute x3, waiting for transfers between devices: 0.01 us -> 0.76 us  [on_device(): mates_of = [lax.ppermute(got, 'row', swap) for got in partner_factors]]
    unnamed x8 -> x24, local copies, waits for them, and re-layouts: 1.72 us -> 2.24 us
  transfers between devices with their start and end apart: 17 -> 17, of which waited for: 9 -> 10; matrix products, arithmetic and copies ran while one was open for 15% -> 15% of each run, Pallas kernels for 0% -> 0%
where the time goes in v21:
time: 67.2 us; the launch traced here: 66.8 us
  waiting for transfers between devices  26.9 us (40%)
  starting transfers between devices  19.9 us (30%)
  matrix products  12.2 us (18%)
  other arithmetic  5.05 us (8%)
  local copies, waits for them, and re-layouts  2.25 us (3%)
    ppermute x3, waiting for transfers between devices, on_device(): received = lax.ppermute(jnp.where(is_upper, q, chain), 'row', pairs)  15.6 us
    dot_general x16, matrix products, product_left_t(): lax.dot_general(left, right, (((0,), (0,)), ((), ())), precision=lax.Prec...  9.02 us
    ppermute x3, starting transfers between devices, on_device(): received = lax.ppermute(jnp.where(is_upper, q, chain), 'row', pairs)  8.73 us
    ppermute x4, starting transfers between devices, col_gather(): by_shift.append(lax.ppermute(part, 'col', perm))  6.73 us
    ppermute x4, waiting for transfers between devices, col_gather(): by_shift.append(lax.ppermute(part, 'col', perm))  5.37 us
    ppermute x3, waiting for transfers between devices, on_device(): partner_factors.append(lax.ppermute(half_s, 'row', pairs))  3.98 us
    ppermute x3, starting transfers between devices, on_device(): partner_factors.append(lax.ppermute(half_s, 'row', pairs))  3.86 us
    dot_general x7, matrix products, product(): jnp.dot(left, right, precision=lax.Precision.HIGH, preferred_element_type...  3.19 us
  transfers between devices with their start and end apart: 17, of which 10 were waited for; matrix products, arithmetic and copies ran while one was open for 15% of the time, Pallas kernels for 0%

profile of v21, /device:TPU:0, one launch (start us, length us, event | category | flops | bytes accessed | tf_op | source)
XLA Modules:
  0.0 66.8 jit_solution(17925862921982573044)
XLA Ops:
  0.0 3.0 %collective-permute-start = (f32[256,128]{1,0:T(8,128)}, f32[256,128]{1,0:T(8,128)S(1)}, u32[]{:S(2)}, u32[]{:S(2)}) collective-permute-start(f32[256,128]{1,0:T(8,128)} %param.9), channel_id=1, source_target_pairs={{0,1},{1,0},{2,3},{3,2},{4,5},{5,4},{6,7},{7,6},{8,9},{9,8},{10,11... | collective-permute-start | bytes 393224 | tf_op jit(solution)/shard_map/ppermute | solution.py:34
  3.0 3.7 %collective-permute-done = f32[256,128]{1,0:T(8,128)S(1)} collective-permute-done((f32[256,128]{1,0:T(8,128)}, f32[256,128]{1,0:T(8,128)S(1)}, u32[]{:S(2)}, u32[]{:S(2)}) %collective-permute-start) | collective-permute-done | bytes 131104 | tf_op jit(solution)/shard_map/ppermute | solution.py:34
  6.7 0.9 %fusion.48 = (f32[256,128]{1,0:T(8,128)S(1)}, f32[256,128]{1,0:T(8,128)S(1)}) fusion(s32[]{:T(128)S(6)} %select_n.301, f32[1,256,128]{2,1,0:T(8,128)} %bitcast.86, f32[1,256,128]{2,1,0:T(8,128)S(1)} %bitcast.89, s32[]{:T(128)S(6)} %select_n.303), kind=kLoop, calls=%fused_computation.98 | loop fusion | flops 65536 | bytes 524296 | tf_op jit(solution)/shard_map/squeeze | solution.py:36
  7.7 0.9 %copy-done.11 = f32[256,128]{1,0:T(8,128)S(1)} copy-done((f32[256,128]{1,0:T(8,128)S(1)}, f32[256,128]{1,0:T(8,128)}, u32[]{:S(2)}) %copy-start.11) | copy-done | bytes 131096
  8.5 1.7 %collective-permute-start.2 = (f32[256,128]{1,0:T(8,128)S(1)}, f32[256,128]{1,0:T(8,128)S(1)}, u32[]{:S(2)}, u32[]{:S(2)}) collective-permute-start(f32[256,128]{1,0:T(8,128)S(1)} %copy-done.11), channel_id=1, source_target_pairs={{0,1},{1,0},{2,3},{3,2},{4,5},{5,4},{6,7},{7,6},{8,9},{9,8},{10,11... | collective-permute-start | bytes 393224 | tf_op jit(solution)/shard_map/ppermute | solution.py:34
  10.8 0.8 %copy-done.9 = f32[512,128]{1,0:T(8,128)S(1)} copy-done((f32[512,128]{1,0:T(8,128)S(1)}, f32[512,128]{1,0:T(8,128)}, u32[]{:S(2)}) %copy-start.9) | copy-done | bytes 262168
  11.6 1.7 %collective-permute-start.1 = (f32[512,128]{1,0:T(8,128)S(1)}, f32[512,128]{1,0:T(8,128)S(1)}, u32[]{:S(2)}, u32[]{:S(2)}) collective-permute-start(f32[512,128]{1,0:T(8,128)S(1)} %copy-done.9), channel_id=1, source_target_pairs={{0,1},{1,0},{2,3},{3,2},{4,5},{5,4},{6,7},{7,6},{8,9},{9,8},{10,11... | collective-permute-start | bytes 786440 | tf_op jit(solution)/shard_map/ppermute | solution.py:34
  13.5 1.3 %collective-permute-start.6 = (f32[128,256]{1,0:T(8,128)S(1)}, f32[128,256]{1,0:T(8,128)S(1)}, u32[]{:S(2)}, u32[]{:S(2)}) collective-permute-start(f32[128,256]{1,0:T(8,128)S(1)} %slice_select_fusion), channel_id=1, source_target_pairs={{16,0},{18,2},{17,1},{19,3}} | collective-permute-start | bytes 393224 | tf_op jit(solution)/shard_map/ppermute | solution.py:76
  14.8 1.3 %collective-permute-start.5 = (f32[128,256]{1,0:T(8,128)S(1)}, f32[128,256]{1,0:T(8,128)S(1)}, u32[]{:S(2)}, u32[]{:S(2)}) collective-permute-start(f32[128,256]{1,0:T(8,128)S(1)} %slice_select_fusion), channel_id=1, source_target_pairs={{8,0},{10,2},{24,16},{26,18},{9,1},{11,3},{25,17},{27,19}} | collective-permute-start | bytes 393224 | tf_op jit(solution)/shard_map/ppermute | solution.py:76
  16.1 1.7 %collective-permute-done.10 = f32[256,128]{1,0:T(8,128)S(1)} collective-permute-done((f32[256,128]{1,0:T(8,128)S(1)}, f32[256,128]{1,0:T(8,128)S(1)}, u32[]{:S(2)}, u32[]{:S(2)}) %collective-permute-start.10) | collective-permute-done | bytes 131104 | tf_op jit(solution)/shard_map/ppermute | solution.py:34
  17.8 1.3 %collective-permute-start.4 = (f32[128,256]{1,0:T(8,128)S(1)}, f32[128,256]{1,0:T(8,128)S(1)}, u32[]{:S(2)}, u32[]{:S(2)}) collective-permute-start(f32[128,256]{1,0:T(8,128)S(1)} %slice_select_fusion), channel_id=1, source_target_pairs={{4,0},{6,2},{12,8},{14,10},{20,16},{22,18},{28,24},{30,26},{5,1},{... | collective-permute-start | bytes 393224 | tf_op jit(solution)/shard_map/ppermute | solution.py:76
  19.6 0.9 %pad_maximum_fusion.1 = f32[3,256,256]{2,1,0:T(8,128)} fusion(f32[1,256,256]{2,1,0:T(8,128)S(1)} %convolution_bitcast_fusion, f32[1,256,256]{2,1,0:T(8,128)S(1)} %fusion.132, f32[1,256,256]{2,1,0:T(8,128)S(1)} %maximum_select_fusion), kind=kLoop, calls=%fused_computation.16 | loop fusion | flops 393216 | bytes 1572864 | tf_op jit(solution)/shard_map/stack | solution.py:56
  20.6 0.7 %collective-permute-done.6 = f32[128,256]{1,0:T(8,128)S(1)} collective-permute-done((f32[128,256]{1,0:T(8,128)S(1)}, f32[128,256]{1,0:T(8,128)S(1)}, u32[]{:S(2)}, u32[]{:S(2)}) %collective-permute-start.6) | collective-permute-done | bytes 131104 | tf_op jit(solution)/shard_map/ppermute | solution.py:76
  21.3 2.6 %collective-permute-done.5 = f32[128,256]{1,0:T(8,128)S(1)} collective-permute-done((f32[128,256]{1,0:T(8,128)S(1)}, f32[128,256]{1,0:T(8,128)S(1)}, u32[]{:S(2)}, u32[]{:S(2)}) %collective-permute-start.5) | collective-permute-done | bytes 131104 | tf_op jit(solution)/shard_map/ppermute | solution.py:76
  23.9 0.7 %collective-permute-done.4 = f32[128,256]{1,0:T(8,128)S(1)} collective-permute-done((f32[128,256]{1,0:T(8,128)S(1)}, f32[128,256]{1,0:T(8,128)S(1)}, u32[]{:S(2)}, u32[]{:S(2)}) %collective-permute-start.4) | collective-permute-done | bytes 131104 | tf_op jit(solution)/shard_map/ppermute | solution.py:76
  24.8 0.5 copy-done.5
  25.3 0.8 %collective-permute-done.7 = f32[128,256]{1,0:T(8,128)} collective-permute-done((f32[128,256]{1,0:T(8,128)S(1)}, f32[128,256]{1,0:T(8,128)}, u32[]{:S(2)}, u32[]{:S(2)}) %collective-permute-start.7) | collective-permute-done | bytes 131104 | tf_op jit(solution)/shard_map/ppermute | solution.py:78
  26.1 0.6 fusion.117
  26.8 0.5 fusion.27
  28.1 1.3 %broadcast_select_fusion = (f32[3,256,256]{2,1,0:T(8,128)S(1)}, f32[3,256,256]{2,1,0:T(8,128)S(1)}) fusion(f32[3,256,256]{2,1,0:T(8,128)} %collective-permute-done.11, pred[]{:T(512)S(6)} %eq.55, f32[1,256,256]{2,1,0:T(8,128)S(1)} %convolution_bitcast_fusion, f32[1,256,256]{2,1,0:T(8,128)S(1)} %fusion.132, f32[1,256,256]{2,1,0:T(8,128)S(1)} %maximum_select_fusion, ...), kind=kLoop, calls=%fused_computation.25 | loop fusion | flops 786432 | bytes 3145730 | tf_op jit(solution)/shard_map/jit(_where)/select_n | solution.py:65
  29.8 1.4 %select_subtract_fusion.1 = (f32[256,256]{1,0:T(8,128)S(1)}, f32[256,256]{1,0:T(8,128)S(1)}) fusion(f32[256,512]{1,0:T(8,128)} %collective-permute-done.12, s32[]{:T(128)S(6)} %select_n.310, f32[256,512]{1,0:T(8,128)S(1)} %convolution_subtract_fusion.1, pred[]{:T(512)S(6)} %eq.55, f32[256,256]{1,0:T(8,128)S(1)} %fusion.20, ...), kind=kOutput, calls=%fused_computation.73 | convolution fusion | flops 100925440 | bytes 2099200 | tf_op jit(solution)/shard_map/dot_general | solution.py:12
  31.7 0.6 collective-permute-start.13
  32.3 1.2 %fusion.55 = f32[256,256]{1,0:T(8,128)S(1)} fusion(f32[256,256]{1,0:T(8,128)S(1)} %get-tuple-element.57, f32[128,256]{1,0:T(8,128)} %collective-permute-done.7, f32[128,256]{1,0:T(8,128)S(1)} %copy-done.6, pred[]{:T(512)S(6)} %eq.59, pred[]{:T(512)S(6)} %and.51), kind=kOutput, calls=%fused_computation.105 | convolution fusion | flops 50397184 | bytes 655362 | tf_op jit(solution)/shard_map/dot_general | solution.py:12
  33.5 1.2 %convolution_add_fusion.5 = f32[256,256]{1,0:T(8,128)S(1)} fusion(f32[256,256]{1,0:T(8,128)S(1)} %fusion.55, f32[256,256]{1,0:T(8,128)S(1)} %get-tuple-element.57, f32[128,256]{1,0:T(8,128)S(1)} %copy-done.6, f32[128,256]{1,0:T(8,128)} %collective-permute-done.7, pred[]{:T(512)S(6)} %eq.59, pred[]{:T(512)S(6)} %and.51), kind=kOutput, calls=%fused_computation.13 | convolution fusion | flops 50462720 | bytes 917506 | tf_op jit(solution)/shard_map/dot_general | solution.py:12
  34.7 5.6 %collective-permute-done.13 = f32[256,256]{1,0:T(8,128)S(1)} collective-permute-done((f32[256,256]{1,0:T(8,128)S(1)}, f32[256,256]{1,0:T(8,128)S(1)}, u32[]{:S(2)}, u32[]{:S(2)}) %collective-permute-start.13) | collective-permute-done | bytes 262176 | tf_op jit(solution)/shard_map/ppermute | solution.py:111
  41.3 3.4 %collective-permute-start.14 = (f32[256,256]{1,0:T(8,128)S(1)}, f32[256,256]{1,0:T(8,128)S(1)}, u32[]{:S(2)}, u32[]{:S(2)}) collective-permute-start(f32[256,256]{1,0:T(8,128)S(1)} %get-tuple-element.61), channel_id=1, source_target_pairs={{0,8},{8,0},{2,10},{10,2},{16,24},{24,16},{18,26},{26,18},{1,9},{9... | collective-permute-start | bytes 786440 | tf_op jit(solution)/shard_map/ppermute | solution.py:111
  45.6 5.4 %collective-permute-done.14 = f32[256,256]{1,0:T(8,128)S(1)} collective-permute-done((f32[256,256]{1,0:T(8,128)S(1)}, f32[256,256]{1,0:T(8,128)S(1)}, u32[]{:S(2)}, u32[]{:S(2)}) %collective-permute-start.14) | collective-permute-done | bytes 262176 | tf_op jit(solution)/shard_map/ppermute | solution.py:111
  51.9 4.7 %collective-permute-start.15 = (f32[256,256]{1,0:T(8,128)S(1)}, f32[256,256]{1,0:T(8,128)S(1)}, u32[]{:S(2)}, u32[]{:S(2)}) collective-permute-start(f32[256,256]{1,0:T(8,128)S(1)} %get-tuple-element.63), channel_id=1, source_target_pairs={{0,16},{16,0},{2,18},{18,2},{1,17},{17,1},{3,19},{19,3}} | collective-permute-start | bytes 786440 | tf_op jit(solution)/shard_map/ppermute | solution.py:111
  57.6 4.6 %collective-permute-done.15 = f32[256,256]{1,0:T(8,128)S(1)} collective-permute-done((f32[256,256]{1,0:T(8,128)S(1)}, f32[256,256]{1,0:T(8,128)S(1)}, u32[]{:S(2)}, u32[]{:S(2)}) %collective-permute-start.15) | collective-permute-done | bytes 262176 | tf_op jit(solution)/shard_map/ppermute | solution.py:111
  62.8 1.2 %broadcast_select_fusion.7 = (f32[256,256]{1,0:T(8,128)S(1)}, f32[256,256]{1,0:T(8,128)S(1)}) fusion(f32[256,256]{1,0:T(8,128)S(1)} %select_select_fusion, pred[]{:T(512)S(6)} %eq.55, f32[256,256]{1,0:T(8,128)S(1)} %fusion.20, f32[256,256]{1,0:T(8,128)S(1)} %get-tuple-element.58, f32[3,256,256]{2,1,0:T(8,128)S(1)} %get-tuple-element.46, ...), kind=kOutput, calls=%fused_computation.138 | convolution fusion | flops 100925440 | bytes 2097157 | tf_op jit(solution)/shard_map/dot_general | solution.py:8
  64.6 1.1 %collective-permute-done.16 = f32[256,256]{1,0:T(8,128)S(1)} collective-permute-done((f32[256,256]{1,0:T(8,128)S(1)}, f32[256,256]{1,0:T(8,128)S(1)}, u32[]{:S(2)}, u32[]{:S(2)}) %collective-permute-start.16) | collective-permute-done | bytes 262176 | tf_op jit(solution)/shard_map/ppermute | solution.py:125
  65.8 1.1 %pad_maximum_fusion = f32[512,512]{1,0:T(8,128)} fusion(f32[256,512]{1,0:T(8,128)S(1)} %convolution_subtract_fusion, f32[256,256]{1,0:T(8,128)S(1)} %get-tuple-element.48, f32[256,256]{1,0:T(8,128)S(1)} %get-tuple-element.47), kind=kLoop, calls=%fused_computation.15 | loop fusion | flops 524288 | bytes 2097152 | tf_op jit(solution)/shard_map/concatenate | solution.py:127
  (69 shorter events, 7.7 us)
Async XLA Ops:
  0.0 6.7 %collective-permute-start = (f32[256,128]{1,0:T(8,128)}, f32[256,128]{1,0:T(8,128)S(1)}, u32[]{:S(2)}, u32[]{:S(2)}) collective-permute-start(f32[256,128]{1,0:T(8,128)} %param.9), channel_id=1, source_target_pairs={{0,1},{1,0},{2,3},{3,2},{4,5},{5,4},{6,7},{7,6},{8,9},{9,8},{10,11... | collective-permute-start | bytes 393224 | tf_op jit(solution)/shard_map/ppermute | solution.py:34
  7.6 0.9 %copy-start.11 = (f32[256,128]{1,0:T(8,128)S(1)}, f32[256,128]{1,0:T(8,128)}, u32[]{:S(2)}) copy-start(f32[256,128]{1,0:T(8,128)} %param.7) | copy-start | bytes 393220
  7.6 2.6 %copy-start.10 = (f32[256,128]{1,0:T(8,128)S(1)}, f32[256,128]{1,0:T(8,128)}, u32[]{:S(2)}) copy-start(f32[256,128]{1,0:T(8,128)} %param.8) | copy-start | bytes 393220
  8.5 12.0 %collective-permute-start.2 = (f32[256,128]{1,0:T(8,128)S(1)}, f32[256,128]{1,0:T(8,128)S(1)}, u32[]{:S(2)}, u32[]{:S(2)}) collective-permute-start(f32[256,128]{1,0:T(8,128)S(1)} %copy-done.11), channel_id=1, source_target_pairs={{0,1},{1,0},{2,3},{3,2},{4,5},{5,4},{6,7},{7,6},{8,9},{9,8},{10,11... | collective-permute-start | bytes 393224 | tf_op jit(solution)/shard_map/ppermute | solution.py:34
  10.3 7.5 %collective-permute-start.10 = (f32[256,128]{1,0:T(8,128)S(1)}, f32[256,128]{1,0:T(8,128)S(1)}, u32[]{:S(2)}, u32[]{:S(2)}) collective-permute-start(f32[256,128]{1,0:T(8,128)S(1)} %copy-done.10), channel_id=1, source_target_pairs={{0,1},{1,0},{2,3},{3,2},{4,5},{5,4},{6,7},{7,6},{8,9},{9,8},{10,11... | collective-permute-start | bytes 393224 | tf_op jit(solution)/shard_map/ppermute | solution.py:34
  10.7 1.0 %copy-start.9 = (f32[512,128]{1,0:T(8,128)S(1)}, f32[512,128]{1,0:T(8,128)}, u32[]{:S(2)}) copy-start(f32[512,128]{1,0:T(8,128)} %param.6) | copy-start | bytes 786436
  10.7 2.8 %collective-permute-start.3 = (f32[128,256]{1,0:T(8,128)S(1)}, f32[128,256]{1,0:T(8,128)S(1)}, u32[]{:S(2)}, u32[]{:S(2)}) collective-permute-start(f32[128,256]{1,0:T(8,128)S(1)} %slice.81), channel_id=1, source_target_pairs={{0,2},{2,0},{4,6},{6,4},{8,10},{10,8},{12,14},{14,12},{16,18},{18,... | collective-permute-start | bytes 393224 | tf_op jit(solution)/shard_map/ppermute | solution.py:68
  11.6 13.0 %collective-permute-start.1 = (f32[512,128]{1,0:T(8,128)S(1)}, f32[512,128]{1,0:T(8,128)S(1)}, u32[]{:S(2)}, u32[]{:S(2)}) collective-permute-start(f32[512,128]{1,0:T(8,128)S(1)} %copy-done.9), channel_id=1, source_target_pairs={{0,1},{1,0},{2,3},{3,2},{4,5},{5,4},{6,7},{7,6},{8,9},{9,8},{10,11... | collective-permute-start | bytes 786440 | tf_op jit(solution)/shard_map/ppermute | solution.py:34
  13.5 7.8 %collective-permute-start.6 = (f32[128,256]{1,0:T(8,128)S(1)}, f32[128,256]{1,0:T(8,128)S(1)}, u32[]{:S(2)}, u32[]{:S(2)}) collective-permute-start(f32[128,256]{1,0:T(8,128)S(1)} %slice_select_fusion), channel_id=1, source_target_pairs={{16,0},{18,2},{17,1},{19,3}} | collective-permute-start | bytes 393224 | tf_op jit(solution)/shard_map/ppermute | solution.py:76
  14.8 9.1 %collective-permute-start.5 = (f32[128,256]{1,0:T(8,128)S(1)}, f32[128,256]{1,0:T(8,128)S(1)}, u32[]{:S(2)}, u32[]{:S(2)}) collective-permute-start(f32[128,256]{1,0:T(8,128)S(1)} %slice_select_fusion), channel_id=1, source_target_pairs={{8,0},{10,2},{24,16},{26,18},{9,1},{11,3},{25,17},{27,19}} | collective-permute-start | bytes 393224 | tf_op jit(solution)/shard_map/ppermute | solution.py:76
  17.8 6.8 %collective-permute-start.4 = (f32[128,256]{1,0:T(8,128)S(1)}, f32[128,256]{1,0:T(8,128)S(1)}, u32[]{:S(2)}, u32[]{:S(2)}) collective-permute-start(f32[128,256]{1,0:T(8,128)S(1)} %slice_select_fusion), channel_id=1, source_target_pairs={{4,0},{6,2},{12,8},{14,10},{20,16},{22,18},{28,24},{30,26},{5,1},{... | collective-permute-start | bytes 393224 | tf_op jit(solution)/shard_map/ppermute | solution.py:76
  20.5 7.6 %collective-permute-start.11 = (f32[3,256,256]{2,1,0:T(8,128)}, f32[3,256,256]{2,1,0:T(8,128)}, u32[]{:S(2)}, u32[]{:S(2)}) collective-permute-start(f32[3,256,256]{2,1,0:T(8,128)} %pad_maximum_fusion.1), channel_id=1, source_target_pairs={{0,2},{2,0},{4,6},{6,4},{8,10},{10,8},{12,14},{14,12},{16,18},{18,... | collective-permute-start | bytes 2359304 | tf_op jit(solution)/shard_map/ppermute | solution.py:63
  21.3 4.0 %collective-permute-start.9 = (f32[128,256]{1,0:T(8,128)S(1)}, f32[128,256]{1,0:T(8,128)S(1)}, u32[]{:S(2)}, u32[]{:S(2)}) collective-permute-start(f32[128,256]{1,0:T(8,128)S(1)} %collective-permute-done.6), channel_id=1, source_target_pairs={{0,2},{2,0},{4,6},{6,4},{8,10},{10,8},{12,14},{14,12},{16,18},{18,... | collective-permute-start | bytes 393224 | tf_op jit(solution)/shard_map/ppermute | solution.py:78
  23.9 0.9 %copy-start.1 = (f32[128,256]{1,0:T(8,128)}, f32[128,256]{1,0:T(8,128)S(1)}, u32[]{:S(2)}) copy-start(f32[128,256]{1,0:T(8,128)S(1)} %collective-permute-done.5) | copy-start | bytes 393220
  23.9 1.4 %collective-permute-start.8 = (f32[128,256]{1,0:T(8,128)S(1)}, f32[128,256]{1,0:T(8,128)S(1)}, u32[]{:S(2)}, u32[]{:S(2)}) collective-permute-start(f32[128,256]{1,0:T(8,128)S(1)} %collective-permute-done.5), channel_id=1, source_target_pairs={{0,2},{2,0},{4,6},{6,4},{8,10},{10,8},{12,14},{14,12},{16,18},{18,... | collective-permute-start | bytes 393224 | tf_op jit(solution)/shard_map/ppermute | solution.py:78
  24.6 0.6 copy-start.5
  24.6 1.5 %collective-permute-start.7 = (f32[128,256]{1,0:T(8,128)S(1)}, f32[128,256]{1,0:T(8,128)}, u32[]{:S(2)}, u32[]{:S(2)}) collective-permute-start(f32[128,256]{1,0:T(8,128)S(1)} %collective-permute-done.4), channel_id=1, source_target_pairs={{0,2},{2,0},{4,6},{6,4},{8,10},{10,8},{12,14},{14,12},{16,18},{18,... | collective-permute-start | bytes 393224 | tf_op jit(solution)/shard_map/ppermute | solution.py:78
  24.6 1.5 %copy-start = (f32[512,512]{1,0:T(8,128)S(1)}, f32[512,512]{1,0:T(8,128)}, u32[]{:S(2)}) copy-start(f32[512,512]{1,0:T(8,128)} %param.5) | copy-start | bytes 3145732
  25.3 0.8 %copy-start.3 = (f32[128,256]{1,0:T(8,128)}, f32[128,256]{1,0:T(8,128)S(1)}, u32[]{:S(2)}) copy-start(f32[128,256]{1,0:T(8,128)S(1)} %collective-permute-done.9) | copy-start | bytes 393220
  25.3 0.8 %copy-start.7 = (f32[128,256]{1,0:T(8,128)}, f32[128,256]{1,0:T(8,128)S(1)}, u32[]{:S(2)}) copy-start(f32[128,256]{1,0:T(8,128)S(1)} %collective-permute-done.8) | copy-start | bytes 393220
  27.7 2.1 %collective-permute-start.12 = (f32[256,512]{1,0:T(8,128)S(1)}, f32[256,512]{1,0:T(8,128)}, u32[]{:S(2)}, u32[]{:S(2)}) collective-permute-start(f32[256,512]{1,0:T(8,128)S(1)} %convolution_subtract_fusion.1), channel_id=1, source_target_pairs={{0,2},{2,0},{4,6},{6,4},{8,10},{10,8},{12,14},{14,12},{16,18},{18,... | collective-permute-start | bytes 1572872 | tf_op jit(solution)/shard_map/ppermute | solution.py:89
  31.3 1.0 %copy-start.6 = (f32[128,256]{1,0:T(8,128)S(1)}, f32[128,256]{1,0:T(8,128)}, u32[]{:S(2)}) copy-start(f32[128,256]{1,0:T(8,128)} %copy-done.5) | copy-start | bytes 393220
  31.7 8.7 %collective-permute-start.13 = (f32[256,256]{1,0:T(8,128)S(1)}, f32[256,256]{1,0:T(8,128)S(1)}, u32[]{:S(2)}, u32[]{:S(2)}) collective-permute-start(f32[256,256]{1,0:T(8,128)S(1)} %get-tuple-element.59), channel_id=1, source_target_pairs={{0,4},{4,0},{2,6},{6,2},{8,12},{12,8},{10,14},{14,10},{16,20},{20,... | collective-permute-start | bytes 786440 | tf_op jit(solution)/shard_map/ppermute | solution.py:111
  40.8 3.8 %copy-start.2 = (f32[128,256]{1,0:T(8,128)S(1)}, f32[128,256]{1,0:T(8,128)}, u32[]{:S(2)}) copy-start(f32[128,256]{1,0:T(8,128)} %copy-done.1) | copy-start | bytes 393220
  40.9 3.8 %copy-start.8 = (f32[128,256]{1,0:T(8,128)S(1)}, f32[128,256]{1,0:T(8,128)}, u32[]{:S(2)}) copy-start(f32[128,256]{1,0:T(8,128)} %copy-done.7) | copy-start | bytes 393220
  41.3 9.8 %collective-permute-start.14 = (f32[256,256]{1,0:T(8,128)S(1)}, f32[256,256]{1,0:T(8,128)S(1)}, u32[]{:S(2)}, u32[]{:S(2)}) collective-permute-start(f32[256,256]{1,0:T(8,128)S(1)} %get-tuple-element.61), channel_id=1, source_target_pairs={{0,8},{8,0},{2,10},{10,2},{16,24},{24,16},{18,26},{26,18},{1,9},{9... | collective-permute-start | bytes 786440 | tf_op jit(solution)/shard_map/ppermute | solution.py:111
  51.5 5.1 %copy-start.4 = (f32[128,256]{1,0:T(8,128)S(1)}, f32[128,256]{1,0:T(8,128)}, u32[]{:S(2)}) copy-start(f32[128,256]{1,0:T(8,128)} %copy-done.3) | copy-start | bytes 393220
  51.9 10.3 %collective-permute-start.15 = (f32[256,256]{1,0:T(8,128)S(1)}, f32[256,256]{1,0:T(8,128)S(1)}, u32[]{:S(2)}, u32[]{:S(2)}) collective-permute-start(f32[256,256]{1,0:T(8,128)S(1)} %get-tuple-element.63), channel_id=1, source_target_pairs={{0,16},{16,0},{2,18},{18,2},{1,17},{17,1},{3,19},{19,3}} | collective-permute-start | bytes 786440 | tf_op jit(solution)/shard_map/ppermute | solution.py:111
  64.1 1.6 %collective-permute-start.16 = (f32[256,256]{1,0:T(8,128)S(1)}, f32[256,256]{1,0:T(8,128)S(1)}, u32[]{:S(2)}, u32[]{:S(2)}) collective-permute-start(f32[256,256]{1,0:T(8,128)S(1)} %get-tuple-element.65), channel_id=1, source_target_pairs={{0,2},{2,0},{4,6},{6,4},{8,10},{10,8},{12,14},{14,12},{16,18},{18,... | collective-permute-start | bytes 786440 | tf_op jit(solution)/shard_map/ppermute | solution.py:125

commit v22 on v19

--- a/solution.py
+++ b/solution.py
@@ -112,8 +112,19 @@
         bottom_rows = jnp.where(is_lower & (core == 0), mates, jnp.where(is_lower, mine, 0.0))
         own_part = product_left_t(top_rows, chain[:hw]) + product_left_t(bottom_rows, chain[hw:])
         own_part, received = lax.optimization_barrier((own_part, received))
-        update = product_left_t(even3[1], received) + q
-        result = jnp.where(is_upper, chain - product(even3[0], update), result)
+        if level == levels - 1:
+            result = lax.cond(
+                is_upper,
+                lambda c, r, qq, old: c - product(even3[0], product_left_t(even3[1], r) + qq),
+                lambda c, r, qq, old: old,
+                chain,
+                received,
+                q,
+                result,
+            )
+        else:
+            update = product_left_t(even3[1], received) + q
+            result = jnp.where(is_upper, chain - product(even3[0], update), result)
         chain = jnp.where(is_lower, chain - own_part - received, chain)
     base_out = jnp.where(base == 0, chain, result)
 

time: 62.8 us -> 68.3 us (1.088)
  waiting for transfers between devices: 27.8 us -> 35.7 us
  starting transfers between devices: 20 us -> 15.7 us
  other arithmetic: 4.13 us -> 5.29 us
    ppermute x3, starting transfers between devices: 8.19 us -> 3.91 us  [on_device(): received = lax.ppermute(jnp.where(is_upper, q, chain), 'row', pairs)]
    ppermute x3, waiting for transfers between devices: 16.3 us -> 19.5 us  [on_device(): received = lax.ppermute(jnp.where(is_upper, q, chain), 'row', pairs)]
    ppermute x3, waiting for transfers between devices: 2.82 us -> 5.44 us  [on_device(): partner_factors.append(lax.ppermute(half_s, 'row', pairs))]
    ppermute x4, waiting for transfers between devices: 7.15 us -> 9.29 us  [col_gather(): by_shift.append(lax.ppermute(part, 'col', perm))]
    select_n x0 -> x2, other arithmetic: none -> 1.11 us  [the longest x1 1.04 us: on_device(): give = jnp.where(core == 0, level0_out, base_out)]
    dot_general x6 -> x5, matrix products: 2.08 us -> 1.77 us  [product(): jnp.dot(left, right, precision=lax.Precision.HIGH, preferred_element_type...]
    dot_general x16 -> x15, matrix products: 6.17 us -> 6.44 us  [product_left_t(): lax.dot_general(left, right, (((0,), (0,)), ((), ())), precision=lax.Prec...]
  transfers between devices with their start and end apart: 17 -> 17, of which waited for: 9 -> 7; matrix products, arithmetic and copies ran while one was open for 15% -> 15% of each run, Pallas kernels for 0% -> 0%
where the time goes in v22:
time: 68.3 us; the launch traced here: 68 us
  waiting for transfers between devices  35.7 us (52%)
  starting transfers between devices  15.7 us (23%)
  matrix products  8.21 us (12%)
  other arithmetic  5.29 us (8%)
  local copies, waits for them, and re-layouts  2.44 us (4%)
    ppermute x3, waiting for transfers between devices, on_device(): received = lax.ppermute(jnp.where(is_upper, q, chain), 'row', pairs)  19.5 us
    ppermute x4, waiting for transfers between devices, col_gather(): by_shift.append(lax.ppermute(part, 'col', perm))  9.29 us
    ppermute x4, starting transfers between devices, col_gather(): by_shift.append(lax.ppermute(part, 'col', perm))  6.73 us
    dot_general x15, matrix products, product_left_t(): lax.dot_general(left, right, (((0,), (0,)), ((), ())), precision=lax.Prec...  6.44 us
    ppermute x3, waiting for transfers between devices, on_device(): partner_factors.append(lax.ppermute(half_s, 'row', pairs))  5.44 us
    ppermute x3, starting transfers between devices, on_device(): received = lax.ppermute(jnp.where(is_upper, q, chain), 'row', pairs)  3.91 us
    ppermute x3, starting transfers between devices, on_device(): partner_factors.append(lax.ppermute(half_s, 'row', pairs))  3.86 us
    dot_general x5, matrix products, product(): jnp.dot(left, right, precision=lax.Precision.HIGH, preferred_element_type...  1.77 us
  transfers between devices with their start and end apart: 17, of which 7 were waited for; matrix products, arithmetic and copies ran while one was open for 15% of the time, Pallas kernels for 0%

profile of v22, /device:TPU:0, one launch (start us, length us, event | category | flops | bytes accessed | tf_op | source)
XLA Modules:
  0.0 68.0 jit_solution(8842575029579920033)
XLA Ops:
  0.0 3.0 %collective-permute-start = (f32[256,128]{1,0:T(8,128)}, f32[256,128]{1,0:T(8,128)S(1)}, u32[]{:S(2)}, u32[]{:S(2)}) collective-permute-start(f32[256,128]{1,0:T(8,128)} %param.11), channel_id=1, source_target_pairs={{0,1},{1,0},{2,3},{3,2},{4,5},{5,4},{6,7},{7,6},{8,9},{9,8},{10,11... | collective-permute-start | bytes 393224 | tf_op jit(solution)/shard_map/ppermute | solution.py:34
  3.0 3.7 %collective-permute-done = f32[256,128]{1,0:T(8,128)S(1)} collective-permute-done((f32[256,128]{1,0:T(8,128)}, f32[256,128]{1,0:T(8,128)S(1)}, u32[]{:S(2)}, u32[]{:S(2)}) %collective-permute-start) | collective-permute-done | bytes 131104 | tf_op jit(solution)/shard_map/ppermute | solution.py:34
  6.7 0.9 %fusion.56 = (f32[256,128]{1,0:T(8,128)S(1)}, f32[256,128]{1,0:T(8,128)S(1)}) fusion(s32[]{:T(128)S(6)} %select_n.305, f32[1,256,128]{2,1,0:T(8,128)} %bitcast.89, f32[1,256,128]{2,1,0:T(8,128)S(1)} %bitcast.92, s32[]{:T(128)S(6)} %select_n.307), kind=kLoop, calls=%fused_computation.104 | loop fusion | flops 65536 | bytes 524296 | tf_op jit(solution)/shard_map/squeeze | solution.py:36
  7.7 0.9 %copy-done.1 = f32[512,128]{1,0:T(8,128)S(1)} copy-done((f32[512,128]{1,0:T(8,128)S(1)}, f32[512,128]{1,0:T(8,128)}, u32[]{:S(2)}) %copy-start.1) | copy-done | bytes 262168
  8.6 1.7 %collective-permute-start.1 = (f32[512,128]{1,0:T(8,128)S(1)}, f32[512,128]{1,0:T(8,128)S(1)}, u32[]{:S(2)}, u32[]{:S(2)}) collective-permute-start(f32[512,128]{1,0:T(8,128)S(1)} %copy-done.1), channel_id=1, source_target_pairs={{0,1},{1,0},{2,3},{3,2},{4,5},{5,4},{6,7},{7,6},{8,9},{9,8},{10,11... | collective-permute-start | bytes 786440 | tf_op jit(solution)/shard_map/ppermute | solution.py:34
  10.8 0.8 %copy-done.2 = f32[256,128]{1,0:T(8,128)S(1)} copy-done((f32[256,128]{1,0:T(8,128)S(1)}, f32[256,128]{1,0:T(8,128)}, u32[]{:S(2)}) %copy-start.2) | copy-done | bytes 131096
  11.6 1.7 %collective-permute-start.7 = (f32[256,128]{1,0:T(8,128)S(1)}, f32[256,128]{1,0:T(8,128)S(1)}, u32[]{:S(2)}, u32[]{:S(2)}) collective-permute-start(f32[256,128]{1,0:T(8,128)S(1)} %copy-done.2), channel_id=1, source_target_pairs={{0,1},{1,0},{2,3},{3,2},{4,5},{5,4},{6,7},{7,6},{8,9},{9,8},{10,11... | collective-permute-start | bytes 393224 | tf_op jit(solution)/shard_map/ppermute | solution.py:34
  13.5 1.3 %collective-permute-start.4 = (f32[128,256]{1,0:T(8,128)S(1)}, f32[128,256]{1,0:T(8,128)S(1)}, u32[]{:S(2)}, u32[]{:S(2)}) collective-permute-start(f32[128,256]{1,0:T(8,128)S(1)} %slice_select_fusion), channel_id=1, source_target_pairs={{4,0},{6,2},{12,8},{14,10},{20,16},{22,18},{28,24},{30,26},{5,1},{... | collective-permute-start | bytes 393224 | tf_op jit(solution)/shard_map/ppermute | solution.py:76
  14.8 1.3 %collective-permute-start.5 = (f32[128,256]{1,0:T(8,128)S(1)}, f32[128,256]{1,0:T(8,128)S(1)}, u32[]{:S(2)}, u32[]{:S(2)}) collective-permute-start(f32[128,256]{1,0:T(8,128)S(1)} %slice_select_fusion), channel_id=1, source_target_pairs={{8,0},{10,2},{24,16},{26,18},{9,1},{11,3},{25,17},{27,19}} | collective-permute-start | bytes 393224 | tf_op jit(solution)/shard_map/ppermute | solution.py:76
  16.1 5.6 %collective-permute-done.7 = f32[256,128]{1,0:T(8,128)S(1)} collective-permute-done((f32[256,128]{1,0:T(8,128)S(1)}, f32[256,128]{1,0:T(8,128)S(1)}, u32[]{:S(2)}, u32[]{:S(2)}) %collective-permute-start.7) | collective-permute-done | bytes 131104 | tf_op jit(solution)/shard_map/ppermute | solution.py:34
  21.7 1.3 %collective-permute-start.6 = (f32[128,256]{1,0:T(8,128)S(1)}, f32[128,256]{1,0:T(8,128)S(1)}, u32[]{:S(2)}, u32[]{:S(2)}) collective-permute-start(f32[128,256]{1,0:T(8,128)S(1)} %slice_select_fusion), channel_id=1, source_target_pairs={{16,0},{18,2},{17,1},{19,3}} | collective-permute-start | bytes 393224 | tf_op jit(solution)/shard_map/ppermute | solution.py:76
  24.0 5.4 %collective-permute-done.6 = f32[128,256]{1,0:T(8,128)S(1)} collective-permute-done((f32[128,256]{1,0:T(8,128)S(1)}, f32[128,256]{1,0:T(8,128)S(1)}, u32[]{:S(2)}, u32[]{:S(2)}) %collective-permute-start.6) | collective-permute-done | bytes 131104 | tf_op jit(solution)/shard_map/ppermute | solution.py:76
  29.4 0.6 fusion.6
  30.1 0.5 fusion.29
  30.6 0.6 convolution_subtract_fusion
  31.4 0.4 collective-permute-start.10
  32.3 1.3 %broadcast_select_fusion = (f32[3,256,256]{2,1,0:T(8,128)S(1)}, f32[3,256,256]{2,1,0:T(8,128)S(1)}) fusion(f32[3,256,256]{2,1,0:T(8,128)} %collective-permute-done.8, pred[]{:T(512)S(6)} %eq.55, f32[1,256,256]{2,1,0:T(8,128)S(1)} %convolution_bitcast_fusion.1, f32[1,256,256]{2,1,0:T(8,128)S(1)} %fusion.143, f32[1,256,256]{2,1,0:T(8,128)S(1)} %maximum_select_fusion, ...), kind=kLoop, calls=%fused_computation.26 | loop fusion | flops 786432 | bytes 3145730 | tf_op jit(solution)/shard_map/jit(_where)/select_n | solution.py:65
  33.6 0.4 fusion.22
  34.1 0.4 select_subtract_fusion.1
  34.5 0.4 broadcast_select_fusion.4
  35.9 7.4 %collective-permute-done.11 = f32[256,256]{1,0:T(8,128)S(1)} collective-permute-done((f32[256,256]{1,0:T(8,128)S(1)}, f32[256,256]{1,0:T(8,128)S(1)}, u32[]{:S(2)}, u32[]{:S(2)}) %collective-permute-start.11) | collective-permute-done | bytes 262176 | tf_op jit(solution)/shard_map/ppermute | solution.py:108
  43.8 1.9 %collective-permute-start.13 = (f32[256,256]{1,0:T(8,128)S(1)}, f32[256,256]{1,0:T(8,128)S(1)}, u32[]{:S(2)}, u32[]{:S(2)}) collective-permute-start(f32[256,256]{1,0:T(8,128)S(1)} %get-tuple-element.111), channel_id=1, source_target_pairs={{0,8},{8,0},{2,10},{10,2},{16,24},{24,16},{18,26},{26,18},{1,9},{9... | collective-permute-start | bytes 786440 | tf_op jit(solution)/shard_map/ppermute | solution.py:108
  45.7 0.4 convolution_add_fusion.1
  47.0 6.2 %collective-permute-done.13 = f32[256,256]{1,0:T(8,128)S(1)} collective-permute-done((f32[256,256]{1,0:T(8,128)S(1)}, f32[256,256]{1,0:T(8,128)S(1)}, u32[]{:S(2)}, u32[]{:S(2)}) %collective-permute-start.13) | collective-permute-done | bytes 262176 | tf_op jit(solution)/shard_map/ppermute | solution.py:108
  53.6 0.4 broadcast_select_fusion.2
  54.0 1.9 %collective-permute-start.15 = (f32[256,256]{1,0:T(8,128)S(1)}, f32[256,256]{1,0:T(8,128)S(1)}, u32[]{:S(2)}, u32[]{:S(2)}) collective-permute-start(f32[256,256]{1,0:T(8,128)S(1)} %get-tuple-element.113), channel_id=1, source_target_pairs={{0,16},{16,0},{2,18},{18,2},{1,17},{17,1},{3,19},{19,3}} | collective-permute-start | bytes 786440 | tf_op jit(solution)/shard_map/ppermute | solution.py:108
  56.6 1.0 %convolution_add_fusion.3 = f32[256,256]{1,0:T(8,128)} fusion(f32[256,256]{1,0:T(8,128)S(1)} %fusion.57, f32[256,256]{1,0:T(8,128)S(1)} %subtract_select_fusion.1, f32[128,256]{1,0:T(8,128)S(1)} %collective-permute-done.6, f32[128,256]{1,0:T(8,128)S(1)} %collective-permute-done.14, pred[]{:T(512)S(6)} %eq.57, pred[]{:T(512)S(6)} %and.53), kind=kOutput, calls=%fused_computation.12 | convolution fusion | flops 50462720 | bytes 917506 | tf_op jit(solution)/shard_map/dot_general | solution.py:12
  57.6 5.9 %collective-permute-done.15 = f32[256,256]{1,0:T(8,128)S(1)} collective-permute-done((f32[256,256]{1,0:T(8,128)S(1)}, f32[256,256]{1,0:T(8,128)S(1)}, u32[]{:S(2)}, u32[]{:S(2)}) %collective-permute-start.15) | collective-permute-done | bytes 262176 | tf_op jit(solution)/shard_map/ppermute | solution.py:108
  63.5 0.8 %conditional.1 = (f32[256,256]{1,0:T(8,128)S(1)}) conditional(s32[]{:T(128)} %convert_element_type.3, (pred[]{:T(512)}, f32[256,256]{1,0:T(8,128)S(1)}, f32[256,256]{1,0:T(8,128)S(1)}, pred[]{:T(512)}, f32[256,256]{1,0:T(8,128)S(1)}, /*index=5*/f32[256,256]{1,0:T(8,128)S(1)}) %tuple.25, (f32[3,256,256]{2,1,0:T(8,128)S(1)}, f32[256,256]{1,0:T(8,128)S(1)}, ...), branch_computations={%region_0.1_spmd, %region_1.2_spmd} | conditional | flops 201457664 | bytes 3932170 | solution.py:116
  64.2 1.0 %broadcast_select_fusion.7 = (f32[256,256]{1,0:T(8,128)S(1)}, f32[256,256]{1,0:T(8,128)S(1)}) fusion(f32[256,256]{1,0:T(8,128)S(1)} %select_subtract_fusion, pred[]{:T(512)S(6)} %eq.55, f32[256,256]{1,0:T(8,128)S(1)} %get-tuple-element.90, f32[256,256]{1,0:T(8,128)S(1)} %subtract_select_fusion.1, f32[256,256]{1,0:T(8,128)S(1)} %collective-permute-done.15, ...), kind=kLoop, calls=%fused_computation.144 | loop fusion | flops 327680 | bytes 1835011 | tf_op jit(solution)/shard_map/jit(_where)/select_n | solution.py:132
  65.4 1.5 %collective-permute-done.16 = f32[256,256]{1,0:T(8,128)S(1)} collective-permute-done((f32[256,256]{1,0:T(8,128)S(1)}, f32[256,256]{1,0:T(8,128)S(1)}, u32[]{:S(2)}, u32[]{:S(2)}) %collective-permute-start.16) | collective-permute-done | bytes 262176 | tf_op jit(solution)/shard_map/ppermute | solution.py:133
  66.9 1.1 %pad_maximum_fusion = f32[512,512]{1,0:T(8,128)} fusion(f32[256,512]{1,0:T(8,128)S(1)} %get-tuple-element.96, f32[256,256]{1,0:T(8,128)S(1)} %get-tuple-element.98, f32[256,256]{1,0:T(8,128)S(1)} %get-tuple-element.97), kind=kLoop, calls=%fused_computation.16 | loop fusion | flops 524288 | bytes 2097152 | tf_op jit(solution)/shard_map/concatenate | solution.py:135
  (58 shorter events, 6.4 us)
Async XLA Ops:
  0.0 6.7 %collective-permute-start = (f32[256,128]{1,0:T(8,128)}, f32[256,128]{1,0:T(8,128)S(1)}, u32[]{:S(2)}, u32[]{:S(2)}) collective-permute-start(f32[256,128]{1,0:T(8,128)} %param.11), channel_id=1, source_target_pairs={{0,1},{1,0},{2,3},{3,2},{4,5},{5,4},{6,7},{7,6},{8,9},{9,8},{10,11... | collective-permute-start | bytes 393224 | tf_op jit(solution)/shard_map/ppermute | solution.py:34
  7.6 1.0 %copy-start.1 = (f32[512,128]{1,0:T(8,128)S(1)}, f32[512,128]{1,0:T(8,128)}, u32[]{:S(2)}) copy-start(f32[512,128]{1,0:T(8,128)} %param.8) | copy-start | bytes 786436
  7.6 2.7 %copy-start.3 = (f32[256,128]{1,0:T(8,128)S(1)}, f32[256,128]{1,0:T(8,128)}, u32[]{:S(2)}) copy-start(f32[256,128]{1,0:T(8,128)} %param.9) | copy-start | bytes 393220
  8.6 15.2 %collective-permute-start.1 = (f32[512,128]{1,0:T(8,128)S(1)}, f32[512,128]{1,0:T(8,128)S(1)}, u32[]{:S(2)}, u32[]{:S(2)}) collective-permute-start(f32[512,128]{1,0:T(8,128)S(1)} %copy-done.1), channel_id=1, source_target_pairs={{0,1},{1,0},{2,3},{3,2},{4,5},{5,4},{6,7},{7,6},{8,9},{9,8},{10,11... | collective-permute-start | bytes 786440 | tf_op jit(solution)/shard_map/ppermute | solution.py:34
  10.3 13.3 %collective-permute-start.2 = (f32[256,128]{1,0:T(8,128)S(1)}, f32[256,128]{1,0:T(8,128)S(1)}, u32[]{:S(2)}, u32[]{:S(2)}) collective-permute-start(f32[256,128]{1,0:T(8,128)S(1)} %copy-done.3), channel_id=1, source_target_pairs={{0,1},{1,0},{2,3},{3,2},{4,5},{5,4},{6,7},{7,6},{8,9},{9,8},{10,11... | collective-permute-start | bytes 393224 | tf_op jit(solution)/shard_map/ppermute | solution.py:34
  10.7 0.9 %copy-start.2 = (f32[256,128]{1,0:T(8,128)S(1)}, f32[256,128]{1,0:T(8,128)}, u32[]{:S(2)}) copy-start(f32[256,128]{1,0:T(8,128)} %param.10) | copy-start | bytes 393220
  10.7 2.7 %collective-permute-start.3 = (f32[128,256]{1,0:T(8,128)S(1)}, f32[128,256]{1,0:T(8,128)S(1)}, u32[]{:S(2)}, u32[]{:S(2)}) collective-permute-start(f32[128,256]{1,0:T(8,128)S(1)} %slice.77), channel_id=1, source_target_pairs={{0,2},{2,0},{4,6},{6,4},{8,10},{10,8},{12,14},{14,12},{16,18},{18,... | collective-permute-start | bytes 393224 | tf_op jit(solution)/shard_map/ppermute | solution.py:68
  11.6 10.1 %collective-permute-start.7 = (f32[256,128]{1,0:T(8,128)S(1)}, f32[256,128]{1,0:T(8,128)S(1)}, u32[]{:S(2)}, u32[]{:S(2)}) collective-permute-start(f32[256,128]{1,0:T(8,128)S(1)} %copy-done.2), channel_id=1, source_target_pairs={{0,1},{1,0},{2,3},{3,2},{4,5},{5,4},{6,7},{7,6},{8,9},{9,8},{10,11... | collective-permute-start | bytes 393224 | tf_op jit(solution)/shard_map/ppermute | solution.py:34
  13.5 10.5 %collective-permute-start.4 = (f32[128,256]{1,0:T(8,128)S(1)}, f32[128,256]{1,0:T(8,128)S(1)}, u32[]{:S(2)}, u32[]{:S(2)}) collective-permute-start(f32[128,256]{1,0:T(8,128)S(1)} %slice_select_fusion), channel_id=1, source_target_pairs={{4,0},{6,2},{12,8},{14,10},{20,16},{22,18},{28,24},{30,26},{5,1},{... | collective-permute-start | bytes 393224 | tf_op jit(solution)/shard_map/ppermute | solution.py:76
  14.8 9.2 %collective-permute-start.5 = (f32[128,256]{1,0:T(8,128)S(1)}, f32[128,256]{1,0:T(8,128)S(1)}, u32[]{:S(2)}, u32[]{:S(2)}) collective-permute-start(f32[128,256]{1,0:T(8,128)S(1)} %slice_select_fusion), channel_id=1, source_target_pairs={{8,0},{10,2},{24,16},{26,18},{9,1},{11,3},{25,17},{27,19}} | collective-permute-start | bytes 393224 | tf_op jit(solution)/shard_map/ppermute | solution.py:76
  21.7 7.7 %collective-permute-start.6 = (f32[128,256]{1,0:T(8,128)S(1)}, f32[128,256]{1,0:T(8,128)S(1)}, u32[]{:S(2)}, u32[]{:S(2)}) collective-permute-start(f32[128,256]{1,0:T(8,128)S(1)} %slice_select_fusion), channel_id=1, source_target_pairs={{16,0},{18,2},{17,1},{19,3}} | collective-permute-start | bytes 393224 | tf_op jit(solution)/shard_map/ppermute | solution.py:76
  23.6 8.8 %collective-permute-start.8 = (f32[3,256,256]{2,1,0:T(8,128)S(1)}, f32[3,256,256]{2,1,0:T(8,128)}, u32[]{:S(2)}, u32[]{:S(2)}) collective-permute-start(f32[3,256,256]{2,1,0:T(8,128)S(1)} %pad_maximum_fusion.1), channel_id=1, source_target_pairs={{0,2},{2,0},{4,6},{6,4},{8,10},{10,8},{12,14},{14,12},{16,18},{18,... | collective-permute-start | bytes 2359304 | tf_op jit(solution)/shard_map/ppermute | solution.py:63
  23.8 5.7 %copy-start = (f32[512,512]{1,0:T(8,128)S(1)}, f32[512,512]{1,0:T(8,128)}, u32[]{:S(2)}) copy-start(f32[512,512]{1,0:T(8,128)} %param.7) | copy-start | bytes 3145732
  31.3 2.8 %collective-permute-start.9 = (f32[256,512]{1,0:T(8,128)S(1)}, f32[256,512]{1,0:T(8,128)S(1)}, u32[]{:S(2)}, u32[]{:S(2)}) collective-permute-start(f32[256,512]{1,0:T(8,128)S(1)} %get-tuple-element.95), channel_id=1, source_target_pairs={{0,2},{2,0},{4,6},{6,4},{8,10},{10,8},{12,14},{14,12},{16,18},{18,... | collective-permute-start | bytes 1572872 | tf_op jit(solution)/shard_map/ppermute | solution.py:86
  31.4 3.5 %collective-permute-start.10 = (f32[128,256]{1,0:T(8,128)S(1)}, f32[128,256]{1,0:T(8,128)S(1)}, u32[]{:S(2)}, u32[]{:S(2)}) collective-permute-start(f32[128,256]{1,0:T(8,128)S(1)} %collective-permute-done.4), channel_id=1, source_target_pairs={{0,2},{2,0},{4,6},{6,4},{8,10},{10,8},{12,14},{14,12},{16,18},{18,... | collective-permute-start | bytes 393224 | tf_op jit(solution)/shard_map/ppermute | solution.py:110
  31.8 14.5 %collective-permute-start.12 = (f32[128,256]{1,0:T(8,128)S(1)}, f32[128,256]{1,0:T(8,128)S(1)}, u32[]{:S(2)}, u32[]{:S(2)}) collective-permute-start(f32[128,256]{1,0:T(8,128)S(1)} %collective-permute-done.5), channel_id=1, source_target_pairs={{0,2},{2,0},{4,6},{6,4},{8,10},{10,8},{12,14},{14,12},{16,18},{18,... | collective-permute-start | bytes 393224 | tf_op jit(solution)/shard_map/ppermute | solution.py:110
  32.0 24.3 %collective-permute-start.14 = (f32[128,256]{1,0:T(8,128)S(1)}, f32[128,256]{1,0:T(8,128)S(1)}, u32[]{:S(2)}, u32[]{:S(2)}) collective-permute-start(f32[128,256]{1,0:T(8,128)S(1)} %collective-permute-done.6), channel_id=1, source_target_pairs={{0,2},{2,0},{4,6},{6,4},{8,10},{10,8},{12,14},{14,12},{16,18},{18,... | collective-permute-start | bytes 393224 | tf_op jit(solution)/shard_map/ppermute | solution.py:110
  34.9 8.4 %collective-permute-start.11 = (f32[256,256]{1,0:T(8,128)S(1)}, f32[256,256]{1,0:T(8,128)S(1)}, u32[]{:S(2)}, u32[]{:S(2)}) collective-permute-start(f32[256,256]{1,0:T(8,128)S(1)} %get-tuple-element.109), channel_id=1, source_target_pairs={{0,4},{4,0},{2,6},{6,2},{8,12},{12,8},{10,14},{14,10},{16,20},{20,... | collective-permute-start | bytes 786440 | tf_op jit(solution)/shard_map/ppermute | solution.py:108
  43.8 9.4 %collective-permute-start.13 = (f32[256,256]{1,0:T(8,128)S(1)}, f32[256,256]{1,0:T(8,128)S(1)}, u32[]{:S(2)}, u32[]{:S(2)}) collective-permute-start(f32[256,256]{1,0:T(8,128)S(1)} %get-tuple-element.111), channel_id=1, source_target_pairs={{0,8},{8,0},{2,10},{10,2},{16,24},{24,16},{18,26},{26,18},{1,9},{9... | collective-permute-start | bytes 786440 | tf_op jit(solution)/shard_map/ppermute | solution.py:108
  54.0 9.4 %collective-permute-start.15 = (f32[256,256]{1,0:T(8,128)S(1)}, f32[256,256]{1,0:T(8,128)S(1)}, u32[]{:S(2)}, u32[]{:S(2)}) collective-permute-start(f32[256,256]{1,0:T(8,128)S(1)} %get-tuple-element.113), channel_id=1, source_target_pairs={{0,16},{16,0},{2,18},{18,2},{1,17},{17,1},{3,19},{19,3}} | collective-permute-start | bytes 786440 | tf_op jit(solution)/shard_map/ppermute | solution.py:108
  65.3 1.6 %collective-permute-start.16 = (f32[256,256]{1,0:T(8,128)S(1)}, f32[256,256]{1,0:T(8,128)S(1)}, u32[]{:S(2)}, u32[]{:S(2)}) collective-permute-start(f32[256,256]{1,0:T(8,128)S(1)} %get-tuple-element.91), channel_id=1, source_target_pairs={{0,2},{2,0},{4,6},{6,4},{8,10},{10,8},{12,14},{14,12},{16,18},{18,... | collective-permute-start | bytes 786440 | tf_op jit(solution)/shard_map/ppermute | solution.py:133

commit v23 on v19

--- a/solution.py
+++ b/solution.py
@@ -83,11 +83,10 @@
     current = leafed[:width]
 
     is_lower = core == 0
-    received = lax.ppermute(current, "row", swap)
+    recv_h = lax.ppermute(lax.dynamic_slice(current, (0, (1 - core) * half), (width, half)), "row", swap)
     own_h = lax.dynamic_slice(current, (0, core * half), (width, half))
     early = product_left_t(jnp.where(is_lower, odd3[1], odd3[2]), own_h)
-    early, received = lax.optimization_barrier((early, received))
-    recv_h = lax.dynamic_slice(received, (0, core * half), (width, half))
+    early, recv_h = lax.optimization_barrier((early, recv_h))
     update = early + product_left_t(jnp.where(is_lower, odd3[2], odd3[1]), recv_h)
     upper_h = jnp.where(is_lower, recv_h, own_h)
     level0_out = upper_h - product(odd3[0], update)

time: 62.8 us -> 62 us (0.987)
  other arithmetic: 4.13 us -> 2.15 us
  waiting for transfers between devices: 27.8 us -> 29.2 us
    select_n x1, other arithmetic: 1.29 us -> 0.18 us  [on_device(): even3 = jnp.where(core == 0, own3, mate3)]
    squeeze x3, other arithmetic: 1.11 us -> 0.23 us  [col_gather(): blocks = [stacked[(me - b) % n_col] for b in range(n_col)]]
    ppermute x3, waiting for transfers between devices: 16.3 us -> 17 us  [on_device(): received = lax.ppermute(jnp.where(is_upper, q, chain), 'row', pairs)]
    unnamed x8 -> x10, local copies, waits for them, and re-layouts: 1.72 us -> 1.72 us
  transfers between devices with their start and end apart: 17 -> 17, of which waited for: 9 -> 10; matrix products, arithmetic and copies ran while one was open for 15% -> 13% of each run, Pallas kernels for 0% -> 0%
where the time goes in v23:
time: 62 us; the launch traced here: 61.7 us
  waiting for transfers between devices  29.2 us (47%)
  starting transfers between devices  19.9 us (32%)
  matrix products  8.21 us (13%)
  other arithmetic  2.15 us (3%)
  local copies, waits for them, and re-layouts  1.83 us (3%)
    ppermute x3, waiting for transfers between devices, on_device(): received = lax.ppermute(jnp.where(is_upper, q, chain), 'row', pairs)  17 us
    ppermute x3, starting transfers between devices, on_device(): received = lax.ppermute(jnp.where(is_upper, q, chain), 'row', pairs)  8.03 us
    ppermute x4, waiting for transfers between devices, col_gather(): by_shift.append(lax.ppermute(part, 'col', perm))  7.3 us
    ppermute x4, starting transfers between devices, col_gather(): by_shift.append(lax.ppermute(part, 'col', perm))  6.66 us
    dot_general x16, matrix products, product_left_t(): lax.dot_general(left, right, (((0,), (0,)), ((), ())), precision=lax.Prec...  6.15 us
    ppermute x3, starting transfers between devices, on_device(): partner_factors.append(lax.ppermute(half_s, 'row', pairs))  3.86 us
    ppermute x3, waiting for transfers between devices, on_device(): partner_factors.append(lax.ppermute(half_s, 'row', pairs))  2.83 us
    dot_general x6, matrix products, product(): jnp.dot(left, right, precision=lax.Precision.HIGH, preferred_element_type...  2.06 us
  transfers between devices with their start and end apart: 17, of which 10 were waited for; matrix products, arithmetic and copies ran while one was open for 13% of the time, Pallas kernels for 0%

profile of v23, /device:TPU:0, one launch (start us, length us, event | category | flops | bytes accessed | tf_op | source)
XLA Modules:
  0.0 61.7 jit_solution(16089219450058765339)
XLA Ops:
  0.0 3.0 %collective-permute-start = (f32[256,128]{1,0:T(8,128)}, f32[256,128]{1,0:T(8,128)S(1)}, u32[]{:S(2)}, u32[]{:S(2)}) collective-permute-start(f32[256,128]{1,0:T(8,128)} %param.9), channel_id=1, source_target_pairs={{0,1},{1,0},{2,3},{3,2},{4,5},{5,4},{6,7},{7,6},{8,9},{9,8},{10,11... | collective-permute-start | bytes 393224 | tf_op jit(solution)/shard_map/ppermute | solution.py:34
  3.0 3.8 %collective-permute-done = f32[256,128]{1,0:T(8,128)S(1)} collective-permute-done((f32[256,128]{1,0:T(8,128)}, f32[256,128]{1,0:T(8,128)S(1)}, u32[]{:S(2)}, u32[]{:S(2)}) %collective-permute-start) | collective-permute-done | bytes 131104 | tf_op jit(solution)/shard_map/ppermute | solution.py:34
  6.9 0.9 %copy-done.4 = f32[256,128]{1,0:T(8,128)S(1)} copy-done((f32[256,128]{1,0:T(8,128)S(1)}, f32[256,128]{1,0:T(8,128)}, u32[]{:S(2)}) %copy-start.4) | copy-done | bytes 131096
  7.7 1.7 %collective-permute-start.2 = (f32[256,128]{1,0:T(8,128)S(1)}, f32[256,128]{1,0:T(8,128)S(1)}, u32[]{:S(2)}, u32[]{:S(2)}) collective-permute-start(f32[256,128]{1,0:T(8,128)S(1)} %copy-done.4), channel_id=1, source_target_pairs={{0,1},{1,0},{2,3},{3,2},{4,5},{5,4},{6,7},{7,6},{8,9},{9,8},{10,11... | collective-permute-start | bytes 393224 | tf_op jit(solution)/shard_map/ppermute | solution.py:34
  10.0 0.8 %copy-done.1 = f32[512,128]{1,0:T(8,128)S(1)} copy-done((f32[512,128]{1,0:T(8,128)S(1)}, f32[512,128]{1,0:T(8,128)}, u32[]{:S(2)}) %copy-start.1) | copy-done | bytes 262168
  10.8 1.7 %collective-permute-start.1 = (f32[512,128]{1,0:T(8,128)S(1)}, f32[512,128]{1,0:T(8,128)S(1)}, u32[]{:S(2)}, u32[]{:S(2)}) collective-permute-start(f32[512,128]{1,0:T(8,128)S(1)} %copy-done.1), channel_id=1, source_target_pairs={{0,1},{1,0},{2,3},{3,2},{4,5},{5,4},{6,7},{7,6},{8,9},{9,8},{10,11... | collective-permute-start | bytes 786440 | tf_op jit(solution)/shard_map/ppermute | solution.py:34
  12.6 1.3 %collective-permute-start.6 = (f32[128,256]{1,0:T(8,128)S(1)}, f32[128,256]{1,0:T(8,128)S(1)}, u32[]{:S(2)}, u32[]{:S(2)}) collective-permute-start(f32[128,256]{1,0:T(8,128)S(1)} %slice_select_fusion), channel_id=1, source_target_pairs={{16,0},{18,2},{17,1},{19,3}} | collective-permute-start | bytes 393224 | tf_op jit(solution)/shard_map/ppermute | solution.py:76
  13.9 1.3 %collective-permute-start.5 = (f32[128,256]{1,0:T(8,128)S(1)}, f32[128,256]{1,0:T(8,128)S(1)}, u32[]{:S(2)}, u32[]{:S(2)}) collective-permute-start(f32[128,256]{1,0:T(8,128)S(1)} %slice_select_fusion), channel_id=1, source_target_pairs={{8,0},{10,2},{24,16},{26,18},{9,1},{11,3},{25,17},{27,19}} | collective-permute-start | bytes 393224 | tf_op jit(solution)/shard_map/ppermute | solution.py:76
  15.2 1.8 %collective-permute-done.7 = f32[256,128]{1,0:T(8,128)S(1)} collective-permute-done((f32[256,128]{1,0:T(8,128)S(1)}, f32[256,128]{1,0:T(8,128)S(1)}, u32[]{:S(2)}, u32[]{:S(2)}) %collective-permute-start.7) | collective-permute-done | bytes 131104 | tf_op jit(solution)/shard_map/ppermute | solution.py:34
  17.0 1.3 %collective-permute-start.4 = (f32[128,256]{1,0:T(8,128)S(1)}, f32[128,256]{1,0:T(8,128)S(1)}, u32[]{:S(2)}, u32[]{:S(2)}) collective-permute-start(f32[128,256]{1,0:T(8,128)S(1)} %slice_select_fusion), channel_id=1, source_target_pairs={{4,0},{6,2},{12,8},{14,10},{20,16},{22,18},{28,24},{30,26},{5,1},{... | collective-permute-start | bytes 393224 | tf_op jit(solution)/shard_map/ppermute | solution.py:76
  19.1 1.8 %collective-permute-done.1 = f32[512,128]{1,0:T(8,128)S(1)} collective-permute-done((f32[512,128]{1,0:T(8,128)S(1)}, f32[512,128]{1,0:T(8,128)S(1)}, u32[]{:S(2)}, u32[]{:S(2)}) %collective-permute-start.1) | collective-permute-done | bytes 262176 | tf_op jit(solution)/shard_map/ppermute | solution.py:34
  21.0 2.0 %collective-permute-done.5 = f32[128,256]{1,0:T(8,128)S(1)} collective-permute-done((f32[128,256]{1,0:T(8,128)S(1)}, f32[128,256]{1,0:T(8,128)S(1)}, u32[]{:S(2)}, u32[]{:S(2)}) %collective-permute-start.5) | collective-permute-done | bytes 131104 | tf_op jit(solution)/shard_map/ppermute | solution.py:76
  23.0 0.8 %collective-permute-done.4 = f32[128,256]{1,0:T(8,128)S(1)} collective-permute-done((f32[128,256]{1,0:T(8,128)S(1)}, f32[128,256]{1,0:T(8,128)S(1)}, u32[]{:S(2)}, u32[]{:S(2)}) %collective-permute-start.4) | collective-permute-done | bytes 131104 | tf_op jit(solution)/shard_map/ppermute | solution.py:76
  23.8 0.5 collective-permute-start.12
  24.3 0.6 %fusion.3 = f32[256,512]{1,0:T(8,128)S(1)} fusion(f32[512,512]{1,0:T(8,128)S(1)} %copy-done, f32[512,256]{1,0:T(8,128)S(1)} %pad_maximum_fusion.2), kind=kOutput, calls=%fused_computation.26 | convolution fusion | flops 403308544 | bytes 2097152 | tf_op jit(solution)/shard_map/dot_general | solution.py:12
  25.0 0.5 fusion.26
  25.5 0.6 convolution_subtract_fusion
  26.2 0.6 collective-permute-start.9
  27.0 0.4 fusion.19
  27.4 0.6 collective-permute-done.9
  27.9 0.4 select_subtract_fusion.1
  28.3 0.4 broadcast_select_fusion.4
  29.5 7.9 %collective-permute-done.11 = f32[256,256]{1,0:T(8,128)S(1)} collective-permute-done((f32[256,256]{1,0:T(8,128)S(1)}, f32[256,256]{1,0:T(8,128)S(1)}, u32[]{:S(2)}, u32[]{:S(2)}) %collective-permute-start.11) | collective-permute-done | bytes 262176 | tf_op jit(solution)/shard_map/ppermute | solution.py:107
  37.4 0.4 broadcast_select_fusion.3
  37.8 3.3 %collective-permute-start.13 = (f32[256,256]{1,0:T(8,128)S(1)}, f32[256,256]{1,0:T(8,128)S(1)}, u32[]{:S(2)}, u32[]{:S(2)}) collective-permute-start(f32[256,256]{1,0:T(8,128)S(1)} %get-tuple-element.57), channel_id=1, source_target_pairs={{0,8},{8,0},{2,10},{10,2},{16,24},{24,16},{18,26},{26,18},{1,9},{9... | collective-permute-start | bytes 786440 | tf_op jit(solution)/shard_map/ppermute | solution.py:107
  42.5 5.0 %collective-permute-done.13 = f32[256,256]{1,0:T(8,128)S(1)} collective-permute-done((f32[256,256]{1,0:T(8,128)S(1)}, f32[256,256]{1,0:T(8,128)S(1)}, u32[]{:S(2)}, u32[]{:S(2)}) %collective-permute-start.13) | collective-permute-done | bytes 262176 | tf_op jit(solution)/shard_map/ppermute | solution.py:107
  47.6 0.4 broadcast_select_fusion.2
  48.0 4.6 %collective-permute-start.15 = (f32[256,256]{1,0:T(8,128)S(1)}, f32[256,256]{1,0:T(8,128)S(1)}, u32[]{:S(2)}, u32[]{:S(2)}) collective-permute-start(f32[256,256]{1,0:T(8,128)S(1)} %get-tuple-element.59), channel_id=1, source_target_pairs={{0,16},{16,0},{2,18},{18,2},{1,17},{17,1},{3,19},{19,3}} | collective-permute-start | bytes 786440 | tf_op jit(solution)/shard_map/ppermute | solution.py:107
  52.6 0.4 convolution_add_fusion.1
  53.9 4.1 %collective-permute-done.15 = f32[256,256]{1,0:T(8,128)S(1)} collective-permute-done((f32[256,256]{1,0:T(8,128)S(1)}, f32[256,256]{1,0:T(8,128)S(1)}, u32[]{:S(2)}, u32[]{:S(2)}) %collective-permute-start.15) | collective-permute-done | bytes 262176 | tf_op jit(solution)/shard_map/ppermute | solution.py:107
  59.1 1.5 %collective-permute-done.16 = f32[256,256]{1,0:T(8,128)S(1)} collective-permute-done((f32[256,256]{1,0:T(8,128)S(1)}, f32[256,256]{1,0:T(8,128)S(1)}, u32[]{:S(2)}, u32[]{:S(2)}) %collective-permute-start.16) | collective-permute-done | bytes 262176 | tf_op jit(solution)/shard_map/ppermute | solution.py:121
  60.7 1.1 %pad_maximum_fusion = f32[512,512]{1,0:T(8,128)} fusion(f32[256,512]{1,0:T(8,128)S(1)} %get-tuple-element.42, f32[256,256]{1,0:T(8,128)S(1)} %get-tuple-element.44, f32[256,256]{1,0:T(8,128)S(1)} %get-tuple-element.43), kind=kLoop, calls=%fused_computation.14 | loop fusion | flops 524288 | bytes 2097152 | tf_op jit(solution)/shard_map/concatenate | solution.py:123
  (55 shorter events, 6.0 us)
Async XLA Ops:
  0.0 6.7 %copy-start.2 = (f32[256,128]{1,0:T(8,128)S(1)}, f32[256,128]{1,0:T(8,128)}, u32[]{:S(2)}) copy-start(f32[256,128]{1,0:T(8,128)} %param.9) | copy-start | bytes 393220
  0.0 6.7 %collective-permute-start = (f32[256,128]{1,0:T(8,128)}, f32[256,128]{1,0:T(8,128)S(1)}, u32[]{:S(2)}, u32[]{:S(2)}) collective-permute-start(f32[256,128]{1,0:T(8,128)} %param.9), channel_id=1, source_target_pairs={{0,1},{1,0},{2,3},{3,2},{4,5},{5,4},{6,7},{7,6},{8,9},{9,8},{10,11... | collective-permute-start | bytes 393224 | tf_op jit(solution)/shard_map/ppermute | solution.py:34
  6.8 0.9 %copy-start.4 = (f32[256,128]{1,0:T(8,128)S(1)}, f32[256,128]{1,0:T(8,128)}, u32[]{:S(2)}) copy-start(f32[256,128]{1,0:T(8,128)} %param.7) | copy-start | bytes 393220
  6.8 2.6 %copy-start.3 = (f32[256,128]{1,0:T(8,128)S(1)}, f32[256,128]{1,0:T(8,128)}, u32[]{:S(2)}) copy-start(f32[256,128]{1,0:T(8,128)} %param.8) | copy-start | bytes 393220
  7.7 11.2 %collective-permute-start.2 = (f32[256,128]{1,0:T(8,128)S(1)}, f32[256,128]{1,0:T(8,128)S(1)}, u32[]{:S(2)}, u32[]{:S(2)}) collective-permute-start(f32[256,128]{1,0:T(8,128)S(1)} %copy-done.4), channel_id=1, source_target_pairs={{0,1},{1,0},{2,3},{3,2},{4,5},{5,4},{6,7},{7,6},{8,9},{9,8},{10,11... | collective-permute-start | bytes 393224 | tf_op jit(solution)/shard_map/ppermute | solution.py:34
  9.4 7.6 %collective-permute-start.7 = (f32[256,128]{1,0:T(8,128)S(1)}, f32[256,128]{1,0:T(8,128)S(1)}, u32[]{:S(2)}, u32[]{:S(2)}) collective-permute-start(f32[256,128]{1,0:T(8,128)S(1)} %copy-done.3), channel_id=1, source_target_pairs={{0,1},{1,0},{2,3},{3,2},{4,5},{5,4},{6,7},{7,6},{8,9},{9,8},{10,11... | collective-permute-start | bytes 393224 | tf_op jit(solution)/shard_map/ppermute | solution.py:34
  9.9 1.0 %copy-start.1 = (f32[512,128]{1,0:T(8,128)S(1)}, f32[512,128]{1,0:T(8,128)}, u32[]{:S(2)}) copy-start(f32[512,128]{1,0:T(8,128)} %param.6) | copy-start | bytes 786436
  9.9 2.7 %collective-permute-start.3 = (f32[128,256]{1,0:T(8,128)S(1)}, f32[128,256]{1,0:T(8,128)S(1)}, u32[]{:S(2)}, u32[]{:S(2)}) collective-permute-start(f32[128,256]{1,0:T(8,128)S(1)} %slice.73), channel_id=1, source_target_pairs={{0,2},{2,0},{4,6},{6,4},{8,10},{10,8},{12,14},{14,12},{16,18},{18,... | collective-permute-start | bytes 393224 | tf_op jit(solution)/shard_map/ppermute | solution.py:68
  10.8 10.0 %collective-permute-start.1 = (f32[512,128]{1,0:T(8,128)S(1)}, f32[512,128]{1,0:T(8,128)S(1)}, u32[]{:S(2)}, u32[]{:S(2)}) collective-permute-start(f32[512,128]{1,0:T(8,128)S(1)} %copy-done.1), channel_id=1, source_target_pairs={{0,1},{1,0},{2,3},{3,2},{4,5},{5,4},{6,7},{7,6},{8,9},{9,8},{10,11... | collective-permute-start | bytes 786440 | tf_op jit(solution)/shard_map/ppermute | solution.py:34
  12.6 8.4 %collective-permute-start.6 = (f32[128,256]{1,0:T(8,128)S(1)}, f32[128,256]{1,0:T(8,128)S(1)}, u32[]{:S(2)}, u32[]{:S(2)}) collective-permute-start(f32[128,256]{1,0:T(8,128)S(1)} %slice_select_fusion), channel_id=1, source_target_pairs={{16,0},{18,2},{17,1},{19,3}} | collective-permute-start | bytes 393224 | tf_op jit(solution)/shard_map/ppermute | solution.py:76
  13.9 9.1 %collective-permute-start.5 = (f32[128,256]{1,0:T(8,128)S(1)}, f32[128,256]{1,0:T(8,128)S(1)}, u32[]{:S(2)}, u32[]{:S(2)}) collective-permute-start(f32[128,256]{1,0:T(8,128)S(1)} %slice_select_fusion), channel_id=1, source_target_pairs={{8,0},{10,2},{24,16},{26,18},{9,1},{11,3},{25,17},{27,19}} | collective-permute-start | bytes 393224 | tf_op jit(solution)/shard_map/ppermute | solution.py:76
  17.0 6.8 %collective-permute-start.4 = (f32[128,256]{1,0:T(8,128)S(1)}, f32[128,256]{1,0:T(8,128)S(1)}, u32[]{:S(2)}, u32[]{:S(2)}) collective-permute-start(f32[128,256]{1,0:T(8,128)S(1)} %slice_select_fusion), channel_id=1, source_target_pairs={{4,0},{6,2},{12,8},{14,10},{20,16},{22,18},{28,24},{30,26},{5,1},{... | collective-permute-start | bytes 393224 | tf_op jit(solution)/shard_map/ppermute | solution.py:76
  18.9 7.9 %collective-permute-start.8 = (f32[3,256,256]{2,1,0:T(8,128)S(1)}, f32[3,256,256]{2,1,0:T(8,128)S(1)}, u32[]{:S(2)}, u32[]{:S(2)}) collective-permute-start(f32[3,256,256]{2,1,0:T(8,128)S(1)} %pad_maximum_fusion.1), channel_id=1, source_target_pairs={{0,2},{2,0},{4,6},{6,4},{8,10},{10,8},{12,14},{14,12},{16,18},{18,... | collective-permute-start | bytes 2359304 | tf_op jit(solution)/shard_map/ppermute | solution.py:63
  20.8 3.5 %copy-start = (f32[512,512]{1,0:T(8,128)S(1)}, f32[512,512]{1,0:T(8,128)}, u32[]{:S(2)}) copy-start(f32[512,512]{1,0:T(8,128)} %param.5) | copy-start | bytes 3145732
  23.8 5.0 %collective-permute-start.10 = (f32[128,256]{1,0:T(8,128)S(1)}, f32[128,256]{1,0:T(8,128)S(1)}, u32[]{:S(2)}, u32[]{:S(2)}) collective-permute-start(f32[128,256]{1,0:T(8,128)S(1)} %collective-permute-done.4), channel_id=1, source_target_pairs={{0,2},{2,0},{4,6},{6,4},{8,10},{10,8},{12,14},{14,12},{16,18},{18,... | collective-permute-start | bytes 393224 | tf_op jit(solution)/shard_map/ppermute | solution.py:109
  23.8 17.7 %collective-permute-start.12 = (f32[128,256]{1,0:T(8,128)S(1)}, f32[128,256]{1,0:T(8,128)S(1)}, u32[]{:S(2)}, u32[]{:S(2)}) collective-permute-start(f32[128,256]{1,0:T(8,128)S(1)} %collective-permute-done.5), channel_id=1, source_target_pairs={{0,2},{2,0},{4,6},{6,4},{8,10},{10,8},{12,14},{14,12},{16,18},{18,... | collective-permute-start | bytes 393224 | tf_op jit(solution)/shard_map/ppermute | solution.py:109
  24.3 28.7 %collective-permute-start.14 = (f32[128,256]{1,0:T(8,128)S(1)}, f32[128,256]{1,0:T(8,128)S(1)}, u32[]{:S(2)}, u32[]{:S(2)}) collective-permute-start(f32[128,256]{1,0:T(8,128)S(1)} %collective-permute-done.6), channel_id=1, source_target_pairs={{0,2},{2,0},{4,6},{6,4},{8,10},{10,8},{12,14},{14,12},{16,18},{18,... | collective-permute-start | bytes 393224 | tf_op jit(solution)/shard_map/ppermute | solution.py:109
  26.2 1.7 %collective-permute-start.9 = (f32[256,256]{1,0:T(8,128)S(1)}, f32[256,256]{1,0:T(8,128)S(1)}, u32[]{:S(2)}, u32[]{:S(2)}) collective-permute-start(f32[256,256]{1,0:T(8,128)S(1)} %constant_dynamic-slice_fusion), channel_id=1, source_target_pairs={{0,2},{2,0},{4,6},{6,4},{8,10},{10,8},{12,14},{14,12},{16,18},{18,... | collective-permute-start | bytes 786440 | tf_op jit(solution)/shard_map/ppermute | solution.py:86
  28.7 8.7 %collective-permute-start.11 = (f32[256,256]{1,0:T(8,128)S(1)}, f32[256,256]{1,0:T(8,128)S(1)}, u32[]{:S(2)}, u32[]{:S(2)}) collective-permute-start(f32[256,256]{1,0:T(8,128)S(1)} %get-tuple-element.55), channel_id=1, source_target_pairs={{0,4},{4,0},{2,6},{6,2},{8,12},{12,8},{10,14},{14,10},{16,20},{20,... | collective-permute-start | bytes 786440 | tf_op jit(solution)/shard_map/ppermute | solution.py:107
  37.8 9.7 %collective-permute-start.13 = (f32[256,256]{1,0:T(8,128)S(1)}, f32[256,256]{1,0:T(8,128)S(1)}, u32[]{:S(2)}, u32[]{:S(2)}) collective-permute-start(f32[256,256]{1,0:T(8,128)S(1)} %get-tuple-element.57), channel_id=1, source_target_pairs={{0,8},{8,0},{2,10},{10,2},{16,24},{24,16},{18,26},{26,18},{1,9},{9... | collective-permute-start | bytes 786440 | tf_op jit(solution)/shard_map/ppermute | solution.py:107
  48.0 10.1 %collective-permute-start.15 = (f32[256,256]{1,0:T(8,128)S(1)}, f32[256,256]{1,0:T(8,128)S(1)}, u32[]{:S(2)}, u32[]{:S(2)}) collective-permute-start(f32[256,256]{1,0:T(8,128)S(1)} %get-tuple-element.59), channel_id=1, source_target_pairs={{0,16},{16,0},{2,18},{18,2},{1,17},{17,1},{3,19},{19,3}} | collective-permute-start | bytes 786440 | tf_op jit(solution)/shard_map/ppermute | solution.py:107
  59.0 1.6 %collective-permute-start.16 = (f32[256,256]{1,0:T(8,128)S(1)}, f32[256,256]{1,0:T(8,128)S(1)}, u32[]{:S(2)}, u32[]{:S(2)}) collective-permute-start(f32[256,256]{1,0:T(8,128)S(1)} %get-tuple-element.61), channel_id=1, source_target_pairs={{0,2},{2,0},{4,6},{6,4},{8,10},{10,8},{12,14},{14,12},{16,18},{18,... | collective-permute-start | bytes 786440 | tf_op jit(solution)/shard_map/ppermute | solution.py:121

commit v24 on v23

--- a/solution.py
+++ b/solution.py
@@ -32,6 +32,10 @@
     for shift in range(1, n_col):
         perm = [(i, (i + shift) % n_col) for i in range(n_col)]
         by_shift.append(lax.ppermute(part, "col", perm))
+    if n_col == 2:
+        first = jnp.where(me == 0, part, by_shift[1])
+        second = jnp.where(me == 0, by_shift[1], part)
+        return jnp.concatenate([first, second], axis=1)
     stacked = jnp.stack(by_shift)
     blocks = [stacked[(me - b) % n_col] for b in range(n_col)]
     return jnp.concatenate(blocks, axis=1)

time: 62 us -> 61.5 us (level)
  waiting for transfers between devices: 29.2 us -> 30.1 us
  local copies, waits for them, and re-layouts: 1.83 us -> 0.99 us
    ppermute x4, waiting for transfers between devices: 7.3 us -> 8.15 us  [col_gather(): by_shift.append(lax.ppermute(part, 'col', perm))]
    unnamed x10, local copies, waits for them, and re-layouts: 1.72 us -> 0.88 us
where the time goes in v24:
time: 61.5 us; the launch traced here: 61.3 us
  waiting for transfers between devices  30.1 us (49%)
  starting transfers between devices  19.6 us (32%)
  matrix products  8.22 us (13%)
  other arithmetic  1.96 us (3%)
  local copies, waits for them, and re-layouts  0.99 us (2%)
    ppermute x3, waiting for transfers between devices, on_device(): received = lax.ppermute(jnp.where(is_upper, q, chain), 'row', pairs)  16.9 us
    ppermute x4, waiting for transfers between devices, col_gather(): by_shift.append(lax.ppermute(part, 'col', perm))  8.15 us
    ppermute x3, starting transfers between devices, on_device(): received = lax.ppermute(jnp.where(is_upper, q, chain), 'row', pairs)  7.73 us
    ppermute x4, starting transfers between devices, col_gather(): by_shift.append(lax.ppermute(part, 'col', perm))  6.73 us
    dot_general x16, matrix products, product_left_t(): lax.dot_general(left, right, (((0,), (0,)), ((), ())), precision=lax.Prec...  6.16 us
    ppermute x3, starting transfers between devices, on_device(): partner_factors.append(lax.ppermute(half_s, 'row', pairs))  3.86 us
    ppermute x3, waiting for transfers between devices, on_device(): partner_factors.append(lax.ppermute(half_s, 'row', pairs))  2.91 us
    dot_general x6, matrix products, product(): jnp.dot(left, right, precision=lax.Precision.HIGH, preferred_element_type...  2.07 us
  transfers between devices with their start and end apart: 17, of which 10 were waited for; matrix products, arithmetic and copies ran while one was open for 13% of the time, Pallas kernels for 0%

profile of v24, /device:TPU:0, one launch (start us, length us, event | category | flops | bytes accessed | tf_op | source)
XLA Modules:
  0.0 61.3 jit_solution(18424678451551704705)
XLA Ops:
  0.0 3.0 %collective-permute-start = (f32[256,128]{1,0:T(8,128)}, f32[256,128]{1,0:T(8,128)S(1)}, u32[]{:S(2)}, u32[]{:S(2)}) collective-permute-start(f32[256,128]{1,0:T(8,128)} %param.9), channel_id=1, source_target_pairs={{0,1},{1,0},{2,3},{3,2},{4,5},{5,4},{6,7},{7,6},{8,9},{9,8},{10,11... | collective-permute-start | bytes 393224 | tf_op jit(solution)/shard_map/ppermute | solution.py:34
  3.0 3.8 %collective-permute-done = f32[256,128]{1,0:T(8,128)S(1)} collective-permute-done((f32[256,128]{1,0:T(8,128)}, f32[256,128]{1,0:T(8,128)S(1)}, u32[]{:S(2)}, u32[]{:S(2)}) %collective-permute-start) | collective-permute-done | bytes 131104 | tf_op jit(solution)/shard_map/ppermute | solution.py:34
  6.8 0.9 %copy-done.4 = f32[256,128]{1,0:T(8,128)S(1)} copy-done((f32[256,128]{1,0:T(8,128)S(1)}, f32[256,128]{1,0:T(8,128)}, u32[]{:S(2)}) %copy-start.4) | copy-done | bytes 131096
  7.7 1.7 %collective-permute-start.2 = (f32[256,128]{1,0:T(8,128)S(1)}, f32[256,128]{1,0:T(8,128)S(1)}, u32[]{:S(2)}, u32[]{:S(2)}) collective-permute-start(f32[256,128]{1,0:T(8,128)S(1)} %copy-done.4), channel_id=1, source_target_pairs={{0,1},{1,0},{2,3},{3,2},{4,5},{5,4},{6,7},{7,6},{8,9},{9,8},{10,11... | collective-permute-start | bytes 393224 | tf_op jit(solution)/shard_map/ppermute | solution.py:34
  9.9 1.7 %collective-permute-start.1 = (f32[512,128]{1,0:T(8,128)S(1)}, f32[512,128]{1,0:T(8,128)S(1)}, u32[]{:S(2)}, u32[]{:S(2)}) collective-permute-start(f32[512,128]{1,0:T(8,128)S(1)} %copy-done.1), channel_id=1, source_target_pairs={{0,1},{1,0},{2,3},{3,2},{4,5},{5,4},{6,7},{7,6},{8,9},{9,8},{10,11... | collective-permute-start | bytes 786440 | tf_op jit(solution)/shard_map/ppermute | solution.py:34
  11.8 1.3 %collective-permute-start.6 = (f32[128,256]{1,0:T(8,128)S(1)}, f32[128,256]{1,0:T(8,128)S(1)}, u32[]{:S(2)}, u32[]{:S(2)}) collective-permute-start(f32[128,256]{1,0:T(8,128)S(1)} %slice_select_fusion), channel_id=1, source_target_pairs={{16,0},{18,2},{17,1},{19,3}} | collective-permute-start | bytes 393224 | tf_op jit(solution)/shard_map/ppermute | solution.py:80
  13.1 1.3 %collective-permute-start.5 = (f32[128,256]{1,0:T(8,128)S(1)}, f32[128,256]{1,0:T(8,128)S(1)}, u32[]{:S(2)}, u32[]{:S(2)}) collective-permute-start(f32[128,256]{1,0:T(8,128)S(1)} %slice_select_fusion), channel_id=1, source_target_pairs={{8,0},{10,2},{24,16},{26,18},{9,1},{11,3},{25,17},{27,19}} | collective-permute-start | bytes 393224 | tf_op jit(solution)/shard_map/ppermute | solution.py:80
  14.4 2.5 %collective-permute-done.7 = f32[256,128]{1,0:T(8,128)S(1)} collective-permute-done((f32[256,128]{1,0:T(8,128)S(1)}, f32[256,128]{1,0:T(8,128)S(1)}, u32[]{:S(2)}, u32[]{:S(2)}) %collective-permute-start.7) | collective-permute-done | bytes 131104 | tf_op jit(solution)/shard_map/ppermute | solution.py:34
  16.9 1.3 %collective-permute-start.4 = (f32[128,256]{1,0:T(8,128)S(1)}, f32[128,256]{1,0:T(8,128)S(1)}, u32[]{:S(2)}, u32[]{:S(2)}) collective-permute-start(f32[128,256]{1,0:T(8,128)S(1)} %slice_select_fusion), channel_id=1, source_target_pairs={{4,0},{6,2},{12,8},{14,10},{20,16},{22,18},{28,24},{30,26},{5,1},{... | collective-permute-start | bytes 393224 | tf_op jit(solution)/shard_map/ppermute | solution.py:80
  19.0 1.8 %collective-permute-done.1 = f32[512,128]{1,0:T(8,128)S(1)} collective-permute-done((f32[512,128]{1,0:T(8,128)S(1)}, f32[512,128]{1,0:T(8,128)S(1)}, u32[]{:S(2)}, u32[]{:S(2)}) %collective-permute-start.1) | collective-permute-done | bytes 262176 | tf_op jit(solution)/shard_map/ppermute | solution.py:34
  20.9 2.1 %collective-permute-done.5 = f32[128,256]{1,0:T(8,128)S(1)} collective-permute-done((f32[128,256]{1,0:T(8,128)S(1)}, f32[128,256]{1,0:T(8,128)S(1)}, u32[]{:S(2)}, u32[]{:S(2)}) %collective-permute-start.5) | collective-permute-done | bytes 131104 | tf_op jit(solution)/shard_map/ppermute | solution.py:80
  23.0 0.8 %collective-permute-done.4 = f32[128,256]{1,0:T(8,128)S(1)} collective-permute-done((f32[128,256]{1,0:T(8,128)S(1)}, f32[128,256]{1,0:T(8,128)S(1)}, u32[]{:S(2)}, u32[]{:S(2)}) %collective-permute-start.4) | collective-permute-done | bytes 131104 | tf_op jit(solution)/shard_map/ppermute | solution.py:80
  23.8 0.5 collective-permute-start.12
  24.3 0.6 %fusion.3 = f32[256,512]{1,0:T(8,128)S(1)} fusion(f32[512,512]{1,0:T(8,128)S(1)} %copy-done, f32[512,256]{1,0:T(8,128)S(1)} %pad_maximum_fusion.2), kind=kOutput, calls=%fused_computation.22 | convolution fusion | flops 403308544 | bytes 2097152 | tf_op jit(solution)/shard_map/dot_general | solution.py:12
  24.9 0.5 fusion.22
  25.4 0.6 convolution_subtract_fusion
  26.2 0.6 collective-permute-start.9
  26.9 0.4 fusion.15
  27.3 0.6 collective-permute-done.9
  27.9 0.4 select_subtract_fusion.1
  28.3 0.4 broadcast_select_fusion.4
  29.4 7.9 %collective-permute-done.11 = f32[256,256]{1,0:T(8,128)S(1)} collective-permute-done((f32[256,256]{1,0:T(8,128)S(1)}, f32[256,256]{1,0:T(8,128)S(1)}, u32[]{:S(2)}, u32[]{:S(2)}) %collective-permute-start.11) | collective-permute-done | bytes 262176 | tf_op jit(solution)/shard_map/ppermute | solution.py:111
  37.4 0.4 broadcast_select_fusion.3
  37.8 3.3 %collective-permute-start.13 = (f32[256,256]{1,0:T(8,128)S(1)}, f32[256,256]{1,0:T(8,128)S(1)}, u32[]{:S(2)}, u32[]{:S(2)}) collective-permute-start(f32[256,256]{1,0:T(8,128)S(1)} %get-tuple-element.57), channel_id=1, source_target_pairs={{0,8},{8,0},{2,10},{10,2},{16,24},{24,16},{18,26},{26,18},{1,9},{9... | collective-permute-start | bytes 786440 | tf_op jit(solution)/shard_map/ppermute | solution.py:111
  42.5 5.0 %collective-permute-done.13 = f32[256,256]{1,0:T(8,128)S(1)} collective-permute-done((f32[256,256]{1,0:T(8,128)S(1)}, f32[256,256]{1,0:T(8,128)S(1)}, u32[]{:S(2)}, u32[]{:S(2)}) %collective-permute-start.13) | collective-permute-done | bytes 262176 | tf_op jit(solution)/shard_map/ppermute | solution.py:111
  47.5 0.4 broadcast_select_fusion.2
  47.9 4.3 %collective-permute-start.15 = (f32[256,256]{1,0:T(8,128)S(1)}, f32[256,256]{1,0:T(8,128)S(1)}, u32[]{:S(2)}, u32[]{:S(2)}) collective-permute-start(f32[256,256]{1,0:T(8,128)S(1)} %get-tuple-element.59), channel_id=1, source_target_pairs={{0,16},{16,0},{2,18},{18,2},{1,17},{17,1},{3,19},{19,3}} | collective-permute-start | bytes 786440 | tf_op jit(solution)/shard_map/ppermute | solution.py:111
  52.3 0.4 convolution_add_fusion.1
  53.6 4.0 %collective-permute-done.15 = f32[256,256]{1,0:T(8,128)S(1)} collective-permute-done((f32[256,256]{1,0:T(8,128)S(1)}, f32[256,256]{1,0:T(8,128)S(1)}, u32[]{:S(2)}, u32[]{:S(2)}) %collective-permute-start.15) | collective-permute-done | bytes 262176 | tf_op jit(solution)/shard_map/ppermute | solution.py:111
  57.6 0.4 convolution_add_fusion.2
  58.7 1.5 %collective-permute-done.16 = f32[256,256]{1,0:T(8,128)S(1)} collective-permute-done((f32[256,256]{1,0:T(8,128)S(1)}, f32[256,256]{1,0:T(8,128)S(1)}, u32[]{:S(2)}, u32[]{:S(2)}) %collective-permute-start.16) | collective-permute-done | bytes 262176 | tf_op jit(solution)/shard_map/ppermute | solution.py:125
  60.2 1.1 %pad_maximum_fusion = f32[512,512]{1,0:T(8,128)} fusion(f32[256,512]{1,0:T(8,128)S(1)} %get-tuple-element.42, f32[256,256]{1,0:T(8,128)S(1)} %get-tuple-element.44, f32[256,256]{1,0:T(8,128)S(1)} %get-tuple-element.43), kind=kLoop, calls=%fused_computation.14 | loop fusion | flops 524288 | bytes 2097152 | tf_op jit(solution)/shard_map/concatenate | solution.py:127
  (55 shorter events, 5.4 us)
Async XLA Ops:
  0.0 6.7 %copy-start.2 = (f32[256,128]{1,0:T(8,128)S(1)}, f32[256,128]{1,0:T(8,128)}, u32[]{:S(2)}) copy-start(f32[256,128]{1,0:T(8,128)} %param.9) | copy-start | bytes 393220
  0.0 6.7 %collective-permute-start = (f32[256,128]{1,0:T(8,128)}, f32[256,128]{1,0:T(8,128)S(1)}, u32[]{:S(2)}, u32[]{:S(2)}) collective-permute-start(f32[256,128]{1,0:T(8,128)} %param.9), channel_id=1, source_target_pairs={{0,1},{1,0},{2,3},{3,2},{4,5},{5,4},{6,7},{7,6},{8,9},{9,8},{10,11... | collective-permute-start | bytes 393224 | tf_op jit(solution)/shard_map/ppermute | solution.py:34
  6.8 0.9 %copy-start.4 = (f32[256,128]{1,0:T(8,128)S(1)}, f32[256,128]{1,0:T(8,128)}, u32[]{:S(2)}) copy-start(f32[256,128]{1,0:T(8,128)} %param.7) | copy-start | bytes 393220
  6.8 2.6 %copy-start.3 = (f32[256,128]{1,0:T(8,128)S(1)}, f32[256,128]{1,0:T(8,128)}, u32[]{:S(2)}) copy-start(f32[256,128]{1,0:T(8,128)} %param.8) | copy-start | bytes 393220
  7.7 2.3 %copy-start.1 = (f32[512,128]{1,0:T(8,128)S(1)}, f32[512,128]{1,0:T(8,128)}, u32[]{:S(2)}) copy-start(f32[512,128]{1,0:T(8,128)} %param.6) | copy-start | bytes 786436
  7.7 11.1 %collective-permute-start.2 = (f32[256,128]{1,0:T(8,128)S(1)}, f32[256,128]{1,0:T(8,128)S(1)}, u32[]{:S(2)}, u32[]{:S(2)}) collective-permute-start(f32[256,128]{1,0:T(8,128)S(1)} %copy-done.4), channel_id=1, source_target_pairs={{0,1},{1,0},{2,3},{3,2},{4,5},{5,4},{6,7},{7,6},{8,9},{9,8},{10,11... | collective-permute-start | bytes 393224 | tf_op jit(solution)/shard_map/ppermute | solution.py:34
  9.4 7.6 %collective-permute-start.7 = (f32[256,128]{1,0:T(8,128)S(1)}, f32[256,128]{1,0:T(8,128)S(1)}, u32[]{:S(2)}, u32[]{:S(2)}) collective-permute-start(f32[256,128]{1,0:T(8,128)S(1)} %copy-done.3), channel_id=1, source_target_pairs={{0,1},{1,0},{2,3},{3,2},{4,5},{5,4},{6,7},{7,6},{8,9},{9,8},{10,11... | collective-permute-start | bytes 393224 | tf_op jit(solution)/shard_map/ppermute | solution.py:34
  9.8 1.9 %collective-permute-start.3 = (f32[128,256]{1,0:T(8,128)S(1)}, f32[128,256]{1,0:T(8,128)S(1)}, u32[]{:S(2)}, u32[]{:S(2)}) collective-permute-start(f32[128,256]{1,0:T(8,128)S(1)} %slice.73), channel_id=1, source_target_pairs={{0,2},{2,0},{4,6},{6,4},{8,10},{10,8},{12,14},{14,12},{16,18},{18,... | collective-permute-start | bytes 393224 | tf_op jit(solution)/shard_map/ppermute | solution.py:72
  9.9 10.9 %collective-permute-start.1 = (f32[512,128]{1,0:T(8,128)S(1)}, f32[512,128]{1,0:T(8,128)S(1)}, u32[]{:S(2)}, u32[]{:S(2)}) collective-permute-start(f32[512,128]{1,0:T(8,128)S(1)} %copy-done.1), channel_id=1, source_target_pairs={{0,1},{1,0},{2,3},{3,2},{4,5},{5,4},{6,7},{7,6},{8,9},{9,8},{10,11... | collective-permute-start | bytes 786440 | tf_op jit(solution)/shard_map/ppermute | solution.py:34
  11.8 9.1 %collective-permute-start.6 = (f32[128,256]{1,0:T(8,128)S(1)}, f32[128,256]{1,0:T(8,128)S(1)}, u32[]{:S(2)}, u32[]{:S(2)}) collective-permute-start(f32[128,256]{1,0:T(8,128)S(1)} %slice_select_fusion), channel_id=1, source_target_pairs={{16,0},{18,2},{17,1},{19,3}} | collective-permute-start | bytes 393224 | tf_op jit(solution)/shard_map/ppermute | solution.py:80
  13.1 9.9 %collective-permute-start.5 = (f32[128,256]{1,0:T(8,128)S(1)}, f32[128,256]{1,0:T(8,128)S(1)}, u32[]{:S(2)}, u32[]{:S(2)}) collective-permute-start(f32[128,256]{1,0:T(8,128)S(1)} %slice_select_fusion), channel_id=1, source_target_pairs={{8,0},{10,2},{24,16},{26,18},{9,1},{11,3},{25,17},{27,19}} | collective-permute-start | bytes 393224 | tf_op jit(solution)/shard_map/ppermute | solution.py:80
  16.9 6.8 %collective-permute-start.4 = (f32[128,256]{1,0:T(8,128)S(1)}, f32[128,256]{1,0:T(8,128)S(1)}, u32[]{:S(2)}, u32[]{:S(2)}) collective-permute-start(f32[128,256]{1,0:T(8,128)S(1)} %slice_select_fusion), channel_id=1, source_target_pairs={{4,0},{6,2},{12,8},{14,10},{20,16},{22,18},{28,24},{30,26},{5,1},{... | collective-permute-start | bytes 393224 | tf_op jit(solution)/shard_map/ppermute | solution.py:80
  18.8 7.9 %collective-permute-start.8 = (f32[3,256,256]{2,1,0:T(8,128)S(1)}, f32[3,256,256]{2,1,0:T(8,128)S(1)}, u32[]{:S(2)}, u32[]{:S(2)}) collective-permute-start(f32[3,256,256]{2,1,0:T(8,128)S(1)} %pad_maximum_fusion.1), channel_id=1, source_target_pairs={{0,2},{2,0},{4,6},{6,4},{8,10},{10,8},{12,14},{14,12},{16,18},{18,... | collective-permute-start | bytes 2359304 | tf_op jit(solution)/shard_map/ppermute | solution.py:67
  18.9 5.4 %copy-start = (f32[512,512]{1,0:T(8,128)S(1)}, f32[512,512]{1,0:T(8,128)}, u32[]{:S(2)}) copy-start(f32[512,512]{1,0:T(8,128)} %param.5) | copy-start | bytes 3145732
  23.8 5.0 %collective-permute-start.10 = (f32[128,256]{1,0:T(8,128)S(1)}, f32[128,256]{1,0:T(8,128)S(1)}, u32[]{:S(2)}, u32[]{:S(2)}) collective-permute-start(f32[128,256]{1,0:T(8,128)S(1)} %collective-permute-done.4), channel_id=1, source_target_pairs={{0,2},{2,0},{4,6},{6,4},{8,10},{10,8},{12,14},{14,12},{16,18},{18,... | collective-permute-start | bytes 393224 | tf_op jit(solution)/shard_map/ppermute | solution.py:113
  23.8 17.7 %collective-permute-start.12 = (f32[128,256]{1,0:T(8,128)S(1)}, f32[128,256]{1,0:T(8,128)S(1)}, u32[]{:S(2)}, u32[]{:S(2)}) collective-permute-start(f32[128,256]{1,0:T(8,128)S(1)} %collective-permute-done.5), channel_id=1, source_target_pairs={{0,2},{2,0},{4,6},{6,4},{8,10},{10,8},{12,14},{14,12},{16,18},{18,... | collective-permute-start | bytes 393224 | tf_op jit(solution)/shard_map/ppermute | solution.py:113
  24.3 28.4 %collective-permute-start.14 = (f32[128,256]{1,0:T(8,128)S(1)}, f32[128,256]{1,0:T(8,128)S(1)}, u32[]{:S(2)}, u32[]{:S(2)}) collective-permute-start(f32[128,256]{1,0:T(8,128)S(1)} %collective-permute-done.6), channel_id=1, source_target_pairs={{0,2},{2,0},{4,6},{6,4},{8,10},{10,8},{12,14},{14,12},{16,18},{18,... | collective-permute-start | bytes 393224 | tf_op jit(solution)/shard_map/ppermute | solution.py:113
  26.2 1.7 %collective-permute-start.9 = (f32[256,256]{1,0:T(8,128)S(1)}, f32[256,256]{1,0:T(8,128)S(1)}, u32[]{:S(2)}, u32[]{:S(2)}) collective-permute-start(f32[256,256]{1,0:T(8,128)S(1)} %constant_dynamic-slice_fusion), channel_id=1, source_target_pairs={{0,2},{2,0},{4,6},{6,4},{8,10},{10,8},{12,14},{14,12},{16,18},{18,... | collective-permute-start | bytes 786440 | tf_op jit(solution)/shard_map/ppermute | solution.py:90
  28.7 8.7 %collective-permute-start.11 = (f32[256,256]{1,0:T(8,128)S(1)}, f32[256,256]{1,0:T(8,128)S(1)}, u32[]{:S(2)}, u32[]{:S(2)}) collective-permute-start(f32[256,256]{1,0:T(8,128)S(1)} %get-tuple-element.55), channel_id=1, source_target_pairs={{0,4},{4,0},{2,6},{6,2},{8,12},{12,8},{10,14},{14,10},{16,20},{20,... | collective-permute-start | bytes 786440 | tf_op jit(solution)/shard_map/ppermute | solution.py:111
  37.8 9.7 %collective-permute-start.13 = (f32[256,256]{1,0:T(8,128)S(1)}, f32[256,256]{1,0:T(8,128)S(1)}, u32[]{:S(2)}, u32[]{:S(2)}) collective-permute-start(f32[256,256]{1,0:T(8,128)S(1)} %get-tuple-element.57), channel_id=1, source_target_pairs={{0,8},{8,0},{2,10},{10,2},{16,24},{24,16},{18,26},{26,18},{1,9},{9... | collective-permute-start | bytes 786440 | tf_op jit(solution)/shard_map/ppermute | solution.py:111
  47.9 9.7 %collective-permute-start.15 = (f32[256,256]{1,0:T(8,128)S(1)}, f32[256,256]{1,0:T(8,128)S(1)}, u32[]{:S(2)}, u32[]{:S(2)}) collective-permute-start(f32[256,256]{1,0:T(8,128)S(1)} %get-tuple-element.59), channel_id=1, source_target_pairs={{0,16},{16,0},{2,18},{18,2},{1,17},{17,1},{3,19},{19,3}} | collective-permute-start | bytes 786440 | tf_op jit(solution)/shard_map/ppermute | solution.py:111
  58.6 1.6 %collective-permute-start.16 = (f32[256,256]{1,0:T(8,128)S(1)}, f32[256,256]{1,0:T(8,128)S(1)}, u32[]{:S(2)}, u32[]{:S(2)}) collective-permute-start(f32[256,256]{1,0:T(8,128)S(1)} %get-tuple-element.61), channel_id=1, source_target_pairs={{0,2},{2,0},{4,6},{6,4},{8,10},{10,8},{12,14},{14,12},{16,18},{18,... | collective-permute-start | bytes 786440 | tf_op jit(solution)/shard_map/ppermute | solution.py:125

commit v25 on v24

--- a/solution.py
+++ b/solution.py
@@ -79,7 +79,10 @@
             pairs += [(i + step, i), (i + step + 1, i + 1)]
         partner_factors.append(lax.ppermute(half_s, "row", pairs))
 
-    leaf_full, leaf_tri, partner_factors = lax.optimization_barrier((leaf_full, leaf_tri, partner_factors))
+    mates_of = [lax.ppermute(got, "row", swap) for got in partner_factors]
+    leaf_full, leaf_tri, partner_factors, mates_of = lax.optimization_barrier(
+        (leaf_full, leaf_tri, partner_factors, mates_of)
+    )
     leaf_vectors = unit_lower(leaf_full)
     leaf_factor = jnp.triu(leaf_tri)
     leaf_w = product_left_t(leaf_factor, product_left_t(leaf_vectors, slab))
@@ -110,7 +113,7 @@
         q = product_left_t(jnp.where(is_upper, even3[2], zeros), chain)
         received = lax.ppermute(jnp.where(is_upper, q, chain), "row", pairs)
         mine = partner_factors[level - 1]
-        mates = lax.ppermute(mine, "row", swap)
+        mates = mates_of[level - 1]
         top_rows = jnp.where(is_lower & (core == 0), mine, jnp.where(is_lower, mates, 0.0))
         bottom_rows = jnp.where(is_lower & (core == 0), mates, jnp.where(is_lower, mine, 0.0))
         own_part = product_left_t(top_rows, chain[:hw]) + product_left_t(bottom_rows, chain[hw:])

time: 61.5 us -> 62.3 us (1.013)
  waiting for transfers between devices: 30.1 us -> 31.7 us
  starting transfers between devices: 19.6 us -> 18.8 us
    ppermute x3, waiting for transfers between devices: 2.91 us -> 4.8 us  [on_device(): partner_factors.append(lax.ppermute(half_s, 'row', pairs))]
    ppermute x4, waiting for transfers between devices: 8.15 us -> 6.31 us  [col_gather(): by_shift.append(lax.ppermute(part, 'col', perm))]
    ppermute x3, waiting for transfers between devices: 0.01 us -> 1.25 us  [on_device(): mates_of = [lax.ppermute(got, 'row', swap) for got in partner_factors]]
  transfers between devices with their start and end apart: 17 -> 17, of which waited for: 10 -> 12; matrix products, arithmetic and copies ran while one was open for 13% -> 9% of each run, Pallas kernels for 0% -> 0%
where the time goes in v25:
time: 62.3 us; the launch traced here: 62.1 us
  waiting for transfers between devices  31.7 us (51%)
  starting transfers between devices  18.8 us (30%)
  matrix products  8.21 us (13%)
  other arithmetic  1.96 us (3%)
  local copies, waits for them, and re-layouts  0.99 us (2%)
    ppermute x3, waiting for transfers between devices, on_device(): received = lax.ppermute(jnp.where(is_upper, q, chain), 'row', pairs)  17 us
    ppermute x3, starting transfers between devices, on_device(): received = lax.ppermute(jnp.where(is_upper, q, chain), 'row', pairs)  7.72 us
    ppermute x4, starting transfers between devices, col_gather(): by_shift.append(lax.ppermute(part, 'col', perm))  6.73 us
    ppermute x4, waiting for transfers between devices, col_gather(): by_shift.append(lax.ppermute(part, 'col', perm))  6.31 us
    dot_general x16, matrix products, product_left_t(): lax.dot_general(left, right, (((0,), (0,)), ((), ())), precision=lax.Prec...  6.14 us
    ppermute x3, waiting for transfers between devices, on_device(): partner_factors.append(lax.ppermute(half_s, 'row', pairs))  4.8 us
    ppermute x3, starting transfers between devices, on_device(): partner_factors.append(lax.ppermute(half_s, 'row', pairs))  3.86 us
    dot_general x6, matrix products, product(): jnp.dot(left, right, precision=lax.Precision.HIGH, preferred_element_type...  2.07 us
  transfers between devices with their start and end apart: 17, of which 12 were waited for; matrix products, arithmetic and copies ran while one was open for 9% of the time, Pallas kernels for 0%

profile of v25, /device:TPU:0, one launch (start us, length us, event | category | flops | bytes accessed | tf_op | source)
XLA Modules:
  0.0 62.1 jit_solution(5686347875612118164)
XLA Ops:
  0.0 3.0 %collective-permute-start = (f32[256,128]{1,0:T(8,128)}, f32[256,128]{1,0:T(8,128)S(1)}, u32[]{:S(2)}, u32[]{:S(2)}) collective-permute-start(f32[256,128]{1,0:T(8,128)} %param.9), channel_id=1, source_target_pairs={{0,1},{1,0},{2,3},{3,2},{4,5},{5,4},{6,7},{7,6},{8,9},{9,8},{10,11... | collective-permute-start | bytes 393224 | tf_op jit(solution)/shard_map/ppermute | solution.py:34
  3.0 3.8 %collective-permute-done = f32[256,128]{1,0:T(8,128)S(1)} collective-permute-done((f32[256,128]{1,0:T(8,128)}, f32[256,128]{1,0:T(8,128)S(1)}, u32[]{:S(2)}, u32[]{:S(2)}) %collective-permute-start) | collective-permute-done | bytes 131104 | tf_op jit(solution)/shard_map/ppermute | solution.py:34
  6.8 0.9 %copy-done.4 = f32[256,128]{1,0:T(8,128)S(1)} copy-done((f32[256,128]{1,0:T(8,128)S(1)}, f32[256,128]{1,0:T(8,128)}, u32[]{:S(2)}) %copy-start.4) | copy-done | bytes 131096
  7.7 1.7 %collective-permute-start.2 = (f32[256,128]{1,0:T(8,128)S(1)}, f32[256,128]{1,0:T(8,128)S(1)}, u32[]{:S(2)}, u32[]{:S(2)}) collective-permute-start(f32[256,128]{1,0:T(8,128)S(1)} %copy-done.4), channel_id=1, source_target_pairs={{0,1},{1,0},{2,3},{3,2},{4,5},{5,4},{6,7},{7,6},{8,9},{9,8},{10,11... | collective-permute-start | bytes 393224 | tf_op jit(solution)/shard_map/ppermute | solution.py:34
  9.9 1.7 %collective-permute-start.1 = (f32[512,128]{1,0:T(8,128)S(1)}, f32[512,128]{1,0:T(8,128)S(1)}, u32[]{:S(2)}, u32[]{:S(2)}) collective-permute-start(f32[512,128]{1,0:T(8,128)S(1)} %copy-done.1), channel_id=1, source_target_pairs={{0,1},{1,0},{2,3},{3,2},{4,5},{5,4},{6,7},{7,6},{8,9},{9,8},{10,11... | collective-permute-start | bytes 786440 | tf_op jit(solution)/shard_map/ppermute | solution.py:34
  11.8 1.3 %collective-permute-start.6 = (f32[128,256]{1,0:T(8,128)S(1)}, f32[128,256]{1,0:T(8,128)S(1)}, u32[]{:S(2)}, u32[]{:S(2)}) collective-permute-start(f32[128,256]{1,0:T(8,128)S(1)} %slice_select_fusion), channel_id=1, source_target_pairs={{16,0},{18,2},{17,1},{19,3}} | collective-permute-start | bytes 393224 | tf_op jit(solution)/shard_map/ppermute | solution.py:80
  13.1 1.3 %collective-permute-start.5 = (f32[128,256]{1,0:T(8,128)S(1)}, f32[128,256]{1,0:T(8,128)S(1)}, u32[]{:S(2)}, u32[]{:S(2)}) collective-permute-start(f32[128,256]{1,0:T(8,128)S(1)} %slice_select_fusion), channel_id=1, source_target_pairs={{8,0},{10,2},{24,16},{26,18},{9,1},{11,3},{25,17},{27,19}} | collective-permute-start | bytes 393224 | tf_op jit(solution)/shard_map/ppermute | solution.py:80
  14.4 2.5 %collective-permute-done.10 = f32[256,128]{1,0:T(8,128)S(1)} collective-permute-done((f32[256,128]{1,0:T(8,128)S(1)}, f32[256,128]{1,0:T(8,128)S(1)}, u32[]{:S(2)}, u32[]{:S(2)}) %collective-permute-start.10) | collective-permute-done | bytes 131104 | tf_op jit(solution)/shard_map/ppermute | solution.py:34
  16.9 1.3 %collective-permute-start.4 = (f32[128,256]{1,0:T(8,128)S(1)}, f32[128,256]{1,0:T(8,128)S(1)}, u32[]{:S(2)}, u32[]{:S(2)}) collective-permute-start(f32[128,256]{1,0:T(8,128)S(1)} %slice_select_fusion), channel_id=1, source_target_pairs={{4,0},{6,2},{12,8},{14,10},{20,16},{22,18},{28,24},{30,26},{5,1},{... | collective-permute-start | bytes 393224 | tf_op jit(solution)/shard_map/ppermute | solution.py:80
  19.0 1.3 %collective-permute-done.6 = f32[128,256]{1,0:T(8,128)S(1)} collective-permute-done((f32[128,256]{1,0:T(8,128)S(1)}, f32[128,256]{1,0:T(8,128)S(1)}, u32[]{:S(2)}, u32[]{:S(2)}) %collective-permute-start.6) | collective-permute-done | bytes 131104 | tf_op jit(solution)/shard_map/ppermute | solution.py:80
  20.3 2.7 %collective-permute-done.5 = f32[128,256]{1,0:T(8,128)S(1)} collective-permute-done((f32[128,256]{1,0:T(8,128)S(1)}, f32[128,256]{1,0:T(8,128)S(1)}, u32[]{:S(2)}, u32[]{:S(2)}) %collective-permute-start.5) | collective-permute-done | bytes 131104 | tf_op jit(solution)/shard_map/ppermute | solution.py:80
  23.0 0.8 %collective-permute-done.4 = f32[128,256]{1,0:T(8,128)S(1)} collective-permute-done((f32[128,256]{1,0:T(8,128)S(1)}, f32[128,256]{1,0:T(8,128)S(1)}, u32[]{:S(2)}, u32[]{:S(2)}) %collective-permute-start.4) | collective-permute-done | bytes 131104 | tf_op jit(solution)/shard_map/ppermute | solution.py:80
  23.9 0.4 collective-permute-done.8
  24.3 0.8 %collective-permute-done.7 = f32[128,256]{1,0:T(8,128)S(1)} collective-permute-done((f32[128,256]{1,0:T(8,128)S(1)}, f32[128,256]{1,0:T(8,128)S(1)}, u32[]{:S(2)}, u32[]{:S(2)}) %collective-permute-start.7) | collective-permute-done | bytes 131104 | tf_op jit(solution)/shard_map/ppermute | solution.py:82
  25.1 0.6 %fusion.3 = f32[256,512]{1,0:T(8,128)S(1)} fusion(f32[512,512]{1,0:T(8,128)S(1)} %copy-done, f32[512,256]{1,0:T(8,128)S(1)} %pad_maximum_fusion.2), kind=kOutput, calls=%fused_computation.22 | convolution fusion | flops 403308544 | bytes 2097152 | tf_op jit(solution)/shard_map/dot_general | solution.py:12
  25.8 0.5 fusion.22
  26.3 0.6 convolution_subtract_fusion
  27.4 0.4 fusion.15
  27.8 0.8 %collective-permute-done.12 = f32[256,256]{1,0:T(8,128)S(1)} collective-permute-done((f32[256,256]{1,0:T(8,128)S(1)}, f32[256,256]{1,0:T(8,128)S(1)}, u32[]{:S(2)}, u32[]{:S(2)}) %collective-permute-start.12) | collective-permute-done | bytes 262176 | tf_op jit(solution)/shard_map/ppermute | solution.py:93
  28.6 0.4 select_subtract_fusion.1
  29.0 0.4 broadcast_select_fusion.4
  30.1 7.7 %collective-permute-done.13 = f32[256,256]{1,0:T(8,128)S(1)} collective-permute-done((f32[256,256]{1,0:T(8,128)S(1)}, f32[256,256]{1,0:T(8,128)S(1)}, u32[]{:S(2)}, u32[]{:S(2)}) %collective-permute-start.13) | collective-permute-done | bytes 262176 | tf_op jit(solution)/shard_map/ppermute | solution.py:114
  38.3 0.4 broadcast_select_fusion.3
  38.7 3.3 %collective-permute-start.14 = (f32[256,256]{1,0:T(8,128)S(1)}, f32[256,256]{1,0:T(8,128)S(1)}, u32[]{:S(2)}, u32[]{:S(2)}) collective-permute-start(f32[256,256]{1,0:T(8,128)S(1)} %get-tuple-element.63), channel_id=1, source_target_pairs={{0,8},{8,0},{2,10},{10,2},{16,24},{24,16},{18,26},{26,18},{1,9},{9... | collective-permute-start | bytes 786440 | tf_op jit(solution)/shard_map/ppermute | solution.py:114
  42.9 5.2 %collective-permute-done.14 = f32[256,256]{1,0:T(8,128)S(1)} collective-permute-done((f32[256,256]{1,0:T(8,128)S(1)}, f32[256,256]{1,0:T(8,128)S(1)}, u32[]{:S(2)}, u32[]{:S(2)}) %collective-permute-start.14) | collective-permute-done | bytes 262176 | tf_op jit(solution)/shard_map/ppermute | solution.py:114
  48.2 0.4 convolution_add_fusion.1
  48.6 0.4 broadcast_select_fusion.2
  49.0 4.3 %collective-permute-start.15 = (f32[256,256]{1,0:T(8,128)S(1)}, f32[256,256]{1,0:T(8,128)S(1)}, u32[]{:S(2)}, u32[]{:S(2)}) collective-permute-start(f32[256,256]{1,0:T(8,128)S(1)} %get-tuple-element.65), channel_id=1, source_target_pairs={{0,16},{16,0},{2,18},{18,2},{1,17},{17,1},{3,19},{19,3}} | collective-permute-start | bytes 786440 | tf_op jit(solution)/shard_map/ppermute | solution.py:114
  54.2 4.1 %collective-permute-done.15 = f32[256,256]{1,0:T(8,128)S(1)} collective-permute-done((f32[256,256]{1,0:T(8,128)S(1)}, f32[256,256]{1,0:T(8,128)S(1)}, u32[]{:S(2)}, u32[]{:S(2)}) %collective-permute-start.15) | collective-permute-done | bytes 262176 | tf_op jit(solution)/shard_map/ppermute | solution.py:114
  58.4 0.4 convolution_add_fusion.2
  59.4 1.5 %collective-permute-done.16 = f32[256,256]{1,0:T(8,128)S(1)} collective-permute-done((f32[256,256]{1,0:T(8,128)S(1)}, f32[256,256]{1,0:T(8,128)S(1)}, u32[]{:S(2)}, u32[]{:S(2)}) %collective-permute-start.16) | collective-permute-done | bytes 262176 | tf_op jit(solution)/shard_map/ppermute | solution.py:128
  61.0 1.1 %pad_maximum_fusion = f32[512,512]{1,0:T(8,128)} fusion(f32[256,512]{1,0:T(8,128)S(1)} %get-tuple-element.48, f32[256,256]{1,0:T(8,128)S(1)} %get-tuple-element.50, f32[256,256]{1,0:T(8,128)S(1)} %get-tuple-element.49), kind=kLoop, calls=%fused_computation.14 | loop fusion | flops 524288 | bytes 2097152 | tf_op jit(solution)/shard_map/concatenate | solution.py:130
  (55 shorter events, 5.7 us)
Async XLA Ops:
  0.0 6.7 %copy-start.2 = (f32[256,128]{1,0:T(8,128)S(1)}, f32[256,128]{1,0:T(8,128)}, u32[]{:S(2)}) copy-start(f32[256,128]{1,0:T(8,128)} %param.9) | copy-start | bytes 393220
  0.0 6.7 %collective-permute-start = (f32[256,128]{1,0:T(8,128)}, f32[256,128]{1,0:T(8,128)S(1)}, u32[]{:S(2)}, u32[]{:S(2)}) collective-permute-start(f32[256,128]{1,0:T(8,128)} %param.9), channel_id=1, source_target_pairs={{0,1},{1,0},{2,3},{3,2},{4,5},{5,4},{6,7},{7,6},{8,9},{9,8},{10,11... | collective-permute-start | bytes 393224 | tf_op jit(solution)/shard_map/ppermute | solution.py:34
  6.8 0.9 %copy-start.4 = (f32[256,128]{1,0:T(8,128)S(1)}, f32[256,128]{1,0:T(8,128)}, u32[]{:S(2)}) copy-start(f32[256,128]{1,0:T(8,128)} %param.7) | copy-start | bytes 393220
  6.8 2.6 %copy-start.3 = (f32[256,128]{1,0:T(8,128)S(1)}, f32[256,128]{1,0:T(8,128)}, u32[]{:S(2)}) copy-start(f32[256,128]{1,0:T(8,128)} %param.8) | copy-start | bytes 393220
  7.7 2.3 %copy-start.1 = (f32[512,128]{1,0:T(8,128)S(1)}, f32[512,128]{1,0:T(8,128)}, u32[]{:S(2)}) copy-start(f32[512,128]{1,0:T(8,128)} %param.6) | copy-start | bytes 786436
  7.7 11.1 %collective-permute-start.2 = (f32[256,128]{1,0:T(8,128)S(1)}, f32[256,128]{1,0:T(8,128)S(1)}, u32[]{:S(2)}, u32[]{:S(2)}) collective-permute-start(f32[256,128]{1,0:T(8,128)S(1)} %copy-done.4), channel_id=1, source_target_pairs={{0,1},{1,0},{2,3},{3,2},{4,5},{5,4},{6,7},{7,6},{8,9},{9,8},{10,11... | collective-permute-start | bytes 393224 | tf_op jit(solution)/shard_map/ppermute | solution.py:34
  9.4 7.6 %collective-permute-start.10 = (f32[256,128]{1,0:T(8,128)S(1)}, f32[256,128]{1,0:T(8,128)S(1)}, u32[]{:S(2)}, u32[]{:S(2)}) collective-permute-start(f32[256,128]{1,0:T(8,128)S(1)} %copy-done.3), channel_id=1, source_target_pairs={{0,1},{1,0},{2,3},{3,2},{4,5},{5,4},{6,7},{7,6},{8,9},{9,8},{10,11... | collective-permute-start | bytes 393224 | tf_op jit(solution)/shard_map/ppermute | solution.py:34
  9.8 1.9 %collective-permute-start.3 = (f32[128,256]{1,0:T(8,128)S(1)}, f32[128,256]{1,0:T(8,128)S(1)}, u32[]{:S(2)}, u32[]{:S(2)}) collective-permute-start(f32[128,256]{1,0:T(8,128)S(1)} %slice.73), channel_id=1, source_target_pairs={{0,2},{2,0},{4,6},{6,4},{8,10},{10,8},{12,14},{14,12},{16,18},{18,... | collective-permute-start | bytes 393224 | tf_op jit(solution)/shard_map/ppermute | solution.py:72
  9.9 13.9 %collective-permute-start.1 = (f32[512,128]{1,0:T(8,128)S(1)}, f32[512,128]{1,0:T(8,128)S(1)}, u32[]{:S(2)}, u32[]{:S(2)}) collective-permute-start(f32[512,128]{1,0:T(8,128)S(1)} %copy-done.1), channel_id=1, source_target_pairs={{0,1},{1,0},{2,3},{3,2},{4,5},{5,4},{6,7},{7,6},{8,9},{9,8},{10,11... | collective-permute-start | bytes 786440 | tf_op jit(solution)/shard_map/ppermute | solution.py:34
  11.8 8.5 %collective-permute-start.6 = (f32[128,256]{1,0:T(8,128)S(1)}, f32[128,256]{1,0:T(8,128)S(1)}, u32[]{:S(2)}, u32[]{:S(2)}) collective-permute-start(f32[128,256]{1,0:T(8,128)S(1)} %slice_select_fusion), channel_id=1, source_target_pairs={{16,0},{18,2},{17,1},{19,3}} | collective-permute-start | bytes 393224 | tf_op jit(solution)/shard_map/ppermute | solution.py:80
  13.1 9.9 %collective-permute-start.5 = (f32[128,256]{1,0:T(8,128)S(1)}, f32[128,256]{1,0:T(8,128)S(1)}, u32[]{:S(2)}, u32[]{:S(2)}) collective-permute-start(f32[128,256]{1,0:T(8,128)S(1)} %slice_select_fusion), channel_id=1, source_target_pairs={{8,0},{10,2},{24,16},{26,18},{9,1},{11,3},{25,17},{27,19}} | collective-permute-start | bytes 393224 | tf_op jit(solution)/shard_map/ppermute | solution.py:80
  16.9 6.8 %collective-permute-start.4 = (f32[128,256]{1,0:T(8,128)S(1)}, f32[128,256]{1,0:T(8,128)S(1)}, u32[]{:S(2)}, u32[]{:S(2)}) collective-permute-start(f32[128,256]{1,0:T(8,128)S(1)} %slice_select_fusion), channel_id=1, source_target_pairs={{4,0},{6,2},{12,8},{14,10},{20,16},{22,18},{28,24},{30,26},{5,1},{... | collective-permute-start | bytes 393224 | tf_op jit(solution)/shard_map/ppermute | solution.py:80
  18.8 8.4 %collective-permute-start.11 = (f32[3,256,256]{2,1,0:T(8,128)S(1)}, f32[3,256,256]{2,1,0:T(8,128)S(1)}, u32[]{:S(2)}, u32[]{:S(2)}) collective-permute-start(f32[3,256,256]{2,1,0:T(8,128)S(1)} %pad_maximum_fusion.1), channel_id=1, source_target_pairs={{0,2},{2,0},{4,6},{6,4},{8,10},{10,8},{12,14},{14,12},{16,18},{18,... | collective-permute-start | bytes 2359304 | tf_op jit(solution)/shard_map/ppermute | solution.py:67
  18.9 6.2 %copy-start = (f32[512,512]{1,0:T(8,128)S(1)}, f32[512,512]{1,0:T(8,128)}, u32[]{:S(2)}) copy-start(f32[512,512]{1,0:T(8,128)} %param.5) | copy-start | bytes 3145732
  20.3 3.6 %collective-permute-start.9 = (f32[128,256]{1,0:T(8,128)S(1)}, f32[128,256]{1,0:T(8,128)S(1)}, u32[]{:S(2)}, u32[]{:S(2)}) collective-permute-start(f32[128,256]{1,0:T(8,128)S(1)} %collective-permute-done.6), channel_id=1, source_target_pairs={{0,2},{2,0},{4,6},{6,4},{8,10},{10,8},{12,14},{14,12},{16,18},{18,... | collective-permute-start | bytes 393224 | tf_op jit(solution)/shard_map/ppermute | solution.py:82
  23.0 1.3 %collective-permute-start.8 = (f32[128,256]{1,0:T(8,128)S(1)}, f32[128,256]{1,0:T(8,128)S(1)}, u32[]{:S(2)}, u32[]{:S(2)}) collective-permute-start(f32[128,256]{1,0:T(8,128)S(1)} %collective-permute-done.5), channel_id=1, source_target_pairs={{0,2},{2,0},{4,6},{6,4},{8,10},{10,8},{12,14},{14,12},{16,18},{18,... | collective-permute-start | bytes 393224 | tf_op jit(solution)/shard_map/ppermute | solution.py:82
  23.8 1.3 %collective-permute-start.7 = (f32[128,256]{1,0:T(8,128)S(1)}, f32[128,256]{1,0:T(8,128)S(1)}, u32[]{:S(2)}, u32[]{:S(2)}) collective-permute-start(f32[128,256]{1,0:T(8,128)S(1)} %collective-permute-done.4), channel_id=1, source_target_pairs={{0,2},{2,0},{4,6},{6,4},{8,10},{10,8},{12,14},{14,12},{16,18},{18,... | collective-permute-start | bytes 393224 | tf_op jit(solution)/shard_map/ppermute | solution.py:82
  27.0 1.6 %collective-permute-start.12 = (f32[256,256]{1,0:T(8,128)S(1)}, f32[256,256]{1,0:T(8,128)S(1)}, u32[]{:S(2)}, u32[]{:S(2)}) collective-permute-start(f32[256,256]{1,0:T(8,128)S(1)} %constant_dynamic-slice_fusion), channel_id=1, source_target_pairs={{0,2},{2,0},{4,6},{6,4},{8,10},{10,8},{12,14},{14,12},{16,18},{18,... | collective-permute-start | bytes 786440 | tf_op jit(solution)/shard_map/ppermute | solution.py:93
  29.4 8.4 %collective-permute-start.13 = (f32[256,256]{1,0:T(8,128)S(1)}, f32[256,256]{1,0:T(8,128)S(1)}, u32[]{:S(2)}, u32[]{:S(2)}) collective-permute-start(f32[256,256]{1,0:T(8,128)S(1)} %get-tuple-element.61), channel_id=1, source_target_pairs={{0,4},{4,0},{2,6},{6,2},{8,12},{12,8},{10,14},{14,10},{16,20},{20,... | collective-permute-start | bytes 786440 | tf_op jit(solution)/shard_map/ppermute | solution.py:114
  38.7 9.4 %collective-permute-start.14 = (f32[256,256]{1,0:T(8,128)S(1)}, f32[256,256]{1,0:T(8,128)S(1)}, u32[]{:S(2)}, u32[]{:S(2)}) collective-permute-start(f32[256,256]{1,0:T(8,128)S(1)} %get-tuple-element.63), channel_id=1, source_target_pairs={{0,8},{8,0},{2,10},{10,2},{16,24},{24,16},{18,26},{26,18},{1,9},{9... | collective-permute-start | bytes 786440 | tf_op jit(solution)/shard_map/ppermute | solution.py:114
  49.0 9.4 %collective-permute-start.15 = (f32[256,256]{1,0:T(8,128)S(1)}, f32[256,256]{1,0:T(8,128)S(1)}, u32[]{:S(2)}, u32[]{:S(2)}) collective-permute-start(f32[256,256]{1,0:T(8,128)S(1)} %get-tuple-element.65), channel_id=1, source_target_pairs={{0,16},{16,0},{2,18},{18,2},{1,17},{17,1},{3,19},{19,3}} | collective-permute-start | bytes 786440 | tf_op jit(solution)/shard_map/ppermute | solution.py:114
  59.3 1.6 %collective-permute-start.16 = (f32[256,256]{1,0:T(8,128)S(1)}, f32[256,256]{1,0:T(8,128)S(1)}, u32[]{:S(2)}, u32[]{:S(2)}) collective-permute-start(f32[256,256]{1,0:T(8,128)S(1)} %get-tuple-element.67), channel_id=1, source_target_pairs={{0,2},{2,0},{4,6},{6,4},{8,10},{10,8},{12,14},{14,12},{16,18},{18,... | collective-permute-start | bytes 786440 | tf_op jit(solution)/shard_map/ppermute | solution.py:128

commit v26 on v24

--- a/solution.py
+++ b/solution.py
@@ -83,8 +83,8 @@
     leaf_vectors = unit_lower(leaf_full)
     leaf_factor = jnp.triu(leaf_tri)
     leaf_w = product_left_t(leaf_factor, product_left_t(leaf_vectors, slab))
-    leafed = slab - product(leaf_vectors, leaf_w)
-    current = leafed[:width]
+    current = slab[:width] - product(leaf_vectors[:width], leaf_w)
+    remainder = slab[width:] - product(leaf_vectors[width:], leaf_w)
 
     is_lower = core == 0
     recv_h = lax.ppermute(lax.dynamic_slice(current, (0, (1 - core) * half), (width, half)), "row", swap)
@@ -124,7 +124,7 @@
     give = jnp.where(core == 0, level0_out, base_out)
     got = lax.ppermute(give, "row", swap)
     top = jnp.concatenate([jnp.where(core == 0, keep, got), jnp.where(core == 0, got, keep)], axis=1)
-    return jnp.concatenate([top, leafed[width:]], axis=0)
+    return jnp.concatenate([top, remainder], axis=0)
 
 
 def solution(mesh):

time: 61.5 us -> 61.3 us (level)
    dot_general x6 -> x7, matrix products: 2.07 us -> 2.25 us  [product(): jnp.dot(left, right, precision=lax.Precision.HIGH, preferred_element_type...]
  transfers between devices with their start and end apart: 17 -> 17, of which waited for: 10 -> 10; matrix products, arithmetic and copies ran while one was open for 13% -> 14% of each run, Pallas kernels for 0% -> 0%
where the time goes in v26:
time: 61.3 us; the launch traced here: 61 us
  waiting for transfers between devices  29.6 us (48%)
  starting transfers between devices  19.6 us (32%)
  matrix products  8.39 us (14%)
  other arithmetic  1.99 us (3%)
  local copies, waits for them, and re-layouts  0.92 us (2%)
    ppermute x3, waiting for transfers between devices, on_device(): received = lax.ppermute(jnp.where(is_upper, q, chain), 'row', pairs)  16.9 us
    ppermute x4, waiting for transfers between devices, col_gather(): by_shift.append(lax.ppermute(part, 'col', perm))  8.15 us
    ppermute x3, starting transfers between devices, on_device(): received = lax.ppermute(jnp.where(is_upper, q, chain), 'row', pairs)  7.73 us
    ppermute x4, starting transfers between devices, col_gather(): by_shift.append(lax.ppermute(part, 'col', perm))  6.73 us
    dot_general x16, matrix products, product_left_t(): lax.dot_general(left, right, (((0,), (0,)), ((), ())), precision=lax.Prec...  6.15 us
    ppermute x3, starting transfers between devices, on_device(): partner_factors.append(lax.ppermute(half_s, 'row', pairs))  3.86 us
    ppermute x3, waiting for transfers between devices, on_device(): partner_factors.append(lax.ppermute(half_s, 'row', pairs))  2.91 us
    dot_general x7, matrix products, product(): jnp.dot(left, right, precision=lax.Precision.HIGH, preferred_element_type...  2.25 us
  transfers between devices with their start and end apart: 17, of which 10 were waited for; matrix products, arithmetic and copies ran while one was open for 14% of the time, Pallas kernels for 0%

profile of v26, /device:TPU:0, one launch (start us, length us, event | category | flops | bytes accessed | tf_op | source)
XLA Modules:
  0.0 61.0 jit_solution(11586142906409857154)
XLA Ops:
  0.0 3.0 %collective-permute-start = (f32[256,128]{1,0:T(8,128)}, f32[256,128]{1,0:T(8,128)S(1)}, u32[]{:S(2)}, u32[]{:S(2)}) collective-permute-start(f32[256,128]{1,0:T(8,128)} %param.9), channel_id=1, source_target_pairs={{0,1},{1,0},{2,3},{3,2},{4,5},{5,4},{6,7},{7,6},{8,9},{9,8},{10,11... | collective-permute-start | bytes 393224 | tf_op jit(solution)/shard_map/ppermute | solution.py:34
  3.0 3.8 %collective-permute-done = f32[256,128]{1,0:T(8,128)S(1)} collective-permute-done((f32[256,128]{1,0:T(8,128)}, f32[256,128]{1,0:T(8,128)S(1)}, u32[]{:S(2)}, u32[]{:S(2)}) %collective-permute-start) | collective-permute-done | bytes 131104 | tf_op jit(solution)/shard_map/ppermute | solution.py:34
  6.8 0.9 %copy-done.4 = f32[256,128]{1,0:T(8,128)S(1)} copy-done((f32[256,128]{1,0:T(8,128)S(1)}, f32[256,128]{1,0:T(8,128)}, u32[]{:S(2)}) %copy-start.4) | copy-done | bytes 131096
  7.7 1.7 %collective-permute-start.2 = (f32[256,128]{1,0:T(8,128)S(1)}, f32[256,128]{1,0:T(8,128)S(1)}, u32[]{:S(2)}, u32[]{:S(2)}) collective-permute-start(f32[256,128]{1,0:T(8,128)S(1)} %copy-done.4), channel_id=1, source_target_pairs={{0,1},{1,0},{2,3},{3,2},{4,5},{5,4},{6,7},{7,6},{8,9},{9,8},{10,11... | collective-permute-start | bytes 393224 | tf_op jit(solution)/shard_map/ppermute | solution.py:34
  9.9 1.7 %collective-permute-start.1 = (f32[512,128]{1,0:T(8,128)S(1)}, f32[512,128]{1,0:T(8,128)S(1)}, u32[]{:S(2)}, u32[]{:S(2)}) collective-permute-start(f32[512,128]{1,0:T(8,128)S(1)} %copy-done.1), channel_id=1, source_target_pairs={{0,1},{1,0},{2,3},{3,2},{4,5},{5,4},{6,7},{7,6},{8,9},{9,8},{10,11... | collective-permute-start | bytes 786440 | tf_op jit(solution)/shard_map/ppermute | solution.py:34
  11.8 1.3 %collective-permute-start.6 = (f32[128,256]{1,0:T(8,128)S(1)}, f32[128,256]{1,0:T(8,128)S(1)}, u32[]{:S(2)}, u32[]{:S(2)}) collective-permute-start(f32[128,256]{1,0:T(8,128)S(1)} %slice_select_fusion), channel_id=1, source_target_pairs={{16,0},{18,2},{17,1},{19,3}} | collective-permute-start | bytes 393224 | tf_op jit(solution)/shard_map/ppermute | solution.py:80
  13.1 1.3 %collective-permute-start.5 = (f32[128,256]{1,0:T(8,128)S(1)}, f32[128,256]{1,0:T(8,128)S(1)}, u32[]{:S(2)}, u32[]{:S(2)}) collective-permute-start(f32[128,256]{1,0:T(8,128)S(1)} %slice_select_fusion), channel_id=1, source_target_pairs={{8,0},{10,2},{24,16},{26,18},{9,1},{11,3},{25,17},{27,19}} | collective-permute-start | bytes 393224 | tf_op jit(solution)/shard_map/ppermute | solution.py:80
  14.4 2.5 %collective-permute-done.7 = f32[256,128]{1,0:T(8,128)S(1)} collective-permute-done((f32[256,128]{1,0:T(8,128)S(1)}, f32[256,128]{1,0:T(8,128)S(1)}, u32[]{:S(2)}, u32[]{:S(2)}) %collective-permute-start.7) | collective-permute-done | bytes 131104 | tf_op jit(solution)/shard_map/ppermute | solution.py:34
  16.9 1.3 %collective-permute-start.4 = (f32[128,256]{1,0:T(8,128)S(1)}, f32[128,256]{1,0:T(8,128)S(1)}, u32[]{:S(2)}, u32[]{:S(2)}) collective-permute-start(f32[128,256]{1,0:T(8,128)S(1)} %slice_select_fusion), channel_id=1, source_target_pairs={{4,0},{6,2},{12,8},{14,10},{20,16},{22,18},{28,24},{30,26},{5,1},{... | collective-permute-start | bytes 393224 | tf_op jit(solution)/shard_map/ppermute | solution.py:80
  19.0 1.8 %collective-permute-done.1 = f32[512,128]{1,0:T(8,128)S(1)} collective-permute-done((f32[512,128]{1,0:T(8,128)S(1)}, f32[512,128]{1,0:T(8,128)S(1)}, u32[]{:S(2)}, u32[]{:S(2)}) %collective-permute-start.1) | collective-permute-done | bytes 262176 | tf_op jit(solution)/shard_map/ppermute | solution.py:34
  20.9 2.1 %collective-permute-done.5 = f32[128,256]{1,0:T(8,128)S(1)} collective-permute-done((f32[128,256]{1,0:T(8,128)S(1)}, f32[128,256]{1,0:T(8,128)S(1)}, u32[]{:S(2)}, u32[]{:S(2)}) %collective-permute-start.5) | collective-permute-done | bytes 131104 | tf_op jit(solution)/shard_map/ppermute | solution.py:80
  23.0 0.8 %collective-permute-done.4 = f32[128,256]{1,0:T(8,128)S(1)} collective-permute-done((f32[128,256]{1,0:T(8,128)S(1)}, f32[128,256]{1,0:T(8,128)S(1)}, u32[]{:S(2)}, u32[]{:S(2)}) %collective-permute-start.4) | collective-permute-done | bytes 131104 | tf_op jit(solution)/shard_map/ppermute | solution.py:80
  23.8 0.5 collective-permute-start.12
  24.3 0.6 %fusion.101 = f32[256,512]{1,0:T(8,128)S(1)} fusion(f32[512,512]{1,0:T(8,128)S(1)} %copy-done, f32[512,256]{1,0:T(8,128)S(1)} %pad_maximum_fusion.2), kind=kOutput, calls=%fused_computation.151 | convolution fusion | flops 403308544 | bytes 2097152 | tf_op jit(solution)/shard_map/dot_general | solution.py:12
  25.0 0.5 fusion.23
  25.9 0.6 collective-permute-start.9
  26.7 0.4 fusion.16
  27.1 0.6 collective-permute-done.9
  27.7 0.4 select_subtract_fusion.1
  28.1 0.4 broadcast_select_fusion.4
  29.2 7.9 %collective-permute-done.11 = f32[256,256]{1,0:T(8,128)S(1)} collective-permute-done((f32[256,256]{1,0:T(8,128)S(1)}, f32[256,256]{1,0:T(8,128)S(1)}, u32[]{:S(2)}, u32[]{:S(2)}) %collective-permute-start.11) | collective-permute-done | bytes 262176 | tf_op jit(solution)/shard_map/ppermute | solution.py:111
  37.2 0.4 broadcast_select_fusion.3
  37.6 3.3 %collective-permute-start.13 = (f32[256,256]{1,0:T(8,128)S(1)}, f32[256,256]{1,0:T(8,128)S(1)}, u32[]{:S(2)}, u32[]{:S(2)}) collective-permute-start(f32[256,256]{1,0:T(8,128)S(1)} %get-tuple-element.55), channel_id=1, source_target_pairs={{0,8},{8,0},{2,10},{10,2},{16,24},{24,16},{18,26},{26,18},{1,9},{9... | collective-permute-start | bytes 786440 | tf_op jit(solution)/shard_map/ppermute | solution.py:111
  40.9 0.4 convolution_add_fusion
  42.2 5.0 %collective-permute-done.13 = f32[256,256]{1,0:T(8,128)S(1)} collective-permute-done((f32[256,256]{1,0:T(8,128)S(1)}, f32[256,256]{1,0:T(8,128)S(1)}, u32[]{:S(2)}, u32[]{:S(2)}) %collective-permute-start.13) | collective-permute-done | bytes 262176 | tf_op jit(solution)/shard_map/ppermute | solution.py:111
  47.3 0.4 broadcast_select_fusion.2
  47.7 4.3 %collective-permute-start.15 = (f32[256,256]{1,0:T(8,128)S(1)}, f32[256,256]{1,0:T(8,128)S(1)}, u32[]{:S(2)}, u32[]{:S(2)}) collective-permute-start(f32[256,256]{1,0:T(8,128)S(1)} %get-tuple-element.57), channel_id=1, source_target_pairs={{0,16},{16,0},{2,18},{18,2},{1,17},{17,1},{3,19},{19,3}} | collective-permute-start | bytes 786440 | tf_op jit(solution)/shard_map/ppermute | solution.py:111
  52.0 0.4 convolution_add_fusion.1
  53.4 4.0 %collective-permute-done.15 = f32[256,256]{1,0:T(8,128)S(1)} collective-permute-done((f32[256,256]{1,0:T(8,128)S(1)}, f32[256,256]{1,0:T(8,128)S(1)}, u32[]{:S(2)}, u32[]{:S(2)}) %collective-permute-start.15) | collective-permute-done | bytes 262176 | tf_op jit(solution)/shard_map/ppermute | solution.py:111
  57.3 0.4 convolution_add_fusion.2
  58.8 1.1 %collective-permute-done.16 = f32[256,256]{1,0:T(8,128)S(1)} collective-permute-done((f32[256,256]{1,0:T(8,128)S(1)}, f32[256,256]{1,0:T(8,128)S(1)}, u32[]{:S(2)}, u32[]{:S(2)}) %collective-permute-start.16) | collective-permute-done | bytes 262176 | tf_op jit(solution)/shard_map/ppermute | solution.py:125
  60.0 1.1 %pad_maximum_fusion = f32[512,512]{1,0:T(8,128)} fusion(f32[256,512]{1,0:T(8,128)S(1)} %convolution_subtract_fusion, f32[256,256]{1,0:T(8,128)S(1)} %get-tuple-element.42, f32[256,256]{1,0:T(8,128)S(1)} %get-tuple-element.41), kind=kLoop, calls=%fused_computation.15 | loop fusion | flops 524288 | bytes 2097152 | tf_op jit(solution)/shard_map/concatenate | solution.py:127
  (56 shorter events, 5.8 us)
Async XLA Ops:
  0.0 6.7 %copy-start.2 = (f32[256,128]{1,0:T(8,128)S(1)}, f32[256,128]{1,0:T(8,128)}, u32[]{:S(2)}) copy-start(f32[256,128]{1,0:T(8,128)} %param.9) | copy-start | bytes 393220
  0.0 6.7 %collective-permute-start = (f32[256,128]{1,0:T(8,128)}, f32[256,128]{1,0:T(8,128)S(1)}, u32[]{:S(2)}, u32[]{:S(2)}) collective-permute-start(f32[256,128]{1,0:T(8,128)} %param.9), channel_id=1, source_target_pairs={{0,1},{1,0},{2,3},{3,2},{4,5},{5,4},{6,7},{7,6},{8,9},{9,8},{10,11... | collective-permute-start | bytes 393224 | tf_op jit(solution)/shard_map/ppermute | solution.py:34
  6.8 0.9 %copy-start.4 = (f32[256,128]{1,0:T(8,128)S(1)}, f32[256,128]{1,0:T(8,128)}, u32[]{:S(2)}) copy-start(f32[256,128]{1,0:T(8,128)} %param.7) | copy-start | bytes 393220
  6.8 2.6 %copy-start.3 = (f32[256,128]{1,0:T(8,128)S(1)}, f32[256,128]{1,0:T(8,128)}, u32[]{:S(2)}) copy-start(f32[256,128]{1,0:T(8,128)} %param.8) | copy-start | bytes 393220
  7.7 2.3 %copy-start.1 = (f32[512,128]{1,0:T(8,128)S(1)}, f32[512,128]{1,0:T(8,128)}, u32[]{:S(2)}) copy-start(f32[512,128]{1,0:T(8,128)} %param.6) | copy-start | bytes 786436
  7.7 11.1 %collective-permute-start.2 = (f32[256,128]{1,0:T(8,128)S(1)}, f32[256,128]{1,0:T(8,128)S(1)}, u32[]{:S(2)}, u32[]{:S(2)}) collective-permute-start(f32[256,128]{1,0:T(8,128)S(1)} %copy-done.4), channel_id=1, source_target_pairs={{0,1},{1,0},{2,3},{3,2},{4,5},{5,4},{6,7},{7,6},{8,9},{9,8},{10,11... | collective-permute-start | bytes 393224 | tf_op jit(solution)/shard_map/ppermute | solution.py:34
  9.4 7.6 %collective-permute-start.7 = (f32[256,128]{1,0:T(8,128)S(1)}, f32[256,128]{1,0:T(8,128)S(1)}, u32[]{:S(2)}, u32[]{:S(2)}) collective-permute-start(f32[256,128]{1,0:T(8,128)S(1)} %copy-done.3), channel_id=1, source_target_pairs={{0,1},{1,0},{2,3},{3,2},{4,5},{5,4},{6,7},{7,6},{8,9},{9,8},{10,11... | collective-permute-start | bytes 393224 | tf_op jit(solution)/shard_map/ppermute | solution.py:34
  9.8 1.9 %collective-permute-start.3 = (f32[128,256]{1,0:T(8,128)S(1)}, f32[128,256]{1,0:T(8,128)S(1)}, u32[]{:S(2)}, u32[]{:S(2)}) collective-permute-start(f32[128,256]{1,0:T(8,128)S(1)} %slice.81), channel_id=1, source_target_pairs={{0,2},{2,0},{4,6},{6,4},{8,10},{10,8},{12,14},{14,12},{16,18},{18,... | collective-permute-start | bytes 393224 | tf_op jit(solution)/shard_map/ppermute | solution.py:72
  9.9 10.9 %collective-permute-start.1 = (f32[512,128]{1,0:T(8,128)S(1)}, f32[512,128]{1,0:T(8,128)S(1)}, u32[]{:S(2)}, u32[]{:S(2)}) collective-permute-start(f32[512,128]{1,0:T(8,128)S(1)} %copy-done.1), channel_id=1, source_target_pairs={{0,1},{1,0},{2,3},{3,2},{4,5},{5,4},{6,7},{7,6},{8,9},{9,8},{10,11... | collective-permute-start | bytes 786440 | tf_op jit(solution)/shard_map/ppermute | solution.py:34
  11.8 9.1 %collective-permute-start.6 = (f32[128,256]{1,0:T(8,128)S(1)}, f32[128,256]{1,0:T(8,128)S(1)}, u32[]{:S(2)}, u32[]{:S(2)}) collective-permute-start(f32[128,256]{1,0:T(8,128)S(1)} %slice_select_fusion), channel_id=1, source_target_pairs={{16,0},{18,2},{17,1},{19,3}} | collective-permute-start | bytes 393224 | tf_op jit(solution)/shard_map/ppermute | solution.py:80
  13.1 9.9 %collective-permute-start.5 = (f32[128,256]{1,0:T(8,128)S(1)}, f32[128,256]{1,0:T(8,128)S(1)}, u32[]{:S(2)}, u32[]{:S(2)}) collective-permute-start(f32[128,256]{1,0:T(8,128)S(1)} %slice_select_fusion), channel_id=1, source_target_pairs={{8,0},{10,2},{24,16},{26,18},{9,1},{11,3},{25,17},{27,19}} | collective-permute-start | bytes 393224 | tf_op jit(solution)/shard_map/ppermute | solution.py:80
  16.9 6.8 %collective-permute-start.4 = (f32[128,256]{1,0:T(8,128)S(1)}, f32[128,256]{1,0:T(8,128)S(1)}, u32[]{:S(2)}, u32[]{:S(2)}) collective-permute-start(f32[128,256]{1,0:T(8,128)S(1)} %slice_select_fusion), channel_id=1, source_target_pairs={{4,0},{6,2},{12,8},{14,10},{20,16},{22,18},{28,24},{30,26},{5,1},{... | collective-permute-start | bytes 393224 | tf_op jit(solution)/shard_map/ppermute | solution.py:80
  18.8 7.7 %collective-permute-start.8 = (f32[3,256,256]{2,1,0:T(8,128)S(1)}, f32[3,256,256]{2,1,0:T(8,128)S(1)}, u32[]{:S(2)}, u32[]{:S(2)}) collective-permute-start(f32[3,256,256]{2,1,0:T(8,128)S(1)} %pad_maximum_fusion.1), channel_id=1, source_target_pairs={{0,2},{2,0},{4,6},{6,4},{8,10},{10,8},{12,14},{14,12},{16,18},{18,... | collective-permute-start | bytes 2359304 | tf_op jit(solution)/shard_map/ppermute | solution.py:67
  18.9 5.4 %copy-start = (f32[512,512]{1,0:T(8,128)S(1)}, f32[512,512]{1,0:T(8,128)}, u32[]{:S(2)}) copy-start(f32[512,512]{1,0:T(8,128)} %param.5) | copy-start | bytes 3145732
  23.8 4.7 %collective-permute-start.10 = (f32[128,256]{1,0:T(8,128)S(1)}, f32[128,256]{1,0:T(8,128)S(1)}, u32[]{:S(2)}, u32[]{:S(2)}) collective-permute-start(f32[128,256]{1,0:T(8,128)S(1)} %collective-permute-done.4), channel_id=1, source_target_pairs={{0,2},{2,0},{4,6},{6,4},{8,10},{10,8},{12,14},{14,12},{16,18},{18,... | collective-permute-start | bytes 393224 | tf_op jit(solution)/shard_map/ppermute | solution.py:113
  23.8 17.5 %collective-permute-start.12 = (f32[128,256]{1,0:T(8,128)S(1)}, f32[128,256]{1,0:T(8,128)S(1)}, u32[]{:S(2)}, u32[]{:S(2)}) collective-permute-start(f32[128,256]{1,0:T(8,128)S(1)} %collective-permute-done.5), channel_id=1, source_target_pairs={{0,2},{2,0},{4,6},{6,4},{8,10},{10,8},{12,14},{14,12},{16,18},{18,... | collective-permute-start | bytes 393224 | tf_op jit(solution)/shard_map/ppermute | solution.py:113
  24.3 28.1 %collective-permute-start.14 = (f32[128,256]{1,0:T(8,128)S(1)}, f32[128,256]{1,0:T(8,128)S(1)}, u32[]{:S(2)}, u32[]{:S(2)}) collective-permute-start(f32[128,256]{1,0:T(8,128)S(1)} %collective-permute-done.6), channel_id=1, source_target_pairs={{0,2},{2,0},{4,6},{6,4},{8,10},{10,8},{12,14},{14,12},{16,18},{18,... | collective-permute-start | bytes 393224 | tf_op jit(solution)/shard_map/ppermute | solution.py:113
  25.9 1.7 %collective-permute-start.9 = (f32[256,256]{1,0:T(8,128)S(1)}, f32[256,256]{1,0:T(8,128)S(1)}, u32[]{:S(2)}, u32[]{:S(2)}) collective-permute-start(f32[256,256]{1,0:T(8,128)S(1)} %constant_dynamic-slice_fusion), channel_id=1, source_target_pairs={{0,2},{2,0},{4,6},{6,4},{8,10},{10,8},{12,14},{14,12},{16,18},{18,... | collective-permute-start | bytes 786440 | tf_op jit(solution)/shard_map/ppermute | solution.py:90
  28.5 8.7 %collective-permute-start.11 = (f32[256,256]{1,0:T(8,128)S(1)}, f32[256,256]{1,0:T(8,128)S(1)}, u32[]{:S(2)}, u32[]{:S(2)}) collective-permute-start(f32[256,256]{1,0:T(8,128)S(1)} %get-tuple-element.53), channel_id=1, source_target_pairs={{0,4},{4,0},{2,6},{6,2},{8,12},{12,8},{10,14},{14,10},{16,20},{20,... | collective-permute-start | bytes 786440 | tf_op jit(solution)/shard_map/ppermute | solution.py:111
  37.6 9.7 %collective-permute-start.13 = (f32[256,256]{1,0:T(8,128)S(1)}, f32[256,256]{1,0:T(8,128)S(1)}, u32[]{:S(2)}, u32[]{:S(2)}) collective-permute-start(f32[256,256]{1,0:T(8,128)S(1)} %get-tuple-element.55), channel_id=1, source_target_pairs={{0,8},{8,0},{2,10},{10,2},{16,24},{24,16},{18,26},{26,18},{1,9},{9... | collective-permute-start | bytes 786440 | tf_op jit(solution)/shard_map/ppermute | solution.py:111
  47.7 9.6 %collective-permute-start.15 = (f32[256,256]{1,0:T(8,128)S(1)}, f32[256,256]{1,0:T(8,128)S(1)}, u32[]{:S(2)}, u32[]{:S(2)}) collective-permute-start(f32[256,256]{1,0:T(8,128)S(1)} %get-tuple-element.57), channel_id=1, source_target_pairs={{0,16},{16,0},{2,18},{18,2},{1,17},{17,1},{3,19},{19,3}} | collective-permute-start | bytes 786440 | tf_op jit(solution)/shard_map/ppermute | solution.py:111
  58.3 1.6 %collective-permute-start.16 = (f32[256,256]{1,0:T(8,128)S(1)}, f32[256,256]{1,0:T(8,128)S(1)}, u32[]{:S(2)}, u32[]{:S(2)}) collective-permute-start(f32[256,256]{1,0:T(8,128)S(1)} %get-tuple-element.59), channel_id=1, source_target_pairs={{0,2},{2,0},{4,6},{6,4},{8,10},{10,8},{12,14},{14,12},{16,18},{18,... | collective-permute-start | bytes 786440 | tf_op jit(solution)/shard_map/ppermute | solution.py:125

commit v27 on v26

--- a/solution.py
+++ b/solution.py
@@ -49,10 +49,10 @@
     width = leaf_t.shape[0]
 
     tree_tri = col_gather(tree_t)
-    tree_tri, leaf_v, leaf_t, tree_v = lax.optimization_barrier((tree_tri, leaf_v, leaf_t, tree_v))
+    tree_full = col_gather(tree_v)
+    tree_tri, tree_full, leaf_v, leaf_t = lax.optimization_barrier((tree_tri, tree_full, leaf_v, leaf_t))
     leaf_full = col_gather(leaf_v)
     leaf_tri = col_gather(leaf_t)
-    tree_full = col_gather(tree_v)
 
     tree_vectors = jnp.triu(tree_full)
     tree_factor = jnp.triu(tree_tri)

time: 61.3 us -> 63.8 us (1.041)
  waiting for transfers between devices: 29.6 us -> 33.1 us
  starting transfers between devices: 19.6 us -> 18.3 us
  other arithmetic: 1.99 us -> 2.71 us
    ppermute x4, waiting for transfers between devices: 8.15 us -> 10.1 us  [col_gather(): by_shift.append(lax.ppermute(part, 'col', perm))]
    ppermute x4, starting transfers between devices: 6.73 us -> 5.09 us  [col_gather(): by_shift.append(lax.ppermute(part, 'col', perm))]
    select_n x4 -> x3, other arithmetic: 0.1 us -> 1 us  [col_gather(): first = jnp.where(me == 0, part, by_shift[1])]
  transfers between devices with their start and end apart: 17 -> 17, of which waited for: 10 -> 11; matrix products, arithmetic and copies ran while one was open for 14% -> 12% of each run, Pallas kernels for 0% -> 0%
where the time goes in v27:
time: 63.8 us; the launch traced here: 63.5 us
  waiting for transfers between devices  33.1 us (52%)
  starting transfers between devices  18.3 us (29%)
  matrix products  8.34 us (13%)
  other arithmetic  2.71 us (4%)
    ppermute x3, waiting for transfers between devices, on_device(): received = lax.ppermute(jnp.where(is_upper, q, chain), 'row', pairs)  17.2 us
    ppermute x4, waiting for transfers between devices, col_gather(): by_shift.append(lax.ppermute(part, 'col', perm))  10.1 us
    ppermute x3, starting transfers between devices, on_device(): received = lax.ppermute(jnp.where(is_upper, q, chain), 'row', pairs)  7.94 us
    dot_general x16, matrix products, product_left_t(): lax.dot_general(left, right, (((0,), (0,)), ((), ())), precision=lax.Prec...  6.14 us
    ppermute x4, starting transfers between devices, col_gather(): by_shift.append(lax.ppermute(part, 'col', perm))  5.09 us
    ppermute x3, starting transfers between devices, on_device(): partner_factors.append(lax.ppermute(half_s, 'row', pairs))  3.88 us
    ppermute x3, waiting for transfers between devices, on_device(): partner_factors.append(lax.ppermute(half_s, 'row', pairs))  3.52 us
    dot_general x7, matrix products, product(): jnp.dot(left, right, precision=lax.Precision.HIGH, preferred_element_type...  2.2 us
  transfers between devices with their start and end apart: 17, of which 11 were waited for; matrix products, arithmetic and copies ran while one was open for 12% of the time, Pallas kernels for 0%

profile of v27, /device:TPU:0, one launch (start us, length us, event | category | flops | bytes accessed | tf_op | source)
XLA Modules:
  0.0 63.5 jit_solution(10896670344300219424)
XLA Ops:
  0.0 3.0 %collective-permute-start.1 = (f32[256,128]{1,0:T(8,128)}, f32[256,128]{1,0:T(8,128)S(1)}, u32[]{:S(2)}, u32[]{:S(2)}) collective-permute-start(f32[256,128]{1,0:T(8,128)} %param.8), channel_id=1, source_target_pairs={{0,1},{1,0},{2,3},{3,2},{4,5},{5,4},{6,7},{7,6},{8,9},{9,8},{10,11... | collective-permute-start | bytes 393224 | tf_op jit(solution)/shard_map/ppermute | solution.py:34
  3.0 4.5 %collective-permute-done.1 = f32[256,128]{1,0:T(8,128)S(1)} collective-permute-done((f32[256,128]{1,0:T(8,128)}, f32[256,128]{1,0:T(8,128)S(1)}, u32[]{:S(2)}, u32[]{:S(2)}) %collective-permute-start.1) | collective-permute-done | bytes 131104 | tf_op jit(solution)/shard_map/ppermute | solution.py:34
  7.6 2.0 %collective-permute-done = f32[256,128]{1,0:T(8,128)S(1)} collective-permute-done((f32[256,128]{1,0:T(8,128)}, f32[256,128]{1,0:T(8,128)S(1)}, u32[]{:S(2)}, u32[]{:S(2)}) %collective-permute-start) | collective-permute-done | bytes 131104 | tf_op jit(solution)/shard_map/ppermute | solution.py:34
  9.6 0.9 %broadcast_select_fusion.14 = (f32[256,128]{1,0:T(8,128)S(1)}, f32[256,128]{1,0:T(8,128)S(1)}, f32[256,128]{1,0:T(8,128)S(1)}, f32[256,128]{1,0:T(8,128)S(1)}) fusion(f32[256,128]{1,0:T(8,128)S(1)} %copy-done.3, f32[256,128]{1,0:T(8,128)S(1)} %collective-permute-done.1, pred[]{:T(512)S(6)} %eq.62, f32[256,128]{1,0:T(8,128)S(1)} %collective-permute-done, ...), kind=kLoop, calls=%fused_computation.131 | loop fusion | flops 131072 | bytes 1048577 | tf_op jit(solution)/shard_map/jit(_where)/select_n | solution.py:36
  11.0 0.5 copy-done.2
  11.6 1.7 %collective-permute-start.3 = (f32[256,128]{1,0:T(8,128)S(1)}, f32[256,128]{1,0:T(8,128)S(1)}, u32[]{:S(2)}, u32[]{:S(2)}) collective-permute-start(f32[256,128]{1,0:T(8,128)S(1)} %copy-done.2), channel_id=1, source_target_pairs={{0,1},{1,0},{2,3},{3,2},{4,5},{5,4},{6,7},{7,6},{8,9},{9,8},{10,11... | collective-permute-start | bytes 393224 | tf_op jit(solution)/shard_map/ppermute | solution.py:34
  14.0 0.6 %collective-permute-done.4 = f32[128,256]{1,0:T(8,128)S(1)} collective-permute-done((f32[128,256]{1,0:T(8,128)S(1)}, f32[128,256]{1,0:T(8,128)S(1)}, u32[]{:S(2)}, u32[]{:S(2)}) %collective-permute-start.4) | collective-permute-done | bytes 131104 | tf_op jit(solution)/shard_map/ppermute | solution.py:72
  14.6 1.3 %collective-permute-start.7 = (f32[128,256]{1,0:T(8,128)S(1)}, f32[128,256]{1,0:T(8,128)S(1)}, u32[]{:S(2)}, u32[]{:S(2)}) collective-permute-start(f32[128,256]{1,0:T(8,128)S(1)} %slice_select_fusion), channel_id=1, source_target_pairs={{16,0},{18,2},{17,1},{19,3}} | collective-permute-start | bytes 393224 | tf_op jit(solution)/shard_map/ppermute | solution.py:80
  15.9 1.3 %collective-permute-start.6 = (f32[128,256]{1,0:T(8,128)S(1)}, f32[128,256]{1,0:T(8,128)S(1)}, u32[]{:S(2)}, u32[]{:S(2)}) collective-permute-start(f32[128,256]{1,0:T(8,128)S(1)} %slice_select_fusion), channel_id=1, source_target_pairs={{8,0},{10,2},{24,16},{26,18},{9,1},{11,3},{25,17},{27,19}} | collective-permute-start | bytes 393224 | tf_op jit(solution)/shard_map/ppermute | solution.py:80
  17.2 1.3 %collective-permute-start.5 = (f32[128,256]{1,0:T(8,128)S(1)}, f32[128,256]{1,0:T(8,128)S(1)}, u32[]{:S(2)}, u32[]{:S(2)}) collective-permute-start(f32[128,256]{1,0:T(8,128)S(1)} %slice_select_fusion), channel_id=1, source_target_pairs={{4,0},{6,2},{12,8},{14,10},{20,16},{22,18},{28,24},{30,26},{5,1},{... | collective-permute-start | bytes 393224 | tf_op jit(solution)/shard_map/ppermute | solution.py:80
  18.6 3.6 %collective-permute-done.2 = f32[512,128]{1,0:T(8,128)S(1)} collective-permute-done((f32[512,128]{1,0:T(8,128)S(1)}, f32[512,128]{1,0:T(8,128)S(1)}, u32[]{:S(2)}, u32[]{:S(2)}) %collective-permute-start.2) | collective-permute-done | bytes 262176 | tf_op jit(solution)/shard_map/ppermute | solution.py:34
  22.2 0.8 %collective-permute-done.7 = f32[128,256]{1,0:T(8,128)S(1)} collective-permute-done((f32[128,256]{1,0:T(8,128)S(1)}, f32[128,256]{1,0:T(8,128)S(1)}, u32[]{:S(2)}, u32[]{:S(2)}) %collective-permute-start.7) | collective-permute-done | bytes 131104 | tf_op jit(solution)/shard_map/ppermute | solution.py:80
  23.1 2.7 %collective-permute-done.6 = f32[128,256]{1,0:T(8,128)S(1)} collective-permute-done((f32[128,256]{1,0:T(8,128)S(1)}, f32[128,256]{1,0:T(8,128)S(1)}, u32[]{:S(2)}, u32[]{:S(2)}) %collective-permute-start.6) | collective-permute-done | bytes 131104 | tf_op jit(solution)/shard_map/ppermute | solution.py:80
  25.8 0.5 collective-permute-start.12
  26.3 0.6 fusion.101
  27.0 0.5 fusion.21
  27.9 0.5 collective-permute-start.9
  28.7 0.4 fusion.14
  29.1 0.6 collective-permute-done.9
  29.6 0.4 select_subtract_fusion.1
  30.0 0.4 broadcast_select_fusion.4
  31.2 7.9 %collective-permute-done.11 = f32[256,256]{1,0:T(8,128)S(1)} collective-permute-done((f32[256,256]{1,0:T(8,128)S(1)}, f32[256,256]{1,0:T(8,128)S(1)}, u32[]{:S(2)}, u32[]{:S(2)}) %collective-permute-start.11) | collective-permute-done | bytes 262176 | tf_op jit(solution)/shard_map/ppermute | solution.py:111
  39.2 0.4 broadcast_select_fusion.3
  39.6 3.2 %collective-permute-start.13 = (f32[256,256]{1,0:T(8,128)S(1)}, f32[256,256]{1,0:T(8,128)S(1)}, u32[]{:S(2)}, u32[]{:S(2)}) collective-permute-start(f32[256,256]{1,0:T(8,128)S(1)} %get-tuple-element.57), channel_id=1, source_target_pairs={{0,8},{8,0},{2,10},{10,2},{16,24},{24,16},{18,26},{26,18},{1,9},{9... | collective-permute-start | bytes 786440 | tf_op jit(solution)/shard_map/ppermute | solution.py:111
  42.7 0.4 convolution_add_fusion
  44.1 5.2 %collective-permute-done.13 = f32[256,256]{1,0:T(8,128)S(1)} collective-permute-done((f32[256,256]{1,0:T(8,128)S(1)}, f32[256,256]{1,0:T(8,128)S(1)}, u32[]{:S(2)}, u32[]{:S(2)}) %collective-permute-start.13) | collective-permute-done | bytes 262176 | tf_op jit(solution)/shard_map/ppermute | solution.py:111
  49.7 4.7 %collective-permute-start.15 = (f32[256,256]{1,0:T(8,128)S(1)}, f32[256,256]{1,0:T(8,128)S(1)}, u32[]{:S(2)}, u32[]{:S(2)}) collective-permute-start(f32[256,256]{1,0:T(8,128)S(1)} %get-tuple-element.59), channel_id=1, source_target_pairs={{0,16},{16,0},{2,18},{18,2},{1,17},{17,1},{3,19},{19,3}} | collective-permute-start | bytes 786440 | tf_op jit(solution)/shard_map/ppermute | solution.py:111
  54.4 0.4 convolution_add_fusion.1
  55.7 4.1 %collective-permute-done.15 = f32[256,256]{1,0:T(8,128)S(1)} collective-permute-done((f32[256,256]{1,0:T(8,128)S(1)}, f32[256,256]{1,0:T(8,128)S(1)}, u32[]{:S(2)}, u32[]{:S(2)}) %collective-permute-start.15) | collective-permute-done | bytes 262176 | tf_op jit(solution)/shard_map/ppermute | solution.py:111
  59.8 0.4 convolution_add_fusion.2
  61.3 1.1 %collective-permute-done.16 = f32[256,256]{1,0:T(8,128)S(1)} collective-permute-done((f32[256,256]{1,0:T(8,128)S(1)}, f32[256,256]{1,0:T(8,128)S(1)}, u32[]{:S(2)}, u32[]{:S(2)}) %collective-permute-start.16) | collective-permute-done | bytes 262176 | tf_op jit(solution)/shard_map/ppermute | solution.py:125
  62.4 1.1 %pad_maximum_fusion = f32[512,512]{1,0:T(8,128)} fusion(f32[256,512]{1,0:T(8,128)S(1)} %convolution_subtract_fusion, f32[256,256]{1,0:T(8,128)S(1)} %get-tuple-element.42, f32[256,256]{1,0:T(8,128)S(1)} %get-tuple-element.41), kind=kLoop, calls=%fused_computation.15 | loop fusion | flops 524288 | bytes 2097152 | tf_op jit(solution)/shard_map/concatenate | solution.py:127
  (52 shorter events, 6.2 us)
Async XLA Ops:
  0.0 9.6 %copy-start.3 = (f32[256,128]{1,0:T(8,128)S(1)}, f32[256,128]{1,0:T(8,128)}, u32[]{:S(2)}) copy-start(f32[256,128]{1,0:T(8,128)} %param.8) | copy-start | bytes 393220
  0.0 7.6 %collective-permute-start.1 = (f32[256,128]{1,0:T(8,128)}, f32[256,128]{1,0:T(8,128)S(1)}, u32[]{:S(2)}, u32[]{:S(2)}) collective-permute-start(f32[256,128]{1,0:T(8,128)} %param.8), channel_id=1, source_target_pairs={{0,1},{1,0},{2,3},{3,2},{4,5},{5,4},{6,7},{7,6},{8,9},{9,8},{10,11... | collective-permute-start | bytes 393224 | tf_op jit(solution)/shard_map/ppermute | solution.py:34
  3.0 6.6 %collective-permute-start = (f32[256,128]{1,0:T(8,128)}, f32[256,128]{1,0:T(8,128)S(1)}, u32[]{:S(2)}, u32[]{:S(2)}) collective-permute-start(f32[256,128]{1,0:T(8,128)} %param.9), channel_id=1, source_target_pairs={{0,1},{1,0},{2,3},{3,2},{4,5},{5,4},{6,7},{7,6},{8,9},{9,8},{10,11... | collective-permute-start | bytes 393224 | tf_op jit(solution)/shard_map/ppermute | solution.py:34
  10.7 0.9 %copy-start.2 = (f32[256,128]{1,0:T(8,128)S(1)}, f32[256,128]{1,0:T(8,128)}, u32[]{:S(2)}) copy-start(f32[256,128]{1,0:T(8,128)} %param.7) | copy-start | bytes 393220
  11.0 2.3 %copy-start.1 = (f32[512,128]{1,0:T(8,128)S(1)}, f32[512,128]{1,0:T(8,128)}, u32[]{:S(2)}) copy-start(f32[512,128]{1,0:T(8,128)} %param.6) | copy-start | bytes 786436
  11.6 5.6 %collective-permute-start.3 = (f32[256,128]{1,0:T(8,128)S(1)}, f32[256,128]{1,0:T(8,128)S(1)}, u32[]{:S(2)}, u32[]{:S(2)}) collective-permute-start(f32[256,128]{1,0:T(8,128)S(1)} %copy-done.2), channel_id=1, source_target_pairs={{0,1},{1,0},{2,3},{3,2},{4,5},{5,4},{6,7},{7,6},{8,9},{9,8},{10,11... | collective-permute-start | bytes 393224 | tf_op jit(solution)/shard_map/ppermute | solution.py:34
  13.2 1.3 %collective-permute-start.4 = (f32[128,256]{1,0:T(8,128)S(1)}, f32[128,256]{1,0:T(8,128)S(1)}, u32[]{:S(2)}, u32[]{:S(2)}) collective-permute-start(f32[128,256]{1,0:T(8,128)S(1)} %slice.81), channel_id=1, source_target_pairs={{0,2},{2,0},{4,6},{6,4},{8,10},{10,8},{12,14},{14,12},{16,18},{18,... | collective-permute-start | bytes 393224 | tf_op jit(solution)/shard_map/ppermute | solution.py:72
  13.3 8.9 %collective-permute-start.2 = (f32[512,128]{1,0:T(8,128)S(1)}, f32[512,128]{1,0:T(8,128)S(1)}, u32[]{:S(2)}, u32[]{:S(2)}) collective-permute-start(f32[512,128]{1,0:T(8,128)S(1)} %copy-done.1), channel_id=1, source_target_pairs={{0,1},{1,0},{2,3},{3,2},{4,5},{5,4},{6,7},{7,6},{8,9},{9,8},{10,11... | collective-permute-start | bytes 786440 | tf_op jit(solution)/shard_map/ppermute | solution.py:34
  13.7 14.8 %collective-permute-start.8 = (f32[3,256,256]{2,1,0:T(8,128)S(1)}, f32[3,256,256]{2,1,0:T(8,128)S(1)}, u32[]{:S(2)}, u32[]{:S(2)}) collective-permute-start(f32[3,256,256]{2,1,0:T(8,128)S(1)} %pad_maximum_fusion.1), channel_id=1, source_target_pairs={{0,2},{2,0},{4,6},{6,4},{8,10},{10,8},{12,14},{14,12},{16,18},{18,... | collective-permute-start | bytes 2359304 | tf_op jit(solution)/shard_map/ppermute | solution.py:67
  14.6 8.4 %collective-permute-start.7 = (f32[128,256]{1,0:T(8,128)S(1)}, f32[128,256]{1,0:T(8,128)S(1)}, u32[]{:S(2)}, u32[]{:S(2)}) collective-permute-start(f32[128,256]{1,0:T(8,128)S(1)} %slice_select_fusion), channel_id=1, source_target_pairs={{16,0},{18,2},{17,1},{19,3}} | collective-permute-start | bytes 393224 | tf_op jit(solution)/shard_map/ppermute | solution.py:80
  15.9 9.9 %collective-permute-start.6 = (f32[128,256]{1,0:T(8,128)S(1)}, f32[128,256]{1,0:T(8,128)S(1)}, u32[]{:S(2)}, u32[]{:S(2)}) collective-permute-start(f32[128,256]{1,0:T(8,128)S(1)} %slice_select_fusion), channel_id=1, source_target_pairs={{8,0},{10,2},{24,16},{26,18},{9,1},{11,3},{25,17},{27,19}} | collective-permute-start | bytes 393224 | tf_op jit(solution)/shard_map/ppermute | solution.py:80
  17.2 8.5 %collective-permute-start.5 = (f32[128,256]{1,0:T(8,128)S(1)}, f32[128,256]{1,0:T(8,128)S(1)}, u32[]{:S(2)}, u32[]{:S(2)}) collective-permute-start(f32[128,256]{1,0:T(8,128)S(1)} %slice_select_fusion), channel_id=1, source_target_pairs={{4,0},{6,2},{12,8},{14,10},{20,16},{22,18},{28,24},{30,26},{5,1},{... | collective-permute-start | bytes 393224 | tf_op jit(solution)/shard_map/ppermute | solution.py:80
  18.6 7.7 %copy-start = (f32[512,512]{1,0:T(8,128)S(1)}, f32[512,512]{1,0:T(8,128)}, u32[]{:S(2)}) copy-start(f32[512,512]{1,0:T(8,128)} %param.5) | copy-start | bytes 3145732
  25.8 4.8 %collective-permute-start.10 = (f32[128,256]{1,0:T(8,128)S(1)}, f32[128,256]{1,0:T(8,128)S(1)}, u32[]{:S(2)}, u32[]{:S(2)}) collective-permute-start(f32[128,256]{1,0:T(8,128)S(1)} %collective-permute-done.5), channel_id=1, source_target_pairs={{0,2},{2,0},{4,6},{6,4},{8,10},{10,8},{12,14},{14,12},{16,18},{18,... | collective-permute-start | bytes 393224 | tf_op jit(solution)/shard_map/ppermute | solution.py:113
  25.8 17.3 %collective-permute-start.12 = (f32[128,256]{1,0:T(8,128)S(1)}, f32[128,256]{1,0:T(8,128)S(1)}, u32[]{:S(2)}, u32[]{:S(2)}) collective-permute-start(f32[128,256]{1,0:T(8,128)S(1)} %collective-permute-done.6), channel_id=1, source_target_pairs={{0,2},{2,0},{4,6},{6,4},{8,10},{10,8},{12,14},{14,12},{16,18},{18,... | collective-permute-start | bytes 393224 | tf_op jit(solution)/shard_map/ppermute | solution.py:113
  26.3 28.5 %collective-permute-start.14 = (f32[128,256]{1,0:T(8,128)S(1)}, f32[128,256]{1,0:T(8,128)S(1)}, u32[]{:S(2)}, u32[]{:S(2)}) collective-permute-start(f32[128,256]{1,0:T(8,128)S(1)} %collective-permute-done.7), channel_id=1, source_target_pairs={{0,2},{2,0},{4,6},{6,4},{8,10},{10,8},{12,14},{14,12},{16,18},{18,... | collective-permute-start | bytes 393224 | tf_op jit(solution)/shard_map/ppermute | solution.py:113
  27.9 1.7 %collective-permute-start.9 = (f32[256,256]{1,0:T(8,128)S(1)}, f32[256,256]{1,0:T(8,128)S(1)}, u32[]{:S(2)}, u32[]{:S(2)}) collective-permute-start(f32[256,256]{1,0:T(8,128)S(1)} %constant_dynamic-slice_fusion), channel_id=1, source_target_pairs={{0,2},{2,0},{4,6},{6,4},{8,10},{10,8},{12,14},{14,12},{16,18},{18,... | collective-permute-start | bytes 786440 | tf_op jit(solution)/shard_map/ppermute | solution.py:90
  30.4 8.7 %collective-permute-start.11 = (f32[256,256]{1,0:T(8,128)S(1)}, f32[256,256]{1,0:T(8,128)S(1)}, u32[]{:S(2)}, u32[]{:S(2)}) collective-permute-start(f32[256,256]{1,0:T(8,128)S(1)} %get-tuple-element.55), channel_id=1, source_target_pairs={{0,4},{4,0},{2,6},{6,2},{8,12},{12,8},{10,14},{14,10},{16,20},{20,... | collective-permute-start | bytes 786440 | tf_op jit(solution)/shard_map/ppermute | solution.py:111
  39.6 9.7 %collective-permute-start.13 = (f32[256,256]{1,0:T(8,128)S(1)}, f32[256,256]{1,0:T(8,128)S(1)}, u32[]{:S(2)}, u32[]{:S(2)}) collective-permute-start(f32[256,256]{1,0:T(8,128)S(1)} %get-tuple-element.57), channel_id=1, source_target_pairs={{0,8},{8,0},{2,10},{10,2},{16,24},{24,16},{18,26},{26,18},{1,9},{9... | collective-permute-start | bytes 786440 | tf_op jit(solution)/shard_map/ppermute | solution.py:111
  49.7 10.1 %collective-permute-start.15 = (f32[256,256]{1,0:T(8,128)S(1)}, f32[256,256]{1,0:T(8,128)S(1)}, u32[]{:S(2)}, u32[]{:S(2)}) collective-permute-start(f32[256,256]{1,0:T(8,128)S(1)} %get-tuple-element.59), channel_id=1, source_target_pairs={{0,16},{16,0},{2,18},{18,2},{1,17},{17,1},{3,19},{19,3}} | collective-permute-start | bytes 786440 | tf_op jit(solution)/shard_map/ppermute | solution.py:111
  60.8 1.6 %collective-permute-start.16 = (f32[256,256]{1,0:T(8,128)S(1)}, f32[256,256]{1,0:T(8,128)S(1)}, u32[]{:S(2)}, u32[]{:S(2)}) collective-permute-start(f32[256,256]{1,0:T(8,128)S(1)} %get-tuple-element.61), channel_id=1, source_target_pairs={{0,2},{2,0},{4,6},{6,4},{8,10},{10,8},{12,14},{14,12},{16,18},{18,... | collective-permute-start | bytes 786440 | tf_op jit(solution)/shard_map/ppermute | solution.py:125
